TPU v7x, 128 devices: a whole 4x4x4 slice. The times are simulated.
128 devices in a mesh: dp: 8 (over x, core), pair: 16 (over z, y).
Axes of the slice: x: 4, y: 4, z: 4, core: 2. Of those that a mesh axis runs over, the one named last changes fastest.
Arguments:
- anchor: bfloat16 [5, 4096, 1024], P(None, ('dp', 'pair')), may hold values from -20 to 20
- partner: bfloat16 [5, 4096, 1024], P(None, ('dp', 'pair')), may hold values from -12 to 12
- counts: int32 [5], replicated, may hold values from 512 to 4096, as said below
- pair_scale: float32 [5], replicated, may hold values from 2 to 8
Outputs:
- loss_value: float32 [], replicated
- grad_anchor: float32 [5, 4096, 1024], P(None, ('dp', 'pair'))
- grad_partner: float32 [5, 4096, 1024], P(None, ('dp', 'pair'))
Inputs may be any that keep to these rules, and one draw needn't show every extreme that they name: The valid samples of pair p are its rows 0 to counts[p] - 1; one pair has all 4096 rows valid.
All inputs are finite; a program needn't handle non-finite values.
Results may differ from a plain program's by a relative error of at most 0.0021.
Values may be sent and summed in bfloat16 or wider, within the bound.
No kernel may reach another device: no remote copies, remote signals or barrier semaphores. Data moves between devices by JAX's collectives and lax.ppermute only.
A program may use at most 128 MiB of HBM per device.

v0:
```python
import math

import jax
import jax.numpy as jnp
from jax import lax
from jax.sharding import PartitionSpec as P

NEG = -1e30


def joined(part, axis, combine):
    gathered = jax.tree.map(lambda a: lax.all_gather(a, axis), part)

    def take(source):
        return jax.tree.map(lambda a: lax.dynamic_index_in_dim(a, source, 0, False), gathered)

    return lax.fori_loop(
        1, lax.axis_size(axis), lambda source, state: combine(state, take(source)), take(0)
    )


def merge_stats(earlier, later):
    highest = jnp.maximum(earlier[0], later[0])
    summed = earlier[1] * jnp.exp(earlier[0] - highest) + later[1] * jnp.exp(later[0] - highest)
    return (highest, summed)


def block_scores(anchor_block, partner_rows, block_valid, col_valid, score_scale):
    scores = (
        jnp.einsum("rd,cd->rc", anchor_block, partner_rows, preferred_element_type=jnp.float32)
        * score_scale
    )
    inside = block_valid[:, None] & col_valid[None, :]
    return (scores, inside)


def local_stats(row_set, col_set, row_global, col_valid, counts, score_scale, tile_rows):
    pair_count = row_set.shape[0]
    total_rows = row_set.shape[1]
    block_count = total_rows // tile_rows
    col_width = col_set.shape[1]
    row_highs, row_sums, col_highs, col_sums = ([], [], [], [])
    for pair_number in range(pair_count):
        anchor_rows = row_set[pair_number]
        partner_rows = col_set[pair_number]
        valid_count = counts[pair_number]
        pair_cols = col_valid[pair_number]

        def local_visit_block(block_index, running):
            high_all, sum_all, col_high, col_sum = running
            start_row = block_index * tile_rows
            block_global = lax.dynamic_slice_in_dim(row_global, start_row, tile_rows, 0)

            def local_live_block(unused):
                anchor_block = lax.dynamic_slice_in_dim(anchor_rows, start_row, tile_rows, 0)
                scores, inside = block_scores(
                    anchor_block, partner_rows, block_global < valid_count, pair_cols, score_scale
                )
                masked = jnp.where(inside, scores, NEG)
                row_high = jnp.max(masked, axis=1)
                row_sum = jnp.sum(
                    jnp.where(inside, jnp.exp(masked - row_high[:, None]), 0.0), axis=1
                )
                block_high = jnp.max(masked, axis=0)
                block_sum = jnp.sum(
                    jnp.where(inside, jnp.exp(masked - block_high[None, :]), 0.0), axis=0
                )
                return (row_high, row_sum, block_high, block_sum)

            def local_empty_block(unused):
                return (
                    jnp.full((tile_rows,), NEG, jnp.float32),
                    jnp.zeros((tile_rows,), jnp.float32),
                    jnp.full((col_width,), NEG, jnp.float32),
                    jnp.zeros((col_width,), jnp.float32),
                )

            row_high, row_sum, block_high, block_sum = lax.cond(
                block_global[0] < valid_count, local_live_block, local_empty_block, 0
            )
            high_all = lax.dynamic_update_slice_in_dim(high_all, row_high, start_row, 0)
            sum_all = lax.dynamic_update_slice_in_dim(sum_all, row_sum, start_row, 0)
            col_high, col_sum = merge_stats((col_high, col_sum), (block_high, block_sum))
            return (high_all, sum_all, col_high, col_sum)

        initial = (
            jnp.full((total_rows,), NEG, jnp.float32),
            jnp.zeros((total_rows,), jnp.float32),
            jnp.full((col_width,), NEG, jnp.float32),
            jnp.zeros((col_width,), jnp.float32),
        )
        high_all, sum_all, col_high, col_sum = lax.fori_loop(
            0, block_count, local_visit_block, initial
        )
        row_highs.append(high_all)
        row_sums.append(sum_all)
        col_highs.append(col_high)
        col_sums.append(col_sum)
    return (jnp.stack(row_highs), jnp.stack(row_sums), jnp.stack(col_highs), jnp.stack(col_sums))


def pair_partials(
    anchor_rows,
    partner_rows,
    row_global,
    pair_cols,
    valid_count,
    row_lse,
    col_lse,
    scale_value,
    score_scale,
    tile_rows,
):
    total_rows = anchor_rows.shape[0]
    block_count = total_rows // tile_rows
    model_width = anchor_rows.shape[1]
    col_width = partner_rows.shape[0]

    def pair_visit_block(block_index, running):
        grad_rows, grad_cols = running
        start_row = block_index * tile_rows
        block_global = lax.dynamic_slice_in_dim(row_global, start_row, tile_rows, 0)

        def pair_live_block(unused):
            anchor_block = lax.dynamic_slice_in_dim(anchor_rows, start_row, tile_rows, 0)
            scores, inside = block_scores(
                anchor_block, partner_rows, block_global < valid_count, pair_cols, score_scale
            )
            block_lse = lax.dynamic_slice_in_dim(row_lse, start_row, tile_rows, 0)
            prob_row = jnp.where(inside, jnp.exp(scores - block_lse[:, None]), 0.0)
            prob_col = jnp.where(inside, jnp.exp(scores - col_lse[None, :]), 0.0)
            weights = (scale_value * 0.5 * (prob_row + prob_col)).astype(jnp.bfloat16)
            part_rows = (
                jnp.dot(weights, partner_rows, preferred_element_type=jnp.float32) * score_scale
            )
            part_cols = (
                jnp.einsum("rc,rd->cd", weights, anchor_block, preferred_element_type=jnp.float32)
                * score_scale
            )
            return (part_rows, part_cols)

        def pair_empty_block(unused):
            return (
                jnp.zeros((tile_rows, model_width), jnp.float32),
                jnp.zeros((col_width, model_width), jnp.float32),
            )

        part_rows, part_cols = lax.cond(
            block_global[0] < valid_count, pair_live_block, pair_empty_block, 0
        )
        grad_rows = lax.dynamic_update_slice_in_dim(grad_rows, part_rows, start_row, 0)
        return (grad_rows, grad_cols + part_cols)

    initial = (
        jnp.zeros((total_rows, model_width), jnp.float32),
        jnp.zeros((col_width, model_width), jnp.float32),
    )
    return lax.fori_loop(0, block_count, pair_visit_block, initial)


def per_device(anchor, partner, counts, pair_scale):
    pair_count, shard_rows, model_width = anchor.shape
    score_scale = 4.0 / math.sqrt(model_width)
    dp_size = lax.axis_size("dp")
    pair_size = lax.axis_size("pair")
    dp_index = lax.axis_index("dp")
    pair_place = lax.axis_index("pair")
    own_first = (dp_index * pair_size + pair_place) * shard_rows
    row_set = lax.all_gather(anchor, "pair", axis=1, tiled=True)
    col_set = lax.all_gather(partner, "dp", axis=1, tiled=True)
    row_first = (dp_index * pair_size + jnp.arange(pair_size, dtype=jnp.int32)) * shard_rows
    col_first = (jnp.arange(dp_size, dtype=jnp.int32) * pair_size + pair_place) * shard_rows
    tile_rows = math.gcd(row_set.shape[1], 128)
    offsets = jnp.arange(shard_rows, dtype=jnp.int32)
    row_global = (row_first[:, None] + offsets[None, :]).reshape(-1)
    col_global = (col_first[:, None] + offsets[None, :]).reshape(-1)
    row_valid = row_global[None, :] < counts[:, None]
    col_valid = col_global[None, :] < counts[:, None]
    row_high, row_sum, col_high, col_sum = local_stats(
        row_set, col_set, row_global, col_valid, counts, score_scale, tile_rows
    )
    row_high, row_sum = joined((row_high, row_sum), "pair", merge_stats)
    col_high, col_sum = joined((col_high, col_sum), "dp", merge_stats)
    row_lse = jnp.where(row_valid, row_high + jnp.log(jnp.where(row_valid, row_sum, 1.0)), 0.0)
    col_lse = jnp.where(col_valid, col_high + jnp.log(jnp.where(col_valid, col_sum, 1.0)), 0.0)
    own_valid = own_first + offsets[None, :] < counts[:, None]
    row_own = lax.dynamic_slice_in_dim(row_lse, pair_place * shard_rows, shard_rows, 1)
    col_own = lax.dynamic_slice_in_dim(col_lse, dp_index * shard_rows, shard_rows, 1)
    positive = (
        jnp.sum(anchor.astype(jnp.float32) * partner.astype(jnp.float32), axis=2) * score_scale
    )
    loss_terms = jnp.where(own_valid, row_own + col_own - 2.0 * positive, 0.0)
    totals = lax.psum(jnp.sum(loss_terms, axis=1), ("dp", "pair"))
    loss_value = jnp.sum(totals / (2.0 * counts.astype(jnp.float32))) / pair_count
    anchor_outs = []
    partner_outs = []
    for pair_number in range(pair_count):
        grad_rows, grad_cols = pair_partials(
            row_set[pair_number],
            col_set[pair_number],
            row_global,
            col_valid[pair_number],
            counts[pair_number],
            row_lse[pair_number],
            col_lse[pair_number],
            pair_scale[pair_number],
            score_scale,
            tile_rows,
        )
        anchor_part = lax.psum_scatter(grad_rows, "pair", scatter_dimension=0, tiled=True)
        partner_part = lax.psum_scatter(grad_cols, "dp", scatter_dimension=0, tiled=True)
        own_term = pair_scale[pair_number] * score_scale
        keep_rows = own_valid[pair_number][:, None]
        anchor_outs.append(
            jnp.where(
                keep_rows, anchor_part - own_term * partner[pair_number].astype(jnp.float32), 0.0
            )
        )
        partner_outs.append(
            jnp.where(
                keep_rows, partner_part - own_term * anchor[pair_number].astype(jnp.float32), 0.0
            )
        )
    return (loss_value, jnp.stack(anchor_outs), jnp.stack(partner_outs))


def solution(mesh):
    in_specs = (P(None, ("dp", "pair"), None), P(None, ("dp", "pair"), None), P(), P())
    out_specs = (P(), P(None, ("dp", "pair"), None), P(None, ("dp", "pair"), None))
    return jax.shard_map(
        per_device, mesh=mesh, in_specs=in_specs, out_specs=out_specs, check_vma=False
    )
```

profile of v0, /device:TPU:0, one launch (start us, length us, event | category | flops | bytes accessed | tf_op | source)
XLA Modules:
  0.0 896.2 jit_solution(7603829063015780967)
XLA Ops:
  12.9 25.4 %all-gather.13.cloned.1.call-done = bf16[5,256,1024]{2,1,0:T(8,128)(2,1)} async-done(((bf16[5,32,1024]{2,1,0:T(8,128)(2,1)}), bf16[5,256,1024]{2,1,0:T(8,128)(2,1)}) %all-gather.13.cloned.1.call-update) | async-done | bytes 2621456 | tf_op jit(solution)/shard_map/all_gather | solution.py:170
  41.0 56.5 %all-gather.11.cloned.1.call-done = bf16[5,512,1024]{2,1,0:T(8,128)(2,1)} async-done(((bf16[5,32,1024]{2,1,0:T(8,128)(2,1)}), bf16[5,512,1024]{2,1,0:T(8,128)(2,1)}) %all-gather.11.cloned.1.call-update) | async-done | bytes 5242896 | tf_op jit(solution)/shard_map/all_gather | solution.py:169
  97.5 4.7 slice_bitcast_fusion
  102.2 24.6 %while.216 = (s32[]{:T(128)}, f32[512]{0:T(512)S(1)}, f32[512]{0:T(512)S(1)}, f32[256]{0:T(256)S(1)}, f32[256]{0:T(256)S(1)}, /*index=5*/s32[512]{0:T(512)S(1)},...) while((s32[]{:T(128)}, f32[512]{0:T(512)S(1)}, ...), condition=%wide.region_7.8_spmd.clone, body=%wide.region_0.7_spmd.clone.sunk | while | flops 67503496 | bytes 1064666 | solution.py:92
  102.9 3.6 conditional.30
  109.1 3.6 conditional.30
  126.8 24.1 %while.217 = (s32[]{:T(128)}, f32[512]{0:T(512)S(1)}, f32[512]{0:T(512)S(1)}, f32[256]{0:T(256)S(1)}, f32[256]{0:T(256)S(1)}, /*index=5*/s32[512]{0:T(512)S(1)},...) while((s32[]{:T(128)}, f32[512]{0:T(512)S(1)}, ...), condition=%wide.region_15.16_spmd.clone, body=%wide.region_8.15_spmd.clone.sunk | while | flops 67503496 | bytes 1064666 | solution.py:92
  151.0 23.7 %while.218 = (s32[]{:T(128)}, f32[512]{0:T(512)S(1)}, f32[512]{0:T(512)S(1)}, f32[256]{0:T(256)S(1)}, f32[256]{0:T(256)S(1)}, /*index=5*/s32[512]{0:T(512)S(1)},...) while((s32[]{:T(128)}, f32[512]{0:T(512)S(1)}, ...), condition=%wide.region_23.24_spmd.clone, body=%wide.region_16.23_spmd.clone.sunk | while | flops 67503496 | bytes 1064666 | solution.py:92
  174.6 24.5 %while.219 = (s32[]{:T(128)}, f32[512]{0:T(512)S(1)}, f32[512]{0:T(512)S(1)}, f32[256]{0:T(256)S(1)}, f32[256]{0:T(256)S(1)}, /*index=5*/s32[512]{0:T(512)S(1)},...) while((s32[]{:T(128)}, f32[512]{0:T(512)S(1)}, ...), condition=%wide.region_31.32_spmd.clone, body=%wide.region_24.31_spmd.clone.sunk | while | flops 67503496 | bytes 1064666 | solution.py:92
  199.2 19.3 %while.220 = (s32[]{:T(128)}, f32[512]{0:T(512)S(1)}, f32[512]{0:T(512)S(1)}, f32[256]{0:T(256)S(1)}, f32[256]{0:T(256)S(1)}, /*index=5*/s32[512]{0:T(512)S(1)},...) while((s32[]{:T(128)}, f32[512]{0:T(512)S(1)}, ...), condition=%wide.region_39.40_spmd.clone, body=%wide.region_32.39_spmd.clone.sunk | while | flops 67503496 | bytes 1065306 | solution.py:92
  218.5 12.8 %all-gather.6 = f32[8,5,256]{2,1,0:T(8,128)S(1)} all-gather(f32[1,5,256]{2,1,0:T(8,128)S(1)} %bitcast.287), channel_id=4, replica_groups=mesh['dp'=8,'pair'=16] {'dp'}, dimensions={0}, use_global_device_ids=true | all-gather | bytes 46080 | tf_op jit(solution)/shard_map/all_gather | solution.py:12
  231.3 12.7 %all-gather.7 = f32[8,5,256]{2,1,0:T(8,128)S(1)} all-gather(f32[1,5,256]{2,1,0:T(8,128)S(1)} %bitcast.288), channel_id=5, replica_groups=mesh['dp'=8,'pair'=16] {'dp'}, dimensions={0}, use_global_device_ids=true | all-gather | bytes 46080 | tf_op jit(solution)/shard_map/all_gather | solution.py:12
  244.3 23.4 %all-gather.4 = f32[16,5,512]{2,1,0:T(8,128)S(1)} all-gather(f32[1,5,512]{2,1,0:T(8,128)S(1)} %bitcast.275), channel_id=2, replica_groups=mesh['dp'=8,'pair'=16] {'pair'}, dimensions={0}, use_global_device_ids=true | all-gather | bytes 174080 | tf_op jit(solution)/shard_map/all_gather | solution.py:12
  267.8 21.6 %all-gather.5 = f32[16,5,512]{2,1,0:T(8,128)S(1)} all-gather(f32[1,5,512]{2,1,0:T(8,128)S(1)} %bitcast.276), channel_id=3, replica_groups=mesh['dp'=8,'pair'=16] {'pair'}, dimensions={0}, use_global_device_ids=true | all-gather | bytes 174080 | tf_op jit(solution)/shard_map/all_gather | solution.py:12
  290.1 11.4 %while.214 = (s32[]{:T(128)}, f32[5,512]{1,0:T(8,128)S(1)}, f32[5,512]{1,0:T(8,128)S(1)}, f32[16,5,512]{2,1,0:T(8,128)S(1)}, f32[16,5,512]{2,1,0:T(8,128)}, /*index=5*/s32[]{:T(128)}, s32[]{:T(128)}, s32[]{:T(128)}) while((s32[]{:T(128)}, f32[5,512]{1,0:T(8,128)S(1)}, f32[5,512]{1,0:T(8,128)S(1)}, f32[16,5,512]{2,1,0:T(8,128)S(1)}, ...), condition=%wide.region_41.42_spmd, body=%wide.region_40.41_spmd.sunk | while | flops 15365 | bytes 61571 | solution.py:17
  303.3 36.0 %while.221 = (s32[]{:T(128)}, f32[512,1024]{1,0:T(8,128)}, f32[256,1024]{1,0:T(8,128)}, s32[512]{0:T(512)S(1)}, s32[]{:T(128)}, /*index=5*/f32[]{:T(128)}, pred[...) while((s32[]{:T(128)}, f32[512,1024]{1,0:T(8,128)}, ...), condition=%wide.region_51.52_spmd.clone, body=%wide.region_48.51_spmd.clone.sunk | while | flops 202539136 | bytes 7542142 | solution.py:158
  304.0 5.3 conditional.35
  312.1 5.3 conditional.35
  321.4 5.4 conditional.35
  330.7 5.4 conditional.35
  341.5 32.1 %while.222 = (s32[]{:T(128)}, f32[512,1024]{1,0:T(8,128)}, f32[256,1024]{1,0:T(8,128)}, s32[512]{0:T(512)S(1)}, s32[]{:T(128)}, /*index=5*/f32[]{:T(128)}, pred[...) while((s32[]{:T(128)}, f32[512,1024]{1,0:T(8,128)}, ...), condition=%wide.region_56.57_spmd.clone, body=%wide.region_53.56_spmd.clone.sunk | while | flops 202539136 | bytes 7542142 | solution.py:158
  342.3 4.3 conditional.36
  349.4 4.3 conditional.36
  357.7 4.3 conditional.36
  366.0 4.3 conditional.36
  375.8 31.4 %while.223 = (s32[]{:T(128)}, f32[512,1024]{1,0:T(8,128)}, f32[256,1024]{1,0:T(8,128)}, s32[512]{0:T(512)S(1)}, s32[]{:T(128)}, /*index=5*/f32[]{:T(128)}, pred[...) while((s32[]{:T(128)}, f32[512,1024]{1,0:T(8,128)}, ...), condition=%wide.region_61.62_spmd.clone, body=%wide.region_58.61_spmd.clone.sunk | while | flops 202539136 | bytes 7542142 | solution.py:158
  376.6 4.2 conditional.37
  383.5 4.2 conditional.37
  391.7 4.2 conditional.37
  399.8 4.2 conditional.37
  409.9 31.8 %while.224 = (s32[]{:T(128)}, f32[512,1024]{1,0:T(8,128)}, f32[256,1024]{1,0:T(8,128)}, s32[512]{0:T(512)S(1)}, s32[]{:T(128)}, /*index=5*/f32[]{:T(128)}, pred[...) while((s32[]{:T(128)}, f32[512,1024]{1,0:T(8,128)}, ...), condition=%wide.region_66.67_spmd.clone, body=%wide.region_63.66_spmd.clone.sunk | while | flops 202539136 | bytes 7542142 | solution.py:158
  410.7 4.2 conditional.38
  417.7 4.2 conditional.38
  426.0 4.2 conditional.38
  434.2 4.2 conditional.38
  443.9 24.4 %while.225 = (s32[]{:T(128)}, f32[512,1024]{1,0:T(8,128)}, f32[256,1024]{1,0:T(8,128)S(1)}, s32[512]{0:T(512)S(1)}, s32[]{:T(128)}, /*index=5*/f32[]{:T(128)}, p...) while((s32[]{:T(128)}, f32[512,1024]{1,0:T(8,128)}, ...), condition=%wide.region_71.72_spmd.clone, body=%wide.region_68.71_spmd.clone.sunk | while | flops 202539136 | bytes 7542142 | solution.py:158
  444.6 4.2 conditional.39
  450.8 4.2 conditional.39
  456.9 4.2 conditional.39
  463.0 4.2 conditional.39
  473.4 63.1 %psum.7 = f32[5]{0:T(128)S(1)} all-reduce(f32[5]{0:T(128)S(1)} %select_reduce_fusion), channel_id=1, replica_groups=mesh['dp'=8,'pair'=16] {'dp','pair'}, use_global_device_ids=true, to_apply=%region_46.47 | all-reduce | flops 5 | bytes 40 | tf_op jit(solution)/shard_map/psum | solution.py:193
  538.9 17.0 %reduce-scatter.13.cloned.1.call-done = f32[32,1024]{1,0:T(8,128)} async-done(((f32[512,1024]{1,0:T(8,128)}), f32[32,1024]{1,0:T(8,128)}) %reduce-scatter.13.cloned.1.call-update) | async-done | bytes 131088 | tf_op jit(solution)/shard_map/reduce_scatter | solution.py:210
  557.0 32.3 %reduce-scatter.25.cloned.1.call-done = f32[32,1024]{1,0:T(8,128)} async-done(((f32[256,1024]{1,0:T(8,128)}), f32[32,1024]{1,0:T(8,128)}) %reduce-scatter.25.cloned.1.call-update) | async-done | bytes 131088 | tf_op jit(solution)/shard_map/reduce_scatter | solution.py:211
  589.3 76.6 %reduce-scatter.15.cloned.1.call-done = f32[32,1024]{1,0:T(8,128)} async-done(((f32[512,1024]{1,0:T(8,128)}), f32[32,1024]{1,0:T(8,128)}) %reduce-scatter.15.cloned.1.call-update) | async-done | bytes 131088 | tf_op jit(solution)/shard_map/reduce_scatter | solution.py:210
  667.0 32.4 %reduce-scatter.27.cloned.1.call-done = f32[32,1024]{1,0:T(8,128)} async-done(((f32[256,1024]{1,0:T(8,128)}), f32[32,1024]{1,0:T(8,128)}) %reduce-scatter.27.cloned.1.call-update) | async-done | bytes 131088 | tf_op jit(solution)/shard_map/reduce_scatter | solution.py:211
  699.4 76.8 %reduce-scatter.17.cloned.1.call-done = f32[32,1024]{1,0:T(8,128)} async-done(((f32[512,1024]{1,0:T(8,128)}), f32[32,1024]{1,0:T(8,128)}) %reduce-scatter.17.cloned.1.call-update) | async-done | bytes 131088 | tf_op jit(solution)/shard_map/reduce_scatter | solution.py:210
  777.2 32.3 %reduce-scatter.29.cloned.1.call-done = f32[32,1024]{1,0:T(8,128)} async-done(((f32[256,1024]{1,0:T(8,128)}), f32[32,1024]{1,0:T(8,128)}) %reduce-scatter.29.cloned.1.call-update) | async-done | bytes 131088 | tf_op jit(solution)/shard_map/reduce_scatter | solution.py:211
  809.5 76.5 %reduce-scatter.19.cloned.1.call-done = f32[32,1024]{1,0:T(8,128)} async-done(((f32[512,1024]{1,0:T(8,128)}), f32[32,1024]{1,0:T(8,128)}) %reduce-scatter.19.cloned.1.call-update) | async-done | bytes 131088 | tf_op jit(solution)/shard_map/reduce_scatter | solution.py:210
  (488 shorter events, 330.0 us)
Async XLA Ops:
  7.2 31.1 %all-gather.13.cloned.1.call-start = ((), (), s32[]{:S(2)}) async-start(), calls=%async_computation.11 | async-start | bytes 2949120 | tf_op jit(solution)/shard_map/all_gather | solution.py:170
  7.9 89.6 %all-gather.11.cloned.1.call-start = ((), (), s32[]{:S(2)}) async-start(), calls=%async_computation.10 | async-start | bytes 5570560 | tf_op jit(solution)/shard_map/all_gather | solution.py:169
  8.6 529.1 %reduce-scatter.21.cloned.1.call-start = ((), (), s32[]{:S(2)}) async-start(), calls=%async_computation.17 | async-start | bytes 1179648 | tf_op jit(solution)/shard_map/reduce_scatter | solution.py:211
  218.4 84.9 %copy-start.1 = (bf16[512,1024]{1,0:T(8,128)(2,1)}, bf16[512,1024]{1,0:T(8,128)(2,1)S(1)}, u32[]{:S(2)}) copy-start(bf16[512,1024]{1,0:T(8,128)(2,1)S(1)} %get-tuple-element.4396) | copy-start | bytes 3145732
  218.4 83.0 %copy-start.5 = (s32[5]{0:T(128)S(1)}, s32[5]{0:T(128)}, u32[]{:S(2)}) copy-start(s32[5]{0:T(128)} %param.50) | copy-start | bytes 64
  289.3 0.7 copy-start.4
  339.3 198.5 %reduce-scatter.11.cloned.1.call-start = ((), (), s32[]{:S(2)}) async-start(), calls=%async_computation.12 | async-start | bytes 2228224 | tf_op jit(solution)/shard_map/reduce_scatter | solution.py:210
  339.9 199.0 %reduce-scatter.23.cloned.1.call-start = ((), (), s32[]{:S(2)}) async-start(), calls=%async_computation.18 | async-start | bytes 1179648 | tf_op jit(solution)/shard_map/reduce_scatter | solution.py:211
  373.6 182.3 %reduce-scatter.13.cloned.1.call-start = ((), (), s32[]{:S(2)}) async-start(), calls=%async_computation.13 | async-start | bytes 2228224 | tf_op jit(solution)/shard_map/reduce_scatter | solution.py:210
  374.2 215.1 %reduce-scatter.25.cloned.1.call-start = ((), (), s32[]{:S(2)}) async-start(), calls=%async_computation.19 | async-start | bytes 1179648 | tf_op jit(solution)/shard_map/reduce_scatter | solution.py:211
  407.3 258.6 %reduce-scatter.15.cloned.1.call-start = ((), (), s32[]{:S(2)}) async-start(), calls=%async_computation.14 | async-start | bytes 2228224 | tf_op jit(solution)/shard_map/reduce_scatter | solution.py:210
  408.0 291.4 %reduce-scatter.27.cloned.1.call-start = ((), (), s32[]{:S(2)}) async-start(), calls=%async_computation.20 | async-start | bytes 1179648 | tf_op jit(solution)/shard_map/reduce_scatter | solution.py:211
  441.7 334.5 %reduce-scatter.17.cloned.1.call-start = ((), (), s32[]{:S(2)}) async-start(), calls=%async_computation.15 | async-start | bytes 2228224 | tf_op jit(solution)/shard_map/reduce_scatter | solution.py:210
  442.2 367.3 %reduce-scatter.29.cloned.1.call-start = ((), (), s32[]{:S(2)}) async-start(), calls=%async_computation.21 | async-start | bytes 1179648 | tf_op jit(solution)/shard_map/reduce_scatter | solution.py:211
  468.4 1.0 copy-start
  468.4 4.0 copy-start.2
  468.4 4.0 copy-start.3
  469.3 416.7 %reduce-scatter.19.cloned.1.call-start = ((), (), s32[]{:S(2)}) async-start(), calls=%async_computation.16 | async-start | bytes 2228224 | tf_op jit(solution)/shard_map/reduce_scatter | solution.py:210
  887.1 0.8 copy-start.6
  887.2 1.0 copy-start.7
Sparse Core Ops, SparseCore 0:
  9.7 28.5 all-gather.12
  40.4 57.0 all-gather.10
  339.4 29.5 reduce-scatter.20
  372.1 73.4 reduce-scatter.10
  448.0 31.0 reduce-scatter.22
  482.5 73.3 reduce-scatter.12
  558.3 30.9 reduce-scatter.24
  592.6 73.2 reduce-scatter.14
  668.4 30.9 reduce-scatter.26
  702.9 73.2 reduce-scatter.16
  778.6 30.9 reduce-scatter.28
  812.7 73.3 reduce-scatter.18
where the time goes:
time: 902 us; the launch traced here: 896 us
  waiting for transfers between devices  430 us (48%)
  blocking collectives  134 us (15%)
  other arithmetic  111 us (12%)
  matrix products  96.2 us (11%)
  local copies, waits for them, and re-layouts  63.8 us (7%)
  loops' own time  41.8 us (5%)
  between operations  19.4 us (2%)
    reduce_scatter x5, waiting for transfers between devices, per_device(): lax.psum_scatter(grad_rows, 'pair', scatter_dimension=0, tiled=True)  247 us
    reduce_scatter x5, waiting for transfers between devices, per_device(): lax.psum_scatter(grad_cols, 'dp', scatter_dimension=0, tiled=True)  97.1 us
    all_gather x4, blocking collectives, joined(): gathered = jax.tree.map(lambda a: lax.all_gather(a, axis), part)  70.5 us
    psum x1, blocking collectives, per_device(): totals = lax.psum(jnp.sum(loss_terms, axis=1), ('dp', 'pair'))  63.1 us
    dot_general x40, matrix products, block_scores(): jnp.einsum('rd,cd->rc', anchor_block, partner_rows, preferred_element_typ...  61.8 us
    all_gather x1, waiting for transfers between devices, per_device(): row_set = lax.all_gather(anchor, 'pair', axis=1, tiled=True)  56.5 us
    add x20, other arithmetic, pair_visit_block(): return (grad_rows, grad_cols + part_cols)  34.6 us
    dot_general x20, matrix products, pair_live_block(): jnp.einsum('rc,rd->cd', weights, anchor_block, preferred_element_type=jnp...  25.5 us
  transfers between devices with their start and end apart: 12, of which 9 were waited for; matrix products, arithmetic and copies ran while one was open for 13% of the time, Pallas kernels for 0%

commit v1 on v0

v1 whole, which is shorter than its diff:
```python
import math

import jax
import jax.numpy as jnp
from jax import lax
from jax.sharding import PartitionSpec as P

NEG = -1e30


def merge_gathered(stats):
    highs = stats[:, 0]
    sums = stats[:, 1]
    highest = jnp.max(highs, axis=0)
    summed = jnp.sum(sums * jnp.exp(highs - highest[None]), axis=0)
    return highest, summed


def per_device(anchor, partner, counts, pair_scale):
    pair_count, shard_rows, model_width = anchor.shape
    score_scale = 4.0 / math.sqrt(model_width)
    dp_size = lax.axis_size("dp")
    pair_size = lax.axis_size("pair")
    dp_index = lax.axis_index("dp")
    pair_place = lax.axis_index("pair")
    own_first = (dp_index * pair_size + pair_place) * shard_rows

    row_set = lax.all_gather(anchor, "pair", axis=1, tiled=True)
    col_set = lax.all_gather(partner, "dp", axis=1, tiled=True)
    row_count = row_set.shape[1]
    offsets = jnp.arange(shard_rows, dtype=jnp.int32)
    row_global = dp_index * row_count + jnp.arange(row_count, dtype=jnp.int32)
    col_first = (jnp.arange(dp_size, dtype=jnp.int32) * pair_size + pair_place) * shard_rows
    col_global = (col_first[:, None] + offsets[None, :]).reshape(-1)
    row_valid = row_global[None, :] < counts[:, None]
    col_valid = col_global[None, :] < counts[:, None]
    inside = row_valid[:, :, None] & col_valid[:, None, :]

    scores = (
        jnp.einsum("prd,pcd->prc", row_set, col_set, preferred_element_type=jnp.float32)
        * score_scale
    )
    masked = jnp.where(inside, scores, NEG)
    row_high = jnp.max(masked, axis=2)
    row_sum = jnp.sum(jnp.where(inside, jnp.exp(masked - row_high[:, :, None]), 0.0), axis=2)
    col_high = jnp.max(masked, axis=1)
    col_sum = jnp.sum(jnp.where(inside, jnp.exp(masked - col_high[:, None, :]), 0.0), axis=1)

    row_stats = lax.all_gather(jnp.stack([row_high, row_sum]), "pair")
    col_stats = lax.all_gather(jnp.stack([col_high, col_sum]), "dp")
    row_high, row_sum = merge_gathered(row_stats)
    col_high, col_sum = merge_gathered(col_stats)
    row_lse = jnp.where(row_valid, row_high + jnp.log(jnp.where(row_valid, row_sum, 1.0)), 0.0)
    col_lse = jnp.where(col_valid, col_high + jnp.log(jnp.where(col_valid, col_sum, 1.0)), 0.0)

    own_valid = own_first + offsets[None, :] < counts[:, None]
    row_own = lax.dynamic_slice_in_dim(row_lse, pair_place * shard_rows, shard_rows, 1)
    col_own = lax.dynamic_slice_in_dim(col_lse, dp_index * shard_rows, shard_rows, 1)
    positive = (
        jnp.sum(anchor.astype(jnp.float32) * partner.astype(jnp.float32), axis=2) * score_scale
    )
    loss_terms = jnp.where(own_valid, row_own + col_own - 2.0 * positive, 0.0)
    totals = lax.psum(jnp.sum(loss_terms, axis=1), ("dp", "pair"))
    loss_value = jnp.sum(totals / (2.0 * counts.astype(jnp.float32))) / pair_count

    prob_row = jnp.where(inside, jnp.exp(scores - row_lse[:, :, None]), 0.0)
    prob_col = jnp.where(inside, jnp.exp(scores - col_lse[:, None, :]), 0.0)
    weights = (pair_scale[:, None, None] * 0.5 * (prob_row + prob_col)).astype(jnp.bfloat16)
    grad_rows = (
        jnp.einsum("prc,pcd->prd", weights, col_set, preferred_element_type=jnp.float32)
        * score_scale
    )
    grad_cols = (
        jnp.einsum("prc,prd->pcd", weights, row_set, preferred_element_type=jnp.float32)
        * score_scale
    )
    anchor_part = lax.psum_scatter(grad_rows, "pair", scatter_dimension=1, tiled=True)
    partner_part = lax.psum_scatter(grad_cols, "dp", scatter_dimension=1, tiled=True)
    own_term = (pair_scale * score_scale)[:, None, None]
    keep_rows = own_valid[:, :, None]
    anchor_out = jnp.where(keep_rows, anchor_part - own_term * partner.astype(jnp.float32), 0.0)
    partner_out = jnp.where(keep_rows, partner_part - own_term * anchor.astype(jnp.float32), 0.0)
    return (loss_value, anchor_out, partner_out)


def solution(mesh):
    in_specs = (P(None, ("dp", "pair"), None), P(None, ("dp", "pair"), None), P(), P())
    out_specs = (P(), P(None, ("dp", "pair"), None), P(None, ("dp", "pair"), None))
    return jax.shard_map(
        per_device, mesh=mesh, in_specs=in_specs, out_specs=out_specs, check_vma=False
    )
```

time: 902 us -> 355 us (0.39)
  waiting for transfers between devices: 430 us -> 211 us
  other arithmetic: 111 us -> 8.11 us
  matrix products: 96.2 us -> 17.6 us
  local copies, waits for them, and re-layouts: 63.8 us -> 0.1 us
  loops' own time: 41.8 us -> 0 us
  blocking collectives: 134 us -> 101 us
    reduce_scatter x10 -> x2, waiting for transfers between devices: 344 us -> 123 us  [the longest x1 92.8 us: per_device(): lax.psum_scatter(grad_rows, 'pair', scatter_dimension=1, tiled=True)]
    dot_general x80 -> x3, matrix products: 96.2 us -> 17.6 us  [the longest x1 7.58 us: per_device(): jnp.einsum('prc,pcd->prd', weights, col_set, preferred_element_type=jnp.f...]
    add x63 -> x1, other arithmetic: 59.9 us -> 0.01 us  [per_device(): row_global = dp_index * row_count + jnp.arange(row_count, dtype=jnp.int32)]
    another operation x52 -> x0, loops' own time: 41.8 us -> none  [the longest x5 13.8 us: local_stats(): lax.fori_loop(0, block_count, local_visit_block, initial)]
    dynamic_update_slice x60 -> x0, local copies, waits for them, and re-layouts: 37.9 us -> none  [the longest x20 17.1 us: pair_visit_block(): lax.dynamic_update_slice_in_dim(grad_rows, part_rows, start_row, 0)]
    all_gather x4 -> x2, blocking collectives: 70.5 us -> 36.7 us  [the longest x1 23.7 us: per_device(): row_stats = lax.all_gather(jnp.stack([row_high, row_sum]), 'pair')]
    lt x40 -> x1, other arithmetic: 25.1 us -> 0.73 us  [per_device(): row_valid = row_global[None, :] < counts[:, None]]
    reduce_sum x21 -> x3, other arithmetic: 17.5 us -> 2.11 us  [the longest x1 2.02 us: per_device(): jnp.sum(jnp.where(inside, jnp.exp(masked - row_high[:, :, None]), 0.0), a...]
  transfers between devices with their start and end apart: 12 -> 4, of which waited for: 9 -> 4; matrix products, arithmetic and copies ran while one was open for 13% -> 3% of each run, Pallas kernels for 0% -> 0%
where the time goes in v1:
time: 355 us; the launch traced here: 354 us
  waiting for transfers between devices  211 us (59%)
  blocking collectives  101 us (28%)
  matrix products  17.6 us (5%)
  between operations  15.6 us (4%)
  other arithmetic  8.11 us (2%)
    reduce_scatter x1, waiting for transfers between devices, per_device(): lax.psum_scatter(grad_rows, 'pair', scatter_dimension=1, tiled=True)  92.8 us
    psum x1, blocking collectives, per_device(): totals = lax.psum(jnp.sum(loss_terms, axis=1), ('dp', 'pair'))  64.5 us
    all_gather x1, waiting for transfers between devices, per_device(): row_set = lax.all_gather(anchor, 'pair', axis=1, tiled=True)  59.2 us
    reduce_scatter x1, waiting for transfers between devices, per_device(): lax.psum_scatter(grad_cols, 'dp', scatter_dimension=1, tiled=True)  30.3 us
    all_gather x1, waiting for transfers between devices, per_device(): col_set = lax.all_gather(partner, 'dp', axis=1, tiled=True)  27.3 us
    all_gather x1, blocking collectives, per_device(): row_stats = lax.all_gather(jnp.stack([row_high, row_sum]), 'pair')  23.7 us
    all_gather x1, blocking collectives, per_device(): col_stats = lax.all_gather(jnp.stack([col_high, col_sum]), 'dp')  13 us
    dot_general x1, matrix products, per_device(): jnp.einsum('prc,pcd->prd', weights, col_set, preferred_element_type=jnp.f...  7.58 us
  transfers between devices with their start and end apart: 4, of which 4 were waited for; matrix products, arithmetic and copies ran while one was open for 3% of the time, Pallas kernels for 0%

profile of v1, /device:TPU:0, one launch (start us, length us, event | category | flops | bytes accessed | tf_op | source)
XLA Modules:
  0.0 353.9 jit_solution(2730051306671288347)
XLA Ops:
  7.2 0.0 all-gather.7.cloned.1.call-start
  7.2 0.7 all-gather.7.cloned.1.call-update
  7.9 0.0 all-gather.5.cloned.1.call-start
  7.9 0.7 all-gather.5.cloned.1.call-update
  8.6 0.0 reduce-scatter.5.cloned.1.call-start
  8.7 0.1 iota_add_fusion
  8.8 0.1 add.96
  8.9 0.7 broadcast_multiply_fusion.2
  9.5 0.7 broadcast_compare_fusion.1
  10.3 0.7 broadcast_compare_fusion
  11.0 27.3 %all-gather.7.cloned.1.call-done = bf16[5,256,1024]{2,1,0:T(8,128)(2,1)} async-done(((bf16[5,32,1024]{2,1,0:T(8,128)(2,1)}), bf16[5,256,1024]{2,1,0:T(8,128)(2,1)}) %all-gather.7.cloned.1.call-update) | async-done | bytes 2621456 | tf_op jit(solution)/shard_map/all_gather | solution.py:29
  38.3 59.2 %all-gather.5.cloned.1.call-done = bf16[5,512,1024]{2,1,0:T(8,128)(2,1)} async-done(((bf16[5,32,1024]{2,1,0:T(8,128)(2,1)}), bf16[5,512,1024]{2,1,0:T(8,128)(2,1)}) %all-gather.5.cloned.1.call-update) | async-done | bytes 5242896 | tf_op jit(solution)/shard_map/all_gather | solution.py:28
  97.5 0.0 copy-start.3
  97.5 5.0 %fusion.6 = (f32[5,512]{1,0:T(8,128)S(1)}, f32[5,256]{1,0:T(8,128)S(1)}, f32[5,512,256]{2,1,0:T(8,128)S(1)}) fusion(pred[5,256]{1,0:T(8,128)(4,1)S(1)} %broadcast_compare_fusion.1, pred[5,512]{1,0:T(8,128)(4,1)S(1)} %broadcast_compare_fusion, bf16[5,512,1024]{2,1,0:T(8,128)(2,1)} %all-gather.5.cloned.1.call-done, ...), kind=kOutput, calls=%fused_computation.13 | convolution fusion | flops 1345450240 | bytes 10504960 | tf_op jit(solution)/shard_map/prd,pcd->prc/dot_general | solution.py:40
  102.5 0.0 copy-start.2
  102.5 2.0 fusion
  104.5 13.0 %all-gather.1 = f32[16,5,256]{2,1,0:T(8,128)S(1)} all-gather(f32[2,5,256]{2,1,0:T(8,128)S(1)} %pad_maximum_fusion.1), channel_id=3, replica_groups=mesh['dp'=8,'pair'=16] {'dp'}, dimensions={0}, use_global_device_ids=true | all-gather | bytes 92160 | tf_op jit(solution)/shard_map/all_gather | solution.py:50
  117.6 0.0 copy-done.2
  117.6 0.1 add_select_fusion.1
  117.7 23.7 %all-gather = f32[32,5,512]{2,1,0:T(8,128)S(1)} all-gather(f32[2,5,512]{2,1,0:T(8,128)S(1)} %pad_maximum_fusion), channel_id=2, replica_groups=mesh['dp'=8,'pair'=16] {'pair'}, dimensions={0}, use_global_device_ids=true | all-gather | bytes 348160 | tf_op jit(solution)/shard_map/all_gather | solution.py:49
  141.4 0.1 fusion.13
  141.5 0.1 add_select_fusion
  141.6 0.0 copy-done.3
  141.6 5.0 %broadcast_multiply_fusion.1 = f32[5,256,1024]{2,1,0:T(8,128)} fusion(bf16[5,512,1024]{2,1,0:T(8,128)(2,1)S(1)} %copy-done.3, f32[5,512,256]{2,1,0:T(8,128)S(1)} %get-tuple-element.12, f32[5,256]{1,0:T(8,128)S(1)} %add_select_fusion.1, f32[5,512]{1,0:T(8,128)S(1)} %add_select_fusion, f32[5]{0:T(128)S(1)} %get-tuple-element.11, ...), kind=kOutput, calls=%fused_computation.11 | convolution fusion | flops 1349386240 | bytes 13126420 | tf_op jit(solution)/shard_map/prc,prd->pcd/dot_general | solution.py:74
  146.6 0.0 reduce-scatter.5.cloned.1.call-update
  146.6 0.0 reduce-scatter.3.cloned.1.call-start
  146.7 7.6 %broadcast_multiply_fusion = f32[5,512,1024]{2,1,0:T(8,128)} fusion(bf16[5,256,1024]{2,1,0:T(8,128)(2,1)} %all-gather.7.cloned.1.call-done, f32[5,512,256]{2,1,0:T(8,128)S(1)} %get-tuple-element.12, f32[5,256]{1,0:T(8,128)S(1)} %add_select_fusion.1, f32[5,512]{1,0:T(8,128)S(1)} %add_select_fusion, f32[5]{0:T(128)S(1)} %get-tuple-element.11, ...), kind=kOutput, calls=%fused_computation.5 | convolution fusion | flops 1350696960 | bytes 15747860 | tf_op jit(solution)/shard_map/prc,pcd->prd/dot_general | solution.py:70
  154.3 0.0 copy-start
  154.3 0.0 copy-start.1
  154.3 0.0 reduce-scatter.3.cloned.1.call-update
  154.3 0.1 broadcast_compare_fusion.2
  154.4 30.3 %reduce-scatter.5.cloned.1.call-done = f32[5,32,1024]{2,1,0:T(8,128)} async-done(((f32[5,256,1024]{2,1,0:T(8,128)}), f32[5,32,1024]{2,1,0:T(8,128)}) %reduce-scatter.5.cloned.1.call-update) | async-done | bytes 655376 | tf_op jit(solution)/shard_map/reduce_scatter | solution.py:78
  184.7 92.8 %reduce-scatter.3.cloned.1.call-done = f32[5,32,1024]{2,1,0:T(8,128)} async-done(((f32[5,512,1024]{2,1,0:T(8,128)}), f32[5,32,1024]{2,1,0:T(8,128)}) %reduce-scatter.3.cloned.1.call-update) | async-done | bytes 655376 | tf_op jit(solution)/shard_map/reduce_scatter | solution.py:77
  277.6 0.0 copy-done
  277.6 0.0 copy-done.1
  277.6 2.7 fusion.8
  280.3 0.2 select_reduce_fusion
  280.5 64.5 %psum.7 = f32[5]{0:T(128)S(1)} all-reduce(f32[5]{0:T(128)S(1)} %select_reduce_fusion), channel_id=1, replica_groups=mesh['dp'=8,'pair'=16] {'dp','pair'}, use_global_device_ids=true, to_apply=%region_10.11 | all-reduce | flops 5 | bytes 40 | tf_op jit(solution)/shard_map/psum | solution.py:63
  345.0 0.6 fusion.18
  (8 shorter events, 0.1 us)
Async XLA Ops:
  7.2 31.1 %all-gather.7.cloned.1.call-start = ((), (), s32[]{:S(2)}) async-start(), calls=%async_computation.3 | async-start | bytes 2949120 | tf_op jit(solution)/shard_map/all_gather | solution.py:29
  7.9 89.6 %all-gather.5.cloned.1.call-start = ((), (), s32[]{:S(2)}) async-start(), calls=%async_computation.2 | async-start | bytes 5570560 | tf_op jit(solution)/shard_map/all_gather | solution.py:28
  8.6 176.1 %reduce-scatter.5.cloned.1.call-start = ((), (), s32[]{:S(2)}) async-start(), calls=%async_computation.5 | async-start | bytes 5898240 | tf_op jit(solution)/shard_map/reduce_scatter | solution.py:78
  97.5 44.1 %copy-start.3 = (bf16[5,512,1024]{2,1,0:T(8,128)(2,1)S(1)}, bf16[5,512,1024]{2,1,0:T(8,128)(2,1)}, u32[]{:S(2)}) copy-start(bf16[5,512,1024]{2,1,0:T(8,128)(2,1)} %all-gather.5.cloned.1.call-done) | copy-start | bytes 15728644
  102.5 15.1 %copy-start.2 = (s32[5]{0:T(128)S(1)}, s32[5]{0:T(128)}, u32[]{:S(2)}) copy-start(s32[5]{0:T(128)} %param.6) | copy-start | bytes 64
  146.6 130.9 %reduce-scatter.3.cloned.1.call-start = ((), (), s32[]{:S(2)}) async-start(), calls=%async_computation.4 | async-start | bytes 11141120 | tf_op jit(solution)/shard_map/reduce_scatter | solution.py:77
  154.3 123.3 %copy-start = (bf16[5,32,1024]{2,1,0:T(8,128)(2,1)S(1)}, bf16[5,32,1024]{2,1,0:T(8,128)(2,1)}, u32[]{:S(2)}) copy-start(bf16[5,32,1024]{2,1,0:T(8,128)(2,1)} %param.5) | copy-start | bytes 983044
  154.3 123.3 %copy-start.1 = (bf16[5,32,1024]{2,1,0:T(8,128)(2,1)S(1)}, bf16[5,32,1024]{2,1,0:T(8,128)(2,1)}, u32[]{:S(2)}) copy-start(bf16[5,32,1024]{2,1,0:T(8,128)(2,1)} %param.4) | copy-start | bytes 983044
Sparse Core Ops, SparseCore 0:
  9.7 28.5 all-gather.6
  40.4 57.0 all-gather.4
  146.8 37.9 reduce-scatter.4
  188.0 89.4 reduce-scatter.2

commit v2 on v1

v2 whole, which is shorter than its diff:
```python
import math

import jax
import jax.numpy as jnp
from jax import lax
from jax.sharding import PartitionSpec as P

NEG = -1e30


def merge_gathered(highs, sums):
    highest = jnp.max(highs, axis=0)
    summed = jnp.sum(sums * jnp.exp(highs - highest[None]), axis=0)
    return highest, summed


def ring_position(offset, size):
    return (offset + size // 2) % size


def ring_gather(shard, axis, size):
    forward = [(i, (i + 1) % size) for i in range(size)]
    backward = [(i, (i - 1) % size) for i in range(size)]
    parts = [None] * size
    parts[ring_position(0, size)] = shard
    ahead = shard
    behind = shard
    forward_steps = size // 2
    backward_steps = size - 1 - forward_steps
    for step in range(1, forward_steps + 1):
        ahead = lax.ppermute(ahead, axis, forward)
        parts[ring_position(-step, size)] = ahead
        if step <= backward_steps:
            behind = lax.ppermute(behind, axis, backward)
            parts[ring_position(step, size)] = behind
    return parts


def ring_reduce_scatter(chunk, extra, axis, size, width):
    forward = [(i, (i + 1) % size) for i in range(size)]
    backward = [(i, (i - 1) % size) for i in range(size)]

    def ahead_part(q):
        return jnp.concatenate([chunk(q, True), extra], axis=1)

    ahead = ahead_part(ring_position(-1, size))
    behind = chunk(ring_position(1, size), False)
    for step in range(1, size):
        ahead = lax.ppermute(ahead, axis, forward) + ahead_part(ring_position(-1 - step, size))
        behind = lax.ppermute(behind, axis, backward) + chunk(ring_position(1 + step, size), False)
    rows = behind.shape[1]
    return jnp.concatenate([ahead[:, :rows], behind], axis=2), ahead[:, rows]


def per_device(anchor, partner, counts, pair_scale):
    pair_count, shard_rows, model_width = anchor.shape
    score_scale = 4.0 / math.sqrt(model_width)
    dp_size = lax.axis_size("dp")
    pair_size = lax.axis_size("pair")
    dp_index = lax.axis_index("dp")
    pair_place = lax.axis_index("pair")
    own_first = (dp_index * pair_size + pair_place) * shard_rows
    offsets = jnp.arange(shard_rows, dtype=jnp.int32)
    own_valid = own_first + offsets[None, :] < counts[:, None]
    positive = (
        jnp.sum(anchor.astype(jnp.float32) * partner.astype(jnp.float32), axis=2) * score_scale
    )
    own_positive = jnp.sum(jnp.where(own_valid, positive, 0.0), axis=1)

    row_set = lax.all_gather(anchor, "pair", axis=1, tiled=True)
    col_set = jnp.concatenate(ring_gather(partner, "dp", dp_size), axis=1)
    row_count = row_set.shape[1]
    col_count = col_set.shape[1]
    row_global = dp_index * row_count + jnp.arange(row_count, dtype=jnp.int32)
    col_owner = (dp_index + jnp.arange(dp_size, dtype=jnp.int32) - dp_size // 2) % dp_size
    col_first = (col_owner * pair_size + pair_place) * shard_rows
    col_global = (col_first[:, None] + offsets[None, :]).reshape(-1)
    row_valid = row_global[None, :] < counts[:, None]
    col_valid = col_global[None, :] < counts[:, None]
    inside = row_valid[:, :, None] & col_valid[:, None, :]

    scores = (
        jnp.einsum("prd,pcd->prc", row_set, col_set, preferred_element_type=jnp.float32)
        * score_scale
    )
    masked = jnp.where(inside, scores, NEG)
    row_high = jnp.max(masked, axis=2)
    row_sum = jnp.sum(jnp.where(inside, jnp.exp(masked - row_high[:, :, None]), 0.0), axis=2)
    col_high = jnp.max(masked, axis=1)
    col_sum = jnp.sum(jnp.where(inside, jnp.exp(masked - col_high[:, None, :]), 0.0), axis=1)

    col_stats = jnp.stack([col_high, col_sum]).reshape(2, pair_count, dp_size, shard_rows)
    col_stats = jnp.roll(col_stats, dp_index - dp_size // 2, axis=2)
    col_stats = lax.all_gather(col_stats, "dp")
    col_high, col_sum = merge_gathered(col_stats[:, 0], col_stats[:, 1])
    col_high = jnp.roll(col_high, dp_size // 2 - dp_index, axis=1).reshape(pair_count, col_count)
    col_sum = jnp.roll(col_sum, dp_size // 2 - dp_index, axis=1).reshape(pair_count, col_count)
    col_lse = jnp.where(col_valid, col_high + jnp.log(jnp.where(col_valid, col_sum, 1.0)), 0.0)

    lanes = jnp.arange(row_count, dtype=jnp.int32)[None, :]
    col_total = jnp.sum(col_lse, axis=1)
    carried = jnp.where(lanes == 0, col_total[:, None], 0.0)
    carried = jnp.where(lanes == 1, own_positive[:, None], carried)
    row_stats = lax.all_gather(jnp.stack([row_high, row_sum, carried]), "pair")
    row_high, row_sum = merge_gathered(row_stats[:, 0], row_stats[:, 1])
    carried = jnp.sum(row_stats[:, 2], axis=0)
    row_lse = jnp.where(row_valid, row_high + jnp.log(jnp.where(row_valid, row_sum, 1.0)), 0.0)
    row_part = jnp.sum(row_lse, axis=1) - 2.0 * carried[:, 1]

    prob_row = jnp.where(inside, jnp.exp(scores - row_lse[:, :, None]), 0.0)
    prob_col = jnp.where(inside, jnp.exp(scores - col_lse[:, None, :]), 0.0)
    weights = (pair_scale[:, None, None] * 0.5 * (prob_row + prob_col)).astype(jnp.bfloat16)
    grad_rows = (
        jnp.einsum("prc,pcd->prd", weights, col_set, preferred_element_type=jnp.float32)
        * score_scale
    )
    grad_cols = (
        jnp.einsum("prc,prd->pcd", weights, row_set, preferred_element_type=jnp.float32)
        * score_scale
    )
    anchor_part = lax.psum_scatter(grad_rows, "pair", scatter_dimension=1, tiled=True)

    half = model_width // 2

    def col_chunk(q, lo):
        block = grad_cols[:, q * shard_rows:(q + 1) * shard_rows]
        return block[:, :, :half] if lo else block[:, :, half:]

    width_lanes = jnp.arange(half, dtype=jnp.int32)[None, :]
    extra = jnp.where(width_lanes == dp_index, row_part[:, None], 0.0)[:, None, :]
    partner_part, row_parts = ring_reduce_scatter(col_chunk, extra, "dp", dp_size, half)

    totals = carried[:, 0] + jnp.sum(row_parts[:, :dp_size], axis=1)
    loss_value = jnp.sum(totals / (2.0 * counts.astype(jnp.float32))) / pair_count

    own_term = (pair_scale * score_scale)[:, None, None]
    keep_rows = own_valid[:, :, None]
    anchor_out = jnp.where(keep_rows, anchor_part - own_term * partner.astype(jnp.float32), 0.0)
    partner_out = jnp.where(keep_rows, partner_part - own_term * anchor.astype(jnp.float32), 0.0)
    return (loss_value, anchor_out, partner_out)


def solution(mesh):
    in_specs = (P(None, ("dp", "pair"), None), P(None, ("dp", "pair"), None), P(), P())
    out_specs = (P(), P(None, ("dp", "pair"), None), P(None, ("dp", "pair"), None))
    return jax.shard_map(
        per_device, mesh=mesh, in_specs=in_specs, out_specs=out_specs, check_vma=False
    )
```

time: 355 us -> 257 us (0.72)
  waiting for transfers between devices: 211 us -> 136 us
  blocking collectives: 101 us -> 37.2 us
  starting transfers between devices: 0.16 us -> 28.9 us
  local copies, waits for them, and re-layouts: 0.1 us -> 6.56 us
  other arithmetic: 8.11 us -> 14.3 us
    ppermute x0 -> x21, waiting for transfers between devices: none -> 113 us  [the longest x7 60.5 us: ring_reduce_scatter(): lax.ppermute(ahead, axis, forward)]
    reduce_scatter x1, waiting for transfers between devices: 92.8 us -> 0.02 us  [per_device(): lax.psum_scatter(grad_rows, 'pair', scatter_dimension=1, tiled=True)]
    psum x1 -> x0, blocking collectives: 64.5 us -> none  [per_device(): totals = lax.psum(jnp.sum(loss_terms, axis=1), ('dp', 'pair'))]
    all_gather x1, waiting for transfers between devices: 59.2 us -> 21.8 us  [per_device(): row_set = lax.all_gather(anchor, 'pair', axis=1, tiled=True)]
    reduce_scatter x1 -> x0, waiting for transfers between devices: 30.3 us -> none  [per_device(): lax.psum_scatter(grad_cols, 'dp', scatter_dimension=1, tiled=True)]
    ppermute x0 -> x21, starting transfers between devices: none -> 28.8 us  [the longest x7 20.5 us: ring_reduce_scatter(): lax.ppermute(behind, axis, backward)]
    all_gather x1 -> x0, waiting for transfers between devices: 27.3 us -> none  [per_device(): col_set = lax.all_gather(partner, 'dp', axis=1, tiled=True)]
    unnamed x8 -> x18, local copies, waits for them, and re-layouts: 0.02 us -> 5.27 us
  transfers between devices with their start and end apart: 4 -> 23, of which waited for: 4 -> 19; matrix products, arithmetic and copies ran while one was open for 3% -> 8% of each run, Pallas kernels for 0% -> 0%
where the time goes in v2:
time: 257 us
  waiting for transfers between devices  136 us (53%)
  blocking collectives  37.2 us (14%)
  starting transfers between devices  28.9 us (11%)
  matrix products  18.3 us (7%)
  between operations  16.1 us (6%)
  other arithmetic  14.3 us (6%)
  local copies, waits for them, and re-layouts  6.56 us (3%)
    ppermute x7, waiting for transfers between devices, ring_reduce_scatter(): lax.ppermute(ahead, axis, forward)  60.5 us
    ppermute x7, waiting for transfers between devices, ring_reduce_scatter(): lax.ppermute(behind, axis, backward)  31.8 us
    all_gather x1, blocking collectives, per_device(): row_stats = lax.all_gather(jnp.stack([row_high, row_sum, carried]), 'pair')  24 us
    all_gather x1, waiting for transfers between devices, per_device(): row_set = lax.all_gather(anchor, 'pair', axis=1, tiled=True)  21.8 us
    ppermute x4, waiting for transfers between devices, ring_gather(): ahead = lax.ppermute(ahead, axis, forward)  20.8 us
    ppermute x7, starting transfers between devices, ring_reduce_scatter(): lax.ppermute(behind, axis, backward)  20.5 us
    all_gather x1, blocking collectives, per_device(): col_stats = lax.all_gather(col_stats, 'dp')  13.2 us
    dot_general x1, matrix products, per_device(): jnp.einsum('prc,pcd->prd', weights, col_set, preferred_element_type=jnp.f...  8.26 us
  transfers between devices with their start and end apart: 23, of which 19 were waited for; matrix products, arithmetic and copies ran while one was open for 8% of the time, Pallas kernels for 0%

profile of v2, /device:TPU:0, one launch (start us, length us, event | category | flops | bytes accessed | tf_op | source)
XLA Modules:
  0.0 256.9 jit_solution(1229007680345445312)
XLA Ops:
  8.0 2.3 collective-permute-start.4
  10.4 1.2 fusion.11
  11.7 6.5 %collective-permute-done = bf16[5,32,1024]{2,1,0:T(8,128)(2,1)S(1)} collective-permute-done((bf16[5,32,1024]{2,1,0:T(8,128)(2,1)}, bf16[5,32,1024]{2,1,0:T(8,128)(2,1)S(1)}, u32[]{:S(2)}, u32[]{:S(2)}) %collective-permute-start) | collective-permute-done | bytes 327712 | tf_op jit(solution)/shard_map/ppermute | solution.py:31
  18.2 0.8 select_reduce_fusion
  19.7 6.2 %collective-permute-done.1 = bf16[5,32,1024]{2,1,0:T(8,128)(2,1)S(1)} collective-permute-done((bf16[5,32,1024]{2,1,0:T(8,128)(2,1)S(1)}, bf16[5,32,1024]{2,1,0:T(8,128)(2,1)S(1)}, u32[]{:S(2)}, u32[]{:S(2)}) %collective-permute-start.1) | collective-permute-done | bytes 327712 | tf_op jit(solution)/shard_map/ppermute | solution.py:31
  26.6 3.0 %collective-permute-start.5 = (bf16[5,32,1024]{2,1,0:T(8,128)(2,1)S(1)}, bf16[5,32,1024]{2,1,0:T(8,128)(2,1)S(1)}, u32[]{:S(2)}, u32[]{:S(2)}) collective-permute-start(bf16[5,32,1024]{2,1,0:T(8,128)(2,1)S(1)} %collective-permute-done.4), channel_id=1, source_target_pairs={{0,112},{16,0},{32,16},{48,32},{64,48},{80,64},{96,80},{112,96},{1... | collective-permute-start | bytes 983048 | tf_op jit(solution)/shard_map/ppermute | solution.py:34
  29.6 4.0 %collective-permute-done.2 = bf16[5,32,1024]{2,1,0:T(8,128)(2,1)S(1)} collective-permute-done((bf16[5,32,1024]{2,1,0:T(8,128)(2,1)S(1)}, bf16[5,32,1024]{2,1,0:T(8,128)(2,1)S(1)}, u32[]{:S(2)}, u32[]{:S(2)}) %collective-permute-start.2) | collective-permute-done | bytes 327712 | tf_op jit(solution)/shard_map/ppermute | solution.py:31
  33.6 0.7 broadcast_compare_fusion
  34.3 3.0 %collective-permute-start.6 = (bf16[5,32,1024]{2,1,0:T(8,128)(2,1)S(1)}, bf16[5,32,1024]{2,1,0:T(8,128)(2,1)S(1)}, u32[]{:S(2)}, u32[]{:S(2)}) collective-permute-start(bf16[5,32,1024]{2,1,0:T(8,128)(2,1)S(1)} %collective-permute-done.5), channel_id=1, source_target_pairs={{0,112},{16,0},{32,16},{48,32},{64,48},{80,64},{96,80},{112,96},{1... | collective-permute-start | bytes 983048 | tf_op jit(solution)/shard_map/ppermute | solution.py:34
  37.3 4.0 %collective-permute-done.3 = bf16[5,32,1024]{2,1,0:T(8,128)(2,1)S(1)} collective-permute-done((bf16[5,32,1024]{2,1,0:T(8,128)(2,1)S(1)}, bf16[5,32,1024]{2,1,0:T(8,128)(2,1)S(1)}, u32[]{:S(2)}, u32[]{:S(2)}) %collective-permute-start.3) | collective-permute-done | bytes 327712 | tf_op jit(solution)/shard_map/ppermute | solution.py:31
  41.3 0.7 constant_dynamic-update-slice_fusion.7
  42.0 0.7 constant_dynamic-update-slice_fusion.6
  42.8 0.8 constant_dynamic-update-slice_fusion.5
  43.5 0.8 constant_dynamic-update-slice_fusion.4
  44.3 0.7 constant_dynamic-update-slice_fusion.3
  45.0 0.7 constant_dynamic-update-slice_fusion.2
  45.8 0.8 constant_dynamic-update-slice_fusion.1
  46.6 0.8 constant_dynamic-update-slice_fusion
  47.3 21.8 %all-gather.4.cloned.1.call-done = bf16[5,512,1024]{2,1,0:T(8,128)(2,1)} async-done(((bf16[5,32,1024]{2,1,0:T(8,128)(2,1)}), bf16[5,512,1024]{2,1,0:T(8,128)(2,1)}) %all-gather.4.cloned.1.call-update) | async-done | bytes 5242896 | tf_op jit(solution)/shard_map/all_gather | solution.py:70
  69.1 5.2 %fusion.8 = (f32[5,512]{1,0:T(8,128)S(1)}, f32[5,256]{1,0:T(8,128)S(1)}, f32[5,256,512]{2,1,0:T(8,128)S(1)}) fusion(pred[5,256]{1,0:T(8,128)(4,1)S(1)} %broadcast_compare_fusion.1, pred[5,512]{1,0:T(8,128)(4,1)S(1)} %broadcast_compare_fusion, bf16[5,256,1024]{2,1,0:T(8,128)(2,1)} %constant_dynamic-update-slice_fusion, ...), kind=kOutput, calls=%fused_computation.25 | convolution fusion | flops 1345450240 | bytes 10504960 | tf_op jit(solution)/shard_map/prd,pcd->prc/dot_general | solution.py:83
  74.4 1.9 fusion
  76.4 13.2 %all-gather = f32[16,5,8,32]{3,2,1,0:T(8,128)S(1)} all-gather(f32[2,5,8,32]{3,2,1,0:T(8,128)S(1)} %fusion.28), channel_id=2, replica_groups=mesh['dp'=8,'pair'=16] {'dp'}, dimensions={0}, use_global_device_ids=true | all-gather | bytes 92160 | tf_op jit(solution)/shard_map/all_gather | solution.py:94
  90.1 24.0 %all-gather.1 = f32[48,5,512]{2,1,0:T(8,128)S(1)} all-gather(f32[3,5,512]{2,1,0:T(8,128)S(1)} %pad_maximum_fusion.8), channel_id=3, replica_groups=mesh['dp'=8,'pair'=16] {'pair'}, dimensions={0}, use_global_device_ids=true | all-gather | bytes 522240 | tf_op jit(solution)/shard_map/all_gather | solution.py:104
  114.5 8.3 %broadcast_multiply_fusion = f32[5,512,1024]{2,1,0:T(8,128)} fusion(bf16[5,256,1024]{2,1,0:T(8,128)(2,1)} %constant_dynamic-update-slice_fusion, f32[5,256,512]{2,1,0:T(8,128)S(1)} %get-tuple-element.28, f32[5,256]{1,0:T(8,128)S(1)} %add_select_fusion.1, f32[5,512]{1,0:T(8,128)S(1)} %get-tuple-element.11, f32[5]{0:T(128)S(1)} %get-tuple-element.27, ...), kind=kOutput, calls=%fused_computation.5 | convolution fusion | flops 1350696960 | bytes 15747860 | tf_op jit(solution)/shard_map/prc,pcd->prd/dot_general | solution.py:114
  122.8 4.8 %broadcast_multiply_fusion.1 = f32[5,256,1024]{2,1,0:T(8,128)S(1)} fusion(bf16[5,512,1024]{2,1,0:T(8,128)(2,1)} %all-gather.4.cloned.1.call-done, f32[5,256,512]{2,1,0:T(8,128)S(1)} %get-tuple-element.28, f32[5,256]{1,0:T(8,128)S(1)} %add_select_fusion.1, f32[5,512]{1,0:T(8,128)S(1)} %get-tuple-element.11, f32[5]{0:T(128)S(1)} %get-tuple-element.27, ...), kind=kOutput, calls=%fused_computation.15 | convolution fusion | flops 1349386240 | bytes 13126420 | tf_op jit(solution)/shard_map/prc,prd->pcd/dot_general | solution.py:118
  127.7 4.6 %collective-permute-done.14 = f32[5,32,512]{2,1,0:T(8,128)S(1)} collective-permute-done((f32[5,32,512]{2,1,0:T(8,128)S(1)}, f32[5,32,512]{2,1,0:T(8,128)S(1)}, u32[]{:S(2)}, u32[]{:S(2)}) %collective-permute-start.14) | collective-permute-done | bytes 327712 | tf_op jit(solution)/shard_map/ppermute | solution.py:50
  132.4 3.1 %collective-permute-start.15 = (f32[5,32,512]{2,1,0:T(8,128)S(1)}, f32[5,32,512]{2,1,0:T(8,128)S(1)}, u32[]{:S(2)}, u32[]{:S(2)}) collective-permute-start(f32[5,32,512]{2,1,0:T(8,128)S(1)} %slice_add_fusion.6), channel_id=1, source_target_pairs={{0,112},{16,0},{32,16},{48,32},{64,48},{80,64},{96,80},{112,96},{1... | collective-permute-start | bytes 983048 | tf_op jit(solution)/shard_map/ppermute | solution.py:50
  135.5 4.6 %collective-permute-done.15 = f32[5,32,512]{2,1,0:T(8,128)S(1)} collective-permute-done((f32[5,32,512]{2,1,0:T(8,128)S(1)}, f32[5,32,512]{2,1,0:T(8,128)S(1)}, u32[]{:S(2)}, u32[]{:S(2)}) %collective-permute-start.15) | collective-permute-done | bytes 327712 | tf_op jit(solution)/shard_map/ppermute | solution.py:50
  140.1 3.5 %collective-permute-start.16 = (f32[5,32,512]{2,1,0:T(8,128)S(1)}, f32[5,32,512]{2,1,0:T(8,128)S(1)}, u32[]{:S(2)}, u32[]{:S(2)}) collective-permute-start(f32[5,32,512]{2,1,0:T(8,128)S(1)} %slice_add_fusion.5), channel_id=1, source_target_pairs={{0,112},{16,0},{32,16},{48,32},{64,48},{80,64},{96,80},{112,96},{1... | collective-permute-start | bytes 983048 | tf_op jit(solution)/shard_map/ppermute | solution.py:50
  143.6 4.6 %collective-permute-done.16 = f32[5,32,512]{2,1,0:T(8,128)S(1)} collective-permute-done((f32[5,32,512]{2,1,0:T(8,128)S(1)}, f32[5,32,512]{2,1,0:T(8,128)S(1)}, u32[]{:S(2)}, u32[]{:S(2)}) %collective-permute-start.16) | collective-permute-done | bytes 327712 | tf_op jit(solution)/shard_map/ppermute | solution.py:50
  148.3 3.5 %collective-permute-start.17 = (f32[5,32,512]{2,1,0:T(8,128)S(1)}, f32[5,32,512]{2,1,0:T(8,128)S(1)}, u32[]{:S(2)}, u32[]{:S(2)}) collective-permute-start(f32[5,32,512]{2,1,0:T(8,128)S(1)} %slice_add_fusion.4), channel_id=1, source_target_pairs={{0,112},{16,0},{32,16},{48,32},{64,48},{80,64},{96,80},{112,96},{1... | collective-permute-start | bytes 983048 | tf_op jit(solution)/shard_map/ppermute | solution.py:50
  151.8 4.6 %collective-permute-done.17 = f32[5,32,512]{2,1,0:T(8,128)S(1)} collective-permute-done((f32[5,32,512]{2,1,0:T(8,128)S(1)}, f32[5,32,512]{2,1,0:T(8,128)S(1)}, u32[]{:S(2)}, u32[]{:S(2)}) %collective-permute-start.17) | collective-permute-done | bytes 327712 | tf_op jit(solution)/shard_map/ppermute | solution.py:50
  156.4 3.5 %collective-permute-start.18 = (f32[5,32,512]{2,1,0:T(8,128)S(1)}, f32[5,32,512]{2,1,0:T(8,128)S(1)}, u32[]{:S(2)}, u32[]{:S(2)}) collective-permute-start(f32[5,32,512]{2,1,0:T(8,128)S(1)} %slice_add_fusion.3), channel_id=1, source_target_pairs={{0,112},{16,0},{32,16},{48,32},{64,48},{80,64},{96,80},{112,96},{1... | collective-permute-start | bytes 983048 | tf_op jit(solution)/shard_map/ppermute | solution.py:50
  160.0 4.6 %collective-permute-done.18 = f32[5,32,512]{2,1,0:T(8,128)S(1)} collective-permute-done((f32[5,32,512]{2,1,0:T(8,128)S(1)}, f32[5,32,512]{2,1,0:T(8,128)S(1)}, u32[]{:S(2)}, u32[]{:S(2)}) %collective-permute-start.18) | collective-permute-done | bytes 327712 | tf_op jit(solution)/shard_map/ppermute | solution.py:50
  164.6 3.5 %collective-permute-start.19 = (f32[5,32,512]{2,1,0:T(8,128)S(1)}, f32[5,32,512]{2,1,0:T(8,128)S(1)}, u32[]{:S(2)}, u32[]{:S(2)}) collective-permute-start(f32[5,32,512]{2,1,0:T(8,128)S(1)} %slice_add_fusion.2), channel_id=1, source_target_pairs={{0,112},{16,0},{32,16},{48,32},{64,48},{80,64},{96,80},{112,96},{1... | collective-permute-start | bytes 983048 | tf_op jit(solution)/shard_map/ppermute | solution.py:50
  168.3 4.5 %collective-permute-done.19 = f32[5,32,512]{2,1,0:T(8,128)S(1)} collective-permute-done((f32[5,32,512]{2,1,0:T(8,128)S(1)}, f32[5,32,512]{2,1,0:T(8,128)S(1)}, u32[]{:S(2)}, u32[]{:S(2)}) %collective-permute-start.19) | collective-permute-done | bytes 327712 | tf_op jit(solution)/shard_map/ppermute | solution.py:50
  172.7 1.0 slice_add_fusion.1
  173.8 3.3 %collective-permute-start.20 = (f32[5,32,512]{2,1,0:T(8,128)S(1)}, f32[5,32,512]{2,1,0:T(8,128)S(1)}, u32[]{:S(2)}, u32[]{:S(2)}) collective-permute-start(f32[5,32,512]{2,1,0:T(8,128)S(1)} %slice_add_fusion.1), channel_id=1, source_target_pairs={{0,112},{16,0},{32,16},{48,32},{64,48},{80,64},{96,80},{112,96},{1... | collective-permute-start | bytes 983048 | tf_op jit(solution)/shard_map/ppermute | solution.py:50
  177.3 4.3 %collective-permute-done.20 = f32[5,32,512]{2,1,0:T(8,128)S(1)} collective-permute-done((f32[5,32,512]{2,1,0:T(8,128)S(1)}, f32[5,32,512]{2,1,0:T(8,128)S(1)}, u32[]{:S(2)}, u32[]{:S(2)}) %collective-permute-start.20) | collective-permute-done | bytes 327712 | tf_op jit(solution)/shard_map/ppermute | solution.py:50
  181.7 2.2 slice_add_fusion
  183.9 9.1 %collective-permute-done.7 = f32[5,33,512]{2,1,0:T(8,128)S(1)} collective-permute-done((f32[5,33,512]{2,1,0:T(8,128)S(1)}, f32[5,33,512]{2,1,0:T(8,128)S(1)}, u32[]{:S(2)}, u32[]{:S(2)}) %collective-permute-start.7) | collective-permute-done | bytes 337952 | tf_op jit(solution)/shard_map/ppermute | solution.py:49
  193.1 8.6 %collective-permute-done.8 = f32[5,33,512]{2,1,0:T(8,128)S(1)} collective-permute-done((f32[5,33,512]{2,1,0:T(8,128)S(1)}, f32[5,33,512]{2,1,0:T(8,128)S(1)}, u32[]{:S(2)}, u32[]{:S(2)}) %collective-permute-start.8) | collective-permute-done | bytes 337952 | tf_op jit(solution)/shard_map/ppermute | solution.py:49
  201.8 8.6 %collective-permute-done.9 = f32[5,33,512]{2,1,0:T(8,128)S(1)} collective-permute-done((f32[5,33,512]{2,1,0:T(8,128)S(1)}, f32[5,33,512]{2,1,0:T(8,128)S(1)}, u32[]{:S(2)}, u32[]{:S(2)}) %collective-permute-start.9) | collective-permute-done | bytes 337952 | tf_op jit(solution)/shard_map/ppermute | solution.py:49
  210.4 8.6 %collective-permute-done.10 = f32[5,33,512]{2,1,0:T(8,128)S(1)} collective-permute-done((f32[5,33,512]{2,1,0:T(8,128)S(1)}, f32[5,33,512]{2,1,0:T(8,128)S(1)}, u32[]{:S(2)}, u32[]{:S(2)}) %collective-permute-start.10) | collective-permute-done | bytes 337952 | tf_op jit(solution)/shard_map/ppermute | solution.py:49
  219.1 8.6 %collective-permute-done.11 = f32[5,33,512]{2,1,0:T(8,128)S(1)} collective-permute-done((f32[5,33,512]{2,1,0:T(8,128)S(1)}, f32[5,33,512]{2,1,0:T(8,128)S(1)}, u32[]{:S(2)}, u32[]{:S(2)}) %collective-permute-start.11) | collective-permute-done | bytes 337952 | tf_op jit(solution)/shard_map/ppermute | solution.py:49
  227.8 8.6 %collective-permute-done.12 = f32[5,33,512]{2,1,0:T(8,128)S(1)} collective-permute-done((f32[5,33,512]{2,1,0:T(8,128)S(1)}, f32[5,33,512]{2,1,0:T(8,128)S(1)}, u32[]{:S(2)}, u32[]{:S(2)}) %collective-permute-start.12) | collective-permute-done | bytes 337952 | tf_op jit(solution)/shard_map/ppermute | solution.py:49
  236.5 8.5 %collective-permute-done.13 = f32[5,33,512]{2,1,0:T(8,128)S(1)} collective-permute-done((f32[5,33,512]{2,1,0:T(8,128)S(1)}, f32[5,33,512]{2,1,0:T(8,128)S(1)}, u32[]{:S(2)}, u32[]{:S(2)}) %collective-permute-start.13) | collective-permute-done | bytes 337952 | tf_op jit(solution)/shard_map/ppermute | solution.py:49
  246.5 2.4 fusion.10
  (77 shorter events, 5.5 us)
Async XLA Ops:
  7.2 37.1 %copy-start.2 = (bf16[5,32,1024]{2,1,0:T(8,128)(2,1)S(1)}, bf16[5,32,1024]{2,1,0:T(8,128)(2,1)}, u32[]{:S(2)}) copy-start(bf16[5,32,1024]{2,1,0:T(8,128)(2,1)} %param.7) | copy-start | bytes 983044
  7.2 62.0 %all-gather.4.cloned.1.call-start = ((), (), s32[]{:S(2)}) async-start(), calls=%async_computation.1 | async-start | bytes 5570560 | tf_op jit(solution)/shard_map/all_gather | solution.py:70
  7.9 238.6 %reduce-scatter.2.cloned.1.call-start = ((), (), s32[]{:S(2)}) async-start(), calls=%async_computation.2 | async-start | bytes 11141120 | tf_op jit(solution)/shard_map/reduce_scatter | solution.py:121
  8.0 18.7 %collective-permute-start.4 = (bf16[5,32,1024]{2,1,0:T(8,128)(2,1)}, bf16[5,32,1024]{2,1,0:T(8,128)(2,1)S(1)}, u32[]{:S(2)}, u32[]{:S(2)}) collective-permute-start(bf16[5,32,1024]{2,1,0:T(8,128)(2,1)} %param.7), channel_id=1, source_target_pairs={{0,112},{16,0},{32,16},{48,32},{64,48},{80,64},{96,80},{112,96},{1... | collective-permute-start | bytes 983048 | tf_op jit(solution)/shard_map/ppermute | solution.py:34
  10.2 7.9 %collective-permute-start = (bf16[5,32,1024]{2,1,0:T(8,128)(2,1)}, bf16[5,32,1024]{2,1,0:T(8,128)(2,1)S(1)}, u32[]{:S(2)}, u32[]{:S(2)}) collective-permute-start(bf16[5,32,1024]{2,1,0:T(8,128)(2,1)} %param.7), channel_id=1, source_target_pairs={{0,16},{16,32},{32,48},{48,64},{64,80},{80,96},{96,112},{112,0},{1... | collective-permute-start | bytes 983048 | tf_op jit(solution)/shard_map/ppermute | solution.py:31
  18.2 7.7 %collective-permute-start.1 = (bf16[5,32,1024]{2,1,0:T(8,128)(2,1)S(1)}, bf16[5,32,1024]{2,1,0:T(8,128)(2,1)S(1)}, u32[]{:S(2)}, u32[]{:S(2)}) collective-permute-start(bf16[5,32,1024]{2,1,0:T(8,128)(2,1)S(1)} %collective-permute-done), channel_id=1, source_target_pairs={{0,16},{16,32},{32,48},{48,64},{64,80},{80,96},{96,112},{112,0},{1... | collective-permute-start | bytes 983048 | tf_op jit(solution)/shard_map/ppermute | solution.py:31
  25.9 7.7 %collective-permute-start.2 = (bf16[5,32,1024]{2,1,0:T(8,128)(2,1)S(1)}, bf16[5,32,1024]{2,1,0:T(8,128)(2,1)S(1)}, u32[]{:S(2)}, u32[]{:S(2)}) collective-permute-start(bf16[5,32,1024]{2,1,0:T(8,128)(2,1)S(1)} %collective-permute-done.1), channel_id=1, source_target_pairs={{0,16},{16,32},{32,48},{48,64},{64,80},{80,96},{96,112},{112,0},{1... | collective-permute-start | bytes 983048 | tf_op jit(solution)/shard_map/ppermute | solution.py:31
  26.6 7.7 %collective-permute-start.5 = (bf16[5,32,1024]{2,1,0:T(8,128)(2,1)S(1)}, bf16[5,32,1024]{2,1,0:T(8,128)(2,1)S(1)}, u32[]{:S(2)}, u32[]{:S(2)}) collective-permute-start(bf16[5,32,1024]{2,1,0:T(8,128)(2,1)S(1)} %collective-permute-done.4), channel_id=1, source_target_pairs={{0,112},{16,0},{32,16},{48,32},{64,48},{80,64},{96,80},{112,96},{1... | collective-permute-start | bytes 983048 | tf_op jit(solution)/shard_map/ppermute | solution.py:34
  33.6 7.7 %collective-permute-start.3 = (bf16[5,32,1024]{2,1,0:T(8,128)(2,1)S(1)}, bf16[5,32,1024]{2,1,0:T(8,128)(2,1)S(1)}, u32[]{:S(2)}, u32[]{:S(2)}) collective-permute-start(bf16[5,32,1024]{2,1,0:T(8,128)(2,1)S(1)} %collective-permute-done.2), channel_id=1, source_target_pairs={{0,16},{16,32},{32,48},{48,64},{64,80},{80,96},{96,112},{112,0},{1... | collective-permute-start | bytes 983048 | tf_op jit(solution)/shard_map/ppermute | solution.py:31
  34.3 12.2 %collective-permute-start.6 = (bf16[5,32,1024]{2,1,0:T(8,128)(2,1)S(1)}, bf16[5,32,1024]{2,1,0:T(8,128)(2,1)S(1)}, u32[]{:S(2)}, u32[]{:S(2)}) collective-permute-start(bf16[5,32,1024]{2,1,0:T(8,128)(2,1)S(1)} %collective-permute-done.5), channel_id=1, source_target_pairs={{0,112},{16,0},{32,16},{48,32},{64,48},{80,64},{96,80},{112,96},{1... | collective-permute-start | bytes 983048 | tf_op jit(solution)/shard_map/ppermute | solution.py:34
  74.3 15.4 %copy-start.4 = (s32[5]{0:T(128)S(1)}, s32[5]{0:T(128)}, u32[]{:S(2)}) copy-start(s32[5]{0:T(128)} %param.8) | copy-start | bytes 64
  127.7 37.0 %copy-start = (f32[5,256,1024]{2,1,0:T(8,128)}, f32[5,256,1024]{2,1,0:T(8,128)S(1)}, u32[]{:S(2)}) copy-start(f32[5,256,1024]{2,1,0:T(8,128)S(1)} %broadcast_multiply_fusion.1) | copy-start | bytes 15728644
  127.7 4.6 %collective-permute-start.14 = (f32[5,32,512]{2,1,0:T(8,128)S(1)}, f32[5,32,512]{2,1,0:T(8,128)S(1)}, u32[]{:S(2)}, u32[]{:S(2)}) collective-permute-start(f32[5,32,512]{2,1,0:T(8,128)S(1)} %slice.154), channel_id=1, source_target_pairs={{0,112},{16,0},{32,16},{48,32},{64,48},{80,64},{96,80},{112,96},{1... | collective-permute-start | bytes 983048 | tf_op jit(solution)/shard_map/ppermute | solution.py:50
  132.4 7.7 %collective-permute-start.15 = (f32[5,32,512]{2,1,0:T(8,128)S(1)}, f32[5,32,512]{2,1,0:T(8,128)S(1)}, u32[]{:S(2)}, u32[]{:S(2)}) collective-permute-start(f32[5,32,512]{2,1,0:T(8,128)S(1)} %slice_add_fusion.6), channel_id=1, source_target_pairs={{0,112},{16,0},{32,16},{48,32},{64,48},{80,64},{96,80},{112,96},{1... | collective-permute-start | bytes 983048 | tf_op jit(solution)/shard_map/ppermute | solution.py:50
  140.1 8.1 %collective-permute-start.16 = (f32[5,32,512]{2,1,0:T(8,128)S(1)}, f32[5,32,512]{2,1,0:T(8,128)S(1)}, u32[]{:S(2)}, u32[]{:S(2)}) collective-permute-start(f32[5,32,512]{2,1,0:T(8,128)S(1)} %slice_add_fusion.5), channel_id=1, source_target_pairs={{0,112},{16,0},{32,16},{48,32},{64,48},{80,64},{96,80},{112,96},{1... | collective-permute-start | bytes 983048 | tf_op jit(solution)/shard_map/ppermute | solution.py:50
  148.3 8.1 %collective-permute-start.17 = (f32[5,32,512]{2,1,0:T(8,128)S(1)}, f32[5,32,512]{2,1,0:T(8,128)S(1)}, u32[]{:S(2)}, u32[]{:S(2)}) collective-permute-start(f32[5,32,512]{2,1,0:T(8,128)S(1)} %slice_add_fusion.4), channel_id=1, source_target_pairs={{0,112},{16,0},{32,16},{48,32},{64,48},{80,64},{96,80},{112,96},{1... | collective-permute-start | bytes 983048 | tf_op jit(solution)/shard_map/ppermute | solution.py:50
  156.4 8.1 %collective-permute-start.18 = (f32[5,32,512]{2,1,0:T(8,128)S(1)}, f32[5,32,512]{2,1,0:T(8,128)S(1)}, u32[]{:S(2)}, u32[]{:S(2)}) collective-permute-start(f32[5,32,512]{2,1,0:T(8,128)S(1)} %slice_add_fusion.3), channel_id=1, source_target_pairs={{0,112},{16,0},{32,16},{48,32},{64,48},{80,64},{96,80},{112,96},{1... | collective-permute-start | bytes 983048 | tf_op jit(solution)/shard_map/ppermute | solution.py:50
  164.6 8.1 %collective-permute-start.19 = (f32[5,32,512]{2,1,0:T(8,128)S(1)}, f32[5,32,512]{2,1,0:T(8,128)S(1)}, u32[]{:S(2)}, u32[]{:S(2)}) collective-permute-start(f32[5,32,512]{2,1,0:T(8,128)S(1)} %slice_add_fusion.2), channel_id=1, source_target_pairs={{0,112},{16,0},{32,16},{48,32},{64,48},{80,64},{96,80},{112,96},{1... | collective-permute-start | bytes 983048 | tf_op jit(solution)/shard_map/ppermute | solution.py:50
  173.8 7.9 %collective-permute-start.20 = (f32[5,32,512]{2,1,0:T(8,128)S(1)}, f32[5,32,512]{2,1,0:T(8,128)S(1)}, u32[]{:S(2)}, u32[]{:S(2)}) collective-permute-start(f32[5,32,512]{2,1,0:T(8,128)S(1)} %slice_add_fusion.1), channel_id=1, source_target_pairs={{0,112},{16,0},{32,16},{48,32},{64,48},{80,64},{96,80},{112,96},{1... | collective-permute-start | bytes 983048 | tf_op jit(solution)/shard_map/ppermute | solution.py:50
  183.9 9.1 %collective-permute-start.7 = (f32[5,33,512]{2,1,0:T(8,128)S(1)}, f32[5,33,512]{2,1,0:T(8,128)S(1)}, u32[]{:S(2)}, u32[]{:S(2)}) collective-permute-start(f32[5,33,512]{2,1,0:T(8,128)S(1)} %pad_maximum_fusion.7), channel_id=1, source_target_pairs={{0,16},{16,32},{32,48},{48,64},{64,80},{80,96},{96,112},{112,0},{1... | collective-permute-start | bytes 1013768 | tf_op jit(solution)/shard_map/ppermute | solution.py:49
  193.1 8.6 %collective-permute-start.8 = (f32[5,33,512]{2,1,0:T(8,128)S(1)}, f32[5,33,512]{2,1,0:T(8,128)S(1)}, u32[]{:S(2)}, u32[]{:S(2)}) collective-permute-start(f32[5,33,512]{2,1,0:T(8,128)S(1)} %fusion.14), channel_id=1, source_target_pairs={{0,16},{16,32},{32,48},{48,64},{64,80},{80,96},{96,112},{112,0},{1... | collective-permute-start | bytes 1013768 | tf_op jit(solution)/shard_map/ppermute | solution.py:49
  201.7 8.6 %collective-permute-start.9 = (f32[5,33,512]{2,1,0:T(8,128)S(1)}, f32[5,33,512]{2,1,0:T(8,128)S(1)}, u32[]{:S(2)}, u32[]{:S(2)}) collective-permute-start(f32[5,33,512]{2,1,0:T(8,128)S(1)} %fusion.15), channel_id=1, source_target_pairs={{0,16},{16,32},{32,48},{48,64},{64,80},{80,96},{96,112},{112,0},{1... | collective-permute-start | bytes 1013768 | tf_op jit(solution)/shard_map/ppermute | solution.py:49
  210.4 8.6 %collective-permute-start.10 = (f32[5,33,512]{2,1,0:T(8,128)S(1)}, f32[5,33,512]{2,1,0:T(8,128)S(1)}, u32[]{:S(2)}, u32[]{:S(2)}) collective-permute-start(f32[5,33,512]{2,1,0:T(8,128)S(1)} %fusion.16), channel_id=1, source_target_pairs={{0,16},{16,32},{32,48},{48,64},{64,80},{80,96},{96,112},{112,0},{1... | collective-permute-start | bytes 1013768 | tf_op jit(solution)/shard_map/ppermute | solution.py:49
  219.0 27.5 %copy-start.1 = (bf16[5,32,1024]{2,1,0:T(8,128)(2,1)S(1)}, bf16[5,32,1024]{2,1,0:T(8,128)(2,1)}, u32[]{:S(2)}) copy-start(bf16[5,32,1024]{2,1,0:T(8,128)(2,1)} %param.6) | copy-start | bytes 983044
  219.0 27.5 %copy-start.3 = (bf16[5,32,1024]{2,1,0:T(8,128)(2,1)S(1)}, bf16[5,32,1024]{2,1,0:T(8,128)(2,1)}, u32[]{:S(2)}) copy-start(bf16[5,32,1024]{2,1,0:T(8,128)(2,1)} %param.7) | copy-start | bytes 983044
  219.1 8.6 %collective-permute-start.11 = (f32[5,33,512]{2,1,0:T(8,128)S(1)}, f32[5,33,512]{2,1,0:T(8,128)S(1)}, u32[]{:S(2)}, u32[]{:S(2)}) collective-permute-start(f32[5,33,512]{2,1,0:T(8,128)S(1)} %fusion.17), channel_id=1, source_target_pairs={{0,16},{16,32},{32,48},{48,64},{64,80},{80,96},{96,112},{112,0},{1... | collective-permute-start | bytes 1013768 | tf_op jit(solution)/shard_map/ppermute | solution.py:49
  227.7 8.6 %collective-permute-start.12 = (f32[5,33,512]{2,1,0:T(8,128)S(1)}, f32[5,33,512]{2,1,0:T(8,128)S(1)}, u32[]{:S(2)}, u32[]{:S(2)}) collective-permute-start(f32[5,33,512]{2,1,0:T(8,128)S(1)} %fusion.18), channel_id=1, source_target_pairs={{0,16},{16,32},{32,48},{48,64},{64,80},{80,96},{96,112},{112,0},{1... | collective-permute-start | bytes 1013768 | tf_op jit(solution)/shard_map/ppermute | solution.py:49
  236.4 8.6 %collective-permute-start.13 = (f32[5,33,512]{2,1,0:T(8,128)S(1)}, f32[5,33,512]{2,1,0:T(8,128)S(1)}, u32[]{:S(2)}, u32[]{:S(2)}) collective-permute-start(f32[5,33,512]{2,1,0:T(8,128)S(1)} %fusion.19), channel_id=1, source_target_pairs={{0,16},{16,32},{32,48},{48,64},{64,80},{80,96},{96,112},{112,0},{1... | collective-permute-start | bytes 1013768 | tf_op jit(solution)/shard_map/ppermute | solution.py:49
Sparse Core Ops, SparseCore 0:
  10.2 58.9 all-gather.3
  122.9 87.9 reduce-scatter.1

commit v3 on v2

--- a/solution.py
+++ b/solution.py
@@ -36,20 +36,31 @@
     return parts
 
 
-def ring_reduce_scatter(chunk, extra, axis, size, width):
-    forward = [(i, (i + 1) % size) for i in range(size)]
-    backward = [(i, (i - 1) % size) for i in range(size)]
+def two_stage_reduce_scatter(grad_cols, extra, axis, size, shard_rows):
+    pair_count, _, width = grad_cols.shape
+    own = lax.axis_index(axis)
+    parity = own % 2
+    chips = size // 2
+    by_chip = grad_cols.reshape(pair_count, chips, 2, shard_rows, width)
+    keep = lax.dynamic_index_in_dim(by_chip, parity, axis=2, keepdims=False)
+    send = lax.dynamic_index_in_dim(by_chip, 1 - parity, axis=2, keepdims=False)
+    body_rows = pair_count * chips * shard_rows
+    send = jnp.concatenate([send.reshape(body_rows, width), extra], axis=0)
+    got = lax.ppermute(send, axis, [(i, i ^ 1) for i in range(size)])
+    summed = keep + got[:body_rows].reshape(pair_count, chips, shard_rows, width)
+    carried = extra + got[body_rows:]
+    chip = own // 2
+    ring = [(i, (i + 2) % size) for i in range(size)]
+    chunk_rows = pair_count * shard_rows
 
-    def ahead_part(q):
-        return jnp.concatenate([chunk(q, True), extra], axis=1)
+    def addend(target):
+        block = lax.dynamic_index_in_dim(summed, target % chips, axis=1, keepdims=False)
+        return jnp.concatenate([block.reshape(chunk_rows, width), carried], axis=0)
 
-    ahead = ahead_part(ring_position(-1, size))
-    behind = chunk(ring_position(1, size), False)
-    for step in range(1, size):
-        ahead = lax.ppermute(ahead, axis, forward) + ahead_part(ring_position(-1 - step, size))
-        behind = lax.ppermute(behind, axis, backward) + chunk(ring_position(1 + step, size), False)
-    rows = behind.shape[1]
-    return jnp.concatenate([ahead[:, :rows], behind], axis=2), ahead[:, rows]
+    running = addend(chip - 1)
+    for step in range(1, chips):
+        running = lax.ppermute(running, axis, ring) + addend(chip - 1 - step)
+    return running[:chunk_rows].reshape(pair_count, shard_rows, width), running[chunk_rows]
 
 
 def per_device(anchor, partner, counts, pair_scale):
@@ -69,11 +80,11 @@
 
     row_set = lax.all_gather(anchor, "pair", axis=1, tiled=True)
     col_set = jnp.concatenate(ring_gather(partner, "dp", dp_size), axis=1)
+    col_set = jnp.roll(col_set, (dp_index - dp_size // 2) * shard_rows, axis=1)
     row_count = row_set.shape[1]
     col_count = col_set.shape[1]
     row_global = dp_index * row_count + jnp.arange(row_count, dtype=jnp.int32)
-    col_owner = (dp_index + jnp.arange(dp_size, dtype=jnp.int32) - dp_size // 2) % dp_size
-    col_first = (col_owner * pair_size + pair_place) * shard_rows
+    col_first = (jnp.arange(dp_size, dtype=jnp.int32) * pair_size + pair_place) * shard_rows
     col_global = (col_first[:, None] + offsets[None, :]).reshape(-1)
     row_valid = row_global[None, :] < counts[:, None]
     col_valid = col_global[None, :] < counts[:, None]
@@ -89,12 +100,8 @@
     col_high = jnp.max(masked, axis=1)
     col_sum = jnp.sum(jnp.where(inside, jnp.exp(masked - col_high[:, None, :]), 0.0), axis=1)
 
-    col_stats = jnp.stack([col_high, col_sum]).reshape(2, pair_count, dp_size, shard_rows)
-    col_stats = jnp.roll(col_stats, dp_index - dp_size // 2, axis=2)
-    col_stats = lax.all_gather(col_stats, "dp")
+    col_stats = lax.all_gather(jnp.stack([col_high, col_sum]), "dp")
     col_high, col_sum = merge_gathered(col_stats[:, 0], col_stats[:, 1])
-    col_high = jnp.roll(col_high, dp_size // 2 - dp_index, axis=1).reshape(pair_count, col_count)
-    col_sum = jnp.roll(col_sum, dp_size // 2 - dp_index, axis=1).reshape(pair_count, col_count)
     col_lse = jnp.where(col_valid, col_high + jnp.log(jnp.where(col_valid, col_sum, 1.0)), 0.0)
 
     lanes = jnp.arange(row_count, dtype=jnp.int32)[None, :]
@@ -120,17 +127,14 @@
     )
     anchor_part = lax.psum_scatter(grad_rows, "pair", scatter_dimension=1, tiled=True)
 
-    half = model_width // 2
+    width_lanes = jnp.arange(model_width, dtype=jnp.int32)[None, :]
+    slots = (jnp.arange(pair_count, dtype=jnp.int32) * dp_size + dp_index)[:, None]
+    loss_row = jnp.sum(jnp.where(width_lanes == slots, row_part[:, None], 0.0), axis=0)
+    extra = jnp.concatenate([loss_row[None], jnp.zeros((7, model_width), jnp.float32)], axis=0)
+    partner_part, loss_row = two_stage_reduce_scatter(grad_cols, extra, "dp", dp_size, shard_rows)
+    row_parts = loss_row[: pair_count * dp_size].reshape(pair_count, dp_size)
 
-    def col_chunk(q, lo):
-        block = grad_cols[:, q * shard_rows:(q + 1) * shard_rows]
-        return block[:, :, :half] if lo else block[:, :, half:]
-
-    width_lanes = jnp.arange(half, dtype=jnp.int32)[None, :]
-    extra = jnp.where(width_lanes == dp_index, row_part[:, None], 0.0)[:, None, :]
-    partner_part, row_parts = ring_reduce_scatter(col_chunk, extra, "dp", dp_size, half)
-
-    totals = carried[:, 0] + jnp.sum(row_parts[:, :dp_size], axis=1)
+    totals = carried[:, 0] + jnp.sum(row_parts, axis=1)
     loss_value = jnp.sum(totals / (2.0 * counts.astype(jnp.float32))) / pair_count
 
     own_term = (pair_scale * score_scale)[:, None, None]

time: 257 us -> 222 us (0.86)
  waiting for transfers between devices: 136 us -> 109 us
  starting transfers between devices: 28.9 us -> 10.8 us
  local copies, waits for them, and re-layouts: 6.56 us -> 17.8 us
    ppermute x14 -> x4, waiting for transfers between devices: 92.2 us -> 57.6 us  [the longest x3 52.5 us: two_stage_reduce_scatter(): running = lax.ppermute(running, axis, ring) + addend(chip - 1 - step)]
    ppermute x14 -> x4, starting transfers between devices: 20.6 us -> 1.41 us  [the longest x3 1.41 us: two_stage_reduce_scatter(): running = lax.ppermute(running, axis, ring) + addend(chip - 1 - step)]
    reduce_scatter x1, waiting for transfers between devices: 0.02 us -> 14.9 us  [per_device(): lax.psum_scatter(grad_rows, 'pair', scatter_dimension=1, tiled=True)]
    unnamed x18 -> x27, local copies, waits for them, and re-layouts: 5.27 us -> 14.1 us
    all_gather x1, waiting for transfers between devices: 21.8 us -> 18 us  [per_device(): row_set = lax.all_gather(anchor, 'pair', axis=1, tiled=True)]
    ppermute x4, waiting for transfers between devices: 20.8 us -> 17.4 us  [ring_gather(): ahead = lax.ppermute(ahead, axis, forward)]
  transfers between devices with their start and end apart: 23 -> 13, of which waited for: 19 -> 10; matrix products, arithmetic and copies ran while one was open for 8% -> 13% of each run, Pallas kernels for 0% -> 0%
where the time goes in v3:
time: 222 us
  waiting for transfers between devices  109 us (49%)
  blocking collectives  37.1 us (17%)
  matrix products  18.3 us (8%)
  local copies, waits for them, and re-layouts  17.8 us (8%)
  between operations  16.1 us (7%)
  other arithmetic  13.3 us (6%)
  starting transfers between devices  10.8 us (5%)
    ppermute x3, waiting for transfers between devices, two_stage_reduce_scatter(): running = lax.ppermute(running, axis, ring) + addend(chip - 1 - step)  52.5 us
    all_gather x1, blocking collectives, per_device(): row_stats = lax.all_gather(jnp.stack([row_high, row_sum, carried]), 'pair')  24 us
    all_gather x1, waiting for transfers between devices, per_device(): row_set = lax.all_gather(anchor, 'pair', axis=1, tiled=True)  18 us
    ppermute x4, waiting for transfers between devices, ring_gather(): ahead = lax.ppermute(ahead, axis, forward)  17.4 us
    reduce_scatter x1, waiting for transfers between devices, per_device(): lax.psum_scatter(grad_rows, 'pair', scatter_dimension=1, tiled=True)  14.9 us
    unnamed x27, local copies, waits for them, and re-layouts  14.1 us
    all_gather x1, blocking collectives, per_device(): col_stats = lax.all_gather(jnp.stack([col_high, col_sum]), 'dp')  13.1 us
    ppermute x3, starting transfers between devices, ring_gather(): behind = lax.ppermute(behind, axis, backward)  9.24 us
  transfers between devices with their start and end apart: 13, of which 10 were waited for; matrix products, arithmetic and copies ran while one was open for 13% of the time, Pallas kernels for 0%

profile of v3, /device:TPU:0, one launch (start us, length us, event | category | flops | bytes accessed | tf_op | source)
XLA Modules:
  0.0 221.9 jit_solution(4666514464861566300)
XLA Ops:
  7.2 0.7 all-gather.4.cloned.1.call-update
  8.0 2.9 %collective-permute-start.4 = (bf16[5,32,1024]{2,1,0:T(8,128)(2,1)}, bf16[5,32,1024]{2,1,0:T(8,128)(2,1)S(1)}, u32[]{:S(2)}, u32[]{:S(2)}) collective-permute-start(bf16[5,32,1024]{2,1,0:T(8,128)(2,1)} %param.5), channel_id=1, source_target_pairs={{0,112},{16,0},{32,16},{48,32},{64,48},{80,64},{96,80},{112,96},{1... | collective-permute-start | bytes 983048 | tf_op jit(solution)/shard_map/ppermute | solution.py:34
  11.1 1.2 fusion.17
  12.3 3.6 %collective-permute-done = bf16[5,32,1024]{2,1,0:T(8,128)(2,1)S(1)} collective-permute-done((bf16[5,32,1024]{2,1,0:T(8,128)(2,1)}, bf16[5,32,1024]{2,1,0:T(8,128)(2,1)S(1)}, u32[]{:S(2)}, u32[]{:S(2)}) %collective-permute-start) | collective-permute-done | bytes 327712 | tf_op jit(solution)/shard_map/ppermute | solution.py:31
  15.9 0.8 select_reduce_fusion.1
  17.4 6.2 %collective-permute-done.1 = bf16[5,32,1024]{2,1,0:T(8,128)(2,1)S(1)} collective-permute-done((bf16[5,32,1024]{2,1,0:T(8,128)(2,1)S(1)}, bf16[5,32,1024]{2,1,0:T(8,128)(2,1)S(1)}, u32[]{:S(2)}, u32[]{:S(2)}) %collective-permute-start.1) | collective-permute-done | bytes 327712 | tf_op jit(solution)/shard_map/ppermute | solution.py:31
  23.6 0.7 broadcast_compare_fusion.1
  24.3 3.0 %collective-permute-start.5 = (bf16[5,32,1024]{2,1,0:T(8,128)(2,1)S(1)}, bf16[5,32,1024]{2,1,0:T(8,128)(2,1)S(1)}, u32[]{:S(2)}, u32[]{:S(2)}) collective-permute-start(bf16[5,32,1024]{2,1,0:T(8,128)(2,1)S(1)} %collective-permute-done.4), channel_id=1, source_target_pairs={{0,112},{16,0},{32,16},{48,32},{64,48},{80,64},{96,80},{112,96},{1... | collective-permute-start | bytes 983048 | tf_op jit(solution)/shard_map/ppermute | solution.py:34
  27.3 4.0 %collective-permute-done.2 = bf16[5,32,1024]{2,1,0:T(8,128)(2,1)S(1)} collective-permute-done((bf16[5,32,1024]{2,1,0:T(8,128)(2,1)S(1)}, bf16[5,32,1024]{2,1,0:T(8,128)(2,1)S(1)}, u32[]{:S(2)}, u32[]{:S(2)}) %collective-permute-start.2) | collective-permute-done | bytes 327712 | tf_op jit(solution)/shard_map/ppermute | solution.py:31
  31.3 0.7 broadcast_compare_fusion
  32.1 3.4 %collective-permute-start.6 = (bf16[5,32,1024]{2,1,0:T(8,128)(2,1)S(1)}, bf16[5,32,1024]{2,1,0:T(8,128)(2,1)S(1)}, u32[]{:S(2)}, u32[]{:S(2)}) collective-permute-start(bf16[5,32,1024]{2,1,0:T(8,128)(2,1)S(1)} %collective-permute-done.5), channel_id=1, source_target_pairs={{0,112},{16,0},{32,16},{48,32},{64,48},{80,64},{96,80},{112,96},{1... | collective-permute-start | bytes 983048 | tf_op jit(solution)/shard_map/ppermute | solution.py:34
  35.4 3.6 %collective-permute-done.3 = bf16[5,32,1024]{2,1,0:T(8,128)(2,1)S(1)} collective-permute-done((bf16[5,32,1024]{2,1,0:T(8,128)(2,1)S(1)}, bf16[5,32,1024]{2,1,0:T(8,128)(2,1)S(1)}, u32[]{:S(2)}, u32[]{:S(2)}) %collective-permute-start.3) | collective-permute-done | bytes 327712 | tf_op jit(solution)/shard_map/ppermute | solution.py:31
  39.0 0.8 constant_dynamic-update-slice_fusion.15
  39.8 0.7 constant_dynamic-update-slice_fusion.14
  40.5 0.7 constant_dynamic-update-slice_fusion.13
  41.3 0.8 constant_dynamic-update-slice_fusion.12
  42.0 0.7 constant_dynamic-update-slice_fusion.11
  42.8 0.8 constant_dynamic-update-slice_fusion.10
  43.6 0.7 constant_dynamic-update-slice_fusion.9
  44.3 0.8 constant_dynamic-update-slice_fusion.8
  45.1 0.7 constant_dynamic-update-slice_fusion.7
  45.8 0.7 constant_dynamic-update-slice_fusion.6
  46.6 0.8 constant_dynamic-update-slice_fusion.5
  47.3 0.8 constant_dynamic-update-slice_fusion.4
  48.1 0.8 constant_dynamic-update-slice_fusion.3
  48.9 0.8 constant_dynamic-update-slice_fusion.2
  49.6 0.8 constant_dynamic-update-slice_fusion.1
  50.4 0.8 constant_dynamic-update-slice_fusion
  51.2 18.0 %all-gather.4.cloned.1.call-done = bf16[5,512,1024]{2,1,0:T(8,128)(2,1)} async-done(((bf16[5,32,1024]{2,1,0:T(8,128)(2,1)}), bf16[5,512,1024]{2,1,0:T(8,128)(2,1)}) %all-gather.4.cloned.1.call-update) | async-done | bytes 5242896 | tf_op jit(solution)/shard_map/all_gather | solution.py:81
  69.1 5.2 %fusion.11 = (f32[5,512]{1,0:T(8,128)S(1)}, f32[5,256]{1,0:T(8,128)S(1)}, f32[5,256,512]{2,1,0:T(8,128)S(1)}) fusion(pred[5,256]{1,0:T(8,128)(4,1)S(1)} %broadcast_compare_fusion.1, pred[5,512]{1,0:T(8,128)(4,1)S(1)} %broadcast_compare_fusion, bf16[5,512,1024]{2,1,0:T(8,128)(2,1)} %all-gather.4.cloned.1.call-done, ...), kind=kOutput, calls=%fused_computation.26 | convolution fusion | flops 1345450240 | bytes 10504964 | tf_op jit(solution)/shard_map/prd,pcd->prc/dot_general | solution.py:94
  74.4 1.9 fusion
  76.3 13.1 %all-gather = f32[16,5,256]{2,1,0:T(8,128)S(1)} all-gather(f32[2,5,256]{2,1,0:T(8,128)S(1)} %pad_maximum_fusion.5), channel_id=2, replica_groups=mesh['dp'=8,'pair'=16] {'dp'}, dimensions={0}, use_global_device_ids=true | all-gather | bytes 92160 | tf_op jit(solution)/shard_map/all_gather | solution.py:103
  89.7 24.0 %all-gather.1 = f32[48,5,512]{2,1,0:T(8,128)S(1)} all-gather(f32[3,5,512]{2,1,0:T(8,128)S(1)} %pad_maximum_fusion.4), channel_id=3, replica_groups=mesh['dp'=8,'pair'=16] {'pair'}, dimensions={0}, use_global_device_ids=true | all-gather | bytes 522240 | tf_op jit(solution)/shard_map/all_gather | solution.py:111
  113.7 0.8 copy-done.3
  114.8 8.3 %broadcast_multiply_fusion = f32[5,512,1024]{2,1,0:T(8,128)} fusion(bf16[5,512,1024]{2,1,0:T(8,128)(2,1)} %constant_dynamic-update-slice_fusion, s32[]{:T(128)S(6)} %select_n.143, f32[5,256,512]{2,1,0:T(8,128)S(1)} %get-tuple-element.21, f32[5,256]{1,0:T(8,128)S(1)} %get-tuple-element.12, f32[5,512]{1,0:T(8,128)S(1)} %get-tuple-element.10, ...), kind=kOutput, calls=%fused_computation.5 | convolution fusion | flops 1350696960 | bytes 15747864 | tf_op jit(solution)/shard_map/prc,pcd->prd/dot_general | solution.py:121
  123.3 1.0 slice_reduce_fusion
  124.6 4.8 %broadcast_multiply_fusion.1 = f32[5,256,1024]{2,1,0:T(8,128)S(1)} fusion(bf16[5,512,1024]{2,1,0:T(8,128)(2,1)} %all-gather.4.cloned.1.call-done, f32[5,256,512]{2,1,0:T(8,128)S(1)} %get-tuple-element.21, f32[5,256]{1,0:T(8,128)S(1)} %get-tuple-element.12, f32[5,512]{1,0:T(8,128)S(1)} %get-tuple-element.10, f32[5]{0:T(128)S(1)} %get-tuple-element.20, ...), kind=kOutput, calls=%fused_computation.17 | convolution fusion | flops 1349386240 | bytes 13126420 | tf_op jit(solution)/shard_map/prc,prd->pcd/dot_general | solution.py:125
  129.9 1.9 copy-done
  131.8 5.1 %collective-permute-done.7 = f32[648,1024]{1,0:T(8,128)} collective-permute-done((f32[648,1024]{1,0:T(8,128)S(1)}, f32[648,1024]{1,0:T(8,128)}, u32[]{:S(2)}, u32[]{:S(2)}) %collective-permute-start.7) | collective-permute-done | bytes 2654240 | tf_op jit(solution)/shard_map/ppermute | solution.py:49
  136.9 2.1 slice.54
  139.0 0.8 bitcast_add_fusion
  140.0 0.8 slice_add_fusion
  140.8 1.3 collective-permute-start.8
  142.0 17.5 %collective-permute-done.8 = f32[168,1024]{1,0:T(8,128)S(1)} collective-permute-done((f32[168,1024]{1,0:T(8,128)S(1)}, f32[168,1024]{1,0:T(8,128)S(1)}, u32[]{:S(2)}, u32[]{:S(2)}) %collective-permute-start.8) | collective-permute-done | bytes 688160 | tf_op jit(solution)/shard_map/ppermute | solution.py:62
  159.7 18.0 %collective-permute-done.9 = f32[168,1024]{1,0:T(8,128)S(1)} collective-permute-done((f32[168,1024]{1,0:T(8,128)S(1)}, f32[168,1024]{1,0:T(8,128)S(1)}, u32[]{:S(2)}, u32[]{:S(2)}) %collective-permute-start.9) | collective-permute-done | bytes 688160 | tf_op jit(solution)/shard_map/ppermute | solution.py:62
  177.9 17.1 %collective-permute-done.10 = f32[168,1024]{1,0:T(8,128)S(1)} collective-permute-done((f32[168,1024]{1,0:T(8,128)S(1)}, f32[168,1024]{1,0:T(8,128)S(1)}, u32[]{:S(2)}, u32[]{:S(2)}) %collective-permute-start.10) | collective-permute-done | bytes 688160 | tf_op jit(solution)/shard_map/ppermute | solution.py:62
  196.6 14.9 %reduce-scatter.2.cloned.1.call-done = f32[5,32,1024]{2,1,0:T(8,128)} async-done(((f32[5,512,1024]{2,1,0:T(8,128)}), f32[5,32,1024]{2,1,0:T(8,128)}) %reduce-scatter.2.cloned.1.call-update) | async-done | bytes 655376 | tf_op jit(solution)/shard_map/reduce_scatter | solution.py:128
  211.6 2.4 %fusion.16 = (f32[5,32,1024]{2,1,0:T(8,128)}, f32[5,32,1024]{2,1,0:T(8,128)}) fusion(f32[5,32,1024]{2,1,0:T(8,128)S(1)} %bitcast.81, bf16[5,32,1024]{2,1,0:T(8,128)(2,1)S(1)} %copy-done.4, f32[5]{0:T(128)S(1)} %get-tuple-element.19, pred[5,32]{1,0:T(8,128)(4,1)S(1)} %broadcast_compare_fusion.2, f32[5,32,1024]{2,1,0:T(8,128)} %reduce-scatter.2.cloned.1.call-done, ...), kind=kLoop, calls=%fused_computation.34 | loop fusion | flops 1310720 | bytes 3276980 | tf_op jit(solution)/shard_map/jit(_where)/select_n | solution.py:143
  (58 shorter events, 4.1 us)
Async XLA Ops:
  7.2 34.9 %copy-start.2 = (bf16[5,32,1024]{2,1,0:T(8,128)(2,1)S(1)}, bf16[5,32,1024]{2,1,0:T(8,128)(2,1)}, u32[]{:S(2)}) copy-start(bf16[5,32,1024]{2,1,0:T(8,128)(2,1)} %param.5) | copy-start | bytes 983044
  7.2 62.0 %all-gather.4.cloned.1.call-start = ((), (), s32[]{:S(2)}) async-start(), calls=%async_computation.1 | async-start | bytes 5570560 | tf_op jit(solution)/shard_map/all_gather | solution.py:81
  7.9 203.6 %reduce-scatter.2.cloned.1.call-start = ((), (), s32[]{:S(2)}) async-start(), calls=%async_computation.2 | async-start | bytes 11141120 | tf_op jit(solution)/shard_map/reduce_scatter | solution.py:128
  8.0 7.9 %collective-permute-start = (bf16[5,32,1024]{2,1,0:T(8,128)(2,1)}, bf16[5,32,1024]{2,1,0:T(8,128)(2,1)S(1)}, u32[]{:S(2)}, u32[]{:S(2)}) collective-permute-start(bf16[5,32,1024]{2,1,0:T(8,128)(2,1)} %param.5), channel_id=1, source_target_pairs={{0,16},{16,32},{32,48},{48,64},{64,80},{80,96},{96,112},{112,0},{1... | collective-permute-start | bytes 983048 | tf_op jit(solution)/shard_map/ppermute | solution.py:31
  8.0 16.4 %collective-permute-start.4 = (bf16[5,32,1024]{2,1,0:T(8,128)(2,1)}, bf16[5,32,1024]{2,1,0:T(8,128)(2,1)S(1)}, u32[]{:S(2)}, u32[]{:S(2)}) collective-permute-start(bf16[5,32,1024]{2,1,0:T(8,128)(2,1)} %param.5), channel_id=1, source_target_pairs={{0,112},{16,0},{32,16},{48,32},{64,48},{80,64},{96,80},{112,96},{1... | collective-permute-start | bytes 983048 | tf_op jit(solution)/shard_map/ppermute | solution.py:34
  15.9 7.7 %collective-permute-start.1 = (bf16[5,32,1024]{2,1,0:T(8,128)(2,1)S(1)}, bf16[5,32,1024]{2,1,0:T(8,128)(2,1)S(1)}, u32[]{:S(2)}, u32[]{:S(2)}) collective-permute-start(bf16[5,32,1024]{2,1,0:T(8,128)(2,1)S(1)} %collective-permute-done), channel_id=1, source_target_pairs={{0,16},{16,32},{32,48},{48,64},{64,80},{80,96},{96,112},{112,0},{1... | collective-permute-start | bytes 983048 | tf_op jit(solution)/shard_map/ppermute | solution.py:31
  23.6 7.7 %collective-permute-start.2 = (bf16[5,32,1024]{2,1,0:T(8,128)(2,1)S(1)}, bf16[5,32,1024]{2,1,0:T(8,128)(2,1)S(1)}, u32[]{:S(2)}, u32[]{:S(2)}) collective-permute-start(bf16[5,32,1024]{2,1,0:T(8,128)(2,1)S(1)} %collective-permute-done.1), channel_id=1, source_target_pairs={{0,16},{16,32},{32,48},{48,64},{64,80},{80,96},{96,112},{112,0},{1... | collective-permute-start | bytes 983048 | tf_op jit(solution)/shard_map/ppermute | solution.py:31
  24.3 7.7 %collective-permute-start.5 = (bf16[5,32,1024]{2,1,0:T(8,128)(2,1)S(1)}, bf16[5,32,1024]{2,1,0:T(8,128)(2,1)S(1)}, u32[]{:S(2)}, u32[]{:S(2)}) collective-permute-start(bf16[5,32,1024]{2,1,0:T(8,128)(2,1)S(1)} %collective-permute-done.4), channel_id=1, source_target_pairs={{0,112},{16,0},{32,16},{48,32},{64,48},{80,64},{96,80},{112,96},{1... | collective-permute-start | bytes 983048 | tf_op jit(solution)/shard_map/ppermute | solution.py:34
  31.3 7.7 %collective-permute-start.3 = (bf16[5,32,1024]{2,1,0:T(8,128)(2,1)S(1)}, bf16[5,32,1024]{2,1,0:T(8,128)(2,1)S(1)}, u32[]{:S(2)}, u32[]{:S(2)}) collective-permute-start(bf16[5,32,1024]{2,1,0:T(8,128)(2,1)S(1)} %collective-permute-done.2), channel_id=1, source_target_pairs={{0,16},{16,32},{32,48},{48,64},{64,80},{80,96},{96,112},{112,0},{1... | collective-permute-start | bytes 983048 | tf_op jit(solution)/shard_map/ppermute | solution.py:31
  32.1 12.3 %collective-permute-start.6 = (bf16[5,32,1024]{2,1,0:T(8,128)(2,1)S(1)}, bf16[5,32,1024]{2,1,0:T(8,128)(2,1)S(1)}, u32[]{:S(2)}, u32[]{:S(2)}) collective-permute-start(bf16[5,32,1024]{2,1,0:T(8,128)(2,1)S(1)} %collective-permute-done.5), channel_id=1, source_target_pairs={{0,112},{16,0},{32,16},{48,32},{64,48},{80,64},{96,80},{112,96},{1... | collective-permute-start | bytes 983048 | tf_op jit(solution)/shard_map/ppermute | solution.py:34
  74.3 15.0 %copy-start.5 = (s32[5]{0:T(128)S(1)}, s32[5]{0:T(128)}, u32[]{:S(2)}) copy-start(s32[5]{0:T(128)} %param.6) | copy-start | bytes 64
  113.7 0.9 copy-start.3
  129.4 2.4 %copy-start = (f32[5,256,1024]{2,1,0:T(8,128)}, f32[5,256,1024]{2,1,0:T(8,128)S(1)}, u32[]{:S(2)}) copy-start(f32[5,256,1024]{2,1,0:T(8,128)S(1)} %broadcast_multiply_fusion.1) | copy-start | bytes 15728644
  131.8 5.1 %collective-permute-start.7 = (f32[648,1024]{1,0:T(8,128)S(1)}, f32[648,1024]{1,0:T(8,128)}, u32[]{:S(2)}, u32[]{:S(2)}) collective-permute-start(f32[648,1024]{1,0:T(8,128)S(1)} %maximum_maximum_fusion), channel_id=1, source_target_pairs={{0,16},{16,0},{32,48},{48,32},{64,80},{80,64},{96,112},{112,96},{1... | collective-permute-start | bytes 7962632 | tf_op jit(solution)/shard_map/ppermute | solution.py:49
  131.8 7.2 %copy-start.1 = (f32[5,256,1024]{2,1,0:T(8,128)S(1)}, f32[5,256,1024]{2,1,0:T(8,128)}, u32[]{:S(2)}) copy-start(f32[5,256,1024]{2,1,0:T(8,128)} %copy-done) | copy-start | bytes 15728644
  140.8 18.8 %collective-permute-start.8 = (f32[168,1024]{1,0:T(8,128)S(1)}, f32[168,1024]{1,0:T(8,128)S(1)}, u32[]{:S(2)}, u32[]{:S(2)}) collective-permute-start(f32[168,1024]{1,0:T(8,128)S(1)} %pad_maximum_fusion.3), channel_id=1, source_target_pairs={{0,32},{16,48},{32,64},{48,80},{64,96},{80,112},{96,0},{112,16},{1... | collective-permute-start | bytes 2064392 | tf_op jit(solution)/shard_map/ppermute | solution.py:62
  159.6 18.0 %collective-permute-start.9 = (f32[168,1024]{1,0:T(8,128)S(1)}, f32[168,1024]{1,0:T(8,128)S(1)}, u32[]{:S(2)}, u32[]{:S(2)}) collective-permute-start(f32[168,1024]{1,0:T(8,128)S(1)} %fusion.12), channel_id=1, source_target_pairs={{0,32},{16,48},{32,64},{48,80},{64,96},{80,112},{96,0},{112,16},{1... | collective-permute-start | bytes 2064392 | tf_op jit(solution)/shard_map/ppermute | solution.py:62
  177.7 33.9 %copy-start.4 = (bf16[5,32,1024]{2,1,0:T(8,128)(2,1)S(1)}, bf16[5,32,1024]{2,1,0:T(8,128)(2,1)}, u32[]{:S(2)}) copy-start(bf16[5,32,1024]{2,1,0:T(8,128)(2,1)} %param.4) | copy-start | bytes 983044
  177.8 17.2 %collective-permute-start.10 = (f32[168,1024]{1,0:T(8,128)S(1)}, f32[168,1024]{1,0:T(8,128)S(1)}, u32[]{:S(2)}, u32[]{:S(2)}) collective-permute-start(f32[168,1024]{1,0:T(8,128)S(1)} %fusion.13), channel_id=1, source_target_pairs={{0,32},{16,48},{32,64},{48,80},{64,96},{80,112},{96,0},{112,16},{1... | collective-permute-start | bytes 2064392 | tf_op jit(solution)/shard_map/ppermute | solution.py:62
Sparse Core Ops, SparseCore 0:
  10.2 58.9 all-gather.3
  123.2 88.2 reduce-scatter.1

commit v4 on v3

--- a/solution.py
+++ b/solution.py
@@ -8,10 +8,21 @@
 NEG = -1e30
 
 
-def merge_gathered(highs, sums):
-    highest = jnp.max(highs, axis=0)
-    summed = jnp.sum(sums * jnp.exp(highs - highest[None]), axis=0)
-    return highest, summed
+def merge_pair(mine, other):
+    highest = jnp.maximum(mine[0], other[0])
+    summed = mine[1] * jnp.exp(mine[0] - highest) + other[1] * jnp.exp(other[0] - highest)
+    return jnp.concatenate([highest[None], summed[None], mine[2:] + other[2:]], axis=0)
+
+
+def butterfly_merge(stats, axis, size):
+    own = lax.axis_index(axis)
+    bit = 1
+    while bit < size:
+        other = lax.ppermute(stats, axis, [(i, i ^ bit) for i in range(size)])
+        lower = (own & bit) == 0
+        stats = merge_pair(jnp.where(lower, stats, other), jnp.where(lower, other, stats))
+        bit *= 2
+    return stats
 
 
 def ring_position(offset, size):
@@ -100,17 +111,16 @@
     col_high = jnp.max(masked, axis=1)
     col_sum = jnp.sum(jnp.where(inside, jnp.exp(masked - col_high[:, None, :]), 0.0), axis=1)
 
-    col_stats = lax.all_gather(jnp.stack([col_high, col_sum]), "dp")
-    col_high, col_sum = merge_gathered(col_stats[:, 0], col_stats[:, 1])
+    col_stats = butterfly_merge(jnp.stack([col_high, col_sum]), "dp", dp_size)
+    col_high, col_sum = col_stats[0], col_stats[1]
     col_lse = jnp.where(col_valid, col_high + jnp.log(jnp.where(col_valid, col_sum, 1.0)), 0.0)
 
     lanes = jnp.arange(row_count, dtype=jnp.int32)[None, :]
     col_total = jnp.sum(col_lse, axis=1)
     carried = jnp.where(lanes == 0, col_total[:, None], 0.0)
     carried = jnp.where(lanes == 1, own_positive[:, None], carried)
-    row_stats = lax.all_gather(jnp.stack([row_high, row_sum, carried]), "pair")
-    row_high, row_sum = merge_gathered(row_stats[:, 0], row_stats[:, 1])
-    carried = jnp.sum(row_stats[:, 2], axis=0)
+    row_stats = butterfly_merge(jnp.stack([row_high, row_sum, carried]), "pair", pair_size)
+    row_high, row_sum, carried = row_stats[0], row_stats[1], row_stats[2]
     row_lse = jnp.where(row_valid, row_high + jnp.log(jnp.where(row_valid, row_sum, 1.0)), 0.0)
     row_part = jnp.sum(row_lse, axis=1) - 2.0 * carried[:, 1]
 

time: 222 us -> 220 us (level)
  blocking collectives: 37.1 us -> 0 us
  waiting for transfers between devices: 109 us -> 126 us
  starting transfers between devices: 10.8 us -> 25.4 us
  local copies, waits for them, and re-layouts: 17.8 us -> 20.3 us
    all_gather x2 -> x0, blocking collectives: 37.1 us -> none  [the longest x1 24 us: per_device(): row_stats = lax.all_gather(jnp.stack([row_high, row_sum, carried]), 'pair')]
    ppermute x0 -> x7, starting transfers between devices: none -> 14.5 us  [butterfly_merge(): other = lax.ppermute(stats, axis, [(i, i ^ bit) for i in range(size)])]
    ppermute x0 -> x7, waiting for transfers between devices: none -> 14 us  [butterfly_merge(): other = lax.ppermute(stats, axis, [(i, i ^ bit) for i in range(size)])]
    unnamed x27 -> x31, local copies, waits for them, and re-layouts: 14.1 us -> 14.2 us
  transfers between devices with their start and end apart: 13 -> 20, of which waited for: 10 -> 17; matrix products, arithmetic and copies ran while one was open for 13% -> 13% of each run, Pallas kernels for 0% -> 0%
where the time goes in v4:
time: 220 us
  waiting for transfers between devices  126 us (57%)
  starting transfers between devices  25.4 us (12%)
  local copies, waits for them, and re-layouts  20.3 us (9%)
  matrix products  18.3 us (8%)
  between operations  16.2 us (7%)
  other arithmetic  13.8 us (6%)
    ppermute x3, waiting for transfers between devices, two_stage_reduce_scatter(): running = lax.ppermute(running, axis, ring) + addend(chip - 1 - step)  51.8 us
    ppermute x4, waiting for transfers between devices, ring_gather(): ahead = lax.ppermute(ahead, axis, forward)  19.1 us
    all_gather x1, waiting for transfers between devices, per_device(): row_set = lax.all_gather(anchor, 'pair', axis=1, tiled=True)  18.1 us
    reduce_scatter x1, waiting for transfers between devices, per_device(): lax.psum_scatter(grad_rows, 'pair', scatter_dimension=1, tiled=True)  16.8 us
    ppermute x7, starting transfers between devices, butterfly_merge(): other = lax.ppermute(stats, axis, [(i, i ^ bit) for i in range(size)])  14.5 us
    unnamed x31, local copies, waits for them, and re-layouts  14.2 us
    ppermute x7, waiting for transfers between devices, butterfly_merge(): other = lax.ppermute(stats, axis, [(i, i ^ bit) for i in range(size)])  14 us
    ppermute x3, starting transfers between devices, ring_gather(): behind = lax.ppermute(behind, axis, backward)  8.88 us
  transfers between devices with their start and end apart: 20, of which 17 were waited for; matrix products, arithmetic and copies ran while one was open for 13% of the time, Pallas kernels for 0%

profile of v4, /device:TPU:0, one launch (start us, length us, event | category | flops | bytes accessed | tf_op | source)
XLA Modules:
  0.0 219.6 jit_solution(9508400766800376050)
XLA Ops:
  8.0 2.9 %collective-permute-start.4 = (bf16[5,32,1024]{2,1,0:T(8,128)(2,1)}, bf16[5,32,1024]{2,1,0:T(8,128)(2,1)S(1)}, u32[]{:S(2)}, u32[]{:S(2)}) collective-permute-start(bf16[5,32,1024]{2,1,0:T(8,128)(2,1)} %param.5), channel_id=1, source_target_pairs={{0,112},{16,0},{32,16},{48,32},{64,48},{80,64},{96,80},{112,96},{1... | collective-permute-start | bytes 983048 | tf_op jit(solution)/shard_map/ppermute | solution.py:45
  10.9 5.0 %collective-permute-done = bf16[5,32,1024]{2,1,0:T(8,128)(2,1)S(1)} collective-permute-done((bf16[5,32,1024]{2,1,0:T(8,128)(2,1)}, bf16[5,32,1024]{2,1,0:T(8,128)(2,1)S(1)}, u32[]{:S(2)}, u32[]{:S(2)}) %collective-permute-start) | collective-permute-done | bytes 327712 | tf_op jit(solution)/shard_map/ppermute | solution.py:42
  16.1 7.5 %collective-permute-done.1 = bf16[5,32,1024]{2,1,0:T(8,128)(2,1)S(1)} collective-permute-done((bf16[5,32,1024]{2,1,0:T(8,128)(2,1)S(1)}, bf16[5,32,1024]{2,1,0:T(8,128)(2,1)S(1)}, u32[]{:S(2)}, u32[]{:S(2)}) %collective-permute-start.1) | collective-permute-done | bytes 327712 | tf_op jit(solution)/shard_map/ppermute | solution.py:42
  23.6 0.8 broadcast_compare_fusion
  24.5 3.0 %collective-permute-start.5 = (bf16[5,32,1024]{2,1,0:T(8,128)(2,1)S(1)}, bf16[5,32,1024]{2,1,0:T(8,128)(2,1)S(1)}, u32[]{:S(2)}, u32[]{:S(2)}) collective-permute-start(bf16[5,32,1024]{2,1,0:T(8,128)(2,1)S(1)} %collective-permute-done.4), channel_id=1, source_target_pairs={{0,112},{16,0},{32,16},{48,32},{64,48},{80,64},{96,80},{112,96},{1... | collective-permute-start | bytes 983048 | tf_op jit(solution)/shard_map/ppermute | solution.py:45
  27.5 3.8 %collective-permute-done.2 = bf16[5,32,1024]{2,1,0:T(8,128)(2,1)S(1)} collective-permute-done((bf16[5,32,1024]{2,1,0:T(8,128)(2,1)S(1)}, bf16[5,32,1024]{2,1,0:T(8,128)(2,1)S(1)}, u32[]{:S(2)}, u32[]{:S(2)}) %collective-permute-start.2) | collective-permute-done | bytes 327712 | tf_op jit(solution)/shard_map/ppermute | solution.py:42
  31.3 1.2 fusion.17
  33.3 3.0 %collective-permute-start.6 = (bf16[5,32,1024]{2,1,0:T(8,128)(2,1)S(1)}, bf16[5,32,1024]{2,1,0:T(8,128)(2,1)S(1)}, u32[]{:S(2)}, u32[]{:S(2)}) collective-permute-start(bf16[5,32,1024]{2,1,0:T(8,128)(2,1)S(1)} %collective-permute-done.5), channel_id=1, source_target_pairs={{0,112},{16,0},{32,16},{48,32},{64,48},{80,64},{96,80},{112,96},{1... | collective-permute-start | bytes 983048 | tf_op jit(solution)/shard_map/ppermute | solution.py:45
  36.3 2.8 %collective-permute-done.3 = bf16[5,32,1024]{2,1,0:T(8,128)(2,1)S(1)} collective-permute-done((bf16[5,32,1024]{2,1,0:T(8,128)(2,1)S(1)}, bf16[5,32,1024]{2,1,0:T(8,128)(2,1)S(1)}, u32[]{:S(2)}, u32[]{:S(2)}) %collective-permute-start.3) | collective-permute-done | bytes 327712 | tf_op jit(solution)/shard_map/ppermute | solution.py:42
  39.0 0.8 constant_dynamic-update-slice_fusion.15
  39.8 0.8 constant_dynamic-update-slice_fusion.14
  41.3 0.8 constant_dynamic-update-slice_fusion.12
  46.6 0.8 constant_dynamic-update-slice_fusion.5
  47.3 0.8 constant_dynamic-update-slice_fusion.4
  51.0 18.1 %all-gather.2.cloned.1.call-done = bf16[5,512,1024]{2,1,0:T(8,128)(2,1)} async-done(((bf16[5,32,1024]{2,1,0:T(8,128)(2,1)}), bf16[5,512,1024]{2,1,0:T(8,128)(2,1)}) %all-gather.2.cloned.1.call-update) | async-done | bytes 5242896 | tf_op jit(solution)/shard_map/all_gather | solution.py:92
  69.2 5.2 %fusion.11 = (f32[5,512]{1,0:T(8,128)S(1)}, f32[5,256]{1,0:T(8,128)S(1)}, f32[5,256,512]{2,1,0:T(8,128)S(1)}) fusion(pred[5,256]{1,0:T(8,128)(4,1)S(1)} %broadcast_compare_fusion.1, pred[5,512]{1,0:T(8,128)(4,1)S(1)} %copy.20, bf16[5,512,1024]{2,1,0:T(8,128)(2,1)} %all-gather.2.cloned.1.call-done, ...), kind=kOutput, calls=%fused_computation.26 | convolution fusion | flops 1345450240 | bytes 10504964 | tf_op jit(solution)/shard_map/prd,pcd->prc/dot_general | solution.py:105
  74.4 1.9 fusion
  76.4 1.2 collective-permute-done.7
  77.6 1.6 collective-permute-start.8
  79.3 2.1 collective-permute-done.8
  81.5 3.1 %collective-permute-start.9 = (f32[2,5,256]{2,1,0:T(8,128)S(1)}, f32[2,5,256]{2,1,0:T(8,128)S(1)}, u32[]{:S(2)}, u32[]{:S(2)}) collective-permute-start(f32[2,5,256]{2,1,0:T(8,128)S(1)} %pad_maximum_fusion.10), channel_id=1, source_target_pairs={{0,64},{16,80},{32,96},{48,112},{64,0},{80,16},{96,32},{112,48},{1... | collective-permute-start | bytes 30728 | tf_op jit(solution)/shard_map/ppermute | solution.py:21
  84.6 2.2 %collective-permute-done.9 = f32[2,5,256]{2,1,0:T(8,128)S(1)} collective-permute-done((f32[2,5,256]{2,1,0:T(8,128)S(1)}, f32[2,5,256]{2,1,0:T(8,128)S(1)}, u32[]{:S(2)}, u32[]{:S(2)}) %collective-permute-start.9) | collective-permute-done | bytes 10272 | tf_op jit(solution)/shard_map/ppermute | solution.py:21
  87.1 1.6 collective-permute-start.10
  88.7 2.5 %collective-permute-done.10 = f32[3,5,512]{2,0,1:T(4,128)S(1)} collective-permute-done((f32[3,5,512]{2,0,1:T(4,128)S(1)}, f32[3,5,512]{2,0,1:T(4,128)S(1)}, u32[]{:S(2)}, u32[]{:S(2)}) %collective-permute-start.10) | collective-permute-done | bytes 30752 | tf_op jit(solution)/shard_map/ppermute | solution.py:21
  91.3 3.1 %collective-permute-start.11 = (f32[3,5,512]{2,0,1:T(4,128)S(1)}, f32[3,5,512]{2,0,1:T(4,128)S(1)}, u32[]{:S(2)}, u32[]{:S(2)}) collective-permute-start(f32[3,5,512]{2,0,1:T(4,128)S(1)} %pad_maximum_fusion.5), channel_id=1, source_target_pairs={{0,2},{1,3},{2,0},{3,1},{4,6},{5,7},{6,4},{7,5},{8,10},{9,11},{10,... | collective-permute-start | bytes 92168 | tf_op jit(solution)/shard_map/ppermute | solution.py:21
  94.4 2.5 %collective-permute-done.11 = f32[3,5,512]{2,0,1:T(4,128)S(1)} collective-permute-done((f32[3,5,512]{2,0,1:T(4,128)S(1)}, f32[3,5,512]{2,0,1:T(4,128)S(1)}, u32[]{:S(2)}, u32[]{:S(2)}) %collective-permute-start.11) | collective-permute-done | bytes 30752 | tf_op jit(solution)/shard_map/ppermute | solution.py:21
  97.1 1.6 collective-permute-start.12
  98.7 2.5 %collective-permute-done.12 = f32[3,5,512]{2,0,1:T(4,128)S(1)} collective-permute-done((f32[3,5,512]{2,0,1:T(4,128)S(1)}, f32[3,5,512]{2,0,1:T(4,128)S(1)}, u32[]{:S(2)}, u32[]{:S(2)}) %collective-permute-start.12) | collective-permute-done | bytes 30752 | tf_op jit(solution)/shard_map/ppermute | solution.py:21
  101.3 3.6 %collective-permute-start.13 = (f32[3,5,512]{2,0,1:T(4,128)S(1)}, f32[3,5,512]{2,0,1:T(4,128)S(1)}, u32[]{:S(2)}, u32[]{:S(2)}) collective-permute-start(f32[3,5,512]{2,0,1:T(4,128)S(1)} %pad_maximum_fusion.7), channel_id=1, source_target_pairs={{0,8},{1,9},{2,10},{3,11},{4,12},{5,13},{6,14},{7,15},{8,0},{9,1},... | collective-permute-start | bytes 92168 | tf_op jit(solution)/shard_map/ppermute | solution.py:21
  104.9 1.2 copy.23
  106.1 1.0 collective-permute-done.13
  107.1 1.2 copy.24
  108.3 1.5 broadcast_select_fusion.1
  109.8 0.9 copy-done.3
  111.0 8.3 %broadcast_multiply_fusion = f32[5,512,1024]{2,1,0:T(8,128)} fusion(bf16[5,512,1024]{2,1,0:T(8,128)(2,1)} %constant_dynamic-update-slice_fusion, s32[]{:T(128)S(6)} %select_n.221, f32[5,256,512]{2,1,0:T(8,128)S(1)} %get-tuple-element.46, f32[5,256]{1,0:T(8,128)S(1)} %get-tuple-element.16, f32[5,512]{1,0:T(8,128)S(1)} %copy.27, f32[5]{0:T(128)S(1)} %get-tuple-element.45, ...), kind=kOutput, calls=%fused_computation.5 | convolution fusion | flops 1350696960 | bytes 15747864 | tf_op jit(solution)/shard_map/prc,pcd->prd/dot_general | solution.py:131
  119.4 1.1 fusion.27
  120.6 4.8 %broadcast_multiply_fusion.1 = f32[5,256,1024]{2,1,0:T(8,128)S(1)} fusion(bf16[5,512,1024]{2,1,0:T(8,128)(2,1)} %all-gather.2.cloned.1.call-done, f32[5,256,512]{2,1,0:T(8,128)S(1)} %get-tuple-element.46, f32[5,256]{1,0:T(8,128)S(1)} %get-tuple-element.16, f32[5,512]{1,0:T(8,128)S(1)} %copy.27, f32[5]{0:T(128)S(1)} %get-tuple-element.45, ...), kind=kOutput, calls=%fused_computation.17 | convolution fusion | flops 1349386240 | bytes 13126420 | tf_op jit(solution)/shard_map/prc,prd->pcd/dot_general | solution.py:135
  125.9 1.9 copy-done
  127.8 5.1 %collective-permute-done.14 = f32[648,1024]{1,0:T(8,128)} collective-permute-done((f32[648,1024]{1,0:T(8,128)S(1)}, f32[648,1024]{1,0:T(8,128)}, u32[]{:S(2)}, u32[]{:S(2)}) %collective-permute-start.14) | collective-permute-done | bytes 2654240 | tf_op jit(solution)/shard_map/ppermute | solution.py:60
  132.9 2.1 slice.223
  135.0 0.8 bitcast_add_fusion
  135.9 0.8 slice_add_fusion.1
  136.8 1.5 collective-permute-start.15
  138.3 17.2 %collective-permute-done.15 = f32[168,1024]{1,0:T(8,128)S(1)} collective-permute-done((f32[168,1024]{1,0:T(8,128)S(1)}, f32[168,1024]{1,0:T(8,128)S(1)}, u32[]{:S(2)}, u32[]{:S(2)}) %collective-permute-start.15) | collective-permute-done | bytes 688160 | tf_op jit(solution)/shard_map/ppermute | solution.py:73
  156.0 17.6 %collective-permute-done.16 = f32[168,1024]{1,0:T(8,128)S(1)} collective-permute-done((f32[168,1024]{1,0:T(8,128)S(1)}, f32[168,1024]{1,0:T(8,128)S(1)}, u32[]{:S(2)}, u32[]{:S(2)}) %collective-permute-start.16) | collective-permute-done | bytes 688160 | tf_op jit(solution)/shard_map/ppermute | solution.py:73
  173.8 17.0 %collective-permute-done.17 = f32[168,1024]{1,0:T(8,128)S(1)} collective-permute-done((f32[168,1024]{1,0:T(8,128)S(1)}, f32[168,1024]{1,0:T(8,128)S(1)}, u32[]{:S(2)}, u32[]{:S(2)}) %collective-permute-start.17) | collective-permute-done | bytes 688160 | tf_op jit(solution)/shard_map/ppermute | solution.py:73
  192.5 16.8 %reduce-scatter.2.cloned.1.call-done = f32[5,32,1024]{2,1,0:T(8,128)} async-done(((f32[5,512,1024]{2,1,0:T(8,128)}), f32[5,32,1024]{2,1,0:T(8,128)}) %reduce-scatter.2.cloned.1.call-update) | async-done | bytes 655376 | tf_op jit(solution)/shard_map/reduce_scatter | solution.py:138
  209.2 2.4 %fusion.16 = (f32[5,32,1024]{2,1,0:T(8,128)}, f32[5,32,1024]{2,1,0:T(8,128)}) fusion(f32[5,32,1024]{2,1,0:T(8,128)S(1)} %bitcast.125, bf16[5,32,1024]{2,1,0:T(8,128)(2,1)S(1)} %copy-done.5, f32[5]{0:T(128)S(1)} %get-tuple-element.44, pred[5,32]{1,0:T(8,128)(4,1)S(1)} %broadcast_compare_fusion.2, f32[5,32,1024]{2,1,0:T(8,128)} %reduce-scatter.2.cloned.1.call-done, ...), kind=kLoop, calls=%fused_computation.34 | loop fusion | flops 1310720 | bytes 3276980 | tf_op jit(solution)/shard_map/jit(_where)/select_n | solution.py:153
  (92 shorter events, 13.9 us)
Async XLA Ops:
  7.2 34.9 %copy-start.2 = (bf16[5,32,1024]{2,1,0:T(8,128)(2,1)S(1)}, bf16[5,32,1024]{2,1,0:T(8,128)(2,1)}, u32[]{:S(2)}) copy-start(bf16[5,32,1024]{2,1,0:T(8,128)(2,1)} %param.5) | copy-start | bytes 983044
  7.2 62.0 %all-gather.2.cloned.1.call-start = ((), (), s32[]{:S(2)}) async-start(), calls=%async_computation.1 | async-start | bytes 5570560 | tf_op jit(solution)/shard_map/all_gather | solution.py:92
  7.9 201.3 %reduce-scatter.2.cloned.1.call-start = ((), (), s32[]{:S(2)}) async-start(), calls=%async_computation.2 | async-start | bytes 11141120 | tf_op jit(solution)/shard_map/reduce_scatter | solution.py:138
  8.0 7.9 %collective-permute-start = (bf16[5,32,1024]{2,1,0:T(8,128)(2,1)}, bf16[5,32,1024]{2,1,0:T(8,128)(2,1)S(1)}, u32[]{:S(2)}, u32[]{:S(2)}) collective-permute-start(bf16[5,32,1024]{2,1,0:T(8,128)(2,1)} %param.5), channel_id=1, source_target_pairs={{0,16},{16,32},{32,48},{48,64},{64,80},{80,96},{96,112},{112,0},{1... | collective-permute-start | bytes 983048 | tf_op jit(solution)/shard_map/ppermute | solution.py:42
  8.0 16.5 %collective-permute-start.4 = (bf16[5,32,1024]{2,1,0:T(8,128)(2,1)}, bf16[5,32,1024]{2,1,0:T(8,128)(2,1)S(1)}, u32[]{:S(2)}, u32[]{:S(2)}) collective-permute-start(bf16[5,32,1024]{2,1,0:T(8,128)(2,1)} %param.5), channel_id=1, source_target_pairs={{0,112},{16,0},{32,16},{48,32},{64,48},{80,64},{96,80},{112,96},{1... | collective-permute-start | bytes 983048 | tf_op jit(solution)/shard_map/ppermute | solution.py:45
  15.9 7.7 %collective-permute-start.1 = (bf16[5,32,1024]{2,1,0:T(8,128)(2,1)S(1)}, bf16[5,32,1024]{2,1,0:T(8,128)(2,1)S(1)}, u32[]{:S(2)}, u32[]{:S(2)}) collective-permute-start(bf16[5,32,1024]{2,1,0:T(8,128)(2,1)S(1)} %collective-permute-done), channel_id=1, source_target_pairs={{0,16},{16,32},{32,48},{48,64},{64,80},{80,96},{96,112},{112,0},{1... | collective-permute-start | bytes 983048 | tf_op jit(solution)/shard_map/ppermute | solution.py:42
  23.6 7.7 %collective-permute-start.2 = (bf16[5,32,1024]{2,1,0:T(8,128)(2,1)S(1)}, bf16[5,32,1024]{2,1,0:T(8,128)(2,1)S(1)}, u32[]{:S(2)}, u32[]{:S(2)}) collective-permute-start(bf16[5,32,1024]{2,1,0:T(8,128)(2,1)S(1)} %collective-permute-done.1), channel_id=1, source_target_pairs={{0,16},{16,32},{32,48},{48,64},{64,80},{80,96},{96,112},{112,0},{1... | collective-permute-start | bytes 983048 | tf_op jit(solution)/shard_map/ppermute | solution.py:42
  24.5 8.8 %collective-permute-start.5 = (bf16[5,32,1024]{2,1,0:T(8,128)(2,1)S(1)}, bf16[5,32,1024]{2,1,0:T(8,128)(2,1)S(1)}, u32[]{:S(2)}, u32[]{:S(2)}) collective-permute-start(bf16[5,32,1024]{2,1,0:T(8,128)(2,1)S(1)} %collective-permute-done.4), channel_id=1, source_target_pairs={{0,112},{16,0},{32,16},{48,32},{64,48},{80,64},{96,80},{112,96},{1... | collective-permute-start | bytes 983048 | tf_op jit(solution)/shard_map/ppermute | solution.py:45
  31.3 7.7 %collective-permute-start.3 = (bf16[5,32,1024]{2,1,0:T(8,128)(2,1)S(1)}, bf16[5,32,1024]{2,1,0:T(8,128)(2,1)S(1)}, u32[]{:S(2)}, u32[]{:S(2)}) collective-permute-start(bf16[5,32,1024]{2,1,0:T(8,128)(2,1)S(1)} %collective-permute-done.2), channel_id=1, source_target_pairs={{0,16},{16,32},{32,48},{48,64},{64,80},{80,96},{96,112},{112,0},{1... | collective-permute-start | bytes 983048 | tf_op jit(solution)/shard_map/ppermute | solution.py:42
  33.3 11.0 %collective-permute-start.6 = (bf16[5,32,1024]{2,1,0:T(8,128)(2,1)S(1)}, bf16[5,32,1024]{2,1,0:T(8,128)(2,1)S(1)}, u32[]{:S(2)}, u32[]{:S(2)}) collective-permute-start(bf16[5,32,1024]{2,1,0:T(8,128)(2,1)S(1)} %collective-permute-done.5), channel_id=1, source_target_pairs={{0,112},{16,0},{32,16},{48,32},{64,48},{80,64},{96,80},{112,96},{1... | collective-permute-start | bytes 983048 | tf_op jit(solution)/shard_map/ppermute | solution.py:45
  74.3 4.8 %copy-start.6 = (s32[5]{0:T(128)S(1)}, s32[5]{0:T(128)}, u32[]{:S(2)}) copy-start(s32[5]{0:T(128)} %param.6) | copy-start | bytes 64
  74.4 30.5 %copy-start.7 = (f32[5]{0:T(128)S(1)}, f32[5]{0:T(128)}, u32[]{:S(2)}) copy-start(f32[5]{0:T(128)} %param.7) | copy-start | bytes 64
  76.3 1.3 collective-permute-start.7
  77.6 3.8 %collective-permute-start.8 = (f32[2,5,256]{2,1,0:T(8,128)S(1)}, f32[2,5,256]{2,1,0:T(8,128)S(1)}, u32[]{:S(2)}, u32[]{:S(2)}) collective-permute-start(f32[2,5,256]{2,1,0:T(8,128)S(1)} %pad_maximum_fusion.9), channel_id=1, source_target_pairs={{0,32},{16,48},{32,0},{48,16},{64,96},{80,112},{96,64},{112,80},{1... | collective-permute-start | bytes 30728 | tf_op jit(solution)/shard_map/ppermute | solution.py:21
  81.5 5.3 %collective-permute-start.9 = (f32[2,5,256]{2,1,0:T(8,128)S(1)}, f32[2,5,256]{2,1,0:T(8,128)S(1)}, u32[]{:S(2)}, u32[]{:S(2)}) collective-permute-start(f32[2,5,256]{2,1,0:T(8,128)S(1)} %pad_maximum_fusion.10), channel_id=1, source_target_pairs={{0,64},{16,80},{32,96},{48,112},{64,0},{80,16},{96,32},{112,48},{1... | collective-permute-start | bytes 30728 | tf_op jit(solution)/shard_map/ppermute | solution.py:21
  87.1 4.1 %collective-permute-start.10 = (f32[3,5,512]{2,0,1:T(4,128)S(1)}, f32[3,5,512]{2,0,1:T(4,128)S(1)}, u32[]{:S(2)}, u32[]{:S(2)}) collective-permute-start(f32[3,5,512]{2,0,1:T(4,128)S(1)} %pad_maximum_fusion.4), channel_id=1, source_target_pairs={{0,1},{1,0},{2,3},{3,2},{4,5},{5,4},{6,7},{7,6},{8,9},{9,8},{10,11... | collective-permute-start | bytes 92168 | tf_op jit(solution)/shard_map/ppermute | solution.py:21
  91.3 5.6 %collective-permute-start.11 = (f32[3,5,512]{2,0,1:T(4,128)S(1)}, f32[3,5,512]{2,0,1:T(4,128)S(1)}, u32[]{:S(2)}, u32[]{:S(2)}) collective-permute-start(f32[3,5,512]{2,0,1:T(4,128)S(1)} %pad_maximum_fusion.5), channel_id=1, source_target_pairs={{0,2},{1,3},{2,0},{3,1},{4,6},{5,7},{6,4},{7,5},{8,10},{9,11},{10,... | collective-permute-start | bytes 92168 | tf_op jit(solution)/shard_map/ppermute | solution.py:21
  97.1 4.1 %collective-permute-start.12 = (f32[3,5,512]{2,0,1:T(4,128)S(1)}, f32[3,5,512]{2,0,1:T(4,128)S(1)}, u32[]{:S(2)}, u32[]{:S(2)}) collective-permute-start(f32[3,5,512]{2,0,1:T(4,128)S(1)} %pad_maximum_fusion.6), channel_id=1, source_target_pairs={{0,4},{1,5},{2,6},{3,7},{4,0},{5,1},{6,2},{7,3},{8,12},{9,13},{10,... | collective-permute-start | bytes 92168 | tf_op jit(solution)/shard_map/ppermute | solution.py:21
  101.3 5.8 %collective-permute-start.13 = (f32[3,5,512]{2,0,1:T(4,128)S(1)}, f32[3,5,512]{2,0,1:T(4,128)S(1)}, u32[]{:S(2)}, u32[]{:S(2)}) collective-permute-start(f32[3,5,512]{2,0,1:T(4,128)S(1)} %pad_maximum_fusion.7), channel_id=1, source_target_pairs={{0,8},{1,9},{2,10},{3,11},{4,12},{5,13},{6,14},{7,15},{8,0},{9,1},... | collective-permute-start | bytes 92168 | tf_op jit(solution)/shard_map/ppermute | solution.py:21
  109.8 0.9 copy-start.3
  109.8 1.1 copy-start.4
  125.4 2.4 %copy-start = (f32[5,256,1024]{2,1,0:T(8,128)}, f32[5,256,1024]{2,1,0:T(8,128)S(1)}, u32[]{:S(2)}) copy-start(f32[5,256,1024]{2,1,0:T(8,128)S(1)} %broadcast_multiply_fusion.1) | copy-start | bytes 15728644
  127.8 5.1 %collective-permute-start.14 = (f32[648,1024]{1,0:T(8,128)S(1)}, f32[648,1024]{1,0:T(8,128)}, u32[]{:S(2)}, u32[]{:S(2)}) collective-permute-start(f32[648,1024]{1,0:T(8,128)S(1)} %maximum_maximum_fusion), channel_id=1, source_target_pairs={{0,16},{16,0},{32,48},{48,32},{64,80},{80,64},{96,112},{112,96},{1... | collective-permute-start | bytes 7962632 | tf_op jit(solution)/shard_map/ppermute | solution.py:60
  127.8 7.2 %copy-start.1 = (f32[5,256,1024]{2,1,0:T(8,128)S(1)}, f32[5,256,1024]{2,1,0:T(8,128)}, u32[]{:S(2)}) copy-start(f32[5,256,1024]{2,1,0:T(8,128)} %copy-done) | copy-start | bytes 15728644
  136.8 18.8 %collective-permute-start.15 = (f32[168,1024]{1,0:T(8,128)S(1)}, f32[168,1024]{1,0:T(8,128)S(1)}, u32[]{:S(2)}, u32[]{:S(2)}) collective-permute-start(f32[168,1024]{1,0:T(8,128)S(1)} %pad_maximum_fusion.3), channel_id=1, source_target_pairs={{0,32},{16,48},{32,64},{48,80},{64,96},{80,112},{96,0},{112,16},{1... | collective-permute-start | bytes 2064392 | tf_op jit(solution)/shard_map/ppermute | solution.py:73
  155.6 17.9 %collective-permute-start.16 = (f32[168,1024]{1,0:T(8,128)S(1)}, f32[168,1024]{1,0:T(8,128)S(1)}, u32[]{:S(2)}, u32[]{:S(2)}) collective-permute-start(f32[168,1024]{1,0:T(8,128)S(1)} %fusion.12), channel_id=1, source_target_pairs={{0,32},{16,48},{32,64},{48,80},{64,96},{80,112},{96,0},{112,16},{1... | collective-permute-start | bytes 2064392 | tf_op jit(solution)/shard_map/ppermute | solution.py:73
  173.6 35.7 %copy-start.5 = (bf16[5,32,1024]{2,1,0:T(8,128)(2,1)S(1)}, bf16[5,32,1024]{2,1,0:T(8,128)(2,1)}, u32[]{:S(2)}) copy-start(bf16[5,32,1024]{2,1,0:T(8,128)(2,1)} %param.4) | copy-start | bytes 983044
  173.7 17.1 %collective-permute-start.17 = (f32[168,1024]{1,0:T(8,128)S(1)}, f32[168,1024]{1,0:T(8,128)S(1)}, u32[]{:S(2)}, u32[]{:S(2)}) collective-permute-start(f32[168,1024]{1,0:T(8,128)S(1)} %fusion.13), channel_id=1, source_target_pairs={{0,32},{16,48},{32,64},{48,80},{64,96},{80,112},{96,0},{112,16},{1... | collective-permute-start | bytes 2064392 | tf_op jit(solution)/shard_map/ppermute | solution.py:73
Sparse Core Ops, SparseCore 0:
  10.2 58.9 all-gather.1
  119.5 89.7 reduce-scatter.1

commit v5 on v4

--- a/solution.py
+++ b/solution.py
@@ -23,6 +23,17 @@
         stats = merge_pair(jnp.where(lower, stats, other), jnp.where(lower, other, stats))
         bit *= 2
     return stats
+
+
+def butterfly_sum(values, axis, size):
+    own = lax.axis_index(axis)
+    bit = 1
+    while bit < size:
+        other = lax.ppermute(values, axis, [(i, i ^ bit) for i in range(size)])
+        lower = (own & bit) == 0
+        values = jnp.where(lower, values, other) + jnp.where(lower, other, values)
+        bit *= 2
+    return values
 
 
 def ring_position(offset, size):
@@ -116,13 +127,11 @@
     col_lse = jnp.where(col_valid, col_high + jnp.log(jnp.where(col_valid, col_sum, 1.0)), 0.0)
 
     lanes = jnp.arange(row_count, dtype=jnp.int32)[None, :]
-    col_total = jnp.sum(col_lse, axis=1)
-    carried = jnp.where(lanes == 0, col_total[:, None], 0.0)
-    carried = jnp.where(lanes == 1, own_positive[:, None], carried)
+    carried = jnp.where(lanes == 0, own_positive[:, None], 0.0)
     row_stats = butterfly_merge(jnp.stack([row_high, row_sum, carried]), "pair", pair_size)
     row_high, row_sum, carried = row_stats[0], row_stats[1], row_stats[2]
     row_lse = jnp.where(row_valid, row_high + jnp.log(jnp.where(row_valid, row_sum, 1.0)), 0.0)
-    row_part = jnp.sum(row_lse, axis=1) - 2.0 * carried[:, 1]
+    row_part = jnp.sum(row_lse, axis=1) - 2.0 * carried[:, 0]
 
     prob_row = jnp.where(inside, jnp.exp(scores - row_lse[:, :, None]), 0.0)
     prob_col = jnp.where(inside, jnp.exp(scores - col_lse[:, None, :]), 0.0)
@@ -144,7 +153,8 @@
     partner_part, loss_row = two_stage_reduce_scatter(grad_cols, extra, "dp", dp_size, shard_rows)
     row_parts = loss_row[: pair_count * dp_size].reshape(pair_count, dp_size)
 
-    totals = carried[:, 0] + jnp.sum(row_parts, axis=1)
+    col_total = butterfly_sum(jnp.sum(col_lse, axis=1), "pair", pair_size)
+    totals = col_total + jnp.sum(row_parts, axis=1)
     loss_value = jnp.sum(totals / (2.0 * counts.astype(jnp.float32))) / pair_count
 
     own_term = (pair_scale * score_scale)[:, None, None]

time: 220 us -> 211 us (0.959)
  waiting for transfers between devices: 126 us -> 110 us
  starting transfers between devices: 25.4 us -> 31.5 us
    ppermute x3, waiting for transfers between devices: 51.8 us -> 38.5 us  [two_stage_reduce_scatter(): running = lax.ppermute(running, axis, ring) + addend(chip - 1 - step)]
    ppermute x0 -> x4, starting transfers between devices: none -> 8.25 us  [butterfly_sum(): other = lax.ppermute(values, axis, [(i, i ^ bit) for i in range(size)])]
    ppermute x0 -> x4, waiting for transfers between devices: none -> 6.65 us  [butterfly_sum(): other = lax.ppermute(values, axis, [(i, i ^ bit) for i in range(size)])]
    ppermute x7, waiting for transfers between devices: 14 us -> 7.8 us  [butterfly_merge(): other = lax.ppermute(stats, axis, [(i, i ^ bit) for i in range(size)])]
    ppermute x4, waiting for transfers between devices: 19.1 us -> 16.3 us  [ring_gather(): ahead = lax.ppermute(ahead, axis, forward)]
  transfers between devices with their start and end apart: 20 -> 24, of which waited for: 17 -> 20; matrix products, arithmetic and copies ran while one was open for 13% -> 14% of each run, Pallas kernels for 0% -> 0%
where the time goes in v5:
time: 211 us
  waiting for transfers between devices  110 us (52%)
  starting transfers between devices  31.5 us (15%)
  local copies, waits for them, and re-layouts  20.6 us (10%)
  matrix products  18.3 us (9%)
  between operations  16.2 us (8%)
  other arithmetic  14.5 us (7%)
    ppermute x3, waiting for transfers between devices, two_stage_reduce_scatter(): running = lax.ppermute(running, axis, ring) + addend(chip - 1 - step)  38.5 us
    all_gather x1, waiting for transfers between devices, per_device(): row_set = lax.all_gather(anchor, 'pair', axis=1, tiled=True)  17.8 us
    ppermute x4, waiting for transfers between devices, ring_gather(): ahead = lax.ppermute(ahead, axis, forward)  16.3 us
    reduce_scatter x1, waiting for transfers between devices, per_device(): lax.psum_scatter(grad_rows, 'pair', scatter_dimension=1, tiled=True)  15.6 us
    unnamed x31, local copies, waits for them, and re-layouts  14.4 us
    ppermute x7, starting transfers between devices, butterfly_merge(): other = lax.ppermute(stats, axis, [(i, i ^ bit) for i in range(size)])  13.2 us
    ppermute x3, starting transfers between devices, ring_gather(): behind = lax.ppermute(behind, axis, backward)  9.41 us
    dot_general x1, matrix products, per_device(): jnp.einsum('prc,pcd->prd', weights, col_set, preferred_element_type=jnp.f...  8.26 us
  transfers between devices with their start and end apart: 24, of which 20 were waited for; matrix products, arithmetic and copies ran while one was open for 14% of the time, Pallas kernels for 0%

profile of v5, /device:TPU:0, one launch (start us, length us, event | category | flops | bytes accessed | tf_op | source)
XLA Modules:
  0.0 210.8 jit_solution(3906028214680772996)
XLA Ops:
  8.0 2.9 %collective-permute-start.4 = (bf16[5,32,1024]{2,1,0:T(8,128)(2,1)}, bf16[5,32,1024]{2,1,0:T(8,128)(2,1)S(1)}, u32[]{:S(2)}, u32[]{:S(2)}) collective-permute-start(bf16[5,32,1024]{2,1,0:T(8,128)(2,1)} %param.5), channel_id=1, source_target_pairs={{0,112},{16,0},{32,16},{48,32},{64,48},{80,64},{96,80},{112,96},{1... | collective-permute-start | bytes 983048 | tf_op jit(solution)/shard_map/ppermute | solution.py:56
  11.7 4.2 %collective-permute-done = bf16[5,32,1024]{2,1,0:T(8,128)(2,1)S(1)} collective-permute-done((bf16[5,32,1024]{2,1,0:T(8,128)(2,1)}, bf16[5,32,1024]{2,1,0:T(8,128)(2,1)S(1)}, u32[]{:S(2)}, u32[]{:S(2)}) %collective-permute-start) | collective-permute-done | bytes 327712 | tf_op jit(solution)/shard_map/ppermute | solution.py:53
  16.2 1.2 fusion.17
  17.4 6.2 %collective-permute-done.1 = bf16[5,32,1024]{2,1,0:T(8,128)(2,1)S(1)} collective-permute-done((bf16[5,32,1024]{2,1,0:T(8,128)(2,1)S(1)}, bf16[5,32,1024]{2,1,0:T(8,128)(2,1)S(1)}, u32[]{:S(2)}, u32[]{:S(2)}) %collective-permute-start.1) | collective-permute-done | bytes 327712 | tf_op jit(solution)/shard_map/ppermute | solution.py:53
  23.6 0.8 select_reduce_fusion.1
  25.2 3.0 %collective-permute-start.5 = (bf16[5,32,1024]{2,1,0:T(8,128)(2,1)S(1)}, bf16[5,32,1024]{2,1,0:T(8,128)(2,1)S(1)}, u32[]{:S(2)}, u32[]{:S(2)}) collective-permute-start(bf16[5,32,1024]{2,1,0:T(8,128)(2,1)S(1)} %collective-permute-done.4), channel_id=1, source_target_pairs={{0,112},{16,0},{32,16},{48,32},{64,48},{80,64},{96,80},{112,96},{1... | collective-permute-start | bytes 983048 | tf_op jit(solution)/shard_map/ppermute | solution.py:56
  28.1 3.2 %collective-permute-done.2 = bf16[5,32,1024]{2,1,0:T(8,128)(2,1)S(1)} collective-permute-done((bf16[5,32,1024]{2,1,0:T(8,128)(2,1)S(1)}, bf16[5,32,1024]{2,1,0:T(8,128)(2,1)S(1)}, u32[]{:S(2)}, u32[]{:S(2)}) %collective-permute-start.2) | collective-permute-done | bytes 327712 | tf_op jit(solution)/shard_map/ppermute | solution.py:53
  31.4 1.3 collective-permute-done.5
  32.7 3.5 %collective-permute-start.6 = (bf16[5,32,1024]{2,1,0:T(8,128)(2,1)S(1)}, bf16[5,32,1024]{2,1,0:T(8,128)(2,1)S(1)}, u32[]{:S(2)}, u32[]{:S(2)}) collective-permute-start(bf16[5,32,1024]{2,1,0:T(8,128)(2,1)S(1)} %collective-permute-done.5), channel_id=1, source_target_pairs={{0,112},{16,0},{32,16},{48,32},{64,48},{80,64},{96,80},{112,96},{1... | collective-permute-start | bytes 983048 | tf_op jit(solution)/shard_map/ppermute | solution.py:56
  36.2 2.8 %collective-permute-done.3 = bf16[5,32,1024]{2,1,0:T(8,128)(2,1)S(1)} collective-permute-done((bf16[5,32,1024]{2,1,0:T(8,128)(2,1)S(1)}, bf16[5,32,1024]{2,1,0:T(8,128)(2,1)S(1)}, u32[]{:S(2)}, u32[]{:S(2)}) %collective-permute-start.3) | collective-permute-done | bytes 327712 | tf_op jit(solution)/shard_map/ppermute | solution.py:53
  42.1 0.8 constant_dynamic-update-slice_fusion.11
  45.1 0.8 constant_dynamic-update-slice_fusion.7
  51.3 17.8 %all-gather.2.cloned.1.call-done = bf16[5,512,1024]{2,1,0:T(8,128)(2,1)} async-done(((bf16[5,32,1024]{2,1,0:T(8,128)(2,1)}), bf16[5,512,1024]{2,1,0:T(8,128)(2,1)}) %all-gather.2.cloned.1.call-update) | async-done | bytes 5242896 | tf_op jit(solution)/shard_map/all_gather | solution.py:103
  69.1 5.2 %fusion.11 = (f32[5,256]{1,0:T(8,128)S(1)}, f32[5,512]{1,0:T(8,128)S(1)}, f32[5,256,512]{2,1,0:T(8,128)S(1)}) fusion(pred[5,256]{1,0:T(8,128)(4,1)S(1)} %broadcast_compare_fusion.1, pred[5,512]{1,0:T(8,128)(4,1)S(1)} %copy.20, bf16[5,512,1024]{2,1,0:T(8,128)(2,1)} %all-gather.2.cloned.1.call-done, ...), kind=kOutput, calls=%fused_computation.26 | convolution fusion | flops 1345450240 | bytes 10504964 | tf_op jit(solution)/shard_map/prd,pcd->prc/dot_general | solution.py:116
  74.3 1.9 fusion
  76.4 1.1 collective-permute-done.7
  77.6 1.5 collective-permute-start.8
  79.1 1.6 collective-permute-start.14
  81.4 1.8 collective-permute-done.14
  83.4 3.1 %collective-permute-start.15 = (f32[3,5,512]{2,0,1:T(4,128)S(1)}, f32[3,5,512]{2,0,1:T(4,128)S(1)}, u32[]{:S(2)}, u32[]{:S(2)}) collective-permute-start(f32[3,5,512]{2,0,1:T(4,128)S(1)} %pad_maximum_fusion.5), channel_id=1, source_target_pairs={{0,2},{1,3},{2,0},{3,1},{4,6},{5,7},{6,4},{7,5},{8,10},{9,11},{10,... | collective-permute-start | bytes 92168 | tf_op jit(solution)/shard_map/ppermute | solution.py:21
  86.5 2.7 %collective-permute-start.9 = (f32[2,5,256]{2,1,0:T(8,128)S(1)}, f32[2,5,256]{2,1,0:T(8,128)S(1)}, u32[]{:S(2)}, u32[]{:S(2)}) collective-permute-start(f32[2,5,256]{2,1,0:T(8,128)S(1)} %pad_maximum_fusion.10), channel_id=1, source_target_pairs={{0,64},{16,80},{32,96},{48,112},{64,0},{80,16},{96,32},{112,48},{1... | collective-permute-start | bytes 30728 | tf_op jit(solution)/shard_map/ppermute | solution.py:21
  89.3 1.2 collective-permute-start.16
  90.5 1.2 collective-permute-done.9
  91.7 1.7 collective-permute-done.16
  93.5 3.0 %collective-permute-start.17 = (f32[3,5,512]{2,0,1:T(4,128)S(1)}, f32[3,5,512]{2,0,1:T(4,128)S(1)}, u32[]{:S(2)}, u32[]{:S(2)}) collective-permute-start(f32[3,5,512]{2,0,1:T(4,128)S(1)} %pad_maximum_fusion.7), channel_id=1, source_target_pairs={{0,8},{1,9},{2,10},{3,11},{4,12},{5,13},{6,14},{7,15},{8,0},{9,1},... | collective-permute-start | bytes 92168 | tf_op jit(solution)/shard_map/ppermute | solution.py:21
  96.7 1.2 copy.23
  98.0 1.4 collective-permute-done.17
  99.3 1.2 copy.24
  100.5 1.5 broadcast_select_fusion.1
  102.1 0.9 copy-done.3
  103.3 8.3 %broadcast_multiply_fusion = f32[5,512,1024]{2,1,0:T(8,128)} fusion(bf16[5,512,1024]{2,1,0:T(8,128)(2,1)} %constant_dynamic-update-slice_fusion, s32[]{:T(128)S(6)} %select_n.255, f32[5,256,512]{2,1,0:T(8,128)S(1)} %get-tuple-element.46, f32[5,256]{1,0:T(8,128)S(1)} %get-tuple-element.8, f32[5,512]{1,0:T(8,128)S(1)} %copy.27, f32[5]{0:T(128)S(1)} %get-tuple-element.45, ...), kind=kOutput, calls=%fused_computation.5 | convolution fusion | flops 1350696960 | bytes 15747864 | tf_op jit(solution)/shard_map/prc,pcd->prd/dot_general | solution.py:140
  111.7 1.1 fusion.20
  112.8 4.8 %broadcast_multiply_fusion.1 = f32[5,256,1024]{2,1,0:T(8,128)S(1)} fusion(bf16[5,512,1024]{2,1,0:T(8,128)(2,1)} %all-gather.2.cloned.1.call-done, f32[5,256,512]{2,1,0:T(8,128)S(1)} %get-tuple-element.46, f32[5,256]{1,0:T(8,128)S(1)} %get-tuple-element.8, f32[5,512]{1,0:T(8,128)S(1)} %copy.27, f32[5]{0:T(128)S(1)} %get-tuple-element.45, ...), kind=kOutput, calls=%fused_computation.17 | convolution fusion | flops 1349386240 | bytes 13126420 | tf_op jit(solution)/shard_map/prc,prd->pcd/dot_general | solution.py:144
  118.1 1.9 copy-done
  120.0 5.1 %collective-permute-done.18 = f32[648,1024]{1,0:T(8,128)} collective-permute-done((f32[648,1024]{1,0:T(8,128)S(1)}, f32[648,1024]{1,0:T(8,128)}, u32[]{:S(2)}, u32[]{:S(2)}) %collective-permute-start.18) | collective-permute-done | bytes 2654240 | tf_op jit(solution)/shard_map/ppermute | solution.py:71
  125.1 2.1 slice.218
  129.4 18.4 %collective-permute-done.19 = f32[168,1024]{1,0:T(8,128)S(1)} collective-permute-done((f32[168,1024]{1,0:T(8,128)S(1)}, f32[168,1024]{1,0:T(8,128)S(1)}, u32[]{:S(2)}, u32[]{:S(2)}) %collective-permute-start.19) | collective-permute-done | bytes 688160 | tf_op jit(solution)/shard_map/ppermute | solution.py:84
  148.0 17.9 %collective-permute-done.20 = f32[168,1024]{1,0:T(8,128)S(1)} collective-permute-done((f32[168,1024]{1,0:T(8,128)S(1)}, f32[168,1024]{1,0:T(8,128)S(1)}, u32[]{:S(2)}, u32[]{:S(2)}) %collective-permute-start.20) | collective-permute-done | bytes 688160 | tf_op jit(solution)/shard_map/ppermute | solution.py:84
  166.2 1.3 collective-permute-start.10
  167.5 2.3 %collective-permute-done.10 = f32[5]{0:T(128)S(1)} collective-permute-done((f32[5]{0:T(128)S(1)}, f32[5]{0:T(128)S(1)}, u32[]{:S(2)}, u32[]{:S(2)}) %collective-permute-start.10) | collective-permute-done | bytes 52 | tf_op jit(solution)/shard_map/ppermute | solution.py:32
  169.7 3.1 %collective-permute-start.11 = (f32[5]{0:T(128)S(1)}, f32[5]{0:T(128)S(1)}, u32[]{:S(2)}, u32[]{:S(2)}) collective-permute-start(f32[5]{0:T(128)S(1)} %fusion.49), channel_id=1, source_target_pairs={{0,2},{1,3},{2,0},{3,1},{4,6},{5,7},{6,4},{7,5},{8,10},{9,11},{10,... | collective-permute-start | bytes 68 | tf_op jit(solution)/shard_map/ppermute | solution.py:32
  172.8 2.0 collective-permute-done.11
  174.8 1.1 collective-permute-start.12
  175.9 2.4 %collective-permute-done.12 = f32[5]{0:T(128)S(1)} collective-permute-done((f32[5]{0:T(128)S(1)}, f32[5]{0:T(128)S(1)}, u32[]{:S(2)}, u32[]{:S(2)}) %collective-permute-start.12) | collective-permute-done | bytes 52 | tf_op jit(solution)/shard_map/ppermute | solution.py:32
  178.3 2.7 %collective-permute-start.13 = (f32[5]{0:T(128)S(1)}, f32[5]{0:T(128)S(1)}, u32[]{:S(2)}, u32[]{:S(2)}) collective-permute-start(f32[5]{0:T(128)S(1)} %fusion.47), channel_id=1, source_target_pairs={{0,8},{1,9},{2,10},{3,11},{4,12},{5,13},{6,14},{7,15},{8,0},{9,1},... | collective-permute-start | bytes 68 | tf_op jit(solution)/shard_map/ppermute | solution.py:32
  181.1 2.1 %collective-permute-done.21 = f32[168,1024]{1,0:T(8,128)S(1)} collective-permute-done((f32[168,1024]{1,0:T(8,128)S(1)}, f32[168,1024]{1,0:T(8,128)S(1)}, u32[]{:S(2)}, u32[]{:S(2)}) %collective-permute-start.21) | collective-permute-done | bytes 688160 | tf_op jit(solution)/shard_map/ppermute | solution.py:84
  184.9 15.6 %reduce-scatter.2.cloned.1.call-done = f32[5,32,1024]{2,1,0:T(8,128)} async-done(((f32[5,512,1024]{2,1,0:T(8,128)}), f32[5,32,1024]{2,1,0:T(8,128)}) %reduce-scatter.2.cloned.1.call-update) | async-done | bytes 655376 | tf_op jit(solution)/shard_map/reduce_scatter | solution.py:147
  200.4 2.4 %fusion.16 = (f32[5,32,1024]{2,1,0:T(8,128)}, f32[5,32,1024]{2,1,0:T(8,128)}) fusion(f32[5,32,1024]{2,1,0:T(8,128)S(1)} %bitcast.117, bf16[5,32,1024]{2,1,0:T(8,128)(2,1)S(1)} %copy-done.5, f32[5]{0:T(128)S(1)} %get-tuple-element.44, pred[5,32]{1,0:T(8,128)(4,1)S(1)} %broadcast_compare_fusion.2, f32[5,32,1024]{2,1,0:T(8,128)} %reduce-scatter.2.cloned.1.call-done, ...), kind=kLoop, calls=%fused_computation.34 | loop fusion | flops 1310720 | bytes 3276980 | tf_op jit(solution)/shard_map/jit(_where)/select_n | solution.py:163
  (103 shorter events, 19.3 us)
Async XLA Ops:
  7.2 34.9 %copy-start.2 = (bf16[5,32,1024]{2,1,0:T(8,128)(2,1)S(1)}, bf16[5,32,1024]{2,1,0:T(8,128)(2,1)}, u32[]{:S(2)}) copy-start(bf16[5,32,1024]{2,1,0:T(8,128)(2,1)} %param.5) | copy-start | bytes 983044
  7.2 61.9 %all-gather.2.cloned.1.call-start = ((), (), s32[]{:S(2)}) async-start(), calls=%async_computation.1 | async-start | bytes 5570560 | tf_op jit(solution)/shard_map/all_gather | solution.py:103
  7.9 192.5 %reduce-scatter.2.cloned.1.call-start = ((), (), s32[]{:S(2)}) async-start(), calls=%async_computation.2 | async-start | bytes 11141120 | tf_op jit(solution)/shard_map/reduce_scatter | solution.py:147
  8.0 7.9 %collective-permute-start = (bf16[5,32,1024]{2,1,0:T(8,128)(2,1)}, bf16[5,32,1024]{2,1,0:T(8,128)(2,1)S(1)}, u32[]{:S(2)}, u32[]{:S(2)}) collective-permute-start(bf16[5,32,1024]{2,1,0:T(8,128)(2,1)} %param.5), channel_id=1, source_target_pairs={{0,16},{16,32},{32,48},{48,64},{64,80},{80,96},{96,112},{112,0},{1... | collective-permute-start | bytes 983048 | tf_op jit(solution)/shard_map/ppermute | solution.py:53
  8.0 17.2 %collective-permute-start.4 = (bf16[5,32,1024]{2,1,0:T(8,128)(2,1)}, bf16[5,32,1024]{2,1,0:T(8,128)(2,1)S(1)}, u32[]{:S(2)}, u32[]{:S(2)}) collective-permute-start(bf16[5,32,1024]{2,1,0:T(8,128)(2,1)} %param.5), channel_id=1, source_target_pairs={{0,112},{16,0},{32,16},{48,32},{64,48},{80,64},{96,80},{112,96},{1... | collective-permute-start | bytes 983048 | tf_op jit(solution)/shard_map/ppermute | solution.py:56
  15.9 7.7 %collective-permute-start.1 = (bf16[5,32,1024]{2,1,0:T(8,128)(2,1)S(1)}, bf16[5,32,1024]{2,1,0:T(8,128)(2,1)S(1)}, u32[]{:S(2)}, u32[]{:S(2)}) collective-permute-start(bf16[5,32,1024]{2,1,0:T(8,128)(2,1)S(1)} %collective-permute-done), channel_id=1, source_target_pairs={{0,16},{16,32},{32,48},{48,64},{64,80},{80,96},{96,112},{112,0},{1... | collective-permute-start | bytes 983048 | tf_op jit(solution)/shard_map/ppermute | solution.py:53
  23.6 7.7 %collective-permute-start.2 = (bf16[5,32,1024]{2,1,0:T(8,128)(2,1)S(1)}, bf16[5,32,1024]{2,1,0:T(8,128)(2,1)S(1)}, u32[]{:S(2)}, u32[]{:S(2)}) collective-permute-start(bf16[5,32,1024]{2,1,0:T(8,128)(2,1)S(1)} %collective-permute-done.1), channel_id=1, source_target_pairs={{0,16},{16,32},{32,48},{48,64},{64,80},{80,96},{96,112},{112,0},{1... | collective-permute-start | bytes 983048 | tf_op jit(solution)/shard_map/ppermute | solution.py:53
  25.2 7.5 %collective-permute-start.5 = (bf16[5,32,1024]{2,1,0:T(8,128)(2,1)S(1)}, bf16[5,32,1024]{2,1,0:T(8,128)(2,1)S(1)}, u32[]{:S(2)}, u32[]{:S(2)}) collective-permute-start(bf16[5,32,1024]{2,1,0:T(8,128)(2,1)S(1)} %collective-permute-done.4), channel_id=1, source_target_pairs={{0,112},{16,0},{32,16},{48,32},{64,48},{80,64},{96,80},{112,96},{1... | collective-permute-start | bytes 983048 | tf_op jit(solution)/shard_map/ppermute | solution.py:56
  31.3 7.7 %collective-permute-start.3 = (bf16[5,32,1024]{2,1,0:T(8,128)(2,1)S(1)}, bf16[5,32,1024]{2,1,0:T(8,128)(2,1)S(1)}, u32[]{:S(2)}, u32[]{:S(2)}) collective-permute-start(bf16[5,32,1024]{2,1,0:T(8,128)(2,1)S(1)} %collective-permute-done.2), channel_id=1, source_target_pairs={{0,16},{16,32},{32,48},{48,64},{64,80},{80,96},{96,112},{112,0},{1... | collective-permute-start | bytes 983048 | tf_op jit(solution)/shard_map/ppermute | solution.py:53
  32.7 11.6 %collective-permute-start.6 = (bf16[5,32,1024]{2,1,0:T(8,128)(2,1)S(1)}, bf16[5,32,1024]{2,1,0:T(8,128)(2,1)S(1)}, u32[]{:S(2)}, u32[]{:S(2)}) collective-permute-start(bf16[5,32,1024]{2,1,0:T(8,128)(2,1)S(1)} %collective-permute-done.5), channel_id=1, source_target_pairs={{0,112},{16,0},{32,16},{48,32},{64,48},{80,64},{96,80},{112,96},{1... | collective-permute-start | bytes 983048 | tf_op jit(solution)/shard_map/ppermute | solution.py:56
  74.3 2.0 copy-start.7
  74.3 22.2 %copy-start.6 = (s32[5]{0:T(128)S(1)}, s32[5]{0:T(128)}, u32[]{:S(2)}) copy-start(s32[5]{0:T(128)} %param.6) | copy-start | bytes 64
  76.3 1.3 collective-permute-start.7
  77.6 3.8 %collective-permute-start.8 = (f32[2,5,256]{2,1,0:T(8,128)S(1)}, f32[2,5,256]{2,1,0:T(8,128)S(1)}, u32[]{:S(2)}, u32[]{:S(2)}) collective-permute-start(f32[2,5,256]{2,1,0:T(8,128)S(1)} %pad_maximum_fusion.9), channel_id=1, source_target_pairs={{0,32},{16,48},{32,0},{48,16},{64,96},{80,112},{96,64},{112,80},{1... | collective-permute-start | bytes 30728 | tf_op jit(solution)/shard_map/ppermute | solution.py:21
  79.1 4.1 %collective-permute-start.14 = (f32[3,5,512]{2,0,1:T(4,128)S(1)}, f32[3,5,512]{2,0,1:T(4,128)S(1)}, u32[]{:S(2)}, u32[]{:S(2)}) collective-permute-start(f32[3,5,512]{2,0,1:T(4,128)S(1)} %pad_maximum_fusion.4), channel_id=1, source_target_pairs={{0,1},{1,0},{2,3},{3,2},{4,5},{5,4},{6,7},{7,6},{8,9},{9,8},{10,11... | collective-permute-start | bytes 92168 | tf_op jit(solution)/shard_map/ppermute | solution.py:21
  83.4 5.8 %collective-permute-start.15 = (f32[3,5,512]{2,0,1:T(4,128)S(1)}, f32[3,5,512]{2,0,1:T(4,128)S(1)}, u32[]{:S(2)}, u32[]{:S(2)}) collective-permute-start(f32[3,5,512]{2,0,1:T(4,128)S(1)} %pad_maximum_fusion.5), channel_id=1, source_target_pairs={{0,2},{1,3},{2,0},{3,1},{4,6},{5,7},{6,4},{7,5},{8,10},{9,11},{10,... | collective-permute-start | bytes 92168 | tf_op jit(solution)/shard_map/ppermute | solution.py:21
  86.5 5.2 %collective-permute-start.9 = (f32[2,5,256]{2,1,0:T(8,128)S(1)}, f32[2,5,256]{2,1,0:T(8,128)S(1)}, u32[]{:S(2)}, u32[]{:S(2)}) collective-permute-start(f32[2,5,256]{2,1,0:T(8,128)S(1)} %pad_maximum_fusion.10), channel_id=1, source_target_pairs={{0,64},{16,80},{32,96},{48,112},{64,0},{80,16},{96,32},{112,48},{1... | collective-permute-start | bytes 30728 | tf_op jit(solution)/shard_map/ppermute | solution.py:21
  89.3 4.1 %collective-permute-start.16 = (f32[3,5,512]{2,0,1:T(4,128)S(1)}, f32[3,5,512]{2,0,1:T(4,128)S(1)}, u32[]{:S(2)}, u32[]{:S(2)}) collective-permute-start(f32[3,5,512]{2,0,1:T(4,128)S(1)} %pad_maximum_fusion.6), channel_id=1, source_target_pairs={{0,4},{1,5},{2,6},{3,7},{4,0},{5,1},{6,2},{7,3},{8,12},{9,13},{10,... | collective-permute-start | bytes 92168 | tf_op jit(solution)/shard_map/ppermute | solution.py:21
  93.5 5.8 %collective-permute-start.17 = (f32[3,5,512]{2,0,1:T(4,128)S(1)}, f32[3,5,512]{2,0,1:T(4,128)S(1)}, u32[]{:S(2)}, u32[]{:S(2)}) collective-permute-start(f32[3,5,512]{2,0,1:T(4,128)S(1)} %pad_maximum_fusion.7), channel_id=1, source_target_pairs={{0,8},{1,9},{2,10},{3,11},{4,12},{5,13},{6,14},{7,15},{8,0},{9,1},... | collective-permute-start | bytes 92168 | tf_op jit(solution)/shard_map/ppermute | solution.py:21
  102.0 0.9 copy-start.3
  102.0 1.2 copy-start.4
  117.7 2.4 %copy-start = (f32[5,256,1024]{2,1,0:T(8,128)}, f32[5,256,1024]{2,1,0:T(8,128)S(1)}, u32[]{:S(2)}) copy-start(f32[5,256,1024]{2,1,0:T(8,128)S(1)} %broadcast_multiply_fusion.1) | copy-start | bytes 15728644
  120.0 5.1 %collective-permute-start.18 = (f32[648,1024]{1,0:T(8,128)S(1)}, f32[648,1024]{1,0:T(8,128)}, u32[]{:S(2)}, u32[]{:S(2)}) collective-permute-start(f32[648,1024]{1,0:T(8,128)S(1)} %maximum_maximum_fusion), channel_id=1, source_target_pairs={{0,16},{16,0},{32,48},{48,32},{64,80},{80,64},{96,112},{112,96},{1... | collective-permute-start | bytes 7962632 | tf_op jit(solution)/shard_map/ppermute | solution.py:71
  120.0 7.2 %copy-start.1 = (f32[5,256,1024]{2,1,0:T(8,128)S(1)}, f32[5,256,1024]{2,1,0:T(8,128)}, u32[]{:S(2)}) copy-start(f32[5,256,1024]{2,1,0:T(8,128)} %copy-done) | copy-start | bytes 15728644
  129.0 18.8 %collective-permute-start.19 = (f32[168,1024]{1,0:T(8,128)S(1)}, f32[168,1024]{1,0:T(8,128)S(1)}, u32[]{:S(2)}, u32[]{:S(2)}) collective-permute-start(f32[168,1024]{1,0:T(8,128)S(1)} %pad_maximum_fusion.3), channel_id=1, source_target_pairs={{0,32},{16,48},{32,64},{48,80},{64,96},{80,112},{96,0},{112,16},{1... | collective-permute-start | bytes 2064392 | tf_op jit(solution)/shard_map/ppermute | solution.py:84
  147.9 18.0 %collective-permute-start.20 = (f32[168,1024]{1,0:T(8,128)S(1)}, f32[168,1024]{1,0:T(8,128)S(1)}, u32[]{:S(2)}, u32[]{:S(2)}) collective-permute-start(f32[168,1024]{1,0:T(8,128)S(1)} %fusion.12), channel_id=1, source_target_pairs={{0,32},{16,48},{32,64},{48,80},{64,96},{80,112},{96,0},{112,16},{1... | collective-permute-start | bytes 2064392 | tf_op jit(solution)/shard_map/ppermute | solution.py:84
  165.9 34.5 %copy-start.5 = (bf16[5,32,1024]{2,1,0:T(8,128)(2,1)S(1)}, bf16[5,32,1024]{2,1,0:T(8,128)(2,1)}, u32[]{:S(2)}) copy-start(bf16[5,32,1024]{2,1,0:T(8,128)(2,1)} %param.4) | copy-start | bytes 983044
  166.0 17.2 %collective-permute-start.21 = (f32[168,1024]{1,0:T(8,128)S(1)}, f32[168,1024]{1,0:T(8,128)S(1)}, u32[]{:S(2)}, u32[]{:S(2)}) collective-permute-start(f32[168,1024]{1,0:T(8,128)S(1)} %fusion.13), channel_id=1, source_target_pairs={{0,32},{16,48},{32,64},{48,80},{64,96},{80,112},{96,0},{112,16},{1... | collective-permute-start | bytes 2064392 | tf_op jit(solution)/shard_map/ppermute | solution.py:84
  166.2 3.6 %collective-permute-start.10 = (f32[5]{0:T(128)S(1)}, f32[5]{0:T(128)S(1)}, u32[]{:S(2)}, u32[]{:S(2)}) collective-permute-start(f32[5]{0:T(128)S(1)} %get-tuple-element.7), channel_id=1, source_target_pairs={{0,1},{1,0},{2,3},{3,2},{4,5},{5,4},{6,7},{7,6},{8,9},{9,8},{10,11... | collective-permute-start | bytes 68 | tf_op jit(solution)/shard_map/ppermute | solution.py:32
  169.7 5.0 %collective-permute-start.11 = (f32[5]{0:T(128)S(1)}, f32[5]{0:T(128)S(1)}, u32[]{:S(2)}, u32[]{:S(2)}) collective-permute-start(f32[5]{0:T(128)S(1)} %fusion.49), channel_id=1, source_target_pairs={{0,2},{1,3},{2,0},{3,1},{4,6},{5,7},{6,4},{7,5},{8,10},{9,11},{10,... | collective-permute-start | bytes 68 | tf_op jit(solution)/shard_map/ppermute | solution.py:32
  174.8 3.5 %collective-permute-start.12 = (f32[5]{0:T(128)S(1)}, f32[5]{0:T(128)S(1)}, u32[]{:S(2)}, u32[]{:S(2)}) collective-permute-start(f32[5]{0:T(128)S(1)} %fusion.48), channel_id=1, source_target_pairs={{0,4},{1,5},{2,6},{3,7},{4,0},{5,1},{6,2},{7,3},{8,12},{9,13},{10,... | collective-permute-start | bytes 68 | tf_op jit(solution)/shard_map/ppermute | solution.py:32
  178.3 5.3 %collective-permute-start.13 = (f32[5]{0:T(128)S(1)}, f32[5]{0:T(128)S(1)}, u32[]{:S(2)}, u32[]{:S(2)}) collective-permute-start(f32[5]{0:T(128)S(1)} %fusion.47), channel_id=1, source_target_pairs={{0,8},{1,9},{2,10},{3,11},{4,12},{5,13},{6,14},{7,15},{8,0},{9,1},... | collective-permute-start | bytes 68 | tf_op jit(solution)/shard_map/ppermute | solution.py:32
Sparse Core Ops, SparseCore 0:
  10.2 58.9 all-gather.1
  111.7 88.6 reduce-scatter.1

commit v6 on v5

--- a/solution.py
+++ b/solution.py
@@ -136,6 +136,7 @@
     prob_row = jnp.where(inside, jnp.exp(scores - row_lse[:, :, None]), 0.0)
     prob_col = jnp.where(inside, jnp.exp(scores - col_lse[:, None, :]), 0.0)
     weights = (pair_scale[:, None, None] * 0.5 * (prob_row + prob_col)).astype(jnp.bfloat16)
+    weights = lax.optimization_barrier(weights)
     grad_rows = (
         jnp.einsum("prc,pcd->prd", weights, col_set, preferred_element_type=jnp.float32)
         * score_scale

time: 211 us -> 211 us (level)
    convert_element_type x0 -> x1, other arithmetic: none -> 2.72 us  [per_device(): (pair_scale[:, None, None] * 0.5 * (prob_row + prob_col)).astype(jnp.bflo...]
    unnamed x31 -> x29, local copies, waits for them, and re-layouts: 14.4 us -> 15.7 us
  transfers between devices with their start and end apart: 24 -> 24, of which waited for: 20 -> 20; matrix products, arithmetic and copies ran while one was open for 14% -> 13% of each run, Pallas kernels for 0% -> 0%
where the time goes in v6:
time: 211 us
  waiting for transfers between devices  111 us (53%)
  starting transfers between devices  31.7 us (15%)
  local copies, waits for them, and re-layouts  20 us (9%)
  matrix products  16.5 us (8%)
  between operations  16.2 us (8%)
  other arithmetic  14.8 us (7%)
    ppermute x3, waiting for transfers between devices, two_stage_reduce_scatter(): running = lax.ppermute(running, axis, ring) + addend(chip - 1 - step)  38.4 us
    reduce_scatter x1, waiting for transfers between devices, per_device(): lax.psum_scatter(grad_rows, 'pair', scatter_dimension=1, tiled=True)  17.6 us
    all_gather x1, waiting for transfers between devices, per_device(): row_set = lax.all_gather(anchor, 'pair', axis=1, tiled=True)  17 us
    ppermute x4, waiting for transfers between devices, ring_gather(): ahead = lax.ppermute(ahead, axis, forward)  16.3 us
    unnamed x29, local copies, waits for them, and re-layouts  15.7 us
    ppermute x7, starting transfers between devices, butterfly_merge(): other = lax.ppermute(stats, axis, [(i, i ^ bit) for i in range(size)])  13 us
    ppermute x3, starting transfers between devices, ring_gather(): behind = lax.ppermute(behind, axis, backward)  9.41 us
    ppermute x7, waiting for transfers between devices, butterfly_merge(): other = lax.ppermute(stats, axis, [(i, i ^ bit) for i in range(size)])  8.7 us
  transfers between devices with their start and end apart: 24, of which 20 were waited for; matrix products, arithmetic and copies ran while one was open for 13% of the time, Pallas kernels for 0%

profile of v6, /device:TPU:0, one launch (start us, length us, event | category | flops | bytes accessed | tf_op | source)
XLA Modules:
  0.0 210.8 jit_solution(13534005508671477531)
XLA Ops:
  8.0 2.9 %collective-permute-start.4 = (bf16[5,32,1024]{2,1,0:T(8,128)(2,1)}, bf16[5,32,1024]{2,1,0:T(8,128)(2,1)S(1)}, u32[]{:S(2)}, u32[]{:S(2)}) collective-permute-start(bf16[5,32,1024]{2,1,0:T(8,128)(2,1)} %param.5), channel_id=1, source_target_pairs={{0,112},{16,0},{32,16},{48,32},{64,48},{80,64},{96,80},{112,96},{1... | collective-permute-start | bytes 983048 | tf_op jit(solution)/shard_map/ppermute | solution.py:56
  10.9 0.8 broadcast_compare_fusion
  11.7 4.2 %collective-permute-done = bf16[5,32,1024]{2,1,0:T(8,128)(2,1)S(1)} collective-permute-done((bf16[5,32,1024]{2,1,0:T(8,128)(2,1)}, bf16[5,32,1024]{2,1,0:T(8,128)(2,1)S(1)}, u32[]{:S(2)}, u32[]{:S(2)}) %collective-permute-start) | collective-permute-done | bytes 327712 | tf_op jit(solution)/shard_map/ppermute | solution.py:53
  16.2 1.2 fusion.17
  17.4 6.2 %collective-permute-done.1 = bf16[5,32,1024]{2,1,0:T(8,128)(2,1)S(1)} collective-permute-done((bf16[5,32,1024]{2,1,0:T(8,128)(2,1)S(1)}, bf16[5,32,1024]{2,1,0:T(8,128)(2,1)S(1)}, u32[]{:S(2)}, u32[]{:S(2)}) %collective-permute-start.1) | collective-permute-done | bytes 327712 | tf_op jit(solution)/shard_map/ppermute | solution.py:53
  23.6 0.8 select_reduce_fusion.1
  25.2 3.0 %collective-permute-start.5 = (bf16[5,32,1024]{2,1,0:T(8,128)(2,1)S(1)}, bf16[5,32,1024]{2,1,0:T(8,128)(2,1)S(1)}, u32[]{:S(2)}, u32[]{:S(2)}) collective-permute-start(bf16[5,32,1024]{2,1,0:T(8,128)(2,1)S(1)} %collective-permute-done.4), channel_id=1, source_target_pairs={{0,112},{16,0},{32,16},{48,32},{64,48},{80,64},{96,80},{112,96},{1... | collective-permute-start | bytes 983048 | tf_op jit(solution)/shard_map/ppermute | solution.py:56
  28.1 3.2 %collective-permute-done.2 = bf16[5,32,1024]{2,1,0:T(8,128)(2,1)S(1)} collective-permute-done((bf16[5,32,1024]{2,1,0:T(8,128)(2,1)S(1)}, bf16[5,32,1024]{2,1,0:T(8,128)(2,1)S(1)}, u32[]{:S(2)}, u32[]{:S(2)}) %collective-permute-start.2) | collective-permute-done | bytes 327712 | tf_op jit(solution)/shard_map/ppermute | solution.py:53
  31.4 1.3 collective-permute-done.5
  32.7 3.5 %collective-permute-start.6 = (bf16[5,32,1024]{2,1,0:T(8,128)(2,1)S(1)}, bf16[5,32,1024]{2,1,0:T(8,128)(2,1)S(1)}, u32[]{:S(2)}, u32[]{:S(2)}) collective-permute-start(bf16[5,32,1024]{2,1,0:T(8,128)(2,1)S(1)} %collective-permute-done.5), channel_id=1, source_target_pairs={{0,112},{16,0},{32,16},{48,32},{64,48},{80,64},{96,80},{112,96},{1... | collective-permute-start | bytes 983048 | tf_op jit(solution)/shard_map/ppermute | solution.py:56
  36.2 2.8 %collective-permute-done.3 = bf16[5,32,1024]{2,1,0:T(8,128)(2,1)S(1)} collective-permute-done((bf16[5,32,1024]{2,1,0:T(8,128)(2,1)S(1)}, bf16[5,32,1024]{2,1,0:T(8,128)(2,1)S(1)}, u32[]{:S(2)}, u32[]{:S(2)}) %collective-permute-start.3) | collective-permute-done | bytes 327712 | tf_op jit(solution)/shard_map/ppermute | solution.py:53
  42.0 1.7 constant_dynamic-update-slice_fusion.11
  46.0 0.8 constant_dynamic-update-slice_fusion.7
  49.1 0.8 constant_dynamic-update-slice_fusion.3
  52.1 17.0 %all-gather.2.cloned.1.call-done = bf16[5,512,1024]{2,1,0:T(8,128)(2,1)} async-done(((bf16[5,32,1024]{2,1,0:T(8,128)(2,1)}), bf16[5,512,1024]{2,1,0:T(8,128)(2,1)}) %all-gather.2.cloned.1.call-update) | async-done | bytes 5242896 | tf_op jit(solution)/shard_map/all_gather | solution.py:103
  69.1 5.2 %fusion.11 = (f32[5,256]{1,0:T(8,128)S(1)}, f32[5,512]{1,0:T(8,128)S(1)}, f32[5,256,512]{2,1,0:T(8,128)S(1)}) fusion(pred[5,256]{1,0:T(8,128)(4,1)S(1)} %broadcast_compare_fusion.1, pred[5,512]{1,0:T(8,128)(4,1)S(1)} %copy.20, bf16[5,512,1024]{2,1,0:T(8,128)(2,1)} %all-gather.2.cloned.1.call-done, ...), kind=kOutput, calls=%fused_computation.26 | convolution fusion | flops 1345450240 | bytes 10504964 | tf_op jit(solution)/shard_map/prd,pcd->prc/dot_general | solution.py:116
  74.3 1.5 copy-done.2
  75.8 1.9 fusion
  77.9 1.1 collective-permute-done.7
  79.0 1.5 collective-permute-start.8
  80.6 1.6 collective-permute-start.14
  82.9 1.8 collective-permute-done.14
  84.8 3.1 %collective-permute-start.15 = (f32[3,5,512]{2,0,1:T(4,128)S(1)}, f32[3,5,512]{2,0,1:T(4,128)S(1)}, u32[]{:S(2)}, u32[]{:S(2)}) collective-permute-start(f32[3,5,512]{2,0,1:T(4,128)S(1)} %pad_maximum_fusion.5), channel_id=1, source_target_pairs={{0,2},{1,3},{2,0},{3,1},{4,6},{5,7},{6,4},{7,5},{8,10},{9,11},{10,... | collective-permute-start | bytes 92168 | tf_op jit(solution)/shard_map/ppermute | solution.py:21
  88.0 2.7 %collective-permute-start.9 = (f32[2,5,256]{2,1,0:T(8,128)S(1)}, f32[2,5,256]{2,1,0:T(8,128)S(1)}, u32[]{:S(2)}, u32[]{:S(2)}) collective-permute-start(f32[2,5,256]{2,1,0:T(8,128)S(1)} %pad_maximum_fusion.10), channel_id=1, source_target_pairs={{0,64},{16,80},{32,96},{48,112},{64,0},{80,16},{96,32},{112,48},{1... | collective-permute-start | bytes 30728 | tf_op jit(solution)/shard_map/ppermute | solution.py:21
  90.8 1.2 collective-permute-start.16
  92.0 1.2 collective-permute-done.9
  93.2 1.7 collective-permute-done.16
  95.0 2.8 %collective-permute-start.17 = (f32[3,5,512]{2,0,1:T(4,128)S(1)}, f32[3,5,512]{2,0,1:T(4,128)S(1)}, u32[]{:S(2)}, u32[]{:S(2)}) collective-permute-start(f32[3,5,512]{2,0,1:T(4,128)S(1)} %pad_maximum_fusion.7), channel_id=1, source_target_pairs={{0,8},{1,9},{2,10},{3,11},{4,12},{5,13},{6,14},{7,15},{8,0},{9,1},... | collective-permute-start | bytes 92168 | tf_op jit(solution)/shard_map/ppermute | solution.py:21
  98.3 2.3 %collective-permute-done.17 = f32[3,5,512]{2,0,1:T(4,128)S(1)} collective-permute-done((f32[3,5,512]{2,0,1:T(4,128)S(1)}, f32[3,5,512]{2,0,1:T(4,128)S(1)}, u32[]{:S(2)}, u32[]{:S(2)}) %collective-permute-start.17) | collective-permute-done | bytes 30752 | tf_op jit(solution)/shard_map/ppermute | solution.py:21
  101.3 2.7 %fusion.4 = bf16[5,512,256]{1,2,0:T(8,128)(2,1)S(1)} fusion(f32[5,256,512]{2,1,0:T(8,128)} %copy-done.2, f32[5,256]{1,0:T(8,128)S(1)} %get-tuple-element.8, f32[5,512]{1,0:T(8,128)S(1)} %copy.27, f32[5]{0:T(128)S(1)} %get-tuple-element.45, pred[5,256]{1,0:T(8,128)(4,1)S(1)} %broadcast_compare_fusion.1, pred[5,512]{1,0:T(8,128)(4,1)S(1)} %copy.20), kind=kLoop, calls=%fused_computation.11 | loop fusion | flops 5898240 | bytes 3951380 | tf_op jit(solution)/shard_map/convert_element_type | solution.py:138
  104.0 7.3 %broadcast_multiply_fusion = f32[5,512,1024]{2,1,0:T(8,128)} fusion(bf16[5,512,256]{1,2,0:T(8,128)(2,1)S(1)} %fusion.4, bf16[5,512,1024]{2,1,0:T(8,128)(2,1)} %constant_dynamic-update-slice_fusion, s32[]{:T(128)S(6)} %select_n.255), kind=kOutput, calls=%fused_computation.5 | convolution fusion | flops 1344798720 | bytes 14417924 | tf_op jit(solution)/shard_map/prc,pcd->prd/dot_general | solution.py:141
  111.6 4.0 %broadcast_multiply_fusion.1 = f32[5,256,1024]{2,1,0:T(8,128)S(1)} fusion(bf16[5,512,256]{1,2,0:T(8,128)(2,1)S(1)} %fusion.4, bf16[5,512,1024]{2,1,0:T(8,128)(2,1)} %all-gather.2.cloned.1.call-done), kind=kOutput, calls=%fused_computation.17 | convolution fusion | flops 1343488000 | bytes 11796480 | tf_op jit(solution)/shard_map/prc,prd->pcd/dot_general | solution.py:145
  116.1 1.9 copy-done
  118.0 5.1 %collective-permute-done.18 = f32[648,1024]{1,0:T(8,128)} collective-permute-done((f32[648,1024]{1,0:T(8,128)S(1)}, f32[648,1024]{1,0:T(8,128)}, u32[]{:S(2)}, u32[]{:S(2)}) %collective-permute-start.18) | collective-permute-done | bytes 2654240 | tf_op jit(solution)/shard_map/ppermute | solution.py:71
  123.1 2.1 slice.218
  126.1 0.8 slice_add_fusion.1
  127.4 18.3 %collective-permute-done.19 = f32[168,1024]{1,0:T(8,128)S(1)} collective-permute-done((f32[168,1024]{1,0:T(8,128)S(1)}, f32[168,1024]{1,0:T(8,128)S(1)}, u32[]{:S(2)}, u32[]{:S(2)}) %collective-permute-start.19) | collective-permute-done | bytes 688160 | tf_op jit(solution)/shard_map/ppermute | solution.py:84
  146.0 18.0 %collective-permute-done.20 = f32[168,1024]{1,0:T(8,128)S(1)} collective-permute-done((f32[168,1024]{1,0:T(8,128)S(1)}, f32[168,1024]{1,0:T(8,128)S(1)}, u32[]{:S(2)}, u32[]{:S(2)}) %collective-permute-start.20) | collective-permute-done | bytes 688160 | tf_op jit(solution)/shard_map/ppermute | solution.py:84
  164.2 1.5 collective-permute-start.10
  165.6 2.1 collective-permute-done.10
  167.7 3.2 %collective-permute-start.11 = (f32[5]{0:T(128)S(1)}, f32[5]{0:T(128)S(1)}, u32[]{:S(2)}, u32[]{:S(2)}) collective-permute-start(f32[5]{0:T(128)S(1)} %fusion.49), channel_id=1, source_target_pairs={{0,2},{1,3},{2,0},{3,1},{4,6},{5,7},{6,4},{7,5},{8,10},{9,11},{10,... | collective-permute-start | bytes 68 | tf_op jit(solution)/shard_map/ppermute | solution.py:32
  171.0 1.8 collective-permute-done.11
  172.8 1.1 collective-permute-start.12
  173.9 2.4 %collective-permute-done.12 = f32[5]{0:T(128)S(1)} collective-permute-done((f32[5]{0:T(128)S(1)}, f32[5]{0:T(128)S(1)}, u32[]{:S(2)}, u32[]{:S(2)}) %collective-permute-start.12) | collective-permute-done | bytes 52 | tf_op jit(solution)/shard_map/ppermute | solution.py:32
  176.3 2.7 %collective-permute-start.13 = (f32[5]{0:T(128)S(1)}, f32[5]{0:T(128)S(1)}, u32[]{:S(2)}, u32[]{:S(2)}) collective-permute-start(f32[5]{0:T(128)S(1)} %fusion.47), channel_id=1, source_target_pairs={{0,8},{1,9},{2,10},{3,11},{4,12},{5,13},{6,14},{7,15},{8,0},{9,1},... | collective-permute-start | bytes 68 | tf_op jit(solution)/shard_map/ppermute | solution.py:32
  179.1 2.1 %collective-permute-done.21 = f32[168,1024]{1,0:T(8,128)S(1)} collective-permute-done((f32[168,1024]{1,0:T(8,128)S(1)}, f32[168,1024]{1,0:T(8,128)S(1)}, u32[]{:S(2)}, u32[]{:S(2)}) %collective-permute-start.21) | collective-permute-done | bytes 688160 | tf_op jit(solution)/shard_map/ppermute | solution.py:84
  182.9 17.6 %reduce-scatter.2.cloned.1.call-done = f32[5,32,1024]{2,1,0:T(8,128)} async-done(((f32[5,512,1024]{2,1,0:T(8,128)}), f32[5,32,1024]{2,1,0:T(8,128)}) %reduce-scatter.2.cloned.1.call-update) | async-done | bytes 655376 | tf_op jit(solution)/shard_map/reduce_scatter | solution.py:148
  200.4 2.4 %fusion.16 = (f32[5,32,1024]{2,1,0:T(8,128)}, f32[5,32,1024]{2,1,0:T(8,128)}) fusion(f32[5,32,1024]{2,1,0:T(8,128)S(1)} %bitcast.117, bf16[5,32,1024]{2,1,0:T(8,128)(2,1)S(1)} %copy-done.4, f32[5]{0:T(128)S(1)} %get-tuple-element.44, pred[5,32]{1,0:T(8,128)(4,1)S(1)} %broadcast_compare_fusion.2, f32[5,32,1024]{2,1,0:T(8,128)} %reduce-scatter.2.cloned.1.call-done, ...), kind=kLoop, calls=%fused_computation.34 | loop fusion | flops 1310720 | bytes 3276980 | tf_op jit(solution)/shard_map/jit(_where)/select_n | solution.py:164
  (102 shorter events, 17.6 us)
Async XLA Ops:
  7.2 41.9 %copy-start.3 = (bf16[5,32,1024]{2,1,0:T(8,128)(2,1)S(1)}, bf16[5,32,1024]{2,1,0:T(8,128)(2,1)}, u32[]{:S(2)}) copy-start(bf16[5,32,1024]{2,1,0:T(8,128)(2,1)} %param.5) | copy-start | bytes 983044
  7.2 61.9 %all-gather.2.cloned.1.call-start = ((), (), s32[]{:S(2)}) async-start(), calls=%async_computation.1 | async-start | bytes 5570560 | tf_op jit(solution)/shard_map/all_gather | solution.py:103
  7.9 192.5 %reduce-scatter.2.cloned.1.call-start = ((), (), s32[]{:S(2)}) async-start(), calls=%async_computation.2 | async-start | bytes 11141120 | tf_op jit(solution)/shard_map/reduce_scatter | solution.py:148
  8.0 7.9 %collective-permute-start = (bf16[5,32,1024]{2,1,0:T(8,128)(2,1)}, bf16[5,32,1024]{2,1,0:T(8,128)(2,1)S(1)}, u32[]{:S(2)}, u32[]{:S(2)}) collective-permute-start(bf16[5,32,1024]{2,1,0:T(8,128)(2,1)} %param.5), channel_id=1, source_target_pairs={{0,16},{16,32},{32,48},{48,64},{64,80},{80,96},{96,112},{112,0},{1... | collective-permute-start | bytes 983048 | tf_op jit(solution)/shard_map/ppermute | solution.py:53
  8.0 17.2 %collective-permute-start.4 = (bf16[5,32,1024]{2,1,0:T(8,128)(2,1)}, bf16[5,32,1024]{2,1,0:T(8,128)(2,1)S(1)}, u32[]{:S(2)}, u32[]{:S(2)}) collective-permute-start(bf16[5,32,1024]{2,1,0:T(8,128)(2,1)} %param.5), channel_id=1, source_target_pairs={{0,112},{16,0},{32,16},{48,32},{64,48},{80,64},{96,80},{112,96},{1... | collective-permute-start | bytes 983048 | tf_op jit(solution)/shard_map/ppermute | solution.py:56
  15.9 7.7 %collective-permute-start.1 = (bf16[5,32,1024]{2,1,0:T(8,128)(2,1)S(1)}, bf16[5,32,1024]{2,1,0:T(8,128)(2,1)S(1)}, u32[]{:S(2)}, u32[]{:S(2)}) collective-permute-start(bf16[5,32,1024]{2,1,0:T(8,128)(2,1)S(1)} %collective-permute-done), channel_id=1, source_target_pairs={{0,16},{16,32},{32,48},{48,64},{64,80},{80,96},{96,112},{112,0},{1... | collective-permute-start | bytes 983048 | tf_op jit(solution)/shard_map/ppermute | solution.py:53
  23.6 7.7 %collective-permute-start.2 = (bf16[5,32,1024]{2,1,0:T(8,128)(2,1)S(1)}, bf16[5,32,1024]{2,1,0:T(8,128)(2,1)S(1)}, u32[]{:S(2)}, u32[]{:S(2)}) collective-permute-start(bf16[5,32,1024]{2,1,0:T(8,128)(2,1)S(1)} %collective-permute-done.1), channel_id=1, source_target_pairs={{0,16},{16,32},{32,48},{48,64},{64,80},{80,96},{96,112},{112,0},{1... | collective-permute-start | bytes 983048 | tf_op jit(solution)/shard_map/ppermute | solution.py:53
  25.2 7.5 %collective-permute-start.5 = (bf16[5,32,1024]{2,1,0:T(8,128)(2,1)S(1)}, bf16[5,32,1024]{2,1,0:T(8,128)(2,1)S(1)}, u32[]{:S(2)}, u32[]{:S(2)}) collective-permute-start(bf16[5,32,1024]{2,1,0:T(8,128)(2,1)S(1)} %collective-permute-done.4), channel_id=1, source_target_pairs={{0,112},{16,0},{32,16},{48,32},{64,48},{80,64},{96,80},{112,96},{1... | collective-permute-start | bytes 983048 | tf_op jit(solution)/shard_map/ppermute | solution.py:56
  31.3 7.7 %collective-permute-start.3 = (bf16[5,32,1024]{2,1,0:T(8,128)(2,1)S(1)}, bf16[5,32,1024]{2,1,0:T(8,128)(2,1)S(1)}, u32[]{:S(2)}, u32[]{:S(2)}) collective-permute-start(bf16[5,32,1024]{2,1,0:T(8,128)(2,1)S(1)} %collective-permute-done.2), channel_id=1, source_target_pairs={{0,16},{16,32},{32,48},{48,64},{64,80},{80,96},{96,112},{112,0},{1... | collective-permute-start | bytes 983048 | tf_op jit(solution)/shard_map/ppermute | solution.py:53
  32.7 12.5 %collective-permute-start.6 = (bf16[5,32,1024]{2,1,0:T(8,128)(2,1)S(1)}, bf16[5,32,1024]{2,1,0:T(8,128)(2,1)S(1)}, u32[]{:S(2)}, u32[]{:S(2)}) collective-permute-start(bf16[5,32,1024]{2,1,0:T(8,128)(2,1)S(1)} %collective-permute-done.5), channel_id=1, source_target_pairs={{0,112},{16,0},{32,16},{48,32},{64,48},{80,64},{96,80},{112,96},{1... | collective-permute-start | bytes 983048 | tf_op jit(solution)/shard_map/ppermute | solution.py:56
  52.1 25.8 %copy-start.6 = (f32[5]{0:T(128)S(1)}, f32[5]{0:T(128)}, u32[]{:S(2)}) copy-start(f32[5]{0:T(128)} %param.7) | copy-start | bytes 64
  52.1 45.8 %copy-start.5 = (s32[5]{0:T(128)S(1)}, s32[5]{0:T(128)}, u32[]{:S(2)}) copy-start(s32[5]{0:T(128)} %param.6) | copy-start | bytes 64
  74.3 1.5 copy-start.2
  77.7 1.3 collective-permute-start.7
  79.0 3.8 %collective-permute-start.8 = (f32[2,5,256]{2,1,0:T(8,128)S(1)}, f32[2,5,256]{2,1,0:T(8,128)S(1)}, u32[]{:S(2)}, u32[]{:S(2)}) collective-permute-start(f32[2,5,256]{2,1,0:T(8,128)S(1)} %pad_maximum_fusion.9), channel_id=1, source_target_pairs={{0,32},{16,48},{32,0},{48,16},{64,96},{80,112},{96,64},{112,80},{1... | collective-permute-start | bytes 30728 | tf_op jit(solution)/shard_map/ppermute | solution.py:21
  80.6 4.1 %collective-permute-start.14 = (f32[3,5,512]{2,0,1:T(4,128)S(1)}, f32[3,5,512]{2,0,1:T(4,128)S(1)}, u32[]{:S(2)}, u32[]{:S(2)}) collective-permute-start(f32[3,5,512]{2,0,1:T(4,128)S(1)} %pad_maximum_fusion.4), channel_id=1, source_target_pairs={{0,1},{1,0},{2,3},{3,2},{4,5},{5,4},{6,7},{7,6},{8,9},{9,8},{10,11... | collective-permute-start | bytes 92168 | tf_op jit(solution)/shard_map/ppermute | solution.py:21
  84.8 5.8 %collective-permute-start.15 = (f32[3,5,512]{2,0,1:T(4,128)S(1)}, f32[3,5,512]{2,0,1:T(4,128)S(1)}, u32[]{:S(2)}, u32[]{:S(2)}) collective-permute-start(f32[3,5,512]{2,0,1:T(4,128)S(1)} %pad_maximum_fusion.5), channel_id=1, source_target_pairs={{0,2},{1,3},{2,0},{3,1},{4,6},{5,7},{6,4},{7,5},{8,10},{9,11},{10,... | collective-permute-start | bytes 92168 | tf_op jit(solution)/shard_map/ppermute | solution.py:21
  88.0 5.2 %collective-permute-start.9 = (f32[2,5,256]{2,1,0:T(8,128)S(1)}, f32[2,5,256]{2,1,0:T(8,128)S(1)}, u32[]{:S(2)}, u32[]{:S(2)}) collective-permute-start(f32[2,5,256]{2,1,0:T(8,128)S(1)} %pad_maximum_fusion.10), channel_id=1, source_target_pairs={{0,64},{16,80},{32,96},{48,112},{64,0},{80,16},{96,32},{112,48},{1... | collective-permute-start | bytes 30728 | tf_op jit(solution)/shard_map/ppermute | solution.py:21
  90.8 4.1 %collective-permute-start.16 = (f32[3,5,512]{2,0,1:T(4,128)S(1)}, f32[3,5,512]{2,0,1:T(4,128)S(1)}, u32[]{:S(2)}, u32[]{:S(2)}) collective-permute-start(f32[3,5,512]{2,0,1:T(4,128)S(1)} %pad_maximum_fusion.6), channel_id=1, source_target_pairs={{0,4},{1,5},{2,6},{3,7},{4,0},{5,1},{6,2},{7,3},{8,12},{9,13},{10,... | collective-permute-start | bytes 92168 | tf_op jit(solution)/shard_map/ppermute | solution.py:21
  95.0 5.6 %collective-permute-start.17 = (f32[3,5,512]{2,0,1:T(4,128)S(1)}, f32[3,5,512]{2,0,1:T(4,128)S(1)}, u32[]{:S(2)}, u32[]{:S(2)}) collective-permute-start(f32[3,5,512]{2,0,1:T(4,128)S(1)} %pad_maximum_fusion.7), channel_id=1, source_target_pairs={{0,8},{1,9},{2,10},{3,11},{4,12},{5,13},{6,14},{7,15},{8,0},{9,1},... | collective-permute-start | bytes 92168 | tf_op jit(solution)/shard_map/ppermute | solution.py:21
  115.7 2.4 %copy-start = (f32[5,256,1024]{2,1,0:T(8,128)}, f32[5,256,1024]{2,1,0:T(8,128)S(1)}, u32[]{:S(2)}) copy-start(f32[5,256,1024]{2,1,0:T(8,128)S(1)} %broadcast_multiply_fusion.1) | copy-start | bytes 15728644
  118.0 5.1 %collective-permute-start.18 = (f32[648,1024]{1,0:T(8,128)S(1)}, f32[648,1024]{1,0:T(8,128)}, u32[]{:S(2)}, u32[]{:S(2)}) collective-permute-start(f32[648,1024]{1,0:T(8,128)S(1)} %maximum_maximum_fusion), channel_id=1, source_target_pairs={{0,16},{16,0},{32,48},{48,32},{64,80},{80,64},{96,112},{112,96},{1... | collective-permute-start | bytes 7962632 | tf_op jit(solution)/shard_map/ppermute | solution.py:71
  118.0 7.1 %copy-start.1 = (f32[5,256,1024]{2,1,0:T(8,128)S(1)}, f32[5,256,1024]{2,1,0:T(8,128)}, u32[]{:S(2)}) copy-start(f32[5,256,1024]{2,1,0:T(8,128)} %copy-done) | copy-start | bytes 15728644
  126.1 74.3 %copy-start.4 = (bf16[5,32,1024]{2,1,0:T(8,128)(2,1)S(1)}, bf16[5,32,1024]{2,1,0:T(8,128)(2,1)}, u32[]{:S(2)}) copy-start(bf16[5,32,1024]{2,1,0:T(8,128)(2,1)} %param.4) | copy-start | bytes 983044
  127.0 18.8 %collective-permute-start.19 = (f32[168,1024]{1,0:T(8,128)S(1)}, f32[168,1024]{1,0:T(8,128)S(1)}, u32[]{:S(2)}, u32[]{:S(2)}) collective-permute-start(f32[168,1024]{1,0:T(8,128)S(1)} %pad_maximum_fusion.3), channel_id=1, source_target_pairs={{0,32},{16,48},{32,64},{48,80},{64,96},{80,112},{96,0},{112,16},{1... | collective-permute-start | bytes 2064392 | tf_op jit(solution)/shard_map/ppermute | solution.py:84
  145.9 18.0 %collective-permute-start.20 = (f32[168,1024]{1,0:T(8,128)S(1)}, f32[168,1024]{1,0:T(8,128)S(1)}, u32[]{:S(2)}, u32[]{:S(2)}) collective-permute-start(f32[168,1024]{1,0:T(8,128)S(1)} %fusion.12), channel_id=1, source_target_pairs={{0,32},{16,48},{32,64},{48,80},{64,96},{80,112},{96,0},{112,16},{1... | collective-permute-start | bytes 2064392 | tf_op jit(solution)/shard_map/ppermute | solution.py:84
  164.0 17.2 %collective-permute-start.21 = (f32[168,1024]{1,0:T(8,128)S(1)}, f32[168,1024]{1,0:T(8,128)S(1)}, u32[]{:S(2)}, u32[]{:S(2)}) collective-permute-start(f32[168,1024]{1,0:T(8,128)S(1)} %fusion.13), channel_id=1, source_target_pairs={{0,32},{16,48},{32,64},{48,80},{64,96},{80,112},{96,0},{112,16},{1... | collective-permute-start | bytes 2064392 | tf_op jit(solution)/shard_map/ppermute | solution.py:84
  164.2 3.6 %collective-permute-start.10 = (f32[5]{0:T(128)S(1)}, f32[5]{0:T(128)S(1)}, u32[]{:S(2)}, u32[]{:S(2)}) collective-permute-start(f32[5]{0:T(128)S(1)} %get-tuple-element.7), channel_id=1, source_target_pairs={{0,1},{1,0},{2,3},{3,2},{4,5},{5,4},{6,7},{7,6},{8,9},{9,8},{10,11... | collective-permute-start | bytes 68 | tf_op jit(solution)/shard_map/ppermute | solution.py:32
  167.7 5.0 %collective-permute-start.11 = (f32[5]{0:T(128)S(1)}, f32[5]{0:T(128)S(1)}, u32[]{:S(2)}, u32[]{:S(2)}) collective-permute-start(f32[5]{0:T(128)S(1)} %fusion.49), channel_id=1, source_target_pairs={{0,2},{1,3},{2,0},{3,1},{4,6},{5,7},{6,4},{7,5},{8,10},{9,11},{10,... | collective-permute-start | bytes 68 | tf_op jit(solution)/shard_map/ppermute | solution.py:32
  172.8 3.5 %collective-permute-start.12 = (f32[5]{0:T(128)S(1)}, f32[5]{0:T(128)S(1)}, u32[]{:S(2)}, u32[]{:S(2)}) collective-permute-start(f32[5]{0:T(128)S(1)} %fusion.48), channel_id=1, source_target_pairs={{0,4},{1,5},{2,6},{3,7},{4,0},{5,1},{6,2},{7,3},{8,12},{9,13},{10,... | collective-permute-start | bytes 68 | tf_op jit(solution)/shard_map/ppermute | solution.py:32
  176.3 5.3 %collective-permute-start.13 = (f32[5]{0:T(128)S(1)}, f32[5]{0:T(128)S(1)}, u32[]{:S(2)}, u32[]{:S(2)}) collective-permute-start(f32[5]{0:T(128)S(1)} %fusion.47), channel_id=1, source_target_pairs={{0,8},{1,9},{2,10},{3,11},{4,12},{5,13},{6,14},{7,15},{8,0},{9,1},... | collective-permute-start | bytes 68 | tf_op jit(solution)/shard_map/ppermute | solution.py:32
Sparse Core Ops, SparseCore 0:
  10.2 58.9 all-gather.1
  111.5 88.8 reduce-scatter.1

commit v7 on v6

--- a/solution.py
+++ b/solution.py
@@ -23,6 +23,23 @@
         stats = merge_pair(jnp.where(lower, stats, other), jnp.where(lower, other, stats))
         bit *= 2
     return stats
+
+
+def group_merge(stats, axis, stride, group):
+    own = lax.axis_index(axis)
+    digit = (own // stride) % group
+    size = lax.axis_size(axis)
+    received = [stats]
+    for shift in range(1, group):
+        perm = [(i, i + ((i // stride + shift) % group - (i // stride) % group) * stride)
+                for i in range(size)]
+        received.append(lax.ppermute(stats, axis, perm))
+    stacked = jnp.stack(received)
+    ordered = jnp.take(stacked, (digit - jnp.arange(group)) % group, axis=0)
+    merged = ordered[0]
+    for member in range(1, group):
+        merged = merge_pair(merged, ordered[member])
+    return merged
 
 
 def butterfly_sum(values, axis, size):
@@ -122,13 +139,15 @@
     col_high = jnp.max(masked, axis=1)
     col_sum = jnp.sum(jnp.where(inside, jnp.exp(masked - col_high[:, None, :]), 0.0), axis=1)
 
-    col_stats = butterfly_merge(jnp.stack([col_high, col_sum]), "dp", dp_size)
+    col_stats = jnp.stack([col_high, col_sum])
+    col_stats = group_merge(group_merge(col_stats, "dp", 1, 2), "dp", 2, dp_size // 2)
     col_high, col_sum = col_stats[0], col_stats[1]
     col_lse = jnp.where(col_valid, col_high + jnp.log(jnp.where(col_valid, col_sum, 1.0)), 0.0)
 
     lanes = jnp.arange(row_count, dtype=jnp.int32)[None, :]
     carried = jnp.where(lanes == 0, own_positive[:, None], 0.0)
-    row_stats = butterfly_merge(jnp.stack([row_high, row_sum, carried]), "pair", pair_size)
+    row_stats = jnp.stack([row_high, row_sum, carried])
+    row_stats = group_merge(group_merge(row_stats, "pair", 1, 4), "pair", 4, pair_size // 4)
     row_high, row_sum, carried = row_stats[0], row_stats[1], row_stats[2]
     row_lse = jnp.where(row_valid, row_high + jnp.log(jnp.where(row_valid, row_sum, 1.0)), 0.0)
     row_part = jnp.sum(row_lse, axis=1) - 2.0 * carried[:, 0]

time: 211 us -> 211 us (level)
  starting transfers between devices: 31.7 us -> 27.1 us
  other arithmetic: 14.8 us -> 18.4 us
    ppermute x4, starting transfers between devices: 8.58 us -> 2.87 us  [butterfly_sum(): other = lax.ppermute(values, axis, [(i, i ^ bit) for i in range(size)])]
    ppermute x4, waiting for transfers between devices: 6.32 us -> 10.8 us  [butterfly_sum(): other = lax.ppermute(values, axis, [(i, i ^ bit) for i in range(size)])]
    reduce_scatter x1, waiting for transfers between devices: 17.6 us -> 13.7 us  [per_device(): lax.psum_scatter(grad_rows, 'pair', scatter_dimension=1, tiled=True)]
    gather x0 -> x4, local copies, waits for them, and re-layouts: none -> 2.39 us  [group_merge(): ordered = jnp.take(stacked, (digit - jnp.arange(group)) % group, axis=0)]
    ppermute x7 -> x10, starting transfers between devices: 13 us -> 12.2 us  [group_merge(): received.append(lax.ppermute(stats, axis, perm))]
    unnamed x29 -> x28, local copies, waits for them, and re-layouts: 15.7 us -> 15 us
    ppermute x7 -> x10, waiting for transfers between devices: 8.7 us -> 8.95 us  [group_merge(): received.append(lax.ppermute(stats, axis, perm))]
  transfers between devices with their start and end apart: 24 -> 27, of which waited for: 20 -> 20; matrix products, arithmetic and copies ran while one was open for 13% -> 15% of each run, Pallas kernels for 0% -> 0%
where the time goes in v7:
time: 211 us; the launch traced here: 210 us
  waiting for transfers between devices  111 us (53%)
  starting transfers between devices  27.1 us (13%)
  local copies, waits for them, and re-layouts  21 us (10%)
  other arithmetic  18.4 us (9%)
  matrix products  16.5 us (8%)
  between operations  16.2 us (8%)
    ppermute x3, waiting for transfers between devices, two_stage_reduce_scatter(): running = lax.ppermute(running, axis, ring) + addend(chip - 1 - step)  37.8 us
    all_gather x1, waiting for transfers between devices, per_device(): row_set = lax.all_gather(anchor, 'pair', axis=1, tiled=True)  16.9 us
    ppermute x4, waiting for transfers between devices, ring_gather(): ahead = lax.ppermute(ahead, axis, forward)  16.5 us
    unnamed x28, local copies, waits for them, and re-layouts  15 us
    reduce_scatter x1, waiting for transfers between devices, per_device(): lax.psum_scatter(grad_rows, 'pair', scatter_dimension=1, tiled=True)  13.7 us
    ppermute x10, starting transfers between devices, group_merge(): received.append(lax.ppermute(stats, axis, perm))  12.2 us
    ppermute x4, waiting for transfers between devices, butterfly_sum(): other = lax.ppermute(values, axis, [(i, i ^ bit) for i in range(size)])  10.8 us
    ppermute x3, starting transfers between devices, ring_gather(): behind = lax.ppermute(behind, axis, backward)  9.41 us
  transfers between devices with their start and end apart: 27, of which 20 were waited for; matrix products, arithmetic and copies ran while one was open for 15% of the time, Pallas kernels for 0%

profile of v7, /device:TPU:0, one launch (start us, length us, event | category | flops | bytes accessed | tf_op | source)
XLA Modules:
  0.0 210.4 jit_solution(16853269041058675096)
XLA Ops:
  8.0 2.9 %collective-permute-start.4 = (bf16[5,32,1024]{2,1,0:T(8,128)(2,1)}, bf16[5,32,1024]{2,1,0:T(8,128)(2,1)S(1)}, u32[]{:S(2)}, u32[]{:S(2)}) collective-permute-start(bf16[5,32,1024]{2,1,0:T(8,128)(2,1)} %param.7), channel_id=1, source_target_pairs={{0,112},{16,0},{32,16},{48,32},{64,48},{80,64},{96,80},{112,96},{1... | collective-permute-start | bytes 983048 | tf_op jit(solution)/shard_map/ppermute | solution.py:73
  11.2 1.2 fusion.17
  12.4 0.8 select_reduce_fusion.1
  13.9 1.9 collective-permute-done
  16.6 7.0 %collective-permute-done.1 = bf16[5,32,1024]{2,1,0:T(8,128)(2,1)S(1)} collective-permute-done((bf16[5,32,1024]{2,1,0:T(8,128)(2,1)S(1)}, bf16[5,32,1024]{2,1,0:T(8,128)(2,1)S(1)}, u32[]{:S(2)}, u32[]{:S(2)}) %collective-permute-start.1) | collective-permute-done | bytes 327712 | tf_op jit(solution)/shard_map/ppermute | solution.py:70
  24.3 3.0 %collective-permute-start.5 = (bf16[5,32,1024]{2,1,0:T(8,128)(2,1)S(1)}, bf16[5,32,1024]{2,1,0:T(8,128)(2,1)S(1)}, u32[]{:S(2)}, u32[]{:S(2)}) collective-permute-start(bf16[5,32,1024]{2,1,0:T(8,128)(2,1)S(1)} %collective-permute-done.4), channel_id=1, source_target_pairs={{0,112},{16,0},{32,16},{48,32},{64,48},{80,64},{96,80},{112,96},{1... | collective-permute-start | bytes 983048 | tf_op jit(solution)/shard_map/ppermute | solution.py:73
  27.3 4.0 %collective-permute-done.2 = bf16[5,32,1024]{2,1,0:T(8,128)(2,1)S(1)} collective-permute-done((bf16[5,32,1024]{2,1,0:T(8,128)(2,1)S(1)}, bf16[5,32,1024]{2,1,0:T(8,128)(2,1)S(1)}, u32[]{:S(2)}, u32[]{:S(2)}) %collective-permute-start.2) | collective-permute-done | bytes 327712 | tf_op jit(solution)/shard_map/ppermute | solution.py:70
  31.9 3.5 %collective-permute-start.6 = (bf16[5,32,1024]{2,1,0:T(8,128)(2,1)S(1)}, bf16[5,32,1024]{2,1,0:T(8,128)(2,1)S(1)}, u32[]{:S(2)}, u32[]{:S(2)}) collective-permute-start(bf16[5,32,1024]{2,1,0:T(8,128)(2,1)S(1)} %collective-permute-done.5), channel_id=1, source_target_pairs={{0,112},{16,0},{32,16},{48,32},{64,48},{80,64},{96,80},{112,96},{1... | collective-permute-start | bytes 983048 | tf_op jit(solution)/shard_map/ppermute | solution.py:73
  35.4 3.6 %collective-permute-done.3 = bf16[5,32,1024]{2,1,0:T(8,128)(2,1)S(1)} collective-permute-done((bf16[5,32,1024]{2,1,0:T(8,128)(2,1)S(1)}, bf16[5,32,1024]{2,1,0:T(8,128)(2,1)S(1)}, u32[]{:S(2)}, u32[]{:S(2)}) %collective-permute-start.3) | collective-permute-done | bytes 327712 | tf_op jit(solution)/shard_map/ppermute | solution.py:70
  39.0 0.8 constant_dynamic-update-slice_fusion.15
  40.6 0.8 constant_dynamic-update-slice_fusion.13
  42.1 1.8 constant_dynamic-update-slice_fusion.11
  46.9 0.8 constant_dynamic-update-slice_fusion.6
  52.3 16.9 %all-gather.2.cloned.1.call-done = bf16[5,512,1024]{2,1,0:T(8,128)(2,1)} async-done(((bf16[5,32,1024]{2,1,0:T(8,128)(2,1)}), bf16[5,512,1024]{2,1,0:T(8,128)(2,1)}) %all-gather.2.cloned.1.call-update) | async-done | bytes 5242896 | tf_op jit(solution)/shard_map/all_gather | solution.py:120
  69.2 5.2 %fusion.11 = (f32[5,256]{1,0:T(8,128)S(1)}, f32[5,512]{1,0:T(8,128)S(1)}, f32[5,256,512]{2,1,0:T(8,128)S(1)}) fusion(pred[5,256]{1,0:T(8,128)(4,1)S(1)} %broadcast_compare_fusion.1, pred[5,512]{1,0:T(8,128)(4,1)S(1)} %broadcast_compare_fusion, bf16[5,512,1024]{2,1,0:T(8,128)(2,1)} %all-gather.2.cloned.1.call-done, ...), kind=kOutput, calls=%fused_computation.30 | convolution fusion | flops 1345450240 | bytes 10504964 | tf_op jit(solution)/shard_map/prd,pcd->prc/dot_general | solution.py:133
  74.4 1.5 copy-done.2
  75.9 1.9 fusion
  78.0 1.1 collective-permute-done.7
  79.8 2.8 %collective-permute-start.10 = (f32[2,5,256]{2,1,0:T(8,128)S(1)}, f32[2,5,256]{2,1,0:T(8,128)S(1)}, u32[]{:S(2)}, u32[]{:S(2)}) collective-permute-start(f32[2,5,256]{2,1,0:T(8,128)S(1)} %get-tuple-element.34), channel_id=1, source_target_pairs={{0,96},{16,112},{32,0},{48,16},{64,32},{80,48},{96,64},{112,80},{1... | collective-permute-start | bytes 30728 | tf_op jit(solution)/shard_map/ppermute | solution.py:36
  82.5 0.8 collective-permute-start.9
  83.4 0.9 collective-permute-start.8
  84.3 2.8 %collective-permute-start.17 = (f32[3,5,512]{2,0,1:T(4,128)S(1)}, f32[3,5,512]{2,0,1:T(4,128)S(1)}, u32[]{:S(2)}, u32[]{:S(2)}) collective-permute-start(f32[3,5,512]{2,0,1:T(4,128)S(1)} %get-tuple-element.32), channel_id=1, source_target_pairs={{0,3},{1,0},{2,1},{3,2},{4,7},{5,4},{6,5},{7,6},{8,11},{9,8},{10,9... | collective-permute-start | bytes 92168 | tf_op jit(solution)/shard_map/ppermute | solution.py:36
  87.1 0.8 collective-permute-start.16
  87.9 0.9 collective-permute-start.15
  89.4 3.2 %collective-permute-done.16 = f32[3,5,512]{2,0,1:T(4,128)S(1)} collective-permute-done((f32[3,5,512]{2,0,1:T(4,128)S(1)}, f32[3,5,512]{2,0,1:T(4,128)S(1)}, u32[]{:S(2)}, u32[]{:S(2)}) %collective-permute-start.16) | collective-permute-done | bytes 30752 | tf_op jit(solution)/shard_map/ppermute | solution.py:36
  94.1 1.6 collective-permute-start.20
  96.4 0.9 collective-permute-start.18
  98.2 3.0 %collective-permute-done.19 = f32[3,5,512]{2,0,1:T(4,128)S(1)} collective-permute-done((f32[3,5,512]{2,0,1:T(4,128)S(1)}, f32[3,5,512]{2,0,1:T(4,128)S(1)}, u32[]{:S(2)}, u32[]{:S(2)}) %collective-permute-start.19) | collective-permute-done | bytes 30752 | tf_op jit(solution)/shard_map/ppermute | solution.py:36
  102.7 2.7 %fusion.4 = bf16[5,512,256]{1,2,0:T(8,128)(2,1)S(1)} fusion(f32[5,256,512]{2,1,0:T(8,128)} %copy-done.2, f32[5,256]{1,0:T(8,128)S(1)} %get-tuple-element.9, f32[5,512]{1,0:T(8,128)S(1)} %get-tuple-element.13, f32[5]{0:T(128)S(1)} %get-tuple-element.40, pred[5,256]{1,0:T(8,128)(4,1)S(1)} %broadcast_compare_fusion.1, pred[5,512]{1,0:T(8,128)(4,1)S(1)} %broadcast_compare_fusion), kind=kLoop, calls=%fused_computation.15 | loop fusion | flops 5898240 | bytes 3951380 | tf_op jit(solution)/shard_map/convert_element_type | solution.py:157
  105.4 7.3 %broadcast_multiply_fusion = f32[5,512,1024]{2,1,0:T(8,128)} fusion(bf16[5,512,256]{1,2,0:T(8,128)(2,1)S(1)} %fusion.4, bf16[5,512,1024]{2,1,0:T(8,128)(2,1)} %constant_dynamic-update-slice_fusion, s32[]{:T(128)S(6)} %select_n.293), kind=kOutput, calls=%fused_computation.9 | convolution fusion | flops 1344798720 | bytes 14417924 | tf_op jit(solution)/shard_map/prc,pcd->prd/dot_general | solution.py:160
  113.2 4.0 %broadcast_multiply_fusion.1 = f32[5,256,1024]{2,1,0:T(8,128)S(1)} fusion(bf16[5,512,256]{1,2,0:T(8,128)(2,1)S(1)} %fusion.4, bf16[5,512,1024]{2,1,0:T(8,128)(2,1)} %all-gather.2.cloned.1.call-done), kind=kOutput, calls=%fused_computation.21 | convolution fusion | flops 1343488000 | bytes 11796480 | tf_op jit(solution)/shard_map/prc,prd->pcd/dot_general | solution.py:164
  117.4 2.0 maximum_maximum_fusion
  119.4 0.9 copy-done
  120.4 5.3 %collective-permute-done.21 = f32[648,1024]{1,0:T(8,128)} collective-permute-done((f32[648,1024]{1,0:T(8,128)}, f32[648,1024]{1,0:T(8,128)}, u32[]{:S(2)}, u32[]{:S(2)}) %collective-permute-start.21) | collective-permute-done | bytes 2654240 | tf_op jit(solution)/shard_map/ppermute | solution.py:88
  125.7 2.1 %slice.312 = f32[640,1024]{1,0:T(8,128)S(1)} slice(f32[648,1024]{1,0:T(8,128)} %collective-permute-done.21), slice={[0:640], [0:1024]} | slice | bytes 5242880 | tf_op jit(solution)/shard_map/slice | solution.py:89
  128.8 0.8 slice_add_fusion
  129.6 1.8 collective-permute-start.22
  131.5 16.9 %collective-permute-done.22 = f32[168,1024]{1,0:T(8,128)S(1)} collective-permute-done((f32[168,1024]{1,0:T(8,128)S(1)}, f32[168,1024]{1,0:T(8,128)S(1)}, u32[]{:S(2)}, u32[]{:S(2)}) %collective-permute-start.22) | collective-permute-done | bytes 688160 | tf_op jit(solution)/shard_map/ppermute | solution.py:101
  149.1 17.4 %collective-permute-done.23 = f32[168,1024]{1,0:T(8,128)S(1)} collective-permute-done((f32[168,1024]{1,0:T(8,128)S(1)}, f32[168,1024]{1,0:T(8,128)S(1)}, u32[]{:S(2)}, u32[]{:S(2)}) %collective-permute-start.23) | collective-permute-done | bytes 688160 | tf_op jit(solution)/shard_map/ppermute | solution.py:101
  166.5 0.9 fusion.13
  167.6 3.5 %collective-permute-done.11 = f32[5]{0:T(128)S(1)} collective-permute-done((f32[5]{0:T(128)S(1)}, f32[5]{0:T(128)S(1)}, u32[]{:S(2)}, u32[]{:S(2)}) %collective-permute-start.11) | collective-permute-done | bytes 52 | tf_op jit(solution)/shard_map/ppermute | solution.py:49
  171.1 1.4 collective-permute-start.12
  172.5 3.7 %collective-permute-done.12 = f32[5]{0:T(128)S(1)} collective-permute-done((f32[5]{0:T(128)S(1)}, f32[5]{0:T(128)S(1)}, u32[]{:S(2)}, u32[]{:S(2)}) %collective-permute-start.12) | collective-permute-done | bytes 52 | tf_op jit(solution)/shard_map/ppermute | solution.py:49
  176.2 3.5 %collective-permute-done.13 = f32[5]{0:T(128)S(1)} collective-permute-done((f32[5]{0:T(128)S(1)}, f32[5]{0:T(128)S(1)}, u32[]{:S(2)}, u32[]{:S(2)}) %collective-permute-start.13) | collective-permute-done | bytes 52 | tf_op jit(solution)/shard_map/ppermute | solution.py:49
  179.7 1.5 collective-permute-start.14
  181.2 3.5 %collective-permute-done.24 = f32[168,1024]{1,0:T(8,128)S(1)} collective-permute-done((f32[168,1024]{1,0:T(8,128)}, f32[168,1024]{1,0:T(8,128)S(1)}, u32[]{:S(2)}, u32[]{:S(2)}) %collective-permute-start.24) | collective-permute-done | bytes 688160 | tf_op jit(solution)/shard_map/ppermute | solution.py:101
  186.4 13.7 %reduce-scatter.2.cloned.1.call-done = f32[5,32,1024]{2,1,0:T(8,128)} async-done(((f32[5,512,1024]{2,1,0:T(8,128)}), f32[5,32,1024]{2,1,0:T(8,128)}) %reduce-scatter.2.cloned.1.call-update) | async-done | bytes 655376 | tf_op jit(solution)/shard_map/reduce_scatter | solution.py:167
  200.0 2.4 %fusion.16 = (f32[5,32,1024]{2,1,0:T(8,128)}, f32[5,32,1024]{2,1,0:T(8,128)}) fusion(f32[5,32,1024]{2,1,0:T(8,128)S(1)} %bitcast.353, bf16[5,32,1024]{2,1,0:T(8,128)(2,1)S(1)} %copy-done.4, f32[5]{0:T(128)S(1)} %get-tuple-element.39, pred[5,32]{1,0:T(8,128)(4,1)S(1)} %broadcast_compare_fusion.2, f32[5,32,1024]{2,1,0:T(8,128)} %reduce-scatter.2.cloned.1.call-done, ...), kind=kLoop, calls=%fused_computation.38 | loop fusion | flops 1310720 | bytes 3276980 | tf_op jit(solution)/shard_map/jit(_where)/select_n | solution.py:183
  (115 shorter events, 22.4 us)
Async XLA Ops:
  7.2 42.1 %copy-start.3 = (bf16[5,32,1024]{2,1,0:T(8,128)(2,1)S(1)}, bf16[5,32,1024]{2,1,0:T(8,128)(2,1)}, u32[]{:S(2)}) copy-start(bf16[5,32,1024]{2,1,0:T(8,128)(2,1)} %param.7) | copy-start | bytes 983044
  7.2 62.0 %all-gather.2.cloned.1.call-start = ((), (), s32[]{:S(2)}) async-start(), calls=%async_computation.1 | async-start | bytes 5570560 | tf_op jit(solution)/shard_map/all_gather | solution.py:120
  7.9 192.1 %reduce-scatter.2.cloned.1.call-start = ((), (), s32[]{:S(2)}) async-start(), calls=%async_computation.2 | async-start | bytes 11141120 | tf_op jit(solution)/shard_map/reduce_scatter | solution.py:167
  8.0 7.9 %collective-permute-start = (bf16[5,32,1024]{2,1,0:T(8,128)(2,1)}, bf16[5,32,1024]{2,1,0:T(8,128)(2,1)S(1)}, u32[]{:S(2)}, u32[]{:S(2)}) collective-permute-start(bf16[5,32,1024]{2,1,0:T(8,128)(2,1)} %param.7), channel_id=1, source_target_pairs={{0,16},{16,32},{32,48},{48,64},{64,80},{80,96},{96,112},{112,0},{1... | collective-permute-start | bytes 983048 | tf_op jit(solution)/shard_map/ppermute | solution.py:70
  8.0 16.4 %collective-permute-start.4 = (bf16[5,32,1024]{2,1,0:T(8,128)(2,1)}, bf16[5,32,1024]{2,1,0:T(8,128)(2,1)S(1)}, u32[]{:S(2)}, u32[]{:S(2)}) collective-permute-start(bf16[5,32,1024]{2,1,0:T(8,128)(2,1)} %param.7), channel_id=1, source_target_pairs={{0,112},{16,0},{32,16},{48,32},{64,48},{80,64},{96,80},{112,96},{1... | collective-permute-start | bytes 983048 | tf_op jit(solution)/shard_map/ppermute | solution.py:73
  15.9 7.7 %collective-permute-start.1 = (bf16[5,32,1024]{2,1,0:T(8,128)(2,1)S(1)}, bf16[5,32,1024]{2,1,0:T(8,128)(2,1)S(1)}, u32[]{:S(2)}, u32[]{:S(2)}) collective-permute-start(bf16[5,32,1024]{2,1,0:T(8,128)(2,1)S(1)} %collective-permute-done), channel_id=1, source_target_pairs={{0,16},{16,32},{32,48},{48,64},{64,80},{80,96},{96,112},{112,0},{1... | collective-permute-start | bytes 983048 | tf_op jit(solution)/shard_map/ppermute | solution.py:70
  23.6 7.7 %collective-permute-start.2 = (bf16[5,32,1024]{2,1,0:T(8,128)(2,1)S(1)}, bf16[5,32,1024]{2,1,0:T(8,128)(2,1)S(1)}, u32[]{:S(2)}, u32[]{:S(2)}) collective-permute-start(bf16[5,32,1024]{2,1,0:T(8,128)(2,1)S(1)} %collective-permute-done.1), channel_id=1, source_target_pairs={{0,16},{16,32},{32,48},{48,64},{64,80},{80,96},{96,112},{112,0},{1... | collective-permute-start | bytes 983048 | tf_op jit(solution)/shard_map/ppermute | solution.py:70
  24.3 7.5 %collective-permute-start.5 = (bf16[5,32,1024]{2,1,0:T(8,128)(2,1)S(1)}, bf16[5,32,1024]{2,1,0:T(8,128)(2,1)S(1)}, u32[]{:S(2)}, u32[]{:S(2)}) collective-permute-start(bf16[5,32,1024]{2,1,0:T(8,128)(2,1)S(1)} %collective-permute-done.4), channel_id=1, source_target_pairs={{0,112},{16,0},{32,16},{48,32},{64,48},{80,64},{96,80},{112,96},{1... | collective-permute-start | bytes 983048 | tf_op jit(solution)/shard_map/ppermute | solution.py:73
  31.3 7.7 %collective-permute-start.3 = (bf16[5,32,1024]{2,1,0:T(8,128)(2,1)S(1)}, bf16[5,32,1024]{2,1,0:T(8,128)(2,1)S(1)}, u32[]{:S(2)}, u32[]{:S(2)}) collective-permute-start(bf16[5,32,1024]{2,1,0:T(8,128)(2,1)S(1)} %collective-permute-done.2), channel_id=1, source_target_pairs={{0,16},{16,32},{32,48},{48,64},{64,80},{80,96},{96,112},{112,0},{1... | collective-permute-start | bytes 983048 | tf_op jit(solution)/shard_map/ppermute | solution.py:70
  31.9 13.5 %collective-permute-start.6 = (bf16[5,32,1024]{2,1,0:T(8,128)(2,1)S(1)}, bf16[5,32,1024]{2,1,0:T(8,128)(2,1)S(1)}, u32[]{:S(2)}, u32[]{:S(2)}) collective-permute-start(bf16[5,32,1024]{2,1,0:T(8,128)(2,1)S(1)} %collective-permute-done.5), channel_id=1, source_target_pairs={{0,112},{16,0},{32,16},{48,32},{64,48},{80,64},{96,80},{112,96},{1... | collective-permute-start | bytes 983048 | tf_op jit(solution)/shard_map/ppermute | solution.py:73
  52.3 45.0 %copy-start.5 = (s32[5]{0:T(128)S(1)}, s32[5]{0:T(128)}, u32[]{:S(2)}) copy-start(s32[5]{0:T(128)} %param.8) | copy-start | bytes 64
  74.4 1.5 copy-start.2
  77.8 1.3 collective-permute-start.7
  79.8 8.1 %collective-permute-start.10 = (f32[2,5,256]{2,1,0:T(8,128)S(1)}, f32[2,5,256]{2,1,0:T(8,128)S(1)}, u32[]{:S(2)}, u32[]{:S(2)}) collective-permute-start(f32[2,5,256]{2,1,0:T(8,128)S(1)} %get-tuple-element.34), channel_id=1, source_target_pairs={{0,96},{16,112},{32,0},{48,16},{64,32},{80,48},{96,64},{112,80},{1... | collective-permute-start | bytes 30728 | tf_op jit(solution)/shard_map/ppermute | solution.py:36
  82.5 6.2 %collective-permute-start.9 = (f32[2,5,256]{2,1,0:T(8,128)S(1)}, f32[2,5,256]{2,1,0:T(8,128)S(1)}, u32[]{:S(2)}, u32[]{:S(2)}) collective-permute-start(f32[2,5,256]{2,1,0:T(8,128)S(1)} %get-tuple-element.34), channel_id=1, source_target_pairs={{0,64},{16,80},{32,96},{48,112},{64,0},{80,16},{96,32},{112,48},{1... | collective-permute-start | bytes 30728 | tf_op jit(solution)/shard_map/ppermute | solution.py:36
  83.4 5.4 %collective-permute-start.8 = (f32[2,5,256]{2,1,0:T(8,128)S(1)}, f32[2,5,256]{2,1,0:T(8,128)S(1)}, u32[]{:S(2)}, u32[]{:S(2)}) collective-permute-start(f32[2,5,256]{2,1,0:T(8,128)S(1)} %get-tuple-element.34), channel_id=1, source_target_pairs={{0,32},{16,48},{32,64},{48,80},{64,96},{80,112},{96,0},{112,16},{1... | collective-permute-start | bytes 30728 | tf_op jit(solution)/shard_map/ppermute | solution.py:36
  84.3 5.2 %collective-permute-start.17 = (f32[3,5,512]{2,0,1:T(4,128)S(1)}, f32[3,5,512]{2,0,1:T(4,128)S(1)}, u32[]{:S(2)}, u32[]{:S(2)}) collective-permute-start(f32[3,5,512]{2,0,1:T(4,128)S(1)} %get-tuple-element.32), channel_id=1, source_target_pairs={{0,3},{1,0},{2,1},{3,2},{4,7},{5,4},{6,5},{7,6},{8,11},{9,8},{10,9... | collective-permute-start | bytes 92168 | tf_op jit(solution)/shard_map/ppermute | solution.py:36
  87.1 5.5 %collective-permute-start.16 = (f32[3,5,512]{2,0,1:T(4,128)S(1)}, f32[3,5,512]{2,0,1:T(4,128)S(1)}, u32[]{:S(2)}, u32[]{:S(2)}) collective-permute-start(f32[3,5,512]{2,0,1:T(4,128)S(1)} %get-tuple-element.32), channel_id=1, source_target_pairs={{0,2},{1,3},{2,0},{3,1},{4,6},{5,7},{6,4},{7,5},{8,10},{9,11},{10,... | collective-permute-start | bytes 92168 | tf_op jit(solution)/shard_map/ppermute | solution.py:36
  87.9 5.2 %collective-permute-start.15 = (f32[3,5,512]{2,0,1:T(4,128)S(1)}, f32[3,5,512]{2,0,1:T(4,128)S(1)}, u32[]{:S(2)}, u32[]{:S(2)}) collective-permute-start(f32[3,5,512]{2,0,1:T(4,128)S(1)} %get-tuple-element.32), channel_id=1, source_target_pairs={{0,1},{1,2},{2,3},{3,0},{4,5},{5,6},{6,7},{7,4},{8,9},{9,10},{10,1... | collective-permute-start | bytes 92168 | tf_op jit(solution)/shard_map/ppermute | solution.py:36
  94.1 4.1 %collective-permute-start.20 = (f32[3,5,512]{2,0,1:T(4,128)S(1)}, f32[3,5,512]{2,0,1:T(4,128)S(1)}, u32[]{:S(2)}, u32[]{:S(2)}) collective-permute-start(f32[3,5,512]{2,0,1:T(4,128)S(1)} %get-tuple-element.30), channel_id=1, source_target_pairs={{0,12},{1,13},{2,14},{3,15},{4,0},{5,1},{6,2},{7,3},{8,4},{9,5},{1... | collective-permute-start | bytes 92168 | tf_op jit(solution)/shard_map/ppermute | solution.py:36
  95.7 5.5 %collective-permute-start.19 = (f32[3,5,512]{2,0,1:T(4,128)S(1)}, f32[3,5,512]{2,0,1:T(4,128)S(1)}, u32[]{:S(2)}, u32[]{:S(2)}) collective-permute-start(f32[3,5,512]{2,0,1:T(4,128)S(1)} %get-tuple-element.30), channel_id=1, source_target_pairs={{0,8},{1,9},{2,10},{3,11},{4,12},{5,13},{6,14},{7,15},{8,0},{9,1},... | collective-permute-start | bytes 92168 | tf_op jit(solution)/shard_map/ppermute | solution.py:36
  96.4 5.2 %collective-permute-start.18 = (f32[3,5,512]{2,0,1:T(4,128)S(1)}, f32[3,5,512]{2,0,1:T(4,128)S(1)}, u32[]{:S(2)}, u32[]{:S(2)}) collective-permute-start(f32[3,5,512]{2,0,1:T(4,128)S(1)} %get-tuple-element.30), channel_id=1, source_target_pairs={{0,4},{1,5},{2,6},{3,7},{4,8},{5,9},{6,10},{7,11},{8,12},{9,13},{1... | collective-permute-start | bytes 92168 | tf_op jit(solution)/shard_map/ppermute | solution.py:36
  117.2 3.2 %copy-start = (f32[5,256,1024]{2,1,0:T(8,128)}, f32[5,256,1024]{2,1,0:T(8,128)S(1)}, u32[]{:S(2)}) copy-start(f32[5,256,1024]{2,1,0:T(8,128)S(1)} %broadcast_multiply_fusion.1) | copy-start | bytes 15728644
  120.4 5.3 %collective-permute-start.21 = (f32[648,1024]{1,0:T(8,128)}, f32[648,1024]{1,0:T(8,128)}, u32[]{:S(2)}, u32[]{:S(2)}) collective-permute-start(f32[648,1024]{1,0:T(8,128)} %maximum_maximum_fusion), channel_id=1, source_target_pairs={{0,16},{16,0},{32,48},{48,32},{64,80},{80,64},{96,112},{112,96},{1... | collective-permute-start | bytes 7962632 | tf_op jit(solution)/shard_map/ppermute | solution.py:88
  120.4 7.4 %copy-start.1 = (f32[5,256,1024]{2,1,0:T(8,128)S(1)}, f32[5,256,1024]{2,1,0:T(8,128)}, u32[]{:S(2)}) copy-start(f32[5,256,1024]{2,1,0:T(8,128)} %copy-done) | copy-start | bytes 15728644
  128.8 71.3 %copy-start.4 = (bf16[5,32,1024]{2,1,0:T(8,128)(2,1)S(1)}, bf16[5,32,1024]{2,1,0:T(8,128)(2,1)}, u32[]{:S(2)}) copy-start(bf16[5,32,1024]{2,1,0:T(8,128)(2,1)} %param.6) | copy-start | bytes 983044
  129.6 18.8 %collective-permute-start.22 = (f32[168,1024]{1,0:T(8,128)S(1)}, f32[168,1024]{1,0:T(8,128)S(1)}, u32[]{:S(2)}, u32[]{:S(2)}) collective-permute-start(f32[168,1024]{1,0:T(8,128)S(1)} %pad_maximum_fusion.3), channel_id=1, source_target_pairs={{0,32},{16,48},{32,64},{48,80},{64,96},{80,112},{96,0},{112,16},{1... | collective-permute-start | bytes 2064392 | tf_op jit(solution)/shard_map/ppermute | solution.py:101
  148.5 18.0 %collective-permute-start.23 = (f32[168,1024]{1,0:T(8,128)S(1)}, f32[168,1024]{1,0:T(8,128)S(1)}, u32[]{:S(2)}, u32[]{:S(2)}) collective-permute-start(f32[168,1024]{1,0:T(8,128)S(1)} %fusion.12), channel_id=1, source_target_pairs={{0,32},{16,48},{32,64},{48,80},{64,96},{80,112},{96,0},{112,16},{1... | collective-permute-start | bytes 2064392 | tf_op jit(solution)/shard_map/ppermute | solution.py:101
  167.4 17.3 %collective-permute-start.24 = (f32[168,1024]{1,0:T(8,128)}, f32[168,1024]{1,0:T(8,128)S(1)}, u32[]{:S(2)}, u32[]{:S(2)}) collective-permute-start(f32[168,1024]{1,0:T(8,128)} %fusion.13), channel_id=1, source_target_pairs={{0,32},{16,48},{32,64},{48,80},{64,96},{80,112},{96,0},{112,16},{1... | collective-permute-start | bytes 2064392 | tf_op jit(solution)/shard_map/ppermute | solution.py:101
  167.5 3.6 %collective-permute-start.11 = (f32[5]{0:T(128)S(1)}, f32[5]{0:T(128)S(1)}, u32[]{:S(2)}, u32[]{:S(2)}) collective-permute-start(f32[5]{0:T(128)S(1)} %get-tuple-element.8), channel_id=1, source_target_pairs={{0,1},{1,0},{2,3},{3,2},{4,5},{5,4},{6,7},{7,6},{8,9},{9,8},{10,11... | collective-permute-start | bytes 68 | tf_op jit(solution)/shard_map/ppermute | solution.py:49
  171.1 5.0 %collective-permute-start.12 = (f32[5]{0:T(128)S(1)}, f32[5]{0:T(128)S(1)}, u32[]{:S(2)}, u32[]{:S(2)}) collective-permute-start(f32[5]{0:T(128)S(1)} %fusion.90), channel_id=1, source_target_pairs={{0,2},{1,3},{2,0},{3,1},{4,6},{5,7},{6,4},{7,5},{8,10},{9,11},{10,... | collective-permute-start | bytes 68 | tf_op jit(solution)/shard_map/ppermute | solution.py:49
  176.2 3.5 %collective-permute-start.13 = (f32[5]{0:T(128)S(1)}, f32[5]{0:T(128)S(1)}, u32[]{:S(2)}, u32[]{:S(2)}) collective-permute-start(f32[5]{0:T(128)S(1)} %fusion.89), channel_id=1, source_target_pairs={{0,4},{1,5},{2,6},{3,7},{4,0},{5,1},{6,2},{7,3},{8,12},{9,13},{10,... | collective-permute-start | bytes 68 | tf_op jit(solution)/shard_map/ppermute | solution.py:49
  179.7 5.4 %collective-permute-start.14 = (f32[5]{0:T(128)S(1)}, f32[5]{0:T(128)S(1)}, u32[]{:S(2)}, u32[]{:S(2)}) collective-permute-start(f32[5]{0:T(128)S(1)} %fusion.88), channel_id=1, source_target_pairs={{0,8},{1,9},{2,10},{3,11},{4,12},{5,13},{6,14},{7,15},{8,0},{9,1},... | collective-permute-start | bytes 68 | tf_op jit(solution)/shard_map/ppermute | solution.py:49
Sparse Core Ops, SparseCore 0:
  10.2 58.9 all-gather.1
  112.9 87.0 reduce-scatter.1

commit v8 on v7

--- a/solution.py
+++ b/solution.py
@@ -3,9 +3,10 @@
 import jax
 import jax.numpy as jnp
 from jax import lax
-from jax.sharding import PartitionSpec as P
+from jax.sharding import Mesh, PartitionSpec as P
 
 NEG = -1e30
+PAIR = ("pz", "py")
 
 
 def merge_pair(mine, other):
@@ -106,9 +107,9 @@
     pair_count, shard_rows, model_width = anchor.shape
     score_scale = 4.0 / math.sqrt(model_width)
     dp_size = lax.axis_size("dp")
-    pair_size = lax.axis_size("pair")
+    pair_size = lax.axis_size(PAIR)
     dp_index = lax.axis_index("dp")
-    pair_place = lax.axis_index("pair")
+    pair_place = lax.axis_index(PAIR)
     own_first = (dp_index * pair_size + pair_place) * shard_rows
     offsets = jnp.arange(shard_rows, dtype=jnp.int32)
     own_valid = own_first + offsets[None, :] < counts[:, None]
@@ -117,7 +118,8 @@
     )
     own_positive = jnp.sum(jnp.where(own_valid, positive, 0.0), axis=1)
 
-    row_set = lax.all_gather(anchor, "pair", axis=1, tiled=True)
+    row_set = lax.all_gather(anchor, "py", axis=1, tiled=True)
+    row_set = lax.all_gather(row_set, "pz", axis=1, tiled=True)
     col_set = jnp.concatenate(ring_gather(partner, "dp", dp_size), axis=1)
     col_set = jnp.roll(col_set, (dp_index - dp_size // 2) * shard_rows, axis=1)
     row_count = row_set.shape[1]
@@ -147,7 +149,7 @@
     lanes = jnp.arange(row_count, dtype=jnp.int32)[None, :]
     carried = jnp.where(lanes == 0, own_positive[:, None], 0.0)
     row_stats = jnp.stack([row_high, row_sum, carried])
-    row_stats = group_merge(group_merge(row_stats, "pair", 1, 4), "pair", 4, pair_size // 4)
+    row_stats = group_merge(group_merge(row_stats, PAIR, 1, 4), PAIR, 4, pair_size // 4)
     row_high, row_sum, carried = row_stats[0], row_stats[1], row_stats[2]
     row_lse = jnp.where(row_valid, row_high + jnp.log(jnp.where(row_valid, row_sum, 1.0)), 0.0)
     row_part = jnp.sum(row_lse, axis=1) - 2.0 * carried[:, 0]
@@ -164,7 +166,8 @@
         jnp.einsum("prc,prd->pcd", weights, row_set, preferred_element_type=jnp.float32)
         * score_scale
     )
-    anchor_part = lax.psum_scatter(grad_rows, "pair", scatter_dimension=1, tiled=True)
+    anchor_part = lax.psum_scatter(grad_rows, "pz", scatter_dimension=1, tiled=True)
+    anchor_part = lax.psum_scatter(anchor_part, "py", scatter_dimension=1, tiled=True)
 
     width_lanes = jnp.arange(model_width, dtype=jnp.int32)[None, :]
     slots = (jnp.arange(pair_count, dtype=jnp.int32) * dp_size + dp_index)[:, None]
@@ -173,7 +176,7 @@
     partner_part, loss_row = two_stage_reduce_scatter(grad_cols, extra, "dp", dp_size, shard_rows)
     row_parts = loss_row[: pair_count * dp_size].reshape(pair_count, dp_size)
 
-    col_total = butterfly_sum(jnp.sum(col_lse, axis=1), "pair", pair_size)
+    col_total = butterfly_sum(jnp.sum(col_lse, axis=1), PAIR, pair_size)
     totals = col_total + jnp.sum(row_parts, axis=1)
     loss_value = jnp.sum(totals / (2.0 * counts.astype(jnp.float32))) / pair_count
 
@@ -185,8 +188,12 @@
 
 
 def solution(mesh):
-    in_specs = (P(None, ("dp", "pair"), None), P(None, ("dp", "pair"), None), P(), P())
-    out_specs = (P(), P(None, ("dp", "pair"), None), P(None, ("dp", "pair"), None))
+    dp_size, pair_size = mesh.devices.shape
+    side = math.isqrt(pair_size)
+    split = Mesh(mesh.devices.reshape(dp_size, pair_size // side, side), ("dp",) + PAIR)
+    rows = P(None, ("dp",) + PAIR, None)
+    in_specs = (rows, rows, P(), P())
+    out_specs = (P(), rows, rows)
     return jax.shard_map(
-        per_device, mesh=mesh, in_specs=in_specs, out_specs=out_specs, check_vma=False
+        per_device, mesh=split, in_specs=in_specs, out_specs=out_specs, check_vma=False
     )

time: 211 us -> 307 us (1.45)
  waiting for transfers between devices: 111 us -> 204 us
  starting transfers between devices: 27.1 us -> 30.3 us
    reduce_scatter x1 -> x2, waiting for transfers between devices: 13.7 us -> 86.5 us  [the longest x1 86.5 us: per_device(): lax.psum_scatter(grad_rows, 'pz', scatter_dimension=1, tiled=True)]
    all_gather x1 -> x2, waiting for transfers between devices: 16.9 us -> 45.4 us  [the longest x1 29.1 us: per_device(): row_set = lax.all_gather(anchor, 'py', axis=1, tiled=True)]
    ppermute x1, waiting for transfers between devices: 5.29 us -> 0.01 us  [two_stage_reduce_scatter(): got = lax.ppermute(send, axis, [(i, i ^ 1) for i in range(size)])]
  transfers between devices with their start and end apart: 27 -> 29, of which waited for: 20 -> 20; matrix products, arithmetic and copies ran while one was open for 15% -> 10% of each run, Pallas kernels for 0% -> 0%
where the time goes in v8:
time: 307 us
  waiting for transfers between devices  204 us (66%)
  starting transfers between devices  30.3 us (10%)
  local copies, waits for them, and re-layouts  21.2 us (7%)
  other arithmetic  18.5 us (6%)
  matrix products  16.5 us (5%)
  between operations  16 us (5%)
    reduce_scatter x1, waiting for transfers between devices, per_device(): lax.psum_scatter(grad_rows, 'pz', scatter_dimension=1, tiled=True)  86.5 us
    ppermute x3, waiting for transfers between devices, two_stage_reduce_scatter(): running = lax.ppermute(running, axis, ring) + addend(chip - 1 - step)  37.7 us
    all_gather x1, waiting for transfers between devices, per_device(): row_set = lax.all_gather(anchor, 'py', axis=1, tiled=True)  29.1 us
    ppermute x4, waiting for transfers between devices, ring_gather(): ahead = lax.ppermute(ahead, axis, forward)  16.5 us
    all_gather x1, waiting for transfers between devices, per_device(): row_set = lax.all_gather(row_set, 'pz', axis=1, tiled=True)  16.3 us
    unnamed x28, local copies, waits for them, and re-layouts  15.1 us
    ppermute x10, starting transfers between devices, group_merge(): received.append(lax.ppermute(stats, axis, perm))  12.8 us
    ppermute x3, starting transfers between devices, ring_gather(): behind = lax.ppermute(behind, axis, backward)  9.41 us
  transfers between devices with their start and end apart: 29, of which 20 were waited for; matrix products, arithmetic and copies ran while one was open for 10% of the time, Pallas kernels for 0%

profile of v8, /device:TPU:0, one launch (start us, length us, event | category | flops | bytes accessed | tf_op | source)
XLA Modules:
  0.0 306.7 jit_solution(6578884859840123474)
XLA Ops:
  8.0 29.1 %all-gather.3.cloned.1.call-done = bf16[5,128,1024]{2,1,0:T(8,128)(2,1)} async-done(((bf16[5,32,1024]{2,1,0:T(8,128)(2,1)}), bf16[5,128,1024]{2,1,0:T(8,128)(2,1)}) %all-gather.3.cloned.1.call-update) | async-done | bytes 1310736 | tf_op jit(solution)/shard_map/all_gather | solution.py:121
  37.2 2.9 collective-permute-start.4
  40.4 1.2 fusion.17
  41.6 0.8 select_reduce_fusion.1
  43.2 1.9 collective-permute-done
  45.8 7.0 %collective-permute-done.1 = bf16[5,32,1024]{2,1,0:T(8,128)(2,1)S(1)} collective-permute-done((bf16[5,32,1024]{2,1,0:T(8,128)(2,1)S(1)}, bf16[5,32,1024]{2,1,0:T(8,128)(2,1)S(1)}, u32[]{:S(2)}, u32[]{:S(2)}) %collective-permute-start.1) | collective-permute-done | bytes 327712 | tf_op jit(solution)/shard_map/ppermute | solution.py:71
  53.5 3.0 collective-permute-start.5
  56.5 4.0 %collective-permute-done.2 = bf16[5,32,1024]{2,1,0:T(8,128)(2,1)S(1)} collective-permute-done((bf16[5,32,1024]{2,1,0:T(8,128)(2,1)S(1)}, bf16[5,32,1024]{2,1,0:T(8,128)(2,1)S(1)}, u32[]{:S(2)}, u32[]{:S(2)}) %collective-permute-start.2) | collective-permute-done | bytes 327712 | tf_op jit(solution)/shard_map/ppermute | solution.py:71
  61.1 3.5 %collective-permute-start.6 = (bf16[5,32,1024]{2,1,0:T(8,128)(2,1)S(1)}, bf16[5,32,1024]{2,1,0:T(8,128)(2,1)S(1)}, u32[]{:S(2)}, u32[]{:S(2)}) collective-permute-start(bf16[5,32,1024]{2,1,0:T(8,128)(2,1)S(1)} %collective-permute-done.5), channel_id=1, source_target_pairs={{0,112},{16,0},{32,16},{48,32},{64,48},{80,64},{96,80},{112,96},{1... | collective-permute-start | bytes 983048 | tf_op jit(solution)/shard_map/ppermute | solution.py:74
  64.6 3.6 %collective-permute-done.3 = bf16[5,32,1024]{2,1,0:T(8,128)(2,1)S(1)} collective-permute-done((bf16[5,32,1024]{2,1,0:T(8,128)(2,1)S(1)}, bf16[5,32,1024]{2,1,0:T(8,128)(2,1)S(1)}, u32[]{:S(2)}, u32[]{:S(2)}) %collective-permute-start.3) | collective-permute-done | bytes 327712 | tf_op jit(solution)/shard_map/ppermute | solution.py:71
  68.2 0.8 constant_dynamic-update-slice_fusion.15
  80.2 16.3 %all-gather.5.cloned.1.call-done = bf16[5,512,1024]{2,1,0:T(8,128)(2,1)} async-done(((bf16[5,128,1024]{2,1,0:T(8,128)(2,1)}), bf16[5,512,1024]{2,1,0:T(8,128)(2,1)}) %all-gather.5.cloned.1.call-update) | async-done | bytes 5242896 | tf_op jit(solution)/shard_map/all_gather | solution.py:122
  96.5 5.2 %fusion.11 = (f32[5,256]{1,0:T(8,128)S(1)}, f32[5,512]{1,0:T(8,128)S(1)}, f32[5,256,512]{2,1,0:T(8,128)S(1)}) fusion(pred[5,256]{1,0:T(8,128)(4,1)S(1)} %broadcast_compare_fusion.1, pred[5,512]{1,0:T(8,128)(4,1)S(1)} %broadcast_compare_fusion, bf16[5,512,1024]{2,1,0:T(8,128)(2,1)} %all-gather.5.cloned.1.call-done, ...), kind=kOutput, calls=%fused_computation.30 | convolution fusion | flops 1345450240 | bytes 10504964 | tf_op jit(solution)/shard_map/prd,pcd->prc/dot_general | solution.py:135
  101.7 1.5 copy-done.2
  103.2 1.9 fusion
  105.3 1.1 collective-permute-done.7
  107.1 2.8 collective-permute-start.10
  109.9 0.8 collective-permute-start.9
  110.7 0.9 collective-permute-start.8
  111.6 2.8 collective-permute-start.17
  114.4 0.8 collective-permute-start.16
  115.2 0.9 collective-permute-start.15
  116.8 3.2 %collective-permute-done.16 = f32[3,5,512]{2,0,1:T(4,128)S(1)} collective-permute-done((f32[3,5,512]{2,0,1:T(4,128)S(1)}, f32[3,5,512]{2,0,1:T(4,128)S(1)}, u32[]{:S(2)}, u32[]{:S(2)}) %collective-permute-start.16) | collective-permute-done | bytes 30752 | tf_op jit(solution)/shard_map/ppermute | solution.py:37
  121.4 1.2 collective-permute-start.20
  122.6 1.9 collective-permute-start.19
  125.5 2.6 collective-permute-done.19
  128.1 1.6 collective-permute-done.18
  130.8 2.7 fusion.4
  133.6 7.3 %broadcast_multiply_fusion = f32[5,512,1024]{2,1,0:T(8,128)} fusion(bf16[5,512,256]{1,2,0:T(8,128)(2,1)S(1)} %fusion.4, bf16[5,512,1024]{2,1,0:T(8,128)(2,1)} %constant_dynamic-update-slice_fusion, s32[]{:T(128)S(6)} %select_n.293), kind=kOutput, calls=%fused_computation.9 | convolution fusion | flops 1344798720 | bytes 14417924 | tf_op jit(solution)/shard_map/prc,pcd->prd/dot_general | solution.py:162
  141.5 4.0 %broadcast_multiply_fusion.1 = f32[5,256,1024]{2,1,0:T(8,128)S(1)} fusion(bf16[5,512,256]{1,2,0:T(8,128)(2,1)S(1)} %fusion.4, bf16[5,512,1024]{2,1,0:T(8,128)(2,1)} %all-gather.5.cloned.1.call-done), kind=kOutput, calls=%fused_computation.21 | convolution fusion | flops 1343488000 | bytes 11796480 | tf_op jit(solution)/shard_map/prc,prd->pcd/dot_general | solution.py:166
  145.7 2.1 maximum_maximum_fusion
  147.8 1.2 copy-done
  149.0 86.5 %reduce-scatter.3.cloned.1.call-done = f32[5,128,1024]{2,1,0:T(8,128)} async-done(((f32[5,512,1024]{2,1,0:T(8,128)}), f32[5,128,1024]{2,1,0:T(8,128)}) %reduce-scatter.3.cloned.1.call-update) | async-done | bytes 2621456 | tf_op jit(solution)/shard_map/reduce_scatter | solution.py:169
  235.6 2.2 slice.312
  237.8 1.0 copy-done.1
  239.9 0.8 slice_add_fusion
  240.7 1.5 collective-permute-start.22
  242.3 17.0 %collective-permute-done.22 = f32[168,1024]{1,0:T(8,128)S(1)} collective-permute-done((f32[168,1024]{1,0:T(8,128)S(1)}, f32[168,1024]{1,0:T(8,128)S(1)}, u32[]{:S(2)}, u32[]{:S(2)}) %collective-permute-start.22) | collective-permute-done | bytes 688160 | tf_op jit(solution)/shard_map/ppermute | solution.py:102
  259.7 17.4 %collective-permute-done.23 = f32[168,1024]{1,0:T(8,128)S(1)} collective-permute-done((f32[168,1024]{1,0:T(8,128)S(1)}, f32[168,1024]{1,0:T(8,128)S(1)}, u32[]{:S(2)}, u32[]{:S(2)}) %collective-permute-start.23) | collective-permute-done | bytes 688160 | tf_op jit(solution)/shard_map/ppermute | solution.py:102
  277.1 0.9 fusion.13
  278.1 1.4 collective-permute-start.11
  279.5 2.2 collective-permute-done.11
  281.7 2.9 collective-permute-start.12
  284.6 2.1 collective-permute-done.12
  286.8 3.4 %collective-permute-done.13 = f32[5]{0:T(128)S(1)} collective-permute-done((f32[5]{0:T(128)S(1)}, f32[5]{0:T(128)S(1)}, u32[]{:S(2)}, u32[]{:S(2)}) %collective-permute-start.13) | collective-permute-done | bytes 52 | tf_op jit(solution)/shard_map/ppermute | solution.py:50
  290.3 1.5 collective-permute-start.14
  291.7 3.3 %collective-permute-done.24 = f32[168,1024]{1,0:T(8,128)S(1)} collective-permute-done((f32[168,1024]{1,0:T(8,128)}, f32[168,1024]{1,0:T(8,128)S(1)}, u32[]{:S(2)}, u32[]{:S(2)}) %collective-permute-start.24) | collective-permute-done | bytes 688160 | tf_op jit(solution)/shard_map/ppermute | solution.py:102
  296.7 2.4 fusion.16
  (121 shorter events, 23.5 us)
Async XLA Ops:
  7.2 64.1 %copy-start.3 = (bf16[5,32,1024]{2,1,0:T(8,128)(2,1)S(1)}, bf16[5,32,1024]{2,1,0:T(8,128)(2,1)}, u32[]{:S(2)}) copy-start(bf16[5,32,1024]{2,1,0:T(8,128)(2,1)} %param.7) | copy-start | bytes 983044
  7.2 29.9 %all-gather.3.cloned.1.call-start = ((), (), s32[]{:S(2)}) async-start(), calls=%async_computation.2 | async-start | bytes 1638400 | tf_op jit(solution)/shard_map/all_gather | solution.py:121
  7.9 88.6 %all-gather.5.cloned.1.call-start = ((), (), s32[]{:S(2)}) async-start(), calls=%async_computation.3 | async-start | bytes 6553600 | tf_op jit(solution)/shard_map/all_gather | solution.py:122
  37.1 198.4 %reduce-scatter.3.cloned.1.call-start = ((), (), s32[]{:S(2)}) async-start(), calls=%async_computation.4 | async-start | bytes 13107200 | tf_op jit(solution)/shard_map/reduce_scatter | solution.py:169
  37.2 7.9 %collective-permute-start = (bf16[5,32,1024]{2,1,0:T(8,128)(2,1)}, bf16[5,32,1024]{2,1,0:T(8,128)(2,1)S(1)}, u32[]{:S(2)}, u32[]{:S(2)}) collective-permute-start(bf16[5,32,1024]{2,1,0:T(8,128)(2,1)} %param.7), channel_id=1, source_target_pairs={{0,16},{16,32},{32,48},{48,64},{64,80},{80,96},{96,112},{112,0},{1... | collective-permute-start | bytes 983048 | tf_op jit(solution)/shard_map/ppermute | solution.py:71
  37.2 16.4 %collective-permute-start.4 = (bf16[5,32,1024]{2,1,0:T(8,128)(2,1)}, bf16[5,32,1024]{2,1,0:T(8,128)(2,1)S(1)}, u32[]{:S(2)}, u32[]{:S(2)}) collective-permute-start(bf16[5,32,1024]{2,1,0:T(8,128)(2,1)} %param.7), channel_id=1, source_target_pairs={{0,112},{16,0},{32,16},{48,32},{64,48},{80,64},{96,80},{112,96},{1... | collective-permute-start | bytes 983048 | tf_op jit(solution)/shard_map/ppermute | solution.py:74
  45.1 7.7 %collective-permute-start.1 = (bf16[5,32,1024]{2,1,0:T(8,128)(2,1)S(1)}, bf16[5,32,1024]{2,1,0:T(8,128)(2,1)S(1)}, u32[]{:S(2)}, u32[]{:S(2)}) collective-permute-start(bf16[5,32,1024]{2,1,0:T(8,128)(2,1)S(1)} %collective-permute-done), channel_id=1, source_target_pairs={{0,16},{16,32},{32,48},{48,64},{64,80},{80,96},{96,112},{112,0},{1... | collective-permute-start | bytes 983048 | tf_op jit(solution)/shard_map/ppermute | solution.py:71
  52.8 7.7 %collective-permute-start.2 = (bf16[5,32,1024]{2,1,0:T(8,128)(2,1)S(1)}, bf16[5,32,1024]{2,1,0:T(8,128)(2,1)S(1)}, u32[]{:S(2)}, u32[]{:S(2)}) collective-permute-start(bf16[5,32,1024]{2,1,0:T(8,128)(2,1)S(1)} %collective-permute-done.1), channel_id=1, source_target_pairs={{0,16},{16,32},{32,48},{48,64},{64,80},{80,96},{96,112},{112,0},{1... | collective-permute-start | bytes 983048 | tf_op jit(solution)/shard_map/ppermute | solution.py:71
  53.5 7.5 %collective-permute-start.5 = (bf16[5,32,1024]{2,1,0:T(8,128)(2,1)S(1)}, bf16[5,32,1024]{2,1,0:T(8,128)(2,1)S(1)}, u32[]{:S(2)}, u32[]{:S(2)}) collective-permute-start(bf16[5,32,1024]{2,1,0:T(8,128)(2,1)S(1)} %collective-permute-done.4), channel_id=1, source_target_pairs={{0,112},{16,0},{32,16},{48,32},{64,48},{80,64},{96,80},{112,96},{1... | collective-permute-start | bytes 983048 | tf_op jit(solution)/shard_map/ppermute | solution.py:74
  60.5 7.7 %collective-permute-start.3 = (bf16[5,32,1024]{2,1,0:T(8,128)(2,1)S(1)}, bf16[5,32,1024]{2,1,0:T(8,128)(2,1)S(1)}, u32[]{:S(2)}, u32[]{:S(2)}) collective-permute-start(bf16[5,32,1024]{2,1,0:T(8,128)(2,1)S(1)} %collective-permute-done.2), channel_id=1, source_target_pairs={{0,16},{16,32},{32,48},{48,64},{64,80},{80,96},{96,112},{112,0},{1... | collective-permute-start | bytes 983048 | tf_op jit(solution)/shard_map/ppermute | solution.py:71
  61.1 12.4 %collective-permute-start.6 = (bf16[5,32,1024]{2,1,0:T(8,128)(2,1)S(1)}, bf16[5,32,1024]{2,1,0:T(8,128)(2,1)S(1)}, u32[]{:S(2)}, u32[]{:S(2)}) collective-permute-start(bf16[5,32,1024]{2,1,0:T(8,128)(2,1)S(1)} %collective-permute-done.5), channel_id=1, source_target_pairs={{0,112},{16,0},{32,16},{48,32},{64,48},{80,64},{96,80},{112,96},{1... | collective-permute-start | bytes 983048 | tf_op jit(solution)/shard_map/ppermute | solution.py:74
  80.2 45.0 %copy-start.5 = (s32[5]{0:T(128)S(1)}, s32[5]{0:T(128)}, u32[]{:S(2)}) copy-start(s32[5]{0:T(128)} %param.8) | copy-start | bytes 64
  101.7 1.5 copy-start.2
  105.2 1.3 collective-permute-start.7
  107.1 8.1 %collective-permute-start.10 = (f32[2,5,256]{2,1,0:T(8,128)S(1)}, f32[2,5,256]{2,1,0:T(8,128)S(1)}, u32[]{:S(2)}, u32[]{:S(2)}) collective-permute-start(f32[2,5,256]{2,1,0:T(8,128)S(1)} %get-tuple-element.34), channel_id=1, source_target_pairs={{0,96},{16,112},{32,0},{48,16},{64,32},{80,48},{96,64},{112,80},{1... | collective-permute-start | bytes 30728 | tf_op jit(solution)/shard_map/ppermute | solution.py:37
  109.9 6.3 %collective-permute-start.9 = (f32[2,5,256]{2,1,0:T(8,128)S(1)}, f32[2,5,256]{2,1,0:T(8,128)S(1)}, u32[]{:S(2)}, u32[]{:S(2)}) collective-permute-start(f32[2,5,256]{2,1,0:T(8,128)S(1)} %get-tuple-element.34), channel_id=1, source_target_pairs={{0,64},{16,80},{32,96},{48,112},{64,0},{80,16},{96,32},{112,48},{1... | collective-permute-start | bytes 30728 | tf_op jit(solution)/shard_map/ppermute | solution.py:37
  110.7 5.4 %collective-permute-start.8 = (f32[2,5,256]{2,1,0:T(8,128)S(1)}, f32[2,5,256]{2,1,0:T(8,128)S(1)}, u32[]{:S(2)}, u32[]{:S(2)}) collective-permute-start(f32[2,5,256]{2,1,0:T(8,128)S(1)} %get-tuple-element.34), channel_id=1, source_target_pairs={{0,32},{16,48},{32,64},{48,80},{64,96},{80,112},{96,0},{112,16},{1... | collective-permute-start | bytes 30728 | tf_op jit(solution)/shard_map/ppermute | solution.py:37
  111.6 5.2 %collective-permute-start.17 = (f32[3,5,512]{2,0,1:T(4,128)S(1)}, f32[3,5,512]{2,0,1:T(4,128)S(1)}, u32[]{:S(2)}, u32[]{:S(2)}) collective-permute-start(f32[3,5,512]{2,0,1:T(4,128)S(1)} %get-tuple-element.32), channel_id=1, source_target_pairs={{0,3},{1,0},{2,1},{3,2},{4,7},{5,4},{6,5},{7,6},{8,11},{9,8},{10,9... | collective-permute-start | bytes 92168 | tf_op jit(solution)/shard_map/ppermute | solution.py:37
  114.4 5.5 %collective-permute-start.16 = (f32[3,5,512]{2,0,1:T(4,128)S(1)}, f32[3,5,512]{2,0,1:T(4,128)S(1)}, u32[]{:S(2)}, u32[]{:S(2)}) collective-permute-start(f32[3,5,512]{2,0,1:T(4,128)S(1)} %get-tuple-element.32), channel_id=1, source_target_pairs={{0,2},{1,3},{2,0},{3,1},{4,6},{5,7},{6,4},{7,5},{8,10},{9,11},{10,... | collective-permute-start | bytes 92168 | tf_op jit(solution)/shard_map/ppermute | solution.py:37
  115.2 5.2 %collective-permute-start.15 = (f32[3,5,512]{2,0,1:T(4,128)S(1)}, f32[3,5,512]{2,0,1:T(4,128)S(1)}, u32[]{:S(2)}, u32[]{:S(2)}) collective-permute-start(f32[3,5,512]{2,0,1:T(4,128)S(1)} %get-tuple-element.32), channel_id=1, source_target_pairs={{0,1},{1,2},{2,3},{3,0},{4,5},{5,6},{6,7},{7,4},{8,9},{9,10},{10,1... | collective-permute-start | bytes 92168 | tf_op jit(solution)/shard_map/ppermute | solution.py:37
  121.4 4.1 %collective-permute-start.20 = (f32[3,5,512]{2,0,1:T(4,128)S(1)}, f32[3,5,512]{2,0,1:T(4,128)S(1)}, u32[]{:S(2)}, u32[]{:S(2)}) collective-permute-start(f32[3,5,512]{2,0,1:T(4,128)S(1)} %get-tuple-element.30), channel_id=1, source_target_pairs={{0,12},{1,13},{2,14},{3,15},{4,0},{5,1},{6,2},{7,3},{8,4},{9,5},{1... | collective-permute-start | bytes 92168 | tf_op jit(solution)/shard_map/ppermute | solution.py:37
  122.6 5.5 %collective-permute-start.19 = (f32[3,5,512]{2,0,1:T(4,128)S(1)}, f32[3,5,512]{2,0,1:T(4,128)S(1)}, u32[]{:S(2)}, u32[]{:S(2)}) collective-permute-start(f32[3,5,512]{2,0,1:T(4,128)S(1)} %get-tuple-element.30), channel_id=1, source_target_pairs={{0,8},{1,9},{2,10},{3,11},{4,12},{5,13},{6,14},{7,15},{8,0},{9,1},... | collective-permute-start | bytes 92168 | tf_op jit(solution)/shard_map/ppermute | solution.py:37
  124.5 5.2 %collective-permute-start.18 = (f32[3,5,512]{2,0,1:T(4,128)S(1)}, f32[3,5,512]{2,0,1:T(4,128)S(1)}, u32[]{:S(2)}, u32[]{:S(2)}) collective-permute-start(f32[3,5,512]{2,0,1:T(4,128)S(1)} %get-tuple-element.30), channel_id=1, source_target_pairs={{0,4},{1,5},{2,6},{3,7},{4,8},{5,9},{6,10},{7,11},{8,12},{9,13},{1... | collective-permute-start | bytes 92168 | tf_op jit(solution)/shard_map/ppermute | solution.py:37
  140.9 155.8 %reduce-scatter.5.cloned.1.call-start = ((), (), s32[]{:S(2)}) async-start(), calls=%async_computation.5 | async-start | bytes 3276800 | tf_op jit(solution)/shard_map/reduce_scatter | solution.py:170
  145.5 3.5 %copy-start = (f32[5,256,1024]{2,1,0:T(8,128)}, f32[5,256,1024]{2,1,0:T(8,128)S(1)}, u32[]{:S(2)}) copy-start(f32[5,256,1024]{2,1,0:T(8,128)S(1)} %broadcast_multiply_fusion.1) | copy-start | bytes 15728644
  149.0 86.6 %collective-permute-start.21 = (f32[648,1024]{1,0:T(8,128)}, f32[648,1024]{1,0:T(8,128)}, u32[]{:S(2)}, u32[]{:S(2)}) collective-permute-start(f32[648,1024]{1,0:T(8,128)} %maximum_maximum_fusion), channel_id=1, source_target_pairs={{0,16},{16,0},{32,48},{48,32},{64,80},{80,64},{96,112},{112,96},{1... | collective-permute-start | bytes 7962632 | tf_op jit(solution)/shard_map/ppermute | solution.py:89
  235.6 3.3 %copy-start.1 = (f32[5,256,1024]{2,1,0:T(8,128)S(1)}, f32[5,256,1024]{2,1,0:T(8,128)}, u32[]{:S(2)}) copy-start(f32[5,256,1024]{2,1,0:T(8,128)} %copy-done) | copy-start | bytes 15728644
  239.8 56.8 %copy-start.4 = (bf16[5,32,1024]{2,1,0:T(8,128)(2,1)S(1)}, bf16[5,32,1024]{2,1,0:T(8,128)(2,1)}, u32[]{:S(2)}) copy-start(bf16[5,32,1024]{2,1,0:T(8,128)(2,1)} %param.6) | copy-start | bytes 983044
  240.7 18.5 %collective-permute-start.22 = (f32[168,1024]{1,0:T(8,128)S(1)}, f32[168,1024]{1,0:T(8,128)S(1)}, u32[]{:S(2)}, u32[]{:S(2)}) collective-permute-start(f32[168,1024]{1,0:T(8,128)S(1)} %pad_maximum_fusion.3), channel_id=1, source_target_pairs={{0,32},{16,48},{32,64},{48,80},{64,96},{80,112},{96,0},{112,16},{1... | collective-permute-start | bytes 2064392 | tf_op jit(solution)/shard_map/ppermute | solution.py:102
  259.3 17.7 %collective-permute-start.23 = (f32[168,1024]{1,0:T(8,128)S(1)}, f32[168,1024]{1,0:T(8,128)S(1)}, u32[]{:S(2)}, u32[]{:S(2)}) collective-permute-start(f32[168,1024]{1,0:T(8,128)S(1)} %fusion.12), channel_id=1, source_target_pairs={{0,32},{16,48},{32,64},{48,80},{64,96},{80,112},{96,0},{112,16},{1... | collective-permute-start | bytes 2064392 | tf_op jit(solution)/shard_map/ppermute | solution.py:102
  278.0 17.0 %collective-permute-start.24 = (f32[168,1024]{1,0:T(8,128)}, f32[168,1024]{1,0:T(8,128)S(1)}, u32[]{:S(2)}, u32[]{:S(2)}) collective-permute-start(f32[168,1024]{1,0:T(8,128)} %fusion.13), channel_id=1, source_target_pairs={{0,32},{16,48},{32,64},{48,80},{64,96},{80,112},{96,0},{112,16},{1... | collective-permute-start | bytes 2064392 | tf_op jit(solution)/shard_map/ppermute | solution.py:102
  278.1 3.6 %collective-permute-start.11 = (f32[5]{0:T(128)S(1)}, f32[5]{0:T(128)S(1)}, u32[]{:S(2)}, u32[]{:S(2)}) collective-permute-start(f32[5]{0:T(128)S(1)} %get-tuple-element.8), channel_id=1, source_target_pairs={{0,1},{1,0},{2,3},{3,2},{4,5},{5,4},{6,7},{7,6},{8,9},{9,8},{10,11... | collective-permute-start | bytes 68 | tf_op jit(solution)/shard_map/ppermute | solution.py:50
  281.7 5.0 %collective-permute-start.12 = (f32[5]{0:T(128)S(1)}, f32[5]{0:T(128)S(1)}, u32[]{:S(2)}, u32[]{:S(2)}) collective-permute-start(f32[5]{0:T(128)S(1)} %fusion.90), channel_id=1, source_target_pairs={{0,2},{1,3},{2,0},{3,1},{4,6},{5,7},{6,4},{7,5},{8,10},{9,11},{10,... | collective-permute-start | bytes 68 | tf_op jit(solution)/shard_map/ppermute | solution.py:50
  286.7 3.5 %collective-permute-start.13 = (f32[5]{0:T(128)S(1)}, f32[5]{0:T(128)S(1)}, u32[]{:S(2)}, u32[]{:S(2)}) collective-permute-start(f32[5]{0:T(128)S(1)} %fusion.89), channel_id=1, source_target_pairs={{0,4},{1,5},{2,6},{3,7},{4,0},{5,1},{6,2},{7,3},{8,12},{9,13},{10,... | collective-permute-start | bytes 68 | tf_op jit(solution)/shard_map/ppermute | solution.py:50
  290.3 5.1 %collective-permute-start.14 = (f32[5]{0:T(128)S(1)}, f32[5]{0:T(128)S(1)}, u32[]{:S(2)}, u32[]{:S(2)}) collective-permute-start(f32[5]{0:T(128)S(1)} %fusion.88), channel_id=1, source_target_pairs={{0,8},{1,9},{2,10},{3,11},{4,12},{5,13},{6,14},{7,15},{8,0},{9,1},... | collective-permute-start | bytes 68 | tf_op jit(solution)/shard_map/ppermute | solution.py:50
Sparse Core Ops, SparseCore 0:
  9.7 27.3 all-gather.2
  38.8 57.7 all-gather.4
  141.0 94.4 reduce-scatter.2
  237.8 33.5 reduce-scatter.4

commit v9 on v6

--- a/solution.py
+++ b/solution.py
@@ -145,7 +145,13 @@
         jnp.einsum("prc,prd->pcd", weights, row_set, preferred_element_type=jnp.float32)
         * score_scale
     )
-    anchor_part = lax.psum_scatter(grad_rows, "pair", scatter_dimension=1, tiled=True)
+    own_term = (pair_scale * score_scale)[:, None, None]
+    own_start = pair_place * shard_rows
+    own_chunk = lax.dynamic_slice_in_dim(grad_rows, own_start, shard_rows, 1)
+    own_chunk = own_chunk - own_term * partner.astype(jnp.float32)
+    grad_rows = lax.dynamic_update_slice_in_dim(grad_rows, own_chunk, own_start, 1)
+    grad_rows = jnp.where(row_valid[:, :, None], grad_rows, 0.0)
+    anchor_out = lax.psum_scatter(grad_rows, "pair", scatter_dimension=1, tiled=True)
 
     width_lanes = jnp.arange(model_width, dtype=jnp.int32)[None, :]
     slots = (jnp.arange(pair_count, dtype=jnp.int32) * dp_size + dp_index)[:, None]
@@ -158,9 +164,7 @@
     totals = col_total + jnp.sum(row_parts, axis=1)
     loss_value = jnp.sum(totals / (2.0 * counts.astype(jnp.float32))) / pair_count
 
-    own_term = (pair_scale * score_scale)[:, None, None]
     keep_rows = own_valid[:, :, None]
-    anchor_out = jnp.where(keep_rows, anchor_part - own_term * partner.astype(jnp.float32), 0.0)
     partner_out = jnp.where(keep_rows, partner_part - own_term * anchor.astype(jnp.float32), 0.0)
     return (loss_value, anchor_out, partner_out)
 

time: 211 us -> 280 us (1.33)
  waiting for transfers between devices: 111 us -> 176 us
  other arithmetic: 14.8 us -> 23.9 us
    reduce_scatter x1, waiting for transfers between devices: 17.6 us -> 68.8 us  [per_device(): lax.psum_scatter(grad_rows, 'pair', scatter_dimension=1, tiled=True)]
    ppermute x3, waiting for transfers between devices: 38.4 us -> 50 us  [two_stage_reduce_scatter(): running = lax.ppermute(running, axis, ring) + addend(chip - 1 - step)]
    select_n x0 -> x1, other arithmetic: none -> 4.78 us  [per_device(): grad_rows = jnp.where(row_valid[:, :, None], grad_rows, 0.0)]
    dot_general x1, matrix products: 7.3 us -> 3.36 us  [per_device(): jnp.einsum('prc,pcd->prd', weights, col_set, preferred_element_type=jnp.f...]
    unnamed x29 -> x25, local copies, waits for them, and re-layouts: 15.7 us -> 13.2 us
  transfers between devices with their start and end apart: 24 -> 24, of which waited for: 20 -> 21; matrix products, arithmetic and copies ran while one was open for 13% -> 8% of each run, Pallas kernels for 0% -> 0%
where the time goes in v9:
time: 280 us; the launch traced here: 279 us
  waiting for transfers between devices  176 us (63%)
  starting transfers between devices  31 us (11%)
  other arithmetic  23.9 us (9%)
  local copies, waits for them, and re-layouts  17.6 us (6%)
  between operations  16.2 us (6%)
  matrix products  14 us (5%)
    reduce_scatter x1, waiting for transfers between devices, per_device(): lax.psum_scatter(grad_rows, 'pair', scatter_dimension=1, tiled=True)  68.8 us
    ppermute x3, waiting for transfers between devices, two_stage_reduce_scatter(): running = lax.ppermute(running, axis, ring) + addend(chip - 1 - step)  50 us
    ppermute x4, waiting for transfers between devices, ring_gather(): ahead = lax.ppermute(ahead, axis, forward)  18.6 us
    all_gather x1, waiting for transfers between devices, per_device(): row_set = lax.all_gather(anchor, 'pair', axis=1, tiled=True)  14.7 us
    unnamed x25, local copies, waits for them, and re-layouts  13.2 us
    ppermute x7, starting transfers between devices, butterfly_merge(): other = lax.ppermute(stats, axis, [(i, i ^ bit) for i in range(size)])  13 us
    ppermute x3, starting transfers between devices, ring_gather(): behind = lax.ppermute(behind, axis, backward)  8.76 us
    ppermute x4, starting transfers between devices, butterfly_sum(): other = lax.ppermute(values, axis, [(i, i ^ bit) for i in range(size)])  8.65 us
  transfers between devices with their start and end apart: 24, of which 21 were waited for; matrix products, arithmetic and copies ran while one was open for 8% of the time, Pallas kernels for 0%

profile of v9, /device:TPU:0, one launch (start us, length us, event | category | flops | bytes accessed | tf_op | source)
XLA Modules:
  0.0 279.2 jit_solution(4347163574807097712)
XLA Ops:
  8.0 2.3 collective-permute-start.4
  11.3 1.2 fusion.17
  12.6 5.6 %collective-permute-done = bf16[5,32,1024]{2,1,0:T(8,128)(2,1)S(1)} collective-permute-done((bf16[5,32,1024]{2,1,0:T(8,128)(2,1)}, bf16[5,32,1024]{2,1,0:T(8,128)(2,1)S(1)}, u32[]{:S(2)}, u32[]{:S(2)}) %collective-permute-start) | collective-permute-done | bytes 327712 | tf_op jit(solution)/shard_map/ppermute | solution.py:53
  18.8 7.0 %collective-permute-done.1 = bf16[5,32,1024]{2,1,0:T(8,128)(2,1)S(1)} collective-permute-done((bf16[5,32,1024]{2,1,0:T(8,128)(2,1)S(1)}, bf16[5,32,1024]{2,1,0:T(8,128)(2,1)S(1)}, u32[]{:S(2)}, u32[]{:S(2)}) %collective-permute-start.1) | collective-permute-done | bytes 327712 | tf_op jit(solution)/shard_map/ppermute | solution.py:53
  25.9 0.8 select_reduce_fusion.1
  27.5 3.0 %collective-permute-start.5 = (bf16[5,32,1024]{2,1,0:T(8,128)(2,1)S(1)}, bf16[5,32,1024]{2,1,0:T(8,128)(2,1)S(1)}, u32[]{:S(2)}, u32[]{:S(2)}) collective-permute-start(bf16[5,32,1024]{2,1,0:T(8,128)(2,1)S(1)} %collective-permute-done.4), channel_id=1, source_target_pairs={{0,112},{16,0},{32,16},{48,32},{64,48},{80,64},{96,80},{112,96},{1... | collective-permute-start | bytes 983048 | tf_op jit(solution)/shard_map/ppermute | solution.py:56
  30.4 3.2 %collective-permute-done.2 = bf16[5,32,1024]{2,1,0:T(8,128)(2,1)S(1)} collective-permute-done((bf16[5,32,1024]{2,1,0:T(8,128)(2,1)S(1)}, bf16[5,32,1024]{2,1,0:T(8,128)(2,1)S(1)}, u32[]{:S(2)}, u32[]{:S(2)}) %collective-permute-start.2) | collective-permute-done | bytes 327712 | tf_op jit(solution)/shard_map/ppermute | solution.py:53
  33.7 1.3 collective-permute-done.5
  35.0 3.5 %collective-permute-start.6 = (bf16[5,32,1024]{2,1,0:T(8,128)(2,1)S(1)}, bf16[5,32,1024]{2,1,0:T(8,128)(2,1)S(1)}, u32[]{:S(2)}, u32[]{:S(2)}) collective-permute-start(bf16[5,32,1024]{2,1,0:T(8,128)(2,1)S(1)} %collective-permute-done.5), channel_id=1, source_target_pairs={{0,112},{16,0},{32,16},{48,32},{64,48},{80,64},{96,80},{112,96},{1... | collective-permute-start | bytes 983048 | tf_op jit(solution)/shard_map/ppermute | solution.py:56
  38.5 2.8 collective-permute-done.3
  44.3 1.8 constant_dynamic-update-slice_fusion.11
  54.4 14.7 %all-gather.2.cloned.1.call-done = bf16[5,512,1024]{2,1,0:T(8,128)(2,1)} async-done(((bf16[5,32,1024]{2,1,0:T(8,128)(2,1)}), bf16[5,512,1024]{2,1,0:T(8,128)(2,1)}) %all-gather.2.cloned.1.call-update) | async-done | bytes 5242896 | tf_op jit(solution)/shard_map/all_gather | solution.py:103
  69.2 6.7 %fusion.11 = (f32[5,256]{1,0:T(8,128)S(1)}, f32[5,512]{1,0:T(8,128)S(1)}, f32[5,256,512]{2,1,0:T(8,128)}) fusion(pred[5,256]{1,0:T(8,128)(4,1)S(1)} %broadcast_compare_fusion.1, pred[5,512]{1,0:T(8,128)(4,1)S(1)} %copy.22, bf16[5,512,1024]{2,1,0:T(8,128)(2,1)} %all-gather.2.cloned.1.call-done, bf16[5,512,1024]{2,1,0:T(8,128)(2,1)} %constant_dynamic-update-slice_fusion, ...), kind=kOutput, calls=%fused_computation.27 | convolution fusion | flops 1345450240 | bytes 10504964 | tf_op jit(solution)/shard_map/prd,pcd->prc/dot_general | solution.py:116
  75.9 3.2 %fusion = (f32[5,256]{1,0:T(8,128)S(1)}, f32[5,512]{1,0:T(8,128)S(1)}) fusion(f32[5,256]{1,0:T(8,128)S(1)} %get-tuple-element.5, pred[5,256]{1,0:T(8,128)(4,1)S(1)} %broadcast_compare_fusion.1, pred[5,512]{1,0:T(8,128)(4,1)S(1)} %copy.22, f32[5,256,512]{2,1,0:T(8,128)} %get-tuple-element.46, f32[5,512]{1,0:T(8,128)S(1)} %get-tuple-element.6), kind=kLoop, calls=%fused_computation.8 | loop fusion | flops 5894400 | bytes 2656000 | tf_op jit(solution)/shard_map/reduce_sum | solution.py:123
  79.3 1.0 collective-permute-done.7
  80.4 1.6 collective-permute-start.8
  82.0 1.6 collective-permute-start.14
  84.2 1.8 collective-permute-done.14
  86.2 3.1 %collective-permute-start.15 = (f32[3,5,512]{2,0,1:T(4,128)S(1)}, f32[3,5,512]{2,0,1:T(4,128)S(1)}, u32[]{:S(2)}, u32[]{:S(2)}) collective-permute-start(f32[3,5,512]{2,0,1:T(4,128)S(1)} %pad_maximum_fusion.5), channel_id=1, source_target_pairs={{0,2},{1,3},{2,0},{3,1},{4,6},{5,7},{6,4},{7,5},{8,10},{9,11},{10,... | collective-permute-start | bytes 92168 | tf_op jit(solution)/shard_map/ppermute | solution.py:21
  89.3 2.7 collective-permute-start.9
  92.1 1.2 collective-permute-start.16
  93.4 1.2 collective-permute-done.9
  94.6 1.7 collective-permute-done.16
  96.4 2.8 %collective-permute-start.17 = (f32[3,5,512]{2,0,1:T(4,128)S(1)}, f32[3,5,512]{2,0,1:T(4,128)S(1)}, u32[]{:S(2)}, u32[]{:S(2)}) collective-permute-start(f32[3,5,512]{2,0,1:T(4,128)S(1)} %pad_maximum_fusion.7), channel_id=1, source_target_pairs={{0,8},{1,9},{2,10},{3,11},{4,12},{5,13},{6,14},{7,15},{8,0},{9,1},... | collective-permute-start | bytes 92168 | tf_op jit(solution)/shard_map/ppermute | solution.py:21
  99.7 2.3 collective-permute-done.17
  102.7 2.7 fusion.4
  105.5 4.0 %broadcast_multiply_fusion.1 = f32[5,256,1024]{2,1,0:T(8,128)S(1)} fusion(bf16[5,512,256]{1,2,0:T(8,128)(2,1)S(1)} %fusion.4, bf16[5,512,1024]{2,1,0:T(8,128)(2,1)} %all-gather.2.cloned.1.call-done), kind=kOutput, calls=%fused_computation.18 | convolution fusion | flops 1343488000 | bytes 11796480 | tf_op jit(solution)/shard_map/prc,prd->pcd/dot_general | solution.py:145
  109.8 2.1 maximum_maximum_fusion
  111.8 0.8 copy-done
  112.7 5.3 %collective-permute-done.18 = f32[648,1024]{1,0:T(8,128)} collective-permute-done((f32[648,1024]{1,0:T(8,128)}, f32[648,1024]{1,0:T(8,128)}, u32[]{:S(2)}, u32[]{:S(2)}) %collective-permute-start.18) | collective-permute-done | bytes 2654240 | tf_op jit(solution)/shard_map/ppermute | solution.py:71
  118.0 2.1 slice.218
  122.3 18.3 %collective-permute-done.19 = f32[168,1024]{1,0:T(8,128)S(1)} collective-permute-done((f32[168,1024]{1,0:T(8,128)S(1)}, f32[168,1024]{1,0:T(8,128)S(1)}, u32[]{:S(2)}, u32[]{:S(2)}) %collective-permute-start.19) | collective-permute-done | bytes 688160 | tf_op jit(solution)/shard_map/ppermute | solution.py:84
  140.6 0.9 fusion.12
  141.5 18.2 %collective-permute-done.20 = f32[168,1024]{1,0:T(8,128)} collective-permute-done((f32[168,1024]{1,0:T(8,128)}, f32[168,1024]{1,0:T(8,128)}, u32[]{:S(2)}, u32[]{:S(2)}) %collective-permute-start.20) | collective-permute-done | bytes 688160 | tf_op jit(solution)/shard_map/ppermute | solution.py:84
  159.7 1.2 fusion.13
  161.1 3.4 %broadcast_multiply_fusion = f32[5,512,1024]{2,1,0:T(8,128)S(1)} fusion(bf16[5,512,256]{1,2,0:T(8,128)(2,1)S(1)} %fusion.4, bf16[5,512,1024]{2,1,0:T(8,128)(2,1)} %constant_dynamic-update-slice_fusion, s32[]{:T(128)S(6)} %select_n.260), kind=kOutput, calls=%fused_computation.6 | convolution fusion | flops 1344798720 | bytes 14417924 | tf_op jit(solution)/shard_map/prc,pcd->prd/dot_general | solution.py:141
  164.4 13.5 %collective-permute-done.21 = f32[168,1024]{1,0:T(8,128)S(1)} collective-permute-done((f32[168,1024]{1,0:T(8,128)S(1)}, f32[168,1024]{1,0:T(8,128)S(1)}, u32[]{:S(2)}, u32[]{:S(2)}) %collective-permute-start.21) | collective-permute-done | bytes 688160 | tf_op jit(solution)/shard_map/ppermute | solution.py:84
  178.1 1.0 fusion.16
  179.1 4.8 %broadcast_select_fusion = f32[5,512,1024]{2,1,0:T(8,128)} fusion(f32[5,512,1024]{2,1,0:T(8,128)S(1)} %get-tuple-element.43, pred[5,512]{1,0:T(8,128)(4,1)S(1)} %copy.22), kind=kLoop, calls=%fused_computation.5 | loop fusion | flops 2621440 | bytes 20974080 | tf_op jit(solution)/shard_map/jit(_where)/select_n | solution.py:153
  183.9 1.5 collective-permute-start.10
  185.5 2.1 collective-permute-done.10
  187.6 3.2 %collective-permute-start.11 = (f32[5]{0:T(128)S(1)}, f32[5]{0:T(128)S(1)}, u32[]{:S(2)}, u32[]{:S(2)}) collective-permute-start(f32[5]{0:T(128)S(1)} %fusion.49), channel_id=1, source_target_pairs={{0,2},{1,3},{2,0},{3,1},{4,6},{5,7},{6,4},{7,5},{8,10},{9,11},{10,... | collective-permute-start | bytes 68 | tf_op jit(solution)/shard_map/ppermute | solution.py:32
  190.8 1.8 collective-permute-done.11
  192.6 1.1 collective-permute-start.12
  193.8 2.4 collective-permute-done.12
  196.2 2.7 collective-permute-start.13
  199.1 2.1 collective-permute-done.13
  202.5 68.8 %reduce-scatter.2.cloned.1.call-done = f32[5,32,1024]{2,1,0:T(8,128)} async-done(((f32[5,512,1024]{2,1,0:T(8,128)}), f32[5,32,1024]{2,1,0:T(8,128)}) %reduce-scatter.2.cloned.1.call-update) | async-done | bytes 655376 | tf_op jit(solution)/shard_map/reduce_scatter | solution.py:154
  (99 shorter events, 20.9 us)
Async XLA Ops:
  7.2 44.3 %copy-start.2 = (bf16[5,32,1024]{2,1,0:T(8,128)(2,1)S(1)}, bf16[5,32,1024]{2,1,0:T(8,128)(2,1)}, u32[]{:S(2)}) copy-start(bf16[5,32,1024]{2,1,0:T(8,128)(2,1)} %param.5) | copy-start | bytes 983044
  7.2 62.0 %all-gather.2.cloned.1.call-start = ((), (), s32[]{:S(2)}) async-start(), calls=%async_computation.1 | async-start | bytes 5570560 | tf_op jit(solution)/shard_map/all_gather | solution.py:103
  7.9 263.4 %reduce-scatter.2.cloned.1.call-start = ((), (), s32[]{:S(2)}) async-start(), calls=%async_computation.2 | async-start | bytes 11141120 | tf_op jit(solution)/shard_map/reduce_scatter | solution.py:154
  8.0 19.5 %collective-permute-start.4 = (bf16[5,32,1024]{2,1,0:T(8,128)(2,1)}, bf16[5,32,1024]{2,1,0:T(8,128)(2,1)S(1)}, u32[]{:S(2)}, u32[]{:S(2)}) collective-permute-start(bf16[5,32,1024]{2,1,0:T(8,128)(2,1)} %param.5), channel_id=1, source_target_pairs={{0,112},{16,0},{32,16},{48,32},{64,48},{80,64},{96,80},{112,96},{1... | collective-permute-start | bytes 983048 | tf_op jit(solution)/shard_map/ppermute | solution.py:56
  10.2 7.9 %collective-permute-start = (bf16[5,32,1024]{2,1,0:T(8,128)(2,1)}, bf16[5,32,1024]{2,1,0:T(8,128)(2,1)S(1)}, u32[]{:S(2)}, u32[]{:S(2)}) collective-permute-start(bf16[5,32,1024]{2,1,0:T(8,128)(2,1)} %param.5), channel_id=1, source_target_pairs={{0,16},{16,32},{32,48},{48,64},{64,80},{80,96},{96,112},{112,0},{1... | collective-permute-start | bytes 983048 | tf_op jit(solution)/shard_map/ppermute | solution.py:53
  18.2 7.7 %collective-permute-start.1 = (bf16[5,32,1024]{2,1,0:T(8,128)(2,1)S(1)}, bf16[5,32,1024]{2,1,0:T(8,128)(2,1)S(1)}, u32[]{:S(2)}, u32[]{:S(2)}) collective-permute-start(bf16[5,32,1024]{2,1,0:T(8,128)(2,1)S(1)} %collective-permute-done), channel_id=1, source_target_pairs={{0,16},{16,32},{32,48},{48,64},{64,80},{80,96},{96,112},{112,0},{1... | collective-permute-start | bytes 983048 | tf_op jit(solution)/shard_map/ppermute | solution.py:53
  25.9 7.7 %collective-permute-start.2 = (bf16[5,32,1024]{2,1,0:T(8,128)(2,1)S(1)}, bf16[5,32,1024]{2,1,0:T(8,128)(2,1)S(1)}, u32[]{:S(2)}, u32[]{:S(2)}) collective-permute-start(bf16[5,32,1024]{2,1,0:T(8,128)(2,1)S(1)} %collective-permute-done.1), channel_id=1, source_target_pairs={{0,16},{16,32},{32,48},{48,64},{64,80},{80,96},{96,112},{112,0},{1... | collective-permute-start | bytes 983048 | tf_op jit(solution)/shard_map/ppermute | solution.py:53
  27.5 7.5 %collective-permute-start.5 = (bf16[5,32,1024]{2,1,0:T(8,128)(2,1)S(1)}, bf16[5,32,1024]{2,1,0:T(8,128)(2,1)S(1)}, u32[]{:S(2)}, u32[]{:S(2)}) collective-permute-start(bf16[5,32,1024]{2,1,0:T(8,128)(2,1)S(1)} %collective-permute-done.4), channel_id=1, source_target_pairs={{0,112},{16,0},{32,16},{48,32},{64,48},{80,64},{96,80},{112,96},{1... | collective-permute-start | bytes 983048 | tf_op jit(solution)/shard_map/ppermute | solution.py:56
  33.6 7.7 %collective-permute-start.3 = (bf16[5,32,1024]{2,1,0:T(8,128)(2,1)S(1)}, bf16[5,32,1024]{2,1,0:T(8,128)(2,1)S(1)}, u32[]{:S(2)}, u32[]{:S(2)}) collective-permute-start(bf16[5,32,1024]{2,1,0:T(8,128)(2,1)S(1)} %collective-permute-done.2), channel_id=1, source_target_pairs={{0,16},{16,32},{32,48},{48,64},{64,80},{80,96},{96,112},{112,0},{1... | collective-permute-start | bytes 983048 | tf_op jit(solution)/shard_map/ppermute | solution.py:53
  35.0 12.6 %collective-permute-start.6 = (bf16[5,32,1024]{2,1,0:T(8,128)(2,1)S(1)}, bf16[5,32,1024]{2,1,0:T(8,128)(2,1)S(1)}, u32[]{:S(2)}, u32[]{:S(2)}) collective-permute-start(bf16[5,32,1024]{2,1,0:T(8,128)(2,1)S(1)} %collective-permute-done.5), channel_id=1, source_target_pairs={{0,112},{16,0},{32,16},{48,32},{64,48},{80,64},{96,80},{112,96},{1... | collective-permute-start | bytes 983048 | tf_op jit(solution)/shard_map/ppermute | solution.py:56
  54.4 44.8 %copy-start.4 = (s32[5]{0:T(128)S(1)}, s32[5]{0:T(128)}, u32[]{:S(2)}) copy-start(s32[5]{0:T(128)} %param.6) | copy-start | bytes 64
  79.1 1.3 collective-permute-start.7
  80.4 3.8 %collective-permute-start.8 = (f32[2,5,256]{2,1,0:T(8,128)S(1)}, f32[2,5,256]{2,1,0:T(8,128)S(1)}, u32[]{:S(2)}, u32[]{:S(2)}) collective-permute-start(f32[2,5,256]{2,1,0:T(8,128)S(1)} %pad_maximum_fusion.9), channel_id=1, source_target_pairs={{0,32},{16,48},{32,0},{48,16},{64,96},{80,112},{96,64},{112,80},{1... | collective-permute-start | bytes 30728 | tf_op jit(solution)/shard_map/ppermute | solution.py:21
  82.0 4.1 %collective-permute-start.14 = (f32[3,5,512]{2,0,1:T(4,128)S(1)}, f32[3,5,512]{2,0,1:T(4,128)S(1)}, u32[]{:S(2)}, u32[]{:S(2)}) collective-permute-start(f32[3,5,512]{2,0,1:T(4,128)S(1)} %pad_maximum_fusion.4), channel_id=1, source_target_pairs={{0,1},{1,0},{2,3},{3,2},{4,5},{5,4},{6,7},{7,6},{8,9},{9,8},{10,11... | collective-permute-start | bytes 92168 | tf_op jit(solution)/shard_map/ppermute | solution.py:21
  86.2 5.8 %collective-permute-start.15 = (f32[3,5,512]{2,0,1:T(4,128)S(1)}, f32[3,5,512]{2,0,1:T(4,128)S(1)}, u32[]{:S(2)}, u32[]{:S(2)}) collective-permute-start(f32[3,5,512]{2,0,1:T(4,128)S(1)} %pad_maximum_fusion.5), channel_id=1, source_target_pairs={{0,2},{1,3},{2,0},{3,1},{4,6},{5,7},{6,4},{7,5},{8,10},{9,11},{10,... | collective-permute-start | bytes 92168 | tf_op jit(solution)/shard_map/ppermute | solution.py:21
  89.3 5.2 %collective-permute-start.9 = (f32[2,5,256]{2,1,0:T(8,128)S(1)}, f32[2,5,256]{2,1,0:T(8,128)S(1)}, u32[]{:S(2)}, u32[]{:S(2)}) collective-permute-start(f32[2,5,256]{2,1,0:T(8,128)S(1)} %pad_maximum_fusion.10), channel_id=1, source_target_pairs={{0,64},{16,80},{32,96},{48,112},{64,0},{80,16},{96,32},{112,48},{1... | collective-permute-start | bytes 30728 | tf_op jit(solution)/shard_map/ppermute | solution.py:21
  92.1 4.1 %collective-permute-start.16 = (f32[3,5,512]{2,0,1:T(4,128)S(1)}, f32[3,5,512]{2,0,1:T(4,128)S(1)}, u32[]{:S(2)}, u32[]{:S(2)}) collective-permute-start(f32[3,5,512]{2,0,1:T(4,128)S(1)} %pad_maximum_fusion.6), channel_id=1, source_target_pairs={{0,4},{1,5},{2,6},{3,7},{4,0},{5,1},{6,2},{7,3},{8,12},{9,13},{10,... | collective-permute-start | bytes 92168 | tf_op jit(solution)/shard_map/ppermute | solution.py:21
  96.4 5.6 %collective-permute-start.17 = (f32[3,5,512]{2,0,1:T(4,128)S(1)}, f32[3,5,512]{2,0,1:T(4,128)S(1)}, u32[]{:S(2)}, u32[]{:S(2)}) collective-permute-start(f32[3,5,512]{2,0,1:T(4,128)S(1)} %pad_maximum_fusion.7), channel_id=1, source_target_pairs={{0,8},{1,9},{2,10},{3,11},{4,12},{5,13},{6,14},{7,15},{8,0},{9,1},... | collective-permute-start | bytes 92168 | tf_op jit(solution)/shard_map/ppermute | solution.py:21
  109.6 3.1 %copy-start = (f32[5,256,1024]{2,1,0:T(8,128)}, f32[5,256,1024]{2,1,0:T(8,128)S(1)}, u32[]{:S(2)}) copy-start(f32[5,256,1024]{2,1,0:T(8,128)S(1)} %broadcast_multiply_fusion.1) | copy-start | bytes 15728644
  112.7 5.3 %collective-permute-start.18 = (f32[648,1024]{1,0:T(8,128)}, f32[648,1024]{1,0:T(8,128)}, u32[]{:S(2)}, u32[]{:S(2)}) collective-permute-start(f32[648,1024]{1,0:T(8,128)} %maximum_maximum_fusion), channel_id=1, source_target_pairs={{0,16},{16,0},{32,48},{48,32},{64,80},{80,64},{96,112},{112,96},{1... | collective-permute-start | bytes 7962632 | tf_op jit(solution)/shard_map/ppermute | solution.py:71
  112.7 7.4 %copy-start.1 = (f32[5,256,1024]{2,1,0:T(8,128)S(1)}, f32[5,256,1024]{2,1,0:T(8,128)}, u32[]{:S(2)}) copy-start(f32[5,256,1024]{2,1,0:T(8,128)} %copy-done) | copy-start | bytes 15728644
  121.8 18.8 %collective-permute-start.19 = (f32[168,1024]{1,0:T(8,128)S(1)}, f32[168,1024]{1,0:T(8,128)S(1)}, u32[]{:S(2)}, u32[]{:S(2)}) collective-permute-start(f32[168,1024]{1,0:T(8,128)S(1)} %pad_maximum_fusion.3), channel_id=1, source_target_pairs={{0,32},{16,48},{32,64},{48,80},{64,96},{80,112},{96,0},{112,16},{1... | collective-permute-start | bytes 2064392 | tf_op jit(solution)/shard_map/ppermute | solution.py:84
  141.5 18.2 %collective-permute-start.20 = (f32[168,1024]{1,0:T(8,128)}, f32[168,1024]{1,0:T(8,128)}, u32[]{:S(2)}, u32[]{:S(2)}) collective-permute-start(f32[168,1024]{1,0:T(8,128)} %fusion.12), channel_id=1, source_target_pairs={{0,32},{16,48},{32,64},{48,80},{64,96},{80,112},{96,0},{112,16},{1... | collective-permute-start | bytes 2064392 | tf_op jit(solution)/shard_map/ppermute | solution.py:84
  160.9 17.0 %collective-permute-start.21 = (f32[168,1024]{1,0:T(8,128)S(1)}, f32[168,1024]{1,0:T(8,128)S(1)}, u32[]{:S(2)}, u32[]{:S(2)}) collective-permute-start(f32[168,1024]{1,0:T(8,128)S(1)} %fusion.13), channel_id=1, source_target_pairs={{0,32},{16,48},{32,64},{48,80},{64,96},{80,112},{96,0},{112,16},{1... | collective-permute-start | bytes 2064392 | tf_op jit(solution)/shard_map/ppermute | solution.py:84
  161.1 17.0 %copy-start.3 = (bf16[5,32,1024]{2,1,0:T(8,128)(2,1)S(1)}, bf16[5,32,1024]{2,1,0:T(8,128)(2,1)}, u32[]{:S(2)}) copy-start(bf16[5,32,1024]{2,1,0:T(8,128)(2,1)} %param.4) | copy-start | bytes 983044
  183.9 3.6 %collective-permute-start.10 = (f32[5]{0:T(128)S(1)}, f32[5]{0:T(128)S(1)}, u32[]{:S(2)}, u32[]{:S(2)}) collective-permute-start(f32[5]{0:T(128)S(1)} %get-tuple-element.7), channel_id=1, source_target_pairs={{0,1},{1,0},{2,3},{3,2},{4,5},{5,4},{6,7},{7,6},{8,9},{9,8},{10,11... | collective-permute-start | bytes 68 | tf_op jit(solution)/shard_map/ppermute | solution.py:32
  187.6 5.0 %collective-permute-start.11 = (f32[5]{0:T(128)S(1)}, f32[5]{0:T(128)S(1)}, u32[]{:S(2)}, u32[]{:S(2)}) collective-permute-start(f32[5]{0:T(128)S(1)} %fusion.49), channel_id=1, source_target_pairs={{0,2},{1,3},{2,0},{3,1},{4,6},{5,7},{6,4},{7,5},{8,10},{9,11},{10,... | collective-permute-start | bytes 68 | tf_op jit(solution)/shard_map/ppermute | solution.py:32
  192.6 3.5 %collective-permute-start.12 = (f32[5]{0:T(128)S(1)}, f32[5]{0:T(128)S(1)}, u32[]{:S(2)}, u32[]{:S(2)}) collective-permute-start(f32[5]{0:T(128)S(1)} %fusion.48), channel_id=1, source_target_pairs={{0,4},{1,5},{2,6},{3,7},{4,0},{5,1},{6,2},{7,3},{8,12},{9,13},{10,... | collective-permute-start | bytes 68 | tf_op jit(solution)/shard_map/ppermute | solution.py:32
  196.2 5.1 %collective-permute-start.13 = (f32[5]{0:T(128)S(1)}, f32[5]{0:T(128)S(1)}, u32[]{:S(2)}, u32[]{:S(2)}) collective-permute-start(f32[5]{0:T(128)S(1)} %fusion.47), channel_id=1, source_target_pairs={{0,8},{1,9},{2,10},{3,11},{4,12},{5,13},{6,14},{7,15},{8,0},{9,1},... | collective-permute-start | bytes 68 | tf_op jit(solution)/shard_map/ppermute | solution.py:32
Sparse Core Ops, SparseCore 0:
  10.2 58.9 all-gather.1
  184.1 87.1 reduce-scatter.1

commit v10 on v6

--- a/solution.py
+++ b/solution.py
@@ -160,8 +160,9 @@
 
     own_term = (pair_scale * score_scale)[:, None, None]
     keep_rows = own_valid[:, :, None]
+    partner_out = jnp.where(keep_rows, partner_part - own_term * anchor.astype(jnp.float32), 0.0)
+    anchor_part, partner_out = lax.optimization_barrier((anchor_part, partner_out))
     anchor_out = jnp.where(keep_rows, anchor_part - own_term * partner.astype(jnp.float32), 0.0)
-    partner_out = jnp.where(keep_rows, partner_part - own_term * anchor.astype(jnp.float32), 0.0)
     return (loss_value, anchor_out, partner_out)
 
 

time: 211 us -> 211 us (level)
  transfers between devices with their start and end apart: 24 -> 24, of which waited for: 20 -> 20; matrix products, arithmetic and copies ran while one was open for 13% -> 14% of each run, Pallas kernels for 0% -> 0%
where the time goes in v10:
time: 211 us; the launch traced here: 210 us
  waiting for transfers between devices  110 us (52%)
  starting transfers between devices  31.6 us (15%)
  local copies, waits for them, and re-layouts  20.3 us (10%)
  matrix products  16.5 us (8%)
  between operations  16.2 us (8%)
  other arithmetic  15.5 us (7%)
    ppermute x3, waiting for transfers between devices, two_stage_reduce_scatter(): running = lax.ppermute(running, axis, ring) + addend(chip - 1 - step)  38.5 us
    all_gather x1, waiting for transfers between devices, per_device(): row_set = lax.all_gather(anchor, 'pair', axis=1, tiled=True)  16.8 us
    reduce_scatter x1, waiting for transfers between devices, per_device(): lax.psum_scatter(grad_rows, 'pair', scatter_dimension=1, tiled=True)  16.5 us
    ppermute x4, waiting for transfers between devices, ring_gather(): ahead = lax.ppermute(ahead, axis, forward)  16.3 us
    unnamed x29, local copies, waits for them, and re-layouts  15.9 us
    ppermute x7, starting transfers between devices, butterfly_merge(): other = lax.ppermute(stats, axis, [(i, i ^ bit) for i in range(size)])  13 us
    ppermute x3, starting transfers between devices, ring_gather(): behind = lax.ppermute(behind, axis, backward)  9.41 us
    ppermute x7, waiting for transfers between devices, butterfly_merge(): other = lax.ppermute(stats, axis, [(i, i ^ bit) for i in range(size)])  8.7 us
  transfers between devices with their start and end apart: 24, of which 20 were waited for; matrix products, arithmetic and copies ran while one was open for 14% of the time, Pallas kernels for 0%

profile of v10, /device:TPU:0, one launch (start us, length us, event | category | flops | bytes accessed | tf_op | source)
XLA Modules:
  0.0 210.4 jit_solution(15621459988645467714)
XLA Ops:
  8.0 2.9 %collective-permute-start.4 = (bf16[5,32,1024]{2,1,0:T(8,128)(2,1)}, bf16[5,32,1024]{2,1,0:T(8,128)(2,1)S(1)}, u32[]{:S(2)}, u32[]{:S(2)}) collective-permute-start(bf16[5,32,1024]{2,1,0:T(8,128)(2,1)} %param.5), channel_id=1, source_target_pairs={{0,112},{16,0},{32,16},{48,32},{64,48},{80,64},{96,80},{112,96},{1... | collective-permute-start | bytes 983048 | tf_op jit(solution)/shard_map/ppermute | solution.py:56
  11.7 4.2 %collective-permute-done = bf16[5,32,1024]{2,1,0:T(8,128)(2,1)S(1)} collective-permute-done((bf16[5,32,1024]{2,1,0:T(8,128)(2,1)}, bf16[5,32,1024]{2,1,0:T(8,128)(2,1)S(1)}, u32[]{:S(2)}, u32[]{:S(2)}) %collective-permute-start) | collective-permute-done | bytes 327712 | tf_op jit(solution)/shard_map/ppermute | solution.py:53
  16.2 1.2 fusion.17
  17.4 6.2 %collective-permute-done.1 = bf16[5,32,1024]{2,1,0:T(8,128)(2,1)S(1)} collective-permute-done((bf16[5,32,1024]{2,1,0:T(8,128)(2,1)S(1)}, bf16[5,32,1024]{2,1,0:T(8,128)(2,1)S(1)}, u32[]{:S(2)}, u32[]{:S(2)}) %collective-permute-start.1) | collective-permute-done | bytes 327712 | tf_op jit(solution)/shard_map/ppermute | solution.py:53
  23.6 0.8 select_reduce_fusion.1
  25.2 3.0 %collective-permute-start.5 = (bf16[5,32,1024]{2,1,0:T(8,128)(2,1)S(1)}, bf16[5,32,1024]{2,1,0:T(8,128)(2,1)S(1)}, u32[]{:S(2)}, u32[]{:S(2)}) collective-permute-start(bf16[5,32,1024]{2,1,0:T(8,128)(2,1)S(1)} %collective-permute-done.4), channel_id=1, source_target_pairs={{0,112},{16,0},{32,16},{48,32},{64,48},{80,64},{96,80},{112,96},{1... | collective-permute-start | bytes 983048 | tf_op jit(solution)/shard_map/ppermute | solution.py:56
  28.1 3.2 %collective-permute-done.2 = bf16[5,32,1024]{2,1,0:T(8,128)(2,1)S(1)} collective-permute-done((bf16[5,32,1024]{2,1,0:T(8,128)(2,1)S(1)}, bf16[5,32,1024]{2,1,0:T(8,128)(2,1)S(1)}, u32[]{:S(2)}, u32[]{:S(2)}) %collective-permute-start.2) | collective-permute-done | bytes 327712 | tf_op jit(solution)/shard_map/ppermute | solution.py:53
  31.4 1.3 collective-permute-done.5
  32.7 3.5 %collective-permute-start.6 = (bf16[5,32,1024]{2,1,0:T(8,128)(2,1)S(1)}, bf16[5,32,1024]{2,1,0:T(8,128)(2,1)S(1)}, u32[]{:S(2)}, u32[]{:S(2)}) collective-permute-start(bf16[5,32,1024]{2,1,0:T(8,128)(2,1)S(1)} %collective-permute-done.5), channel_id=1, source_target_pairs={{0,112},{16,0},{32,16},{48,32},{64,48},{80,64},{96,80},{112,96},{1... | collective-permute-start | bytes 983048 | tf_op jit(solution)/shard_map/ppermute | solution.py:56
  36.2 2.8 %collective-permute-done.3 = bf16[5,32,1024]{2,1,0:T(8,128)(2,1)S(1)} collective-permute-done((bf16[5,32,1024]{2,1,0:T(8,128)(2,1)S(1)}, bf16[5,32,1024]{2,1,0:T(8,128)(2,1)S(1)}, u32[]{:S(2)}, u32[]{:S(2)}) %collective-permute-start.3) | collective-permute-done | bytes 327712 | tf_op jit(solution)/shard_map/ppermute | solution.py:53
  42.1 1.7 constant_dynamic-update-slice_fusion.11
  46.1 0.8 constant_dynamic-update-slice_fusion.7
  51.5 0.8 constant_dynamic-update-slice_fusion
  52.3 16.8 %all-gather.2.cloned.1.call-done = bf16[5,512,1024]{2,1,0:T(8,128)(2,1)} async-done(((bf16[5,32,1024]{2,1,0:T(8,128)(2,1)}), bf16[5,512,1024]{2,1,0:T(8,128)(2,1)}) %all-gather.2.cloned.1.call-update) | async-done | bytes 5242896 | tf_op jit(solution)/shard_map/all_gather | solution.py:103
  69.1 5.2 %fusion.11 = (f32[5,256]{1,0:T(8,128)S(1)}, f32[5,512]{1,0:T(8,128)S(1)}, f32[5,256,512]{2,1,0:T(8,128)S(1)}) fusion(pred[5,256]{1,0:T(8,128)(4,1)S(1)} %broadcast_compare_fusion.1, pred[5,512]{1,0:T(8,128)(4,1)S(1)} %copy.20, bf16[5,512,1024]{2,1,0:T(8,128)(2,1)} %all-gather.2.cloned.1.call-done, ...), kind=kOutput, calls=%fused_computation.26 | convolution fusion | flops 1345450240 | bytes 10504964 | tf_op jit(solution)/shard_map/prd,pcd->prc/dot_general | solution.py:116
  74.3 1.5 copy-done.2
  75.8 1.9 fusion
  77.9 1.1 collective-permute-done.7
  79.0 1.5 collective-permute-start.8
  80.6 1.6 collective-permute-start.14
  82.9 1.8 collective-permute-done.14
  84.8 3.1 %collective-permute-start.15 = (f32[3,5,512]{2,0,1:T(4,128)S(1)}, f32[3,5,512]{2,0,1:T(4,128)S(1)}, u32[]{:S(2)}, u32[]{:S(2)}) collective-permute-start(f32[3,5,512]{2,0,1:T(4,128)S(1)} %pad_maximum_fusion.5), channel_id=1, source_target_pairs={{0,2},{1,3},{2,0},{3,1},{4,6},{5,7},{6,4},{7,5},{8,10},{9,11},{10,... | collective-permute-start | bytes 92168 | tf_op jit(solution)/shard_map/ppermute | solution.py:21
  88.0 2.7 %collective-permute-start.9 = (f32[2,5,256]{2,1,0:T(8,128)S(1)}, f32[2,5,256]{2,1,0:T(8,128)S(1)}, u32[]{:S(2)}, u32[]{:S(2)}) collective-permute-start(f32[2,5,256]{2,1,0:T(8,128)S(1)} %pad_maximum_fusion.10), channel_id=1, source_target_pairs={{0,64},{16,80},{32,96},{48,112},{64,0},{80,16},{96,32},{112,48},{1... | collective-permute-start | bytes 30728 | tf_op jit(solution)/shard_map/ppermute | solution.py:21
  90.8 1.2 collective-permute-start.16
  92.0 1.2 collective-permute-done.9
  93.2 1.7 collective-permute-done.16
  95.0 2.8 %collective-permute-start.17 = (f32[3,5,512]{2,0,1:T(4,128)S(1)}, f32[3,5,512]{2,0,1:T(4,128)S(1)}, u32[]{:S(2)}, u32[]{:S(2)}) collective-permute-start(f32[3,5,512]{2,0,1:T(4,128)S(1)} %pad_maximum_fusion.7), channel_id=1, source_target_pairs={{0,8},{1,9},{2,10},{3,11},{4,12},{5,13},{6,14},{7,15},{8,0},{9,1},... | collective-permute-start | bytes 92168 | tf_op jit(solution)/shard_map/ppermute | solution.py:21
  98.3 2.3 %collective-permute-done.17 = f32[3,5,512]{2,0,1:T(4,128)S(1)} collective-permute-done((f32[3,5,512]{2,0,1:T(4,128)S(1)}, f32[3,5,512]{2,0,1:T(4,128)S(1)}, u32[]{:S(2)}, u32[]{:S(2)}) %collective-permute-start.17) | collective-permute-done | bytes 30752 | tf_op jit(solution)/shard_map/ppermute | solution.py:21
  101.3 2.7 %fusion.4 = bf16[5,512,256]{1,2,0:T(8,128)(2,1)S(1)} fusion(f32[5,256,512]{2,1,0:T(8,128)} %copy-done.2, f32[5,256]{1,0:T(8,128)S(1)} %get-tuple-element.12, f32[5,512]{1,0:T(8,128)S(1)} %copy.27, f32[5]{0:T(128)S(1)} %get-tuple-element.47, pred[5,256]{1,0:T(8,128)(4,1)S(1)} %broadcast_compare_fusion.1, pred[5,512]{1,0:T(8,128)(4,1)S(1)} %copy.20), kind=kLoop, calls=%fused_computation.11 | loop fusion | flops 5898240 | bytes 3951380 | tf_op jit(solution)/shard_map/convert_element_type | solution.py:138
  104.1 7.3 %broadcast_multiply_fusion = f32[5,512,1024]{2,1,0:T(8,128)} fusion(bf16[5,512,256]{1,2,0:T(8,128)(2,1)S(1)} %fusion.4, bf16[5,512,1024]{2,1,0:T(8,128)(2,1)} %constant_dynamic-update-slice_fusion, s32[]{:T(128)S(6)} %select_n.255), kind=kOutput, calls=%fused_computation.5 | convolution fusion | flops 1344798720 | bytes 14417924 | tf_op jit(solution)/shard_map/prc,pcd->prd/dot_general | solution.py:141
  111.6 4.0 %broadcast_multiply_fusion.1 = f32[5,256,1024]{2,1,0:T(8,128)S(1)} fusion(bf16[5,512,256]{1,2,0:T(8,128)(2,1)S(1)} %fusion.4, bf16[5,512,1024]{2,1,0:T(8,128)(2,1)} %all-gather.2.cloned.1.call-done), kind=kOutput, calls=%fused_computation.17 | convolution fusion | flops 1343488000 | bytes 11796480 | tf_op jit(solution)/shard_map/prc,prd->pcd/dot_general | solution.py:145
  116.1 1.9 copy-done
  118.0 5.1 %collective-permute-done.18 = f32[648,1024]{1,0:T(8,128)} collective-permute-done((f32[648,1024]{1,0:T(8,128)S(1)}, f32[648,1024]{1,0:T(8,128)}, u32[]{:S(2)}, u32[]{:S(2)}) %collective-permute-start.18) | collective-permute-done | bytes 2654240 | tf_op jit(solution)/shard_map/ppermute | solution.py:71
  123.1 2.1 slice.218
  126.2 0.8 slice_add_fusion.1
  127.5 18.3 %collective-permute-done.19 = f32[168,1024]{1,0:T(8,128)S(1)} collective-permute-done((f32[168,1024]{1,0:T(8,128)S(1)}, f32[168,1024]{1,0:T(8,128)S(1)}, u32[]{:S(2)}, u32[]{:S(2)}) %collective-permute-start.19) | collective-permute-done | bytes 688160 | tf_op jit(solution)/shard_map/ppermute | solution.py:84
  146.0 18.0 %collective-permute-done.20 = f32[168,1024]{1,0:T(8,128)S(1)} collective-permute-done((f32[168,1024]{1,0:T(8,128)S(1)}, f32[168,1024]{1,0:T(8,128)S(1)}, u32[]{:S(2)}, u32[]{:S(2)}) %collective-permute-start.20) | collective-permute-done | bytes 688160 | tf_op jit(solution)/shard_map/ppermute | solution.py:84
  164.2 1.5 collective-permute-start.10
  165.6 2.1 collective-permute-done.10
  167.7 3.2 %collective-permute-start.11 = (f32[5]{0:T(128)S(1)}, f32[5]{0:T(128)S(1)}, u32[]{:S(2)}, u32[]{:S(2)}) collective-permute-start(f32[5]{0:T(128)S(1)} %fusion.49), channel_id=1, source_target_pairs={{0,2},{1,3},{2,0},{3,1},{4,6},{5,7},{6,4},{7,5},{8,10},{9,11},{10,... | collective-permute-start | bytes 68 | tf_op jit(solution)/shard_map/ppermute | solution.py:32
  171.0 1.8 collective-permute-done.11
  172.8 1.1 collective-permute-start.12
  173.9 2.4 %collective-permute-done.12 = f32[5]{0:T(128)S(1)} collective-permute-done((f32[5]{0:T(128)S(1)}, f32[5]{0:T(128)S(1)}, u32[]{:S(2)}, u32[]{:S(2)}) %collective-permute-start.12) | collective-permute-done | bytes 52 | tf_op jit(solution)/shard_map/ppermute | solution.py:32
  176.3 2.6 %collective-permute-start.13 = (f32[5]{0:T(128)S(1)}, f32[5]{0:T(128)S(1)}, u32[]{:S(2)}, u32[]{:S(2)}) collective-permute-start(f32[5]{0:T(128)S(1)} %fusion.47), channel_id=1, source_target_pairs={{0,8},{1,9},{2,10},{3,11},{4,12},{5,13},{6,14},{7,15},{8,0},{9,1},... | collective-permute-start | bytes 68 | tf_op jit(solution)/shard_map/ppermute | solution.py:32
  179.0 2.3 %collective-permute-done.21 = f32[168,1024]{1,0:T(8,128)S(1)} collective-permute-done((f32[168,1024]{1,0:T(8,128)S(1)}, f32[168,1024]{1,0:T(8,128)S(1)}, u32[]{:S(2)}, u32[]{:S(2)}) %collective-permute-start.21) | collective-permute-done | bytes 688160 | tf_op jit(solution)/shard_map/ppermute | solution.py:84
  182.9 1.0 fusion.16
  183.9 16.5 %reduce-scatter.2.cloned.1.call-done = f32[5,32,1024]{2,1,0:T(8,128)} async-done(((f32[5,512,1024]{2,1,0:T(8,128)}), f32[5,32,1024]{2,1,0:T(8,128)}) %reduce-scatter.2.cloned.1.call-update) | async-done | bytes 655376 | tf_op jit(solution)/shard_map/reduce_scatter | solution.py:148
  200.4 2.1 fusion.19
  (103 shorter events, 18.6 us)
Async XLA Ops:
  7.2 42.0 %copy-start.3 = (bf16[5,32,1024]{2,1,0:T(8,128)(2,1)S(1)}, bf16[5,32,1024]{2,1,0:T(8,128)(2,1)}, u32[]{:S(2)}) copy-start(bf16[5,32,1024]{2,1,0:T(8,128)(2,1)} %param.5) | copy-start | bytes 983044
  7.2 61.9 %all-gather.2.cloned.1.call-start = ((), (), s32[]{:S(2)}) async-start(), calls=%async_computation.1 | async-start | bytes 5570560 | tf_op jit(solution)/shard_map/all_gather | solution.py:103
  7.9 192.5 %reduce-scatter.2.cloned.1.call-start = ((), (), s32[]{:S(2)}) async-start(), calls=%async_computation.2 | async-start | bytes 11141120 | tf_op jit(solution)/shard_map/reduce_scatter | solution.py:148
  8.0 7.9 %collective-permute-start = (bf16[5,32,1024]{2,1,0:T(8,128)(2,1)}, bf16[5,32,1024]{2,1,0:T(8,128)(2,1)S(1)}, u32[]{:S(2)}, u32[]{:S(2)}) collective-permute-start(bf16[5,32,1024]{2,1,0:T(8,128)(2,1)} %param.5), channel_id=1, source_target_pairs={{0,16},{16,32},{32,48},{48,64},{64,80},{80,96},{96,112},{112,0},{1... | collective-permute-start | bytes 983048 | tf_op jit(solution)/shard_map/ppermute | solution.py:53
  8.0 17.2 %collective-permute-start.4 = (bf16[5,32,1024]{2,1,0:T(8,128)(2,1)}, bf16[5,32,1024]{2,1,0:T(8,128)(2,1)S(1)}, u32[]{:S(2)}, u32[]{:S(2)}) collective-permute-start(bf16[5,32,1024]{2,1,0:T(8,128)(2,1)} %param.5), channel_id=1, source_target_pairs={{0,112},{16,0},{32,16},{48,32},{64,48},{80,64},{96,80},{112,96},{1... | collective-permute-start | bytes 983048 | tf_op jit(solution)/shard_map/ppermute | solution.py:56
  15.9 7.7 %collective-permute-start.1 = (bf16[5,32,1024]{2,1,0:T(8,128)(2,1)S(1)}, bf16[5,32,1024]{2,1,0:T(8,128)(2,1)S(1)}, u32[]{:S(2)}, u32[]{:S(2)}) collective-permute-start(bf16[5,32,1024]{2,1,0:T(8,128)(2,1)S(1)} %collective-permute-done), channel_id=1, source_target_pairs={{0,16},{16,32},{32,48},{48,64},{64,80},{80,96},{96,112},{112,0},{1... | collective-permute-start | bytes 983048 | tf_op jit(solution)/shard_map/ppermute | solution.py:53
  23.6 7.7 %collective-permute-start.2 = (bf16[5,32,1024]{2,1,0:T(8,128)(2,1)S(1)}, bf16[5,32,1024]{2,1,0:T(8,128)(2,1)S(1)}, u32[]{:S(2)}, u32[]{:S(2)}) collective-permute-start(bf16[5,32,1024]{2,1,0:T(8,128)(2,1)S(1)} %collective-permute-done.1), channel_id=1, source_target_pairs={{0,16},{16,32},{32,48},{48,64},{64,80},{80,96},{96,112},{112,0},{1... | collective-permute-start | bytes 983048 | tf_op jit(solution)/shard_map/ppermute | solution.py:53
  25.2 7.5 %collective-permute-start.5 = (bf16[5,32,1024]{2,1,0:T(8,128)(2,1)S(1)}, bf16[5,32,1024]{2,1,0:T(8,128)(2,1)S(1)}, u32[]{:S(2)}, u32[]{:S(2)}) collective-permute-start(bf16[5,32,1024]{2,1,0:T(8,128)(2,1)S(1)} %collective-permute-done.4), channel_id=1, source_target_pairs={{0,112},{16,0},{32,16},{48,32},{64,48},{80,64},{96,80},{112,96},{1... | collective-permute-start | bytes 983048 | tf_op jit(solution)/shard_map/ppermute | solution.py:56
  31.3 7.7 %collective-permute-start.3 = (bf16[5,32,1024]{2,1,0:T(8,128)(2,1)S(1)}, bf16[5,32,1024]{2,1,0:T(8,128)(2,1)S(1)}, u32[]{:S(2)}, u32[]{:S(2)}) collective-permute-start(bf16[5,32,1024]{2,1,0:T(8,128)(2,1)S(1)} %collective-permute-done.2), channel_id=1, source_target_pairs={{0,16},{16,32},{32,48},{48,64},{64,80},{80,96},{96,112},{112,0},{1... | collective-permute-start | bytes 983048 | tf_op jit(solution)/shard_map/ppermute | solution.py:53
  32.7 12.6 %collective-permute-start.6 = (bf16[5,32,1024]{2,1,0:T(8,128)(2,1)S(1)}, bf16[5,32,1024]{2,1,0:T(8,128)(2,1)S(1)}, u32[]{:S(2)}, u32[]{:S(2)}) collective-permute-start(bf16[5,32,1024]{2,1,0:T(8,128)(2,1)S(1)} %collective-permute-done.5), channel_id=1, source_target_pairs={{0,112},{16,0},{32,16},{48,32},{64,48},{80,64},{96,80},{112,96},{1... | collective-permute-start | bytes 983048 | tf_op jit(solution)/shard_map/ppermute | solution.py:56
  52.3 25.5 %copy-start.6 = (f32[5]{0:T(128)S(1)}, f32[5]{0:T(128)}, u32[]{:S(2)}) copy-start(f32[5]{0:T(128)} %param.7) | copy-start | bytes 64
  52.3 45.5 %copy-start.5 = (s32[5]{0:T(128)S(1)}, s32[5]{0:T(128)}, u32[]{:S(2)}) copy-start(s32[5]{0:T(128)} %param.6) | copy-start | bytes 64
  74.3 1.5 copy-start.2
  77.7 1.3 collective-permute-start.7
  79.0 3.8 %collective-permute-start.8 = (f32[2,5,256]{2,1,0:T(8,128)S(1)}, f32[2,5,256]{2,1,0:T(8,128)S(1)}, u32[]{:S(2)}, u32[]{:S(2)}) collective-permute-start(f32[2,5,256]{2,1,0:T(8,128)S(1)} %pad_maximum_fusion.9), channel_id=1, source_target_pairs={{0,32},{16,48},{32,0},{48,16},{64,96},{80,112},{96,64},{112,80},{1... | collective-permute-start | bytes 30728 | tf_op jit(solution)/shard_map/ppermute | solution.py:21
  80.6 4.1 %collective-permute-start.14 = (f32[3,5,512]{2,0,1:T(4,128)S(1)}, f32[3,5,512]{2,0,1:T(4,128)S(1)}, u32[]{:S(2)}, u32[]{:S(2)}) collective-permute-start(f32[3,5,512]{2,0,1:T(4,128)S(1)} %pad_maximum_fusion.4), channel_id=1, source_target_pairs={{0,1},{1,0},{2,3},{3,2},{4,5},{5,4},{6,7},{7,6},{8,9},{9,8},{10,11... | collective-permute-start | bytes 92168 | tf_op jit(solution)/shard_map/ppermute | solution.py:21
  84.8 5.8 %collective-permute-start.15 = (f32[3,5,512]{2,0,1:T(4,128)S(1)}, f32[3,5,512]{2,0,1:T(4,128)S(1)}, u32[]{:S(2)}, u32[]{:S(2)}) collective-permute-start(f32[3,5,512]{2,0,1:T(4,128)S(1)} %pad_maximum_fusion.5), channel_id=1, source_target_pairs={{0,2},{1,3},{2,0},{3,1},{4,6},{5,7},{6,4},{7,5},{8,10},{9,11},{10,... | collective-permute-start | bytes 92168 | tf_op jit(solution)/shard_map/ppermute | solution.py:21
  88.0 5.2 %collective-permute-start.9 = (f32[2,5,256]{2,1,0:T(8,128)S(1)}, f32[2,5,256]{2,1,0:T(8,128)S(1)}, u32[]{:S(2)}, u32[]{:S(2)}) collective-permute-start(f32[2,5,256]{2,1,0:T(8,128)S(1)} %pad_maximum_fusion.10), channel_id=1, source_target_pairs={{0,64},{16,80},{32,96},{48,112},{64,0},{80,16},{96,32},{112,48},{1... | collective-permute-start | bytes 30728 | tf_op jit(solution)/shard_map/ppermute | solution.py:21
  90.8 4.1 %collective-permute-start.16 = (f32[3,5,512]{2,0,1:T(4,128)S(1)}, f32[3,5,512]{2,0,1:T(4,128)S(1)}, u32[]{:S(2)}, u32[]{:S(2)}) collective-permute-start(f32[3,5,512]{2,0,1:T(4,128)S(1)} %pad_maximum_fusion.6), channel_id=1, source_target_pairs={{0,4},{1,5},{2,6},{3,7},{4,0},{5,1},{6,2},{7,3},{8,12},{9,13},{10,... | collective-permute-start | bytes 92168 | tf_op jit(solution)/shard_map/ppermute | solution.py:21
  95.0 5.6 %collective-permute-start.17 = (f32[3,5,512]{2,0,1:T(4,128)S(1)}, f32[3,5,512]{2,0,1:T(4,128)S(1)}, u32[]{:S(2)}, u32[]{:S(2)}) collective-permute-start(f32[3,5,512]{2,0,1:T(4,128)S(1)} %pad_maximum_fusion.7), channel_id=1, source_target_pairs={{0,8},{1,9},{2,10},{3,11},{4,12},{5,13},{6,14},{7,15},{8,0},{9,1},... | collective-permute-start | bytes 92168 | tf_op jit(solution)/shard_map/ppermute | solution.py:21
  115.7 2.4 %copy-start = (f32[5,256,1024]{2,1,0:T(8,128)}, f32[5,256,1024]{2,1,0:T(8,128)S(1)}, u32[]{:S(2)}) copy-start(f32[5,256,1024]{2,1,0:T(8,128)S(1)} %broadcast_multiply_fusion.1) | copy-start | bytes 15728644
  118.0 5.1 %collective-permute-start.18 = (f32[648,1024]{1,0:T(8,128)S(1)}, f32[648,1024]{1,0:T(8,128)}, u32[]{:S(2)}, u32[]{:S(2)}) collective-permute-start(f32[648,1024]{1,0:T(8,128)S(1)} %maximum_maximum_fusion), channel_id=1, source_target_pairs={{0,16},{16,0},{32,48},{48,32},{64,80},{80,64},{96,112},{112,96},{1... | collective-permute-start | bytes 7962632 | tf_op jit(solution)/shard_map/ppermute | solution.py:71
  118.0 7.1 %copy-start.1 = (f32[5,256,1024]{2,1,0:T(8,128)S(1)}, f32[5,256,1024]{2,1,0:T(8,128)}, u32[]{:S(2)}) copy-start(f32[5,256,1024]{2,1,0:T(8,128)} %copy-done) | copy-start | bytes 15728644
  126.1 56.7 %copy-start.4 = (bf16[5,32,1024]{2,1,0:T(8,128)(2,1)S(1)}, bf16[5,32,1024]{2,1,0:T(8,128)(2,1)}, u32[]{:S(2)}) copy-start(bf16[5,32,1024]{2,1,0:T(8,128)(2,1)} %param.4) | copy-start | bytes 983044
  127.0 18.8 %collective-permute-start.19 = (f32[168,1024]{1,0:T(8,128)S(1)}, f32[168,1024]{1,0:T(8,128)S(1)}, u32[]{:S(2)}, u32[]{:S(2)}) collective-permute-start(f32[168,1024]{1,0:T(8,128)S(1)} %pad_maximum_fusion.3), channel_id=1, source_target_pairs={{0,32},{16,48},{32,64},{48,80},{64,96},{80,112},{96,0},{112,16},{1... | collective-permute-start | bytes 2064392 | tf_op jit(solution)/shard_map/ppermute | solution.py:84
  145.9 18.0 %collective-permute-start.20 = (f32[168,1024]{1,0:T(8,128)S(1)}, f32[168,1024]{1,0:T(8,128)S(1)}, u32[]{:S(2)}, u32[]{:S(2)}) collective-permute-start(f32[168,1024]{1,0:T(8,128)S(1)} %fusion.12), channel_id=1, source_target_pairs={{0,32},{16,48},{32,64},{48,80},{64,96},{80,112},{96,0},{112,16},{1... | collective-permute-start | bytes 2064392 | tf_op jit(solution)/shard_map/ppermute | solution.py:84
  164.0 17.2 %collective-permute-start.21 = (f32[168,1024]{1,0:T(8,128)S(1)}, f32[168,1024]{1,0:T(8,128)S(1)}, u32[]{:S(2)}, u32[]{:S(2)}) collective-permute-start(f32[168,1024]{1,0:T(8,128)S(1)} %fusion.13), channel_id=1, source_target_pairs={{0,32},{16,48},{32,64},{48,80},{64,96},{80,112},{96,0},{112,16},{1... | collective-permute-start | bytes 2064392 | tf_op jit(solution)/shard_map/ppermute | solution.py:84
  164.2 3.6 %collective-permute-start.10 = (f32[5]{0:T(128)S(1)}, f32[5]{0:T(128)S(1)}, u32[]{:S(2)}, u32[]{:S(2)}) collective-permute-start(f32[5]{0:T(128)S(1)} %get-tuple-element.11), channel_id=1, source_target_pairs={{0,1},{1,0},{2,3},{3,2},{4,5},{5,4},{6,7},{7,6},{8,9},{9,8},{10,11... | collective-permute-start | bytes 68 | tf_op jit(solution)/shard_map/ppermute | solution.py:32
  167.7 5.0 %collective-permute-start.11 = (f32[5]{0:T(128)S(1)}, f32[5]{0:T(128)S(1)}, u32[]{:S(2)}, u32[]{:S(2)}) collective-permute-start(f32[5]{0:T(128)S(1)} %fusion.49), channel_id=1, source_target_pairs={{0,2},{1,3},{2,0},{3,1},{4,6},{5,7},{6,4},{7,5},{8,10},{9,11},{10,... | collective-permute-start | bytes 68 | tf_op jit(solution)/shard_map/ppermute | solution.py:32
  172.8 3.5 %collective-permute-start.12 = (f32[5]{0:T(128)S(1)}, f32[5]{0:T(128)S(1)}, u32[]{:S(2)}, u32[]{:S(2)}) collective-permute-start(f32[5]{0:T(128)S(1)} %fusion.48), channel_id=1, source_target_pairs={{0,4},{1,5},{2,6},{3,7},{4,0},{5,1},{6,2},{7,3},{8,12},{9,13},{10,... | collective-permute-start | bytes 68 | tf_op jit(solution)/shard_map/ppermute | solution.py:32
  176.3 5.3 %collective-permute-start.13 = (f32[5]{0:T(128)S(1)}, f32[5]{0:T(128)S(1)}, u32[]{:S(2)}, u32[]{:S(2)}) collective-permute-start(f32[5]{0:T(128)S(1)} %fusion.47), channel_id=1, source_target_pairs={{0,8},{1,9},{2,10},{3,11},{4,12},{5,13},{6,14},{7,15},{8,0},{9,1},... | collective-permute-start | bytes 68 | tf_op jit(solution)/shard_map/ppermute | solution.py:32
Sparse Core Ops, SparseCore 0:
  10.2 58.9 all-gather.1
  111.5 88.8 reduce-scatter.1

commit v11 on v6

--- a/solution.py
+++ b/solution.py
@@ -100,10 +100,10 @@
     )
     own_positive = jnp.sum(jnp.where(own_valid, positive, 0.0), axis=1)
 
-    row_set = lax.all_gather(anchor, "pair", axis=1, tiled=True)
+    row_blocks = lax.all_gather(anchor, "pair", axis=0)
     col_set = jnp.concatenate(ring_gather(partner, "dp", dp_size), axis=1)
     col_set = jnp.roll(col_set, (dp_index - dp_size // 2) * shard_rows, axis=1)
-    row_count = row_set.shape[1]
+    row_count = row_blocks.shape[0] * shard_rows
     col_count = col_set.shape[1]
     row_global = dp_index * row_count + jnp.arange(row_count, dtype=jnp.int32)
     col_first = (jnp.arange(dp_size, dtype=jnp.int32) * pair_size + pair_place) * shard_rows
@@ -113,9 +113,9 @@
     inside = row_valid[:, :, None] & col_valid[:, None, :]
 
     scores = (
-        jnp.einsum("prd,pcd->prc", row_set, col_set, preferred_element_type=jnp.float32)
+        jnp.einsum("kprd,pcd->pkrc", row_blocks, col_set, preferred_element_type=jnp.float32)
         * score_scale
-    )
+    ).reshape(pair_count, row_count, col_count)
     masked = jnp.where(inside, scores, NEG)
     row_high = jnp.max(masked, axis=2)
     row_sum = jnp.sum(jnp.where(inside, jnp.exp(masked - row_high[:, :, None]), 0.0), axis=2)
@@ -137,15 +137,18 @@
     prob_col = jnp.where(inside, jnp.exp(scores - col_lse[:, None, :]), 0.0)
     weights = (pair_scale[:, None, None] * 0.5 * (prob_row + prob_col)).astype(jnp.bfloat16)
     weights = lax.optimization_barrier(weights)
+    weight_blocks = weights.reshape(pair_count, pair_size, shard_rows, col_count)
     grad_rows = (
-        jnp.einsum("prc,pcd->prd", weights, col_set, preferred_element_type=jnp.float32)
+        jnp.einsum("pkrc,pcd->kprd", weight_blocks, col_set, preferred_element_type=jnp.float32)
         * score_scale
     )
     grad_cols = (
-        jnp.einsum("prc,prd->pcd", weights, row_set, preferred_element_type=jnp.float32)
+        jnp.einsum("pkrc,kprd->pcd", weight_blocks, row_blocks, preferred_element_type=jnp.float32)
         * score_scale
     )
-    anchor_part = lax.psum_scatter(grad_rows, "pair", scatter_dimension=1, tiled=True)
+    anchor_part = lax.psum_scatter(
+        grad_rows.reshape(-1, model_width), "pair", scatter_dimension=0, tiled=True
+    ).reshape(pair_count, shard_rows, model_width)
 
     width_lanes = jnp.arange(model_width, dtype=jnp.int32)[None, :]
     slots = (jnp.arange(pair_count, dtype=jnp.int32) * dp_size + dp_index)[:, None]

time: 211 us -> 213 us (level)
  local copies, waits for them, and re-layouts: 20 us -> 27.7 us
  matrix products: 16.5 us -> 12 us
  other arithmetic: 14.8 us -> 18.3 us
  waiting for transfers between devices: 111 us -> 108 us
    mul x0 -> x1, local copies, waits for them, and re-layouts: none -> 5.11 us  [per_device(): jnp.einsum('pkrc,pcd->kprd', weight_blocks, col_set, preferred_element_ty...]
    dot_general x3, matrix products: 16.5 us -> 12 us  [the longest x1 4.62 us: per_device(): jnp.einsum('kprd,pcd->pkrc', row_blocks, col_set, preferred_element_type=...]
    ppermute x4, waiting for transfers between devices: 16.3 us -> 19.7 us  [ring_gather(): ahead = lax.ppermute(ahead, axis, forward)]
    all_gather x1, waiting for transfers between devices: 17 us -> 14.8 us  [per_device(): row_blocks = lax.all_gather(anchor, 'pair', axis=0)]
    unnamed x29 -> x33, local copies, waits for them, and re-layouts: 15.7 us -> 16.3 us
  transfers between devices with their start and end apart: 24 -> 24, of which waited for: 20 -> 18; matrix products, arithmetic and copies ran while one was open for 13% -> 15% of each run, Pallas kernels for 0% -> 0%
where the time goes in v11:
time: 213 us
  waiting for transfers between devices  108 us (51%)
  starting transfers between devices  30.3 us (14%)
  local copies, waits for them, and re-layouts  27.7 us (13%)
  other arithmetic  18.3 us (9%)
  between operations  16.2 us (8%)
  matrix products  12 us (6%)
    ppermute x3, waiting for transfers between devices, two_stage_reduce_scatter(): running = lax.ppermute(running, axis, ring) + addend(chip - 1 - step)  38.2 us
    ppermute x4, waiting for transfers between devices, ring_gather(): ahead = lax.ppermute(ahead, axis, forward)  19.7 us
    reduce_scatter x1, waiting for transfers between devices, per_device(): lax.psum_scatter(grad_rows.reshape(-1, model_width), 'pair', scatter_dime...  16.3 us
    unnamed x33, local copies, waits for them, and re-layouts  16.3 us
    all_gather x1, waiting for transfers between devices, per_device(): row_blocks = lax.all_gather(anchor, 'pair', axis=0)  14.8 us
    ppermute x7, starting transfers between devices, butterfly_merge(): other = lax.ppermute(stats, axis, [(i, i ^ bit) for i in range(size)])  13.2 us
    ppermute x4, starting transfers between devices, butterfly_sum(): other = lax.ppermute(values, axis, [(i, i ^ bit) for i in range(size)])  8.26 us
    ppermute x3, starting transfers between devices, ring_gather(): behind = lax.ppermute(behind, axis, backward)  8.21 us
  transfers between devices with their start and end apart: 24, of which 18 were waited for; matrix products, arithmetic and copies ran while one was open for 15% of the time, Pallas kernels for 0%

profile of v11, /device:TPU:0, one launch (start us, length us, event | category | flops | bytes accessed | tf_op | source)
XLA Modules:
  0.0 212.8 jit_solution(10724259299526979242)
XLA Ops:
  8.0 2.3 %collective-permute-start.4 = (bf16[5,32,1024]{2,1,0:T(8,128)(2,1)}, bf16[5,32,1024]{2,1,0:T(8,128)(2,1)S(1)}, u32[]{:S(2)}, u32[]{:S(2)}) collective-permute-start(bf16[5,32,1024]{2,1,0:T(8,128)(2,1)} %param.5), channel_id=1, source_target_pairs={{0,112},{16,0},{32,16},{48,32},{64,48},{80,64},{96,80},{112,96},{1... | collective-permute-start | bytes 983048 | tf_op jit(solution)/shard_map/ppermute | solution.py:56
  11.3 1.2 fusion.29
  13.3 4.9 %collective-permute-done = bf16[5,32,1024]{2,1,0:T(8,128)(2,1)S(1)} collective-permute-done((bf16[5,32,1024]{2,1,0:T(8,128)(2,1)}, bf16[5,32,1024]{2,1,0:T(8,128)(2,1)S(1)}, u32[]{:S(2)}, u32[]{:S(2)}) %collective-permute-start) | collective-permute-done | bytes 327712 | tf_op jit(solution)/shard_map/ppermute | solution.py:53
  19.7 6.1 %collective-permute-done.1 = bf16[5,32,1024]{2,1,0:T(8,128)(2,1)S(1)} collective-permute-done((bf16[5,32,1024]{2,1,0:T(8,128)(2,1)S(1)}, bf16[5,32,1024]{2,1,0:T(8,128)(2,1)S(1)}, u32[]{:S(2)}, u32[]{:S(2)}) %collective-permute-start.1) | collective-permute-done | bytes 327712 | tf_op jit(solution)/shard_map/ppermute | solution.py:53
  26.0 3.0 %collective-permute-start.5 = (bf16[5,32,1024]{2,1,0:T(8,128)(2,1)S(1)}, bf16[5,32,1024]{2,1,0:T(8,128)(2,1)S(1)}, u32[]{:S(2)}, u32[]{:S(2)}) collective-permute-start(bf16[5,32,1024]{2,1,0:T(8,128)(2,1)S(1)} %collective-permute-done.4), channel_id=1, source_target_pairs={{0,112},{16,0},{32,16},{48,32},{64,48},{80,64},{96,80},{112,96},{1... | collective-permute-start | bytes 983048 | tf_op jit(solution)/shard_map/ppermute | solution.py:56
  28.9 4.7 %collective-permute-done.2 = bf16[5,32,1024]{2,1,0:T(8,128)(2,1)S(1)} collective-permute-done((bf16[5,32,1024]{2,1,0:T(8,128)(2,1)S(1)}, bf16[5,32,1024]{2,1,0:T(8,128)(2,1)S(1)}, u32[]{:S(2)}, u32[]{:S(2)}) %collective-permute-start.2) | collective-permute-done | bytes 327712 | tf_op jit(solution)/shard_map/ppermute | solution.py:53
  34.3 3.0 %collective-permute-start.6 = (bf16[5,32,1024]{2,1,0:T(8,128)(2,1)S(1)}, bf16[5,32,1024]{2,1,0:T(8,128)(2,1)S(1)}, u32[]{:S(2)}, u32[]{:S(2)}) collective-permute-start(bf16[5,32,1024]{2,1,0:T(8,128)(2,1)S(1)} %collective-permute-done.5), channel_id=1, source_target_pairs={{0,112},{16,0},{32,16},{48,32},{64,48},{80,64},{96,80},{112,96},{1... | collective-permute-start | bytes 983048 | tf_op jit(solution)/shard_map/ppermute | solution.py:56
  37.3 4.0 %collective-permute-done.3 = bf16[5,32,1024]{2,1,0:T(8,128)(2,1)S(1)} collective-permute-done((bf16[5,32,1024]{2,1,0:T(8,128)(2,1)S(1)}, bf16[5,32,1024]{2,1,0:T(8,128)(2,1)S(1)}, u32[]{:S(2)}, u32[]{:S(2)}) %collective-permute-start.3) | collective-permute-done | bytes 327712 | tf_op jit(solution)/shard_map/ppermute | solution.py:53
  44.3 1.8 constant_dynamic-update-slice_fusion.11
  54.3 14.8 %all-gather.3.cloned.1.call-done = bf16[80,32,1024]{2,1,0:T(8,128)(2,1)} async-done(((bf16[5,32,1024]{2,1,0:T(8,128)(2,1)}), bf16[80,32,1024]{2,1,0:T(8,128)(2,1)}) %all-gather.3.cloned.1.call-update) | async-done | bytes 5242896 | tf_op jit(solution)/shard_map/all_gather | solution.py:103
  69.1 4.6 %fusion.18 = (f32[5,256]{1,0:T(8,128)S(1)}, f32[5,256,16,32]{1,3,2,0:T(8,128)S(1)}) fusion(pred[5,256]{1,0:T(8,128)(4,1)S(1)} %broadcast_compare_fusion.2, pred[5,16,32]{2,1,0:T(8,128)(4,1)S(1)} %broadcast_compare_fusion.1, bf16[16,5,32,1024]{3,2,1,0:T(8,128)(2,1)} %bitcast.148, bf16[5,512,1024]{2,1,0:T(8,128)(2,1)} %constant_dynamic-update-slice_fusion, ...), kind=kOutput, calls=%fused_computation.27 | convolution fusion | flops 1344797440 | bytes 10494724 | tf_op jit(solution)/shard_map/kprd,pcd->pkrc/dot_general | solution.py:116
  73.8 1.3 fusion.7
  75.2 1.4 fusion.8
  76.9 1.5 collective-permute-start.8
  78.5 1.6 collective-permute-start.14
  80.7 1.8 collective-permute-done.14
  82.7 3.1 %collective-permute-start.15 = (f32[3,5,512]{2,0,1:T(4,128)S(1)}, f32[3,5,512]{2,0,1:T(4,128)S(1)}, u32[]{:S(2)}, u32[]{:S(2)}) collective-permute-start(f32[3,5,512]{2,0,1:T(4,128)S(1)} %pad_maximum_fusion.5), channel_id=1, source_target_pairs={{0,2},{1,3},{2,0},{3,1},{4,6},{5,7},{6,4},{7,5},{8,10},{9,11},{10,... | collective-permute-start | bytes 92168 | tf_op jit(solution)/shard_map/ppermute | solution.py:21
  85.8 2.7 %collective-permute-start.9 = (f32[2,5,256]{2,1,0:T(8,128)S(1)}, f32[2,5,256]{2,1,0:T(8,128)S(1)}, u32[]{:S(2)}, u32[]{:S(2)}) collective-permute-start(f32[2,5,256]{2,1,0:T(8,128)S(1)} %pad_maximum_fusion.10), channel_id=1, source_target_pairs={{0,64},{16,80},{32,96},{48,112},{64,0},{80,16},{96,32},{112,48},{1... | collective-permute-start | bytes 30728 | tf_op jit(solution)/shard_map/ppermute | solution.py:21
  88.6 1.2 collective-permute-start.16
  89.9 1.2 collective-permute-done.9
  91.0 1.7 collective-permute-done.16
  92.9 3.0 %collective-permute-start.17 = (f32[3,5,512]{2,0,1:T(4,128)S(1)}, f32[3,5,512]{2,0,1:T(4,128)S(1)}, u32[]{:S(2)}, u32[]{:S(2)}) collective-permute-start(f32[3,5,512]{2,0,1:T(4,128)S(1)} %pad_maximum_fusion.7), channel_id=1, source_target_pairs={{0,8},{1,9},{2,10},{3,11},{4,12},{5,13},{6,14},{7,15},{8,0},{9,1},... | collective-permute-start | bytes 92168 | tf_op jit(solution)/shard_map/ppermute | solution.py:21
  96.1 1.2 copy.39
  97.3 1.3 collective-permute-done.17
  98.6 1.2 copy.40
  99.8 1.5 broadcast_select_fusion.1
  101.3 0.9 copy-done.3
  102.6 1.4 fusion.6
  104.0 1.1 copy-done.6
  105.1 3.3 %multiply_bitcast_fusion = f32[16,5,32,1024]{3,2,0,1:T(8,128)S(1)} fusion(bf16[5,16,32,256]{3,2,1,0:T(8,128)(2,1)S(1)} %bitcast.139, bf16[5,512,1024]{2,1,0:T(8,128)(2,1)} %constant_dynamic-update-slice_fusion, s32[]{:T(128)S(6)} %select_n.261), kind=kOutput, calls=%fused_computation | convolution fusion | flops 1344798720 | bytes 14417924 | tf_op jit(solution)/shard_map/pkrc,pcd->kprd/dot_general | solution.py:142
  108.4 5.1 %copy.45 = f32[16,5,32,1024]{3,2,1,0:T(8,128)} copy(f32[16,5,32,1024]{3,2,0,1:T(8,128)S(1)} %multiply_bitcast_fusion) | data formatting | bytes 20971520 | tf_op jit(solution)/shard_map/mul | solution.py:142
  113.6 1.1 fusion.32
  114.9 4.1 %bitcast_multiply_fusion = f32[5,256,1024]{2,1,0:T(8,128)S(1)} fusion(bf16[5,16,32,256]{3,2,1,0:T(8,128)(2,1)S(1)} %bitcast.140, bf16[16,5,32,1024]{3,2,1,0:T(8,128)(2,1)} %bitcast.149), kind=kOutput, calls=%fused_computation.1 | convolution fusion | flops 1343488000 | bytes 11796480 | tf_op jit(solution)/shard_map/pkrc,kprd->pcd/dot_general | solution.py:146
  119.5 1.9 copy-done
  121.4 5.1 %collective-permute-done.18 = f32[648,1024]{1,0:T(8,128)} collective-permute-done((f32[648,1024]{1,0:T(8,128)S(1)}, f32[648,1024]{1,0:T(8,128)}, u32[]{:S(2)}, u32[]{:S(2)}) %collective-permute-start.18) | collective-permute-done | bytes 2654240 | tf_op jit(solution)/shard_map/ppermute | solution.py:71
  126.5 2.1 slice.218
  130.8 18.4 %collective-permute-done.19 = f32[168,1024]{1,0:T(8,128)S(1)} collective-permute-done((f32[168,1024]{1,0:T(8,128)S(1)}, f32[168,1024]{1,0:T(8,128)S(1)}, u32[]{:S(2)}, u32[]{:S(2)}) %collective-permute-start.19) | collective-permute-done | bytes 688160 | tf_op jit(solution)/shard_map/ppermute | solution.py:84
  149.4 17.9 %collective-permute-done.20 = f32[168,1024]{1,0:T(8,128)S(1)} collective-permute-done((f32[168,1024]{1,0:T(8,128)S(1)}, f32[168,1024]{1,0:T(8,128)S(1)}, u32[]{:S(2)}, u32[]{:S(2)}) %collective-permute-start.20) | collective-permute-done | bytes 688160 | tf_op jit(solution)/shard_map/ppermute | solution.py:84
  167.5 1.3 collective-permute-start.10
  168.8 2.3 %collective-permute-done.10 = f32[5]{0:T(128)S(1)} collective-permute-done((f32[5]{0:T(128)S(1)}, f32[5]{0:T(128)S(1)}, u32[]{:S(2)}, u32[]{:S(2)}) %collective-permute-start.10) | collective-permute-done | bytes 52 | tf_op jit(solution)/shard_map/ppermute | solution.py:32
  171.1 2.9 %collective-permute-start.11 = (f32[5]{0:T(128)S(1)}, f32[5]{0:T(128)S(1)}, u32[]{:S(2)}, u32[]{:S(2)}) collective-permute-start(f32[5]{0:T(128)S(1)} %fusion.61), channel_id=1, source_target_pairs={{0,2},{1,3},{2,0},{3,1},{4,6},{5,7},{6,4},{7,5},{8,10},{9,11},{10,... | collective-permute-start | bytes 68 | tf_op jit(solution)/shard_map/ppermute | solution.py:32
  174.0 2.1 collective-permute-done.11
  176.1 1.2 collective-permute-start.12
  177.3 2.4 %collective-permute-done.12 = f32[5]{0:T(128)S(1)} collective-permute-done((f32[5]{0:T(128)S(1)}, f32[5]{0:T(128)S(1)}, u32[]{:S(2)}, u32[]{:S(2)}) %collective-permute-start.12) | collective-permute-done | bytes 52 | tf_op jit(solution)/shard_map/ppermute | solution.py:32
  179.7 2.9 %collective-permute-start.13 = (f32[5]{0:T(128)S(1)}, f32[5]{0:T(128)S(1)}, u32[]{:S(2)}, u32[]{:S(2)}) collective-permute-start(f32[5]{0:T(128)S(1)} %fusion.59), channel_id=1, source_target_pairs={{0,8},{1,9},{2,10},{3,11},{4,12},{5,13},{6,14},{7,15},{8,0},{9,1},... | collective-permute-start | bytes 68 | tf_op jit(solution)/shard_map/ppermute | solution.py:32
  182.5 2.0 collective-permute-done.21
  186.1 16.3 %reduce-scatter.2.cloned.1.call-done = f32[160,1024]{1,0:T(8,128)} async-done(((f32[2560,1024]{1,0:T(8,128)}), f32[160,1024]{1,0:T(8,128)}) %reduce-scatter.2.cloned.1.call-update) | async-done | bytes 655376 | tf_op jit(solution)/shard_map/reduce_scatter | solution.py:149
  202.5 2.4 %fusion.28 = (f32[5,32,1024]{2,1,0:T(8,128)}, f32[5,32,1024]{2,1,0:T(8,128)}) fusion(f32[5,32,1024]{2,1,0:T(8,128)S(1)} %bitcast.136, bf16[5,32,1024]{2,1,0:T(8,128)(2,1)S(1)} %copy-done.5, f32[5]{0:T(128)S(1)} %get-tuple-element.42, pred[5,32]{1,0:T(8,128)(4,1)S(1)} %broadcast_compare_fusion.3, f32[5,32,1024]{2,1,0:T(8,128)} %bitcast.141, ...), kind=kLoop, calls=%fused_computation.40 | loop fusion | flops 1310720 | bytes 3276980 | tf_op jit(solution)/shard_map/jit(_where)/select_n | solution.py:167
  (110 shorter events, 22.4 us)
Async XLA Ops:
  7.2 44.1 %copy-start.2 = (bf16[5,32,1024]{2,1,0:T(8,128)(2,1)S(1)}, bf16[5,32,1024]{2,1,0:T(8,128)(2,1)}, u32[]{:S(2)}) copy-start(bf16[5,32,1024]{2,1,0:T(8,128)(2,1)} %param.5) | copy-start | bytes 983044
  7.2 62.0 %all-gather.3.cloned.1.call-start = ((), (), s32[]{:S(2)}) async-start(), calls=%async_computation.2 | async-start | bytes 5570560 | tf_op jit(solution)/shard_map/all_gather | solution.py:103
  7.9 194.6 %reduce-scatter.2.cloned.1.call-start = ((), (), s32[]{:S(2)}) async-start(), calls=%async_computation.1 | async-start | bytes 11141120 | tf_op jit(solution)/shard_map/reduce_scatter | solution.py:149
  8.0 18.0 %collective-permute-start.4 = (bf16[5,32,1024]{2,1,0:T(8,128)(2,1)}, bf16[5,32,1024]{2,1,0:T(8,128)(2,1)S(1)}, u32[]{:S(2)}, u32[]{:S(2)}) collective-permute-start(bf16[5,32,1024]{2,1,0:T(8,128)(2,1)} %param.5), channel_id=1, source_target_pairs={{0,112},{16,0},{32,16},{48,32},{64,48},{80,64},{96,80},{112,96},{1... | collective-permute-start | bytes 983048 | tf_op jit(solution)/shard_map/ppermute | solution.py:56
  10.2 7.9 %collective-permute-start = (bf16[5,32,1024]{2,1,0:T(8,128)(2,1)}, bf16[5,32,1024]{2,1,0:T(8,128)(2,1)S(1)}, u32[]{:S(2)}, u32[]{:S(2)}) collective-permute-start(bf16[5,32,1024]{2,1,0:T(8,128)(2,1)} %param.5), channel_id=1, source_target_pairs={{0,16},{16,32},{32,48},{48,64},{64,80},{80,96},{96,112},{112,0},{1... | collective-permute-start | bytes 983048 | tf_op jit(solution)/shard_map/ppermute | solution.py:53
  18.2 7.7 %collective-permute-start.1 = (bf16[5,32,1024]{2,1,0:T(8,128)(2,1)S(1)}, bf16[5,32,1024]{2,1,0:T(8,128)(2,1)S(1)}, u32[]{:S(2)}, u32[]{:S(2)}) collective-permute-start(bf16[5,32,1024]{2,1,0:T(8,128)(2,1)S(1)} %collective-permute-done), channel_id=1, source_target_pairs={{0,16},{16,32},{32,48},{48,64},{64,80},{80,96},{96,112},{112,0},{1... | collective-permute-start | bytes 983048 | tf_op jit(solution)/shard_map/ppermute | solution.py:53
  25.9 7.7 %collective-permute-start.2 = (bf16[5,32,1024]{2,1,0:T(8,128)(2,1)S(1)}, bf16[5,32,1024]{2,1,0:T(8,128)(2,1)S(1)}, u32[]{:S(2)}, u32[]{:S(2)}) collective-permute-start(bf16[5,32,1024]{2,1,0:T(8,128)(2,1)S(1)} %collective-permute-done.1), channel_id=1, source_target_pairs={{0,16},{16,32},{32,48},{48,64},{64,80},{80,96},{96,112},{112,0},{1... | collective-permute-start | bytes 983048 | tf_op jit(solution)/shard_map/ppermute | solution.py:53
  26.0 8.4 %collective-permute-start.5 = (bf16[5,32,1024]{2,1,0:T(8,128)(2,1)S(1)}, bf16[5,32,1024]{2,1,0:T(8,128)(2,1)S(1)}, u32[]{:S(2)}, u32[]{:S(2)}) collective-permute-start(bf16[5,32,1024]{2,1,0:T(8,128)(2,1)S(1)} %collective-permute-done.4), channel_id=1, source_target_pairs={{0,112},{16,0},{32,16},{48,32},{64,48},{80,64},{96,80},{112,96},{1... | collective-permute-start | bytes 983048 | tf_op jit(solution)/shard_map/ppermute | solution.py:56
  33.6 7.7 %collective-permute-start.3 = (bf16[5,32,1024]{2,1,0:T(8,128)(2,1)S(1)}, bf16[5,32,1024]{2,1,0:T(8,128)(2,1)S(1)}, u32[]{:S(2)}, u32[]{:S(2)}) collective-permute-start(bf16[5,32,1024]{2,1,0:T(8,128)(2,1)S(1)} %collective-permute-done.2), channel_id=1, source_target_pairs={{0,16},{16,32},{32,48},{48,64},{64,80},{80,96},{96,112},{112,0},{1... | collective-permute-start | bytes 983048 | tf_op jit(solution)/shard_map/ppermute | solution.py:53
  34.3 13.2 %collective-permute-start.6 = (bf16[5,32,1024]{2,1,0:T(8,128)(2,1)S(1)}, bf16[5,32,1024]{2,1,0:T(8,128)(2,1)S(1)}, u32[]{:S(2)}, u32[]{:S(2)}) collective-permute-start(bf16[5,32,1024]{2,1,0:T(8,128)(2,1)S(1)} %collective-permute-done.5), channel_id=1, source_target_pairs={{0,112},{16,0},{32,16},{48,32},{64,48},{80,64},{96,80},{112,96},{1... | collective-permute-start | bytes 983048 | tf_op jit(solution)/shard_map/ppermute | solution.py:56
  73.8 22.1 %copy-start.8 = (s32[5]{0:T(128)S(1)}, s32[5]{0:T(128)}, u32[]{:S(2)}) copy-start(s32[5]{0:T(128)} %param.6) | copy-start | bytes 64
  75.1 1.7 collective-permute-start.7
  76.9 3.8 %collective-permute-start.8 = (f32[2,5,256]{2,1,0:T(8,128)S(1)}, f32[2,5,256]{2,1,0:T(8,128)S(1)}, u32[]{:S(2)}, u32[]{:S(2)}) collective-permute-start(f32[2,5,256]{2,1,0:T(8,128)S(1)} %pad_maximum_fusion.9), channel_id=1, source_target_pairs={{0,32},{16,48},{32,0},{48,16},{64,96},{80,112},{96,64},{112,80},{1... | collective-permute-start | bytes 30728 | tf_op jit(solution)/shard_map/ppermute | solution.py:21
  78.5 4.1 %collective-permute-start.14 = (f32[3,5,512]{2,0,1:T(4,128)S(1)}, f32[3,5,512]{2,0,1:T(4,128)S(1)}, u32[]{:S(2)}, u32[]{:S(2)}) collective-permute-start(f32[3,5,512]{2,0,1:T(4,128)S(1)} %pad_maximum_fusion.4), channel_id=1, source_target_pairs={{0,1},{1,0},{2,3},{3,2},{4,5},{5,4},{6,7},{7,6},{8,9},{9,8},{10,11... | collective-permute-start | bytes 92168 | tf_op jit(solution)/shard_map/ppermute | solution.py:21
  82.7 5.8 %collective-permute-start.15 = (f32[3,5,512]{2,0,1:T(4,128)S(1)}, f32[3,5,512]{2,0,1:T(4,128)S(1)}, u32[]{:S(2)}, u32[]{:S(2)}) collective-permute-start(f32[3,5,512]{2,0,1:T(4,128)S(1)} %pad_maximum_fusion.5), channel_id=1, source_target_pairs={{0,2},{1,3},{2,0},{3,1},{4,6},{5,7},{6,4},{7,5},{8,10},{9,11},{10,... | collective-permute-start | bytes 92168 | tf_op jit(solution)/shard_map/ppermute | solution.py:21
  85.8 5.2 %collective-permute-start.9 = (f32[2,5,256]{2,1,0:T(8,128)S(1)}, f32[2,5,256]{2,1,0:T(8,128)S(1)}, u32[]{:S(2)}, u32[]{:S(2)}) collective-permute-start(f32[2,5,256]{2,1,0:T(8,128)S(1)} %pad_maximum_fusion.10), channel_id=1, source_target_pairs={{0,64},{16,80},{32,96},{48,112},{64,0},{80,16},{96,32},{112,48},{1... | collective-permute-start | bytes 30728 | tf_op jit(solution)/shard_map/ppermute | solution.py:21
  88.6 4.1 %collective-permute-start.16 = (f32[3,5,512]{2,0,1:T(4,128)S(1)}, f32[3,5,512]{2,0,1:T(4,128)S(1)}, u32[]{:S(2)}, u32[]{:S(2)}) collective-permute-start(f32[3,5,512]{2,0,1:T(4,128)S(1)} %pad_maximum_fusion.6), channel_id=1, source_target_pairs={{0,4},{1,5},{2,6},{3,7},{4,0},{5,1},{6,2},{7,3},{8,12},{9,13},{10,... | collective-permute-start | bytes 92168 | tf_op jit(solution)/shard_map/ppermute | solution.py:21
  92.9 5.8 %collective-permute-start.17 = (f32[3,5,512]{2,0,1:T(4,128)S(1)}, f32[3,5,512]{2,0,1:T(4,128)S(1)}, u32[]{:S(2)}, u32[]{:S(2)}) collective-permute-start(f32[3,5,512]{2,0,1:T(4,128)S(1)} %pad_maximum_fusion.7), channel_id=1, source_target_pairs={{0,8},{1,9},{2,10},{3,11},{4,12},{5,13},{6,14},{7,15},{8,0},{9,1},... | collective-permute-start | bytes 92168 | tf_op jit(solution)/shard_map/ppermute | solution.py:21
  101.3 0.9 copy-start.3
  101.3 1.1 copy-start.4
  104.0 1.1 copy-start.6
  113.5 1.5 copy-start.7
  119.0 2.4 %copy-start = (f32[5,256,1024]{2,1,0:T(8,128)}, f32[5,256,1024]{2,1,0:T(8,128)S(1)}, u32[]{:S(2)}) copy-start(f32[5,256,1024]{2,1,0:T(8,128)S(1)} %bitcast_multiply_fusion) | copy-start | bytes 15728644
  121.4 5.1 %collective-permute-start.18 = (f32[648,1024]{1,0:T(8,128)S(1)}, f32[648,1024]{1,0:T(8,128)}, u32[]{:S(2)}, u32[]{:S(2)}) collective-permute-start(f32[648,1024]{1,0:T(8,128)S(1)} %maximum_maximum_fusion), channel_id=1, source_target_pairs={{0,16},{16,0},{32,48},{48,32},{64,80},{80,64},{96,112},{112,96},{1... | collective-permute-start | bytes 7962632 | tf_op jit(solution)/shard_map/ppermute | solution.py:71
  121.4 7.2 %copy-start.1 = (f32[5,256,1024]{2,1,0:T(8,128)S(1)}, f32[5,256,1024]{2,1,0:T(8,128)}, u32[]{:S(2)}) copy-start(f32[5,256,1024]{2,1,0:T(8,128)} %copy-done) | copy-start | bytes 15728644
  129.5 72.9 %copy-start.5 = (bf16[5,32,1024]{2,1,0:T(8,128)(2,1)S(1)}, bf16[5,32,1024]{2,1,0:T(8,128)(2,1)}, u32[]{:S(2)}) copy-start(bf16[5,32,1024]{2,1,0:T(8,128)(2,1)} %param.4) | copy-start | bytes 983044
  130.4 18.8 %collective-permute-start.19 = (f32[168,1024]{1,0:T(8,128)S(1)}, f32[168,1024]{1,0:T(8,128)S(1)}, u32[]{:S(2)}, u32[]{:S(2)}) collective-permute-start(f32[168,1024]{1,0:T(8,128)S(1)} %pad_maximum_fusion.3), channel_id=1, source_target_pairs={{0,32},{16,48},{32,64},{48,80},{64,96},{80,112},{96,0},{112,16},{1... | collective-permute-start | bytes 2064392 | tf_op jit(solution)/shard_map/ppermute | solution.py:84
  149.3 18.0 %collective-permute-start.20 = (f32[168,1024]{1,0:T(8,128)S(1)}, f32[168,1024]{1,0:T(8,128)S(1)}, u32[]{:S(2)}, u32[]{:S(2)}) collective-permute-start(f32[168,1024]{1,0:T(8,128)S(1)} %fusion.24), channel_id=1, source_target_pairs={{0,32},{16,48},{32,64},{48,80},{64,96},{80,112},{96,0},{112,16},{1... | collective-permute-start | bytes 2064392 | tf_op jit(solution)/shard_map/ppermute | solution.py:84
  167.4 17.1 %collective-permute-start.21 = (f32[168,1024]{1,0:T(8,128)S(1)}, f32[168,1024]{1,0:T(8,128)S(1)}, u32[]{:S(2)}, u32[]{:S(2)}) collective-permute-start(f32[168,1024]{1,0:T(8,128)S(1)} %fusion.25), channel_id=1, source_target_pairs={{0,32},{16,48},{32,64},{48,80},{64,96},{80,112},{96,0},{112,16},{1... | collective-permute-start | bytes 2064392 | tf_op jit(solution)/shard_map/ppermute | solution.py:84
  167.5 3.6 %collective-permute-start.10 = (f32[5]{0:T(128)S(1)}, f32[5]{0:T(128)S(1)}, u32[]{:S(2)}, u32[]{:S(2)}) collective-permute-start(f32[5]{0:T(128)S(1)} %get-tuple-element.5), channel_id=1, source_target_pairs={{0,1},{1,0},{2,3},{3,2},{4,5},{5,4},{6,7},{7,6},{8,9},{9,8},{10,11... | collective-permute-start | bytes 68 | tf_op jit(solution)/shard_map/ppermute | solution.py:32
  171.1 5.0 %collective-permute-start.11 = (f32[5]{0:T(128)S(1)}, f32[5]{0:T(128)S(1)}, u32[]{:S(2)}, u32[]{:S(2)}) collective-permute-start(f32[5]{0:T(128)S(1)} %fusion.61), channel_id=1, source_target_pairs={{0,2},{1,3},{2,0},{3,1},{4,6},{5,7},{6,4},{7,5},{8,10},{9,11},{10,... | collective-permute-start | bytes 68 | tf_op jit(solution)/shard_map/ppermute | solution.py:32
  176.1 3.5 %collective-permute-start.12 = (f32[5]{0:T(128)S(1)}, f32[5]{0:T(128)S(1)}, u32[]{:S(2)}, u32[]{:S(2)}) collective-permute-start(f32[5]{0:T(128)S(1)} %fusion.60), channel_id=1, source_target_pairs={{0,4},{1,5},{2,6},{3,7},{4,0},{5,1},{6,2},{7,3},{8,12},{9,13},{10,... | collective-permute-start | bytes 68 | tf_op jit(solution)/shard_map/ppermute | solution.py:32
  179.7 5.2 %collective-permute-start.13 = (f32[5]{0:T(128)S(1)}, f32[5]{0:T(128)S(1)}, u32[]{:S(2)}, u32[]{:S(2)}) collective-permute-start(f32[5]{0:T(128)S(1)} %fusion.59), channel_id=1, source_target_pairs={{0,8},{1,9},{2,10},{3,11},{4,12},{5,13},{6,14},{7,15},{8,0},{9,1},... | collective-permute-start | bytes 68 | tf_op jit(solution)/shard_map/ppermute | solution.py:32
Sparse Core Ops, SparseCore 0:
  10.1 58.9 all-gather.2
  113.6 88.8 reduce-scatter.1

commit v12 on v6

--- a/solution.py
+++ b/solution.py
@@ -14,13 +14,14 @@
     return jnp.concatenate([highest[None], summed[None], mine[2:] + other[2:]], axis=0)
 
 
-def butterfly_merge(stats, axis, size):
+def butterfly_merge(stats, axis, size, bit=1, other=None):
     own = lax.axis_index(axis)
-    bit = 1
     while bit < size:
-        other = lax.ppermute(stats, axis, [(i, i ^ bit) for i in range(size)])
+        if other is None:
+            other = lax.ppermute(stats, axis, [(i, i ^ bit) for i in range(size)])
         lower = (own & bit) == 0
         stats = merge_pair(jnp.where(lower, stats, other), jnp.where(lower, other, stats))
+        other = None
         bit *= 2
     return stats
 
@@ -122,16 +123,19 @@
     col_high = jnp.max(masked, axis=1)
     col_sum = jnp.sum(jnp.where(inside, jnp.exp(masked - col_high[:, None, :]), 0.0), axis=1)
 
-    col_stats = butterfly_merge(jnp.stack([col_high, col_sum]), "dp", dp_size)
-    col_high, col_sum = col_stats[0], col_stats[1]
-    col_lse = jnp.where(col_valid, col_high + jnp.log(jnp.where(col_valid, col_sum, 1.0)), 0.0)
-
     lanes = jnp.arange(row_count, dtype=jnp.int32)[None, :]
     carried = jnp.where(lanes == 0, own_positive[:, None], 0.0)
-    row_stats = butterfly_merge(jnp.stack([row_high, row_sum, carried]), "pair", pair_size)
+    row_stats = jnp.stack([row_high, row_sum, carried])
+    row_first = lax.ppermute(row_stats, "pair", [(i, i ^ 1) for i in range(pair_size)])
+    col_stats, row_first = lax.optimization_barrier((jnp.stack([col_high, col_sum]), row_first))
+    row_stats = butterfly_merge(row_stats, "pair", pair_size, 1, row_first)
     row_high, row_sum, carried = row_stats[0], row_stats[1], row_stats[2]
     row_lse = jnp.where(row_valid, row_high + jnp.log(jnp.where(row_valid, row_sum, 1.0)), 0.0)
     row_part = jnp.sum(row_lse, axis=1) - 2.0 * carried[:, 0]
+
+    col_stats = butterfly_merge(col_stats, "dp", dp_size)
+    col_high, col_sum = col_stats[0], col_stats[1]
+    col_lse = jnp.where(col_valid, col_high + jnp.log(jnp.where(col_valid, col_sum, 1.0)), 0.0)
 
     prob_row = jnp.where(inside, jnp.exp(scores - row_lse[:, :, None]), 0.0)
     prob_col = jnp.where(inside, jnp.exp(scores - col_lse[:, None, :]), 0.0)

time: 211 us -> 211 us (level)
    ppermute x0 -> x1, waiting for transfers between devices: none -> 2.51 us  [per_device(): lax.ppermute(row_stats, 'pair', [(i, i ^ 1) for i in range(pair_size)])]
    ppermute x7 -> x6, waiting for transfers between devices: 8.7 us -> 6.44 us  [butterfly_merge(): other = lax.ppermute(stats, axis, [(i, i ^ bit) for i in range(size)])]
    ppermute x7 -> x6, starting transfers between devices: 13 us -> 11.2 us  [butterfly_merge(): other = lax.ppermute(stats, axis, [(i, i ^ bit) for i in range(size)])]
    unnamed x29 -> x27, local copies, waits for them, and re-layouts: 15.7 us -> 15.9 us
  transfers between devices with their start and end apart: 24 -> 24, of which waited for: 20 -> 19; matrix products, arithmetic and copies ran while one was open for 13% -> 13% of each run, Pallas kernels for 0% -> 0%
where the time goes in v12:
time: 211 us
  waiting for transfers between devices  112 us (53%)
  starting transfers between devices  30.1 us (14%)
  local copies, waits for them, and re-layouts  20.3 us (10%)
  matrix products  16.5 us (8%)
  between operations  16.2 us (8%)
  other arithmetic  15.5 us (7%)
    ppermute x3, waiting for transfers between devices, two_stage_reduce_scatter(): running = lax.ppermute(running, axis, ring) + addend(chip - 1 - step)  38.8 us
    reduce_scatter x1, waiting for transfers between devices, per_device(): lax.psum_scatter(grad_rows, 'pair', scatter_dimension=1, tiled=True)  17.7 us
    all_gather x1, waiting for transfers between devices, per_device(): row_set = lax.all_gather(anchor, 'pair', axis=1, tiled=True)  16.8 us
    unnamed x27, local copies, waits for them, and re-layouts  15.9 us
    ppermute x4, waiting for transfers between devices, ring_gather(): ahead = lax.ppermute(ahead, axis, forward)  15.6 us
    ppermute x6, starting transfers between devices, butterfly_merge(): other = lax.ppermute(stats, axis, [(i, i ^ bit) for i in range(size)])  11.2 us
    ppermute x3, starting transfers between devices, ring_gather(): behind = lax.ppermute(behind, axis, backward)  9.41 us
    ppermute x4, starting transfers between devices, butterfly_sum(): other = lax.ppermute(values, axis, [(i, i ^ bit) for i in range(size)])  7.41 us
  transfers between devices with their start and end apart: 24, of which 19 were waited for; matrix products, arithmetic and copies ran while one was open for 13% of the time, Pallas kernels for 0%

profile of v12, /device:TPU:0, one launch (start us, length us, event | category | flops | bytes accessed | tf_op | source)
XLA Modules:
  0.0 210.9 jit_solution(1005704290587100007)
XLA Ops:
  8.0 2.9 %collective-permute-start.4 = (bf16[5,32,1024]{2,1,0:T(8,128)(2,1)}, bf16[5,32,1024]{2,1,0:T(8,128)(2,1)S(1)}, u32[]{:S(2)}, u32[]{:S(2)}) collective-permute-start(bf16[5,32,1024]{2,1,0:T(8,128)(2,1)} %param.5), channel_id=1, source_target_pairs={{0,112},{16,0},{32,16},{48,32},{64,48},{80,64},{96,80},{112,96},{1... | collective-permute-start | bytes 983048 | tf_op jit(solution)/shard_map/ppermute | solution.py:57
  11.1 0.8 broadcast_compare_fusion
  12.0 1.2 fusion.17
  13.3 2.6 %collective-permute-done = bf16[5,32,1024]{2,1,0:T(8,128)(2,1)S(1)} collective-permute-done((bf16[5,32,1024]{2,1,0:T(8,128)(2,1)}, bf16[5,32,1024]{2,1,0:T(8,128)(2,1)S(1)}, u32[]{:S(2)}, u32[]{:S(2)}) %collective-permute-start) | collective-permute-done | bytes 327712 | tf_op jit(solution)/shard_map/ppermute | solution.py:54
  16.6 7.0 %collective-permute-done.1 = bf16[5,32,1024]{2,1,0:T(8,128)(2,1)S(1)} collective-permute-done((bf16[5,32,1024]{2,1,0:T(8,128)(2,1)S(1)}, bf16[5,32,1024]{2,1,0:T(8,128)(2,1)S(1)}, u32[]{:S(2)}, u32[]{:S(2)}) %collective-permute-start.1) | collective-permute-done | bytes 327712 | tf_op jit(solution)/shard_map/ppermute | solution.py:54
  23.6 0.8 select_reduce_fusion.1
  25.2 3.0 %collective-permute-start.5 = (bf16[5,32,1024]{2,1,0:T(8,128)(2,1)S(1)}, bf16[5,32,1024]{2,1,0:T(8,128)(2,1)S(1)}, u32[]{:S(2)}, u32[]{:S(2)}) collective-permute-start(bf16[5,32,1024]{2,1,0:T(8,128)(2,1)S(1)} %collective-permute-done.4), channel_id=1, source_target_pairs={{0,112},{16,0},{32,16},{48,32},{64,48},{80,64},{96,80},{112,96},{1... | collective-permute-start | bytes 983048 | tf_op jit(solution)/shard_map/ppermute | solution.py:57
  28.1 3.2 %collective-permute-done.2 = bf16[5,32,1024]{2,1,0:T(8,128)(2,1)S(1)} collective-permute-done((bf16[5,32,1024]{2,1,0:T(8,128)(2,1)S(1)}, bf16[5,32,1024]{2,1,0:T(8,128)(2,1)S(1)}, u32[]{:S(2)}, u32[]{:S(2)}) %collective-permute-start.2) | collective-permute-done | bytes 327712 | tf_op jit(solution)/shard_map/ppermute | solution.py:54
  31.4 1.3 collective-permute-done.5
  32.7 3.5 %collective-permute-start.6 = (bf16[5,32,1024]{2,1,0:T(8,128)(2,1)S(1)}, bf16[5,32,1024]{2,1,0:T(8,128)(2,1)S(1)}, u32[]{:S(2)}, u32[]{:S(2)}) collective-permute-start(bf16[5,32,1024]{2,1,0:T(8,128)(2,1)S(1)} %collective-permute-done.5), channel_id=1, source_target_pairs={{0,112},{16,0},{32,16},{48,32},{64,48},{80,64},{96,80},{112,96},{1... | collective-permute-start | bytes 983048 | tf_op jit(solution)/shard_map/ppermute | solution.py:57
  36.2 2.8 %collective-permute-done.3 = bf16[5,32,1024]{2,1,0:T(8,128)(2,1)S(1)} collective-permute-done((bf16[5,32,1024]{2,1,0:T(8,128)(2,1)S(1)}, bf16[5,32,1024]{2,1,0:T(8,128)(2,1)S(1)}, u32[]{:S(2)}, u32[]{:S(2)}) %collective-permute-start.3) | collective-permute-done | bytes 327712 | tf_op jit(solution)/shard_map/ppermute | solution.py:54
  42.1 1.7 constant_dynamic-update-slice_fusion.11
  46.1 0.8 constant_dynamic-update-slice_fusion.7
  51.5 0.8 constant_dynamic-update-slice_fusion
  52.3 16.8 %all-gather.2.cloned.1.call-done = bf16[5,512,1024]{2,1,0:T(8,128)(2,1)} async-done(((bf16[5,32,1024]{2,1,0:T(8,128)(2,1)}), bf16[5,512,1024]{2,1,0:T(8,128)(2,1)}) %all-gather.2.cloned.1.call-update) | async-done | bytes 5242896 | tf_op jit(solution)/shard_map/all_gather | solution.py:104
  69.1 5.2 %fusion.10 = (f32[5,512]{1,0:T(8,128)S(1)}, f32[5,256]{1,0:T(8,128)S(1)}, f32[5,256,512]{2,1,0:T(8,128)S(1)}) fusion(pred[5,256]{1,0:T(8,128)(4,1)S(1)} %broadcast_compare_fusion.1, pred[5,512]{1,0:T(8,128)(4,1)S(1)} %copy.20, bf16[5,512,1024]{2,1,0:T(8,128)(2,1)} %all-gather.2.cloned.1.call-done, ...), kind=kOutput, calls=%fused_computation.25 | convolution fusion | flops 1345450240 | bytes 10504964 | tf_op jit(solution)/shard_map/prd,pcd->prc/dot_general | solution.py:117
  74.3 1.5 copy-done.2
  75.8 1.9 fusion.1
  77.8 1.6 collective-permute-start.7
  79.4 2.5 %collective-permute-done.7 = f32[3,5,512]{2,0,1:T(4,128)S(1)} collective-permute-done((f32[3,5,512]{2,0,1:T(4,128)S(1)}, f32[3,5,512]{2,0,1:T(4,128)S(1)}, u32[]{:S(2)}, u32[]{:S(2)}) %collective-permute-start.7) | collective-permute-done | bytes 30752 | tf_op jit(solution)/shard_map/ppermute | solution.py:129
  82.0 1.1 collective-permute-done.8
  83.1 1.5 collective-permute-start.9
  84.7 3.1 %collective-permute-start.15 = (f32[3,5,512]{2,0,1:T(4,128)S(1)}, f32[3,5,512]{2,0,1:T(4,128)S(1)}, u32[]{:S(2)}, u32[]{:S(2)}) collective-permute-start(f32[3,5,512]{2,0,1:T(4,128)S(1)} %pad_maximum_fusion.5), channel_id=1, source_target_pairs={{0,2},{1,3},{2,0},{3,1},{4,6},{5,7},{6,4},{7,5},{8,10},{9,11},{10,... | collective-permute-start | bytes 92168 | tf_op jit(solution)/shard_map/ppermute | solution.py:21
  87.8 2.8 %collective-permute-start.10 = (f32[2,5,256]{2,1,0:T(8,128)S(1)}, f32[2,5,256]{2,1,0:T(8,128)S(1)}, u32[]{:S(2)}, u32[]{:S(2)}) collective-permute-start(f32[2,5,256]{2,1,0:T(8,128)S(1)} %pad_maximum_fusion.10), channel_id=1, source_target_pairs={{0,64},{16,80},{32,96},{48,112},{64,0},{80,16},{96,32},{112,48},{1... | collective-permute-start | bytes 30728 | tf_op jit(solution)/shard_map/ppermute | solution.py:21
  90.8 1.1 collective-permute-start.16
  91.9 1.3 collective-permute-done.10
  93.2 1.7 collective-permute-done.16
  95.0 2.7 %collective-permute-start.17 = (f32[3,5,512]{2,0,1:T(4,128)S(1)}, f32[3,5,512]{2,0,1:T(4,128)S(1)}, u32[]{:S(2)}, u32[]{:S(2)}) collective-permute-start(f32[3,5,512]{2,0,1:T(4,128)S(1)} %pad_maximum_fusion.7), channel_id=1, source_target_pairs={{0,8},{1,9},{2,10},{3,11},{4,12},{5,13},{6,14},{7,15},{8,0},{9,1},... | collective-permute-start | bytes 92168 | tf_op jit(solution)/shard_map/ppermute | solution.py:21
  98.2 2.4 %collective-permute-done.17 = f32[3,5,512]{2,0,1:T(4,128)S(1)} collective-permute-done((f32[3,5,512]{2,0,1:T(4,128)S(1)}, f32[3,5,512]{2,0,1:T(4,128)S(1)}, u32[]{:S(2)}, u32[]{:S(2)}) %collective-permute-start.17) | collective-permute-done | bytes 30752 | tf_op jit(solution)/shard_map/ppermute | solution.py:21
  101.3 2.7 %fusion.4 = bf16[5,512,256]{1,2,0:T(8,128)(2,1)S(1)} fusion(f32[5,256,512]{2,1,0:T(8,128)} %copy-done.2, f32[5,256]{1,0:T(8,128)S(1)} %get-tuple-element.12, f32[5,512]{1,0:T(8,128)S(1)} %copy.27, f32[5]{0:T(128)S(1)} %get-tuple-element.49, pred[5,256]{1,0:T(8,128)(4,1)S(1)} %broadcast_compare_fusion.1, pred[5,512]{1,0:T(8,128)(4,1)S(1)} %copy.20), kind=kLoop, calls=%fused_computation.11 | loop fusion | flops 5898240 | bytes 3951380 | tf_op jit(solution)/shard_map/convert_element_type | solution.py:142
  104.0 7.3 %broadcast_multiply_fusion = f32[5,512,1024]{2,1,0:T(8,128)} fusion(bf16[5,512,256]{1,2,0:T(8,128)(2,1)S(1)} %fusion.4, bf16[5,512,1024]{2,1,0:T(8,128)(2,1)} %constant_dynamic-update-slice_fusion, s32[]{:T(128)S(6)} %select_n.255), kind=kOutput, calls=%fused_computation.5 | convolution fusion | flops 1344798720 | bytes 14417924 | tf_op jit(solution)/shard_map/prc,pcd->prd/dot_general | solution.py:145
  111.6 4.0 %broadcast_multiply_fusion.1 = f32[5,256,1024]{2,1,0:T(8,128)S(1)} fusion(bf16[5,512,256]{1,2,0:T(8,128)(2,1)S(1)} %fusion.4, bf16[5,512,1024]{2,1,0:T(8,128)(2,1)} %all-gather.2.cloned.1.call-done), kind=kOutput, calls=%fused_computation.17 | convolution fusion | flops 1343488000 | bytes 11796480 | tf_op jit(solution)/shard_map/prc,prd->pcd/dot_general | solution.py:149
  116.1 1.9 copy-done
  118.0 5.1 %collective-permute-done.18 = f32[648,1024]{1,0:T(8,128)} collective-permute-done((f32[648,1024]{1,0:T(8,128)S(1)}, f32[648,1024]{1,0:T(8,128)}, u32[]{:S(2)}, u32[]{:S(2)}) %collective-permute-start.18) | collective-permute-done | bytes 2654240 | tf_op jit(solution)/shard_map/ppermute | solution.py:72
  123.1 2.1 slice.218
  126.1 0.8 slice_add_fusion.1
  127.3 18.4 %collective-permute-done.19 = f32[168,1024]{1,0:T(8,128)S(1)} collective-permute-done((f32[168,1024]{1,0:T(8,128)S(1)}, f32[168,1024]{1,0:T(8,128)S(1)}, u32[]{:S(2)}, u32[]{:S(2)}) %collective-permute-start.19) | collective-permute-done | bytes 688160 | tf_op jit(solution)/shard_map/ppermute | solution.py:85
  145.9 17.9 %collective-permute-done.20 = f32[168,1024]{1,0:T(8,128)S(1)} collective-permute-done((f32[168,1024]{1,0:T(8,128)S(1)}, f32[168,1024]{1,0:T(8,128)S(1)}, u32[]{:S(2)}, u32[]{:S(2)}) %collective-permute-start.20) | collective-permute-done | bytes 688160 | tf_op jit(solution)/shard_map/ppermute | solution.py:85
  164.1 1.2 collective-permute-start.11
  165.3 2.4 %collective-permute-done.11 = f32[5]{0:T(128)S(1)} collective-permute-done((f32[5]{0:T(128)S(1)}, f32[5]{0:T(128)S(1)}, u32[]{:S(2)}, u32[]{:S(2)}) %collective-permute-start.11) | collective-permute-done | bytes 52 | tf_op jit(solution)/shard_map/ppermute | solution.py:33
  167.7 2.7 %collective-permute-start.12 = (f32[5]{0:T(128)S(1)}, f32[5]{0:T(128)S(1)}, u32[]{:S(2)}, u32[]{:S(2)}) collective-permute-start(f32[5]{0:T(128)S(1)} %fusion.49), channel_id=1, source_target_pairs={{0,2},{1,3},{2,0},{3,1},{4,6},{5,7},{6,4},{7,5},{8,10},{9,11},{10,... | collective-permute-start | bytes 68 | tf_op jit(solution)/shard_map/ppermute | solution.py:33
  170.4 2.3 %collective-permute-done.12 = f32[5]{0:T(128)S(1)} collective-permute-done((f32[5]{0:T(128)S(1)}, f32[5]{0:T(128)S(1)}, u32[]{:S(2)}, u32[]{:S(2)}) %collective-permute-start.12) | collective-permute-done | bytes 52 | tf_op jit(solution)/shard_map/ppermute | solution.py:33
  172.7 1.0 collective-permute-start.13
  173.8 2.5 %collective-permute-done.13 = f32[5]{0:T(128)S(1)} collective-permute-done((f32[5]{0:T(128)S(1)}, f32[5]{0:T(128)S(1)}, u32[]{:S(2)}, u32[]{:S(2)}) %collective-permute-start.13) | collective-permute-done | bytes 52 | tf_op jit(solution)/shard_map/ppermute | solution.py:33
  176.3 2.5 %collective-permute-start.14 = (f32[5]{0:T(128)S(1)}, f32[5]{0:T(128)S(1)}, u32[]{:S(2)}, u32[]{:S(2)}) collective-permute-start(f32[5]{0:T(128)S(1)} %fusion.47), channel_id=1, source_target_pairs={{0,8},{1,9},{2,10},{3,11},{4,12},{5,13},{6,14},{7,15},{8,0},{9,1},... | collective-permute-start | bytes 68 | tf_op jit(solution)/shard_map/ppermute | solution.py:33
  178.8 2.4 %collective-permute-done.21 = f32[168,1024]{1,0:T(8,128)S(1)} collective-permute-done((f32[168,1024]{1,0:T(8,128)S(1)}, f32[168,1024]{1,0:T(8,128)S(1)}, u32[]{:S(2)}, u32[]{:S(2)}) %collective-permute-start.21) | collective-permute-done | bytes 688160 | tf_op jit(solution)/shard_map/ppermute | solution.py:85
  182.8 17.7 %reduce-scatter.2.cloned.1.call-done = f32[5,32,1024]{2,1,0:T(8,128)} async-done(((f32[5,512,1024]{2,1,0:T(8,128)}), f32[5,32,1024]{2,1,0:T(8,128)}) %reduce-scatter.2.cloned.1.call-update) | async-done | bytes 655376 | tf_op jit(solution)/shard_map/reduce_scatter | solution.py:152
  200.6 2.4 %fusion.16 = (f32[5,32,1024]{2,1,0:T(8,128)}, f32[5,32,1024]{2,1,0:T(8,128)}) fusion(f32[5,32,1024]{2,1,0:T(8,128)S(1)} %bitcast.117, bf16[5,32,1024]{2,1,0:T(8,128)(2,1)S(1)} %copy-done.4, f32[5]{0:T(128)S(1)} %get-tuple-element.48, pred[5,32]{1,0:T(8,128)(4,1)S(1)} %broadcast_compare_fusion.2, f32[5,32,1024]{2,1,0:T(8,128)} %reduce-scatter.2.cloned.1.call-done, ...), kind=kLoop, calls=%fused_computation.34 | loop fusion | flops 1310720 | bytes 3276980 | tf_op jit(solution)/shard_map/jit(_where)/select_n | solution.py:168
  (100 shorter events, 17.6 us)
Async XLA Ops:
  7.2 42.0 %copy-start.3 = (bf16[5,32,1024]{2,1,0:T(8,128)(2,1)S(1)}, bf16[5,32,1024]{2,1,0:T(8,128)(2,1)}, u32[]{:S(2)}) copy-start(bf16[5,32,1024]{2,1,0:T(8,128)(2,1)} %param.5) | copy-start | bytes 983044
  7.2 61.9 %all-gather.2.cloned.1.call-start = ((), (), s32[]{:S(2)}) async-start(), calls=%async_computation.1 | async-start | bytes 5570560 | tf_op jit(solution)/shard_map/all_gather | solution.py:104
  7.9 192.6 %reduce-scatter.2.cloned.1.call-start = ((), (), s32[]{:S(2)}) async-start(), calls=%async_computation.2 | async-start | bytes 11141120 | tf_op jit(solution)/shard_map/reduce_scatter | solution.py:152
  8.0 7.9 %collective-permute-start = (bf16[5,32,1024]{2,1,0:T(8,128)(2,1)}, bf16[5,32,1024]{2,1,0:T(8,128)(2,1)S(1)}, u32[]{:S(2)}, u32[]{:S(2)}) collective-permute-start(bf16[5,32,1024]{2,1,0:T(8,128)(2,1)} %param.5), channel_id=1, source_target_pairs={{0,16},{16,32},{32,48},{48,64},{64,80},{80,96},{96,112},{112,0},{1... | collective-permute-start | bytes 983048 | tf_op jit(solution)/shard_map/ppermute | solution.py:54
  8.0 17.2 %collective-permute-start.4 = (bf16[5,32,1024]{2,1,0:T(8,128)(2,1)}, bf16[5,32,1024]{2,1,0:T(8,128)(2,1)S(1)}, u32[]{:S(2)}, u32[]{:S(2)}) collective-permute-start(bf16[5,32,1024]{2,1,0:T(8,128)(2,1)} %param.5), channel_id=1, source_target_pairs={{0,112},{16,0},{32,16},{48,32},{64,48},{80,64},{96,80},{112,96},{1... | collective-permute-start | bytes 983048 | tf_op jit(solution)/shard_map/ppermute | solution.py:57
  15.9 7.7 %collective-permute-start.1 = (bf16[5,32,1024]{2,1,0:T(8,128)(2,1)S(1)}, bf16[5,32,1024]{2,1,0:T(8,128)(2,1)S(1)}, u32[]{:S(2)}, u32[]{:S(2)}) collective-permute-start(bf16[5,32,1024]{2,1,0:T(8,128)(2,1)S(1)} %collective-permute-done), channel_id=1, source_target_pairs={{0,16},{16,32},{32,48},{48,64},{64,80},{80,96},{96,112},{112,0},{1... | collective-permute-start | bytes 983048 | tf_op jit(solution)/shard_map/ppermute | solution.py:54
  23.6 7.7 %collective-permute-start.2 = (bf16[5,32,1024]{2,1,0:T(8,128)(2,1)S(1)}, bf16[5,32,1024]{2,1,0:T(8,128)(2,1)S(1)}, u32[]{:S(2)}, u32[]{:S(2)}) collective-permute-start(bf16[5,32,1024]{2,1,0:T(8,128)(2,1)S(1)} %collective-permute-done.1), channel_id=1, source_target_pairs={{0,16},{16,32},{32,48},{48,64},{64,80},{80,96},{96,112},{112,0},{1... | collective-permute-start | bytes 983048 | tf_op jit(solution)/shard_map/ppermute | solution.py:54
  25.2 7.5 %collective-permute-start.5 = (bf16[5,32,1024]{2,1,0:T(8,128)(2,1)S(1)}, bf16[5,32,1024]{2,1,0:T(8,128)(2,1)S(1)}, u32[]{:S(2)}, u32[]{:S(2)}) collective-permute-start(bf16[5,32,1024]{2,1,0:T(8,128)(2,1)S(1)} %collective-permute-done.4), channel_id=1, source_target_pairs={{0,112},{16,0},{32,16},{48,32},{64,48},{80,64},{96,80},{112,96},{1... | collective-permute-start | bytes 983048 | tf_op jit(solution)/shard_map/ppermute | solution.py:57
  31.3 7.7 %collective-permute-start.3 = (bf16[5,32,1024]{2,1,0:T(8,128)(2,1)S(1)}, bf16[5,32,1024]{2,1,0:T(8,128)(2,1)S(1)}, u32[]{:S(2)}, u32[]{:S(2)}) collective-permute-start(bf16[5,32,1024]{2,1,0:T(8,128)(2,1)S(1)} %collective-permute-done.2), channel_id=1, source_target_pairs={{0,16},{16,32},{32,48},{48,64},{64,80},{80,96},{96,112},{112,0},{1... | collective-permute-start | bytes 983048 | tf_op jit(solution)/shard_map/ppermute | solution.py:54
  32.7 12.6 %collective-permute-start.6 = (bf16[5,32,1024]{2,1,0:T(8,128)(2,1)S(1)}, bf16[5,32,1024]{2,1,0:T(8,128)(2,1)S(1)}, u32[]{:S(2)}, u32[]{:S(2)}) collective-permute-start(bf16[5,32,1024]{2,1,0:T(8,128)(2,1)S(1)} %collective-permute-done.5), channel_id=1, source_target_pairs={{0,112},{16,0},{32,16},{48,32},{64,48},{80,64},{96,80},{112,96},{1... | collective-permute-start | bytes 983048 | tf_op jit(solution)/shard_map/ppermute | solution.py:57
  52.3 45.4 %copy-start.5 = (s32[5]{0:T(128)S(1)}, s32[5]{0:T(128)}, u32[]{:S(2)}) copy-start(s32[5]{0:T(128)} %param.6) | copy-start | bytes 64
  74.3 1.5 copy-start.2
  77.8 4.1 %collective-permute-start.7 = (f32[3,5,512]{2,0,1:T(4,128)S(1)}, f32[3,5,512]{2,0,1:T(4,128)S(1)}, u32[]{:S(2)}, u32[]{:S(2)}) collective-permute-start(f32[3,5,512]{2,0,1:T(4,128)S(1)} %pad_maximum_fusion.4), channel_id=1, source_target_pairs={{0,1},{1,0},{2,3},{3,2},{4,5},{5,4},{6,7},{7,6},{8,9},{9,8},{10,11... | collective-permute-start | bytes 92168 | tf_op jit(solution)/shard_map/ppermute | solution.py:129
  81.9 1.2 collective-permute-start.8
  83.1 4.7 %collective-permute-start.9 = (f32[2,5,256]{2,1,0:T(8,128)S(1)}, f32[2,5,256]{2,1,0:T(8,128)S(1)}, u32[]{:S(2)}, u32[]{:S(2)}) collective-permute-start(f32[2,5,256]{2,1,0:T(8,128)S(1)} %pad_maximum_fusion.9), channel_id=1, source_target_pairs={{0,32},{16,48},{32,0},{48,16},{64,96},{80,112},{96,64},{112,80},{1... | collective-permute-start | bytes 30728 | tf_op jit(solution)/shard_map/ppermute | solution.py:21
  84.7 5.9 %collective-permute-start.15 = (f32[3,5,512]{2,0,1:T(4,128)S(1)}, f32[3,5,512]{2,0,1:T(4,128)S(1)}, u32[]{:S(2)}, u32[]{:S(2)}) collective-permute-start(f32[3,5,512]{2,0,1:T(4,128)S(1)} %pad_maximum_fusion.5), channel_id=1, source_target_pairs={{0,2},{1,3},{2,0},{3,1},{4,6},{5,7},{6,4},{7,5},{8,10},{9,11},{10,... | collective-permute-start | bytes 92168 | tf_op jit(solution)/shard_map/ppermute | solution.py:21
  87.8 5.3 %collective-permute-start.10 = (f32[2,5,256]{2,1,0:T(8,128)S(1)}, f32[2,5,256]{2,1,0:T(8,128)S(1)}, u32[]{:S(2)}, u32[]{:S(2)}) collective-permute-start(f32[2,5,256]{2,1,0:T(8,128)S(1)} %pad_maximum_fusion.10), channel_id=1, source_target_pairs={{0,64},{16,80},{32,96},{48,112},{64,0},{80,16},{96,32},{112,48},{1... | collective-permute-start | bytes 30728 | tf_op jit(solution)/shard_map/ppermute | solution.py:21
  90.8 4.1 %collective-permute-start.16 = (f32[3,5,512]{2,0,1:T(4,128)S(1)}, f32[3,5,512]{2,0,1:T(4,128)S(1)}, u32[]{:S(2)}, u32[]{:S(2)}) collective-permute-start(f32[3,5,512]{2,0,1:T(4,128)S(1)} %pad_maximum_fusion.6), channel_id=1, source_target_pairs={{0,4},{1,5},{2,6},{3,7},{4,0},{5,1},{6,2},{7,3},{8,12},{9,13},{10,... | collective-permute-start | bytes 92168 | tf_op jit(solution)/shard_map/ppermute | solution.py:21
  95.0 5.6 %collective-permute-start.17 = (f32[3,5,512]{2,0,1:T(4,128)S(1)}, f32[3,5,512]{2,0,1:T(4,128)S(1)}, u32[]{:S(2)}, u32[]{:S(2)}) collective-permute-start(f32[3,5,512]{2,0,1:T(4,128)S(1)} %pad_maximum_fusion.7), channel_id=1, source_target_pairs={{0,8},{1,9},{2,10},{3,11},{4,12},{5,13},{6,14},{7,15},{8,0},{9,1},... | collective-permute-start | bytes 92168 | tf_op jit(solution)/shard_map/ppermute | solution.py:21
  115.6 2.4 %copy-start = (f32[5,256,1024]{2,1,0:T(8,128)}, f32[5,256,1024]{2,1,0:T(8,128)S(1)}, u32[]{:S(2)}) copy-start(f32[5,256,1024]{2,1,0:T(8,128)S(1)} %broadcast_multiply_fusion.1) | copy-start | bytes 15728644
  118.0 5.1 %collective-permute-start.18 = (f32[648,1024]{1,0:T(8,128)S(1)}, f32[648,1024]{1,0:T(8,128)}, u32[]{:S(2)}, u32[]{:S(2)}) collective-permute-start(f32[648,1024]{1,0:T(8,128)S(1)} %maximum_maximum_fusion), channel_id=1, source_target_pairs={{0,16},{16,0},{32,48},{48,32},{64,80},{80,64},{96,112},{112,96},{1... | collective-permute-start | bytes 7962632 | tf_op jit(solution)/shard_map/ppermute | solution.py:72
  118.0 7.1 %copy-start.1 = (f32[5,256,1024]{2,1,0:T(8,128)S(1)}, f32[5,256,1024]{2,1,0:T(8,128)}, u32[]{:S(2)}) copy-start(f32[5,256,1024]{2,1,0:T(8,128)} %copy-done) | copy-start | bytes 15728644
  126.1 74.4 %copy-start.4 = (bf16[5,32,1024]{2,1,0:T(8,128)(2,1)S(1)}, bf16[5,32,1024]{2,1,0:T(8,128)(2,1)}, u32[]{:S(2)}) copy-start(bf16[5,32,1024]{2,1,0:T(8,128)(2,1)} %param.4) | copy-start | bytes 983044
  127.0 18.8 %collective-permute-start.19 = (f32[168,1024]{1,0:T(8,128)S(1)}, f32[168,1024]{1,0:T(8,128)S(1)}, u32[]{:S(2)}, u32[]{:S(2)}) collective-permute-start(f32[168,1024]{1,0:T(8,128)S(1)} %pad_maximum_fusion.3), channel_id=1, source_target_pairs={{0,32},{16,48},{32,64},{48,80},{64,96},{80,112},{96,0},{112,16},{1... | collective-permute-start | bytes 2064392 | tf_op jit(solution)/shard_map/ppermute | solution.py:85
  145.9 18.0 %collective-permute-start.20 = (f32[168,1024]{1,0:T(8,128)S(1)}, f32[168,1024]{1,0:T(8,128)S(1)}, u32[]{:S(2)}, u32[]{:S(2)}) collective-permute-start(f32[168,1024]{1,0:T(8,128)S(1)} %fusion.12), channel_id=1, source_target_pairs={{0,32},{16,48},{32,64},{48,80},{64,96},{80,112},{96,0},{112,16},{1... | collective-permute-start | bytes 2064392 | tf_op jit(solution)/shard_map/ppermute | solution.py:85
  164.0 17.2 %collective-permute-start.21 = (f32[168,1024]{1,0:T(8,128)S(1)}, f32[168,1024]{1,0:T(8,128)S(1)}, u32[]{:S(2)}, u32[]{:S(2)}) collective-permute-start(f32[168,1024]{1,0:T(8,128)S(1)} %fusion.13), channel_id=1, source_target_pairs={{0,32},{16,48},{32,64},{48,80},{64,96},{80,112},{96,0},{112,16},{1... | collective-permute-start | bytes 2064392 | tf_op jit(solution)/shard_map/ppermute | solution.py:85
  164.1 3.6 %collective-permute-start.11 = (f32[5]{0:T(128)S(1)}, f32[5]{0:T(128)S(1)}, u32[]{:S(2)}, u32[]{:S(2)}) collective-permute-start(f32[5]{0:T(128)S(1)} %get-tuple-element.11), channel_id=1, source_target_pairs={{0,1},{1,0},{2,3},{3,2},{4,5},{5,4},{6,7},{7,6},{8,9},{9,8},{10,11... | collective-permute-start | bytes 68 | tf_op jit(solution)/shard_map/ppermute | solution.py:33
  167.7 5.0 %collective-permute-start.12 = (f32[5]{0:T(128)S(1)}, f32[5]{0:T(128)S(1)}, u32[]{:S(2)}, u32[]{:S(2)}) collective-permute-start(f32[5]{0:T(128)S(1)} %fusion.49), channel_id=1, source_target_pairs={{0,2},{1,3},{2,0},{3,1},{4,6},{5,7},{6,4},{7,5},{8,10},{9,11},{10,... | collective-permute-start | bytes 68 | tf_op jit(solution)/shard_map/ppermute | solution.py:33
  172.7 3.5 %collective-permute-start.13 = (f32[5]{0:T(128)S(1)}, f32[5]{0:T(128)S(1)}, u32[]{:S(2)}, u32[]{:S(2)}) collective-permute-start(f32[5]{0:T(128)S(1)} %fusion.48), channel_id=1, source_target_pairs={{0,4},{1,5},{2,6},{3,7},{4,0},{5,1},{6,2},{7,3},{8,12},{9,13},{10,... | collective-permute-start | bytes 68 | tf_op jit(solution)/shard_map/ppermute | solution.py:33
  176.3 5.3 %collective-permute-start.14 = (f32[5]{0:T(128)S(1)}, f32[5]{0:T(128)S(1)}, u32[]{:S(2)}, u32[]{:S(2)}) collective-permute-start(f32[5]{0:T(128)S(1)} %fusion.47), channel_id=1, source_target_pairs={{0,8},{1,9},{2,10},{3,11},{4,12},{5,13},{6,14},{7,15},{8,0},{9,1},... | collective-permute-start | bytes 68 | tf_op jit(solution)/shard_map/ppermute | solution.py:33
Sparse Core Ops, SparseCore 0:
  10.2 58.9 all-gather.1
  111.5 89.0 reduce-scatter.1

commit v13 on v6

--- a/solution.py
+++ b/solution.py
@@ -72,17 +72,52 @@
     summed = keep + got[:body_rows].reshape(pair_count, chips, shard_rows, width)
     carried = extra + got[body_rows:]
     chip = own // 2
-    ring = [(i, (i + 2) % size) for i in range(size)]
+    sign = 1 - 2 * parity
+    ring = [(i, (i + (2 if i % 2 == 0 else -2)) % size) for i in range(size)]
     chunk_rows = pair_count * shard_rows
 
     def addend(target):
         block = lax.dynamic_index_in_dim(summed, target % chips, axis=1, keepdims=False)
         return jnp.concatenate([block.reshape(chunk_rows, width), carried], axis=0)
 
-    running = addend(chip - 1)
+    running = addend(chip - sign)
     for step in range(1, chips):
-        running = lax.ppermute(running, axis, ring) + addend(chip - 1 - step)
+        running = lax.ppermute(running, axis, ring) + addend(chip - sign * (1 + step))
     return running[:chunk_rows].reshape(pair_count, shard_rows, width), running[chunk_rows]
+
+
+def pair_ring_reduce_scatter(blocks, side):
+    pair_count, _, rows, width = blocks.shape
+    dp_size = lax.axis_size("dp")
+    pair_size = side * side
+    parity = lax.axis_index("dp") % 2
+    sign = 1 - 2 * parity
+    place = lax.axis_index("pair")
+    z_own = place // side
+    y_own = place % side
+
+    def ring(step_of):
+        return [(d * pair_size + k, d * pair_size + step_of(k, 1 if d % 2 == 0 else -1))
+                for d in range(dp_size) for k in range(pair_size)]
+
+    along_y = ring(lambda k, s: (k // side) * side + (k % side + s) % side)
+    along_z = ring(lambda k, s: ((k // side + s) % side) * side + k % side)
+    grid = blocks.reshape(pair_count, side, side, rows, width)
+
+    def y_part(step):
+        return lax.dynamic_index_in_dim(grid, (y_own - sign * (1 + step)) % side, 2, False)
+
+    running = y_part(0)
+    for step in range(1, side):
+        running = lax.ppermute(running, ("dp", "pair"), along_y) + y_part(step)
+
+    def z_part(step):
+        return lax.dynamic_index_in_dim(running, (z_own - sign * (1 + step)) % side, 1, False)
+
+    total = z_part(0)
+    for step in range(1, side):
+        total = lax.ppermute(total, ("dp", "pair"), along_z) + z_part(step)
+    return total
 
 
 def per_device(anchor, partner, counts, pair_scale):
@@ -137,8 +172,16 @@
     prob_col = jnp.where(inside, jnp.exp(scores - col_lse[:, None, :]), 0.0)
     weights = (pair_scale[:, None, None] * 0.5 * (prob_row + prob_col)).astype(jnp.bfloat16)
     weights = lax.optimization_barrier(weights)
+    ring_width = model_width // 8
+    main_width = model_width - ring_width
+    col_main = col_set[:, :, :main_width]
+    col_ring = col_set[:, :, main_width:]
     grad_rows = (
-        jnp.einsum("prc,pcd->prd", weights, col_set, preferred_element_type=jnp.float32)
+        jnp.einsum("prc,pcd->prd", weights, col_main, preferred_element_type=jnp.float32)
+        * score_scale
+    )
+    grad_ring = (
+        jnp.einsum("prc,pcd->prd", weights, col_ring, preferred_element_type=jnp.float32)
         * score_scale
     )
     grad_cols = (
@@ -146,6 +189,11 @@
         * score_scale
     )
     anchor_part = lax.psum_scatter(grad_rows, "pair", scatter_dimension=1, tiled=True)
+    side = math.isqrt(pair_size)
+    ring_part = pair_ring_reduce_scatter(
+        grad_ring.reshape(pair_count, pair_size, shard_rows, ring_width), side
+    )
+    anchor_part = jnp.concatenate([anchor_part, ring_part], axis=2)
 
     width_lanes = jnp.arange(model_width, dtype=jnp.int32)[None, :]
     slots = (jnp.arange(pair_count, dtype=jnp.int32) * dp_size + dp_index)[:, None]

time: 211 us -> 215 us (1.019)
  waiting for transfers between devices: 111 us -> 105 us
  other arithmetic: 14.8 us -> 19.8 us
  starting transfers between devices: 31.7 us -> 35.3 us
    ppermute x4, waiting for transfers between devices: 6.32 us -> 0.01 us  [butterfly_sum(): other = lax.ppermute(values, axis, [(i, i ^ bit) for i in range(size)])]
    ppermute x3 -> x9, starting transfers between devices: 0.58 us -> 5.98 us  [the longest x3 2.06 us: pair_ring_reduce_scatter(): running = lax.ppermute(running, ('dp', 'pair'), along_y) + y_part(step)]
    ppermute x1, waiting for transfers between devices: 5.08 us -> 0.01 us  [two_stage_reduce_scatter(): got = lax.ppermute(send, axis, [(i, i ^ 1) for i in range(size)])]
    ppermute x3 -> x9, waiting for transfers between devices: 38.4 us -> 42.6 us  [the longest x3 26.6 us: pair_ring_reduce_scatter(): running = lax.ppermute(running, ('dp', 'pair'), along_y) + y_part(step)]
    dot_general x1 -> x2, matrix products: 7.3 us -> 8.4 us  [the longest x1 6.79 us: per_device(): jnp.einsum('prc,pcd->prd', weights, col_main, preferred_element_type=jnp....]
  transfers between devices with their start and end apart: 24 -> 30, of which waited for: 20 -> 21; matrix products, arithmetic and copies ran while one was open for 13% -> 15% of each run, Pallas kernels for 0% -> 0%
where the time goes in v13:
time: 215 us; the launch traced here: 214 us
  waiting for transfers between devices  105 us (49%)
  starting transfers between devices  35.3 us (16%)
  local copies, waits for them, and re-layouts  20.2 us (9%)
  other arithmetic  19.8 us (9%)
  matrix products  17.6 us (8%)
  between operations  16.3 us (8%)
    ppermute x3, waiting for transfers between devices, pair_ring_reduce_scatter(): running = lax.ppermute(running, ('dp', 'pair'), along_y) + y_part(step)  26.6 us
    all_gather x1, waiting for transfers between devices, per_device(): row_set = lax.all_gather(anchor, 'pair', axis=1, tiled=True)  17.9 us
    reduce_scatter x1, waiting for transfers between devices, per_device(): lax.psum_scatter(grad_rows, 'pair', scatter_dimension=1, tiled=True)  17.2 us
    ppermute x4, waiting for transfers between devices, ring_gather(): ahead = lax.ppermute(ahead, axis, forward)  16.3 us
    unnamed x29, local copies, waits for them, and re-layouts  14.5 us
    ppermute x3, waiting for transfers between devices, pair_ring_reduce_scatter(): total = lax.ppermute(total, ('dp', 'pair'), along_z) + z_part(step)  13.9 us
    ppermute x7, starting transfers between devices, butterfly_merge(): other = lax.ppermute(stats, axis, [(i, i ^ bit) for i in range(size)])  13 us
    ppermute x3, starting transfers between devices, ring_gather(): behind = lax.ppermute(behind, axis, backward)  9.41 us
  transfers between devices with their start and end apart: 30, of which 21 were waited for; matrix products, arithmetic and copies ran while one was open for 15% of the time, Pallas kernels for 0%

profile of v13, /device:TPU:0, one launch (start us, length us, event | category | flops | bytes accessed | tf_op | source)
XLA Modules:
  0.0 214.0 jit_solution(17518241607228172563)
XLA Ops:
  8.0 2.9 %collective-permute-start.4 = (bf16[5,32,1024]{2,1,0:T(8,128)(2,1)}, bf16[5,32,1024]{2,1,0:T(8,128)(2,1)S(1)}, u32[]{:S(2)}, u32[]{:S(2)}) collective-permute-start(bf16[5,32,1024]{2,1,0:T(8,128)(2,1)} %param.5), channel_id=1, source_target_pairs={{0,112},{16,0},{32,16},{48,32},{64,48},{80,64},{96,80},{112,96},{1... | collective-permute-start | bytes 983048 | tf_op jit(solution)/shard_map/ppermute | solution.py:56
  11.7 4.2 %collective-permute-done = bf16[5,32,1024]{2,1,0:T(8,128)(2,1)S(1)} collective-permute-done((bf16[5,32,1024]{2,1,0:T(8,128)(2,1)}, bf16[5,32,1024]{2,1,0:T(8,128)(2,1)S(1)}, u32[]{:S(2)}, u32[]{:S(2)}) %collective-permute-start) | collective-permute-done | bytes 327712 | tf_op jit(solution)/shard_map/ppermute | solution.py:53
  16.2 1.2 fusion.17
  17.4 6.2 %collective-permute-done.1 = bf16[5,32,1024]{2,1,0:T(8,128)(2,1)S(1)} collective-permute-done((bf16[5,32,1024]{2,1,0:T(8,128)(2,1)S(1)}, bf16[5,32,1024]{2,1,0:T(8,128)(2,1)S(1)}, u32[]{:S(2)}, u32[]{:S(2)}) %collective-permute-start.1) | collective-permute-done | bytes 327712 | tf_op jit(solution)/shard_map/ppermute | solution.py:53
  25.2 3.0 %collective-permute-start.5 = (bf16[5,32,1024]{2,1,0:T(8,128)(2,1)S(1)}, bf16[5,32,1024]{2,1,0:T(8,128)(2,1)S(1)}, u32[]{:S(2)}, u32[]{:S(2)}) collective-permute-start(bf16[5,32,1024]{2,1,0:T(8,128)(2,1)S(1)} %collective-permute-done.4), channel_id=1, source_target_pairs={{0,112},{16,0},{32,16},{48,32},{64,48},{80,64},{96,80},{112,96},{1... | collective-permute-start | bytes 983048 | tf_op jit(solution)/shard_map/ppermute | solution.py:56
  28.1 3.2 %collective-permute-done.2 = bf16[5,32,1024]{2,1,0:T(8,128)(2,1)S(1)} collective-permute-done((bf16[5,32,1024]{2,1,0:T(8,128)(2,1)S(1)}, bf16[5,32,1024]{2,1,0:T(8,128)(2,1)S(1)}, u32[]{:S(2)}, u32[]{:S(2)}) %collective-permute-start.2) | collective-permute-done | bytes 327712 | tf_op jit(solution)/shard_map/ppermute | solution.py:53
  31.4 1.3 collective-permute-done.5
  32.7 3.5 %collective-permute-start.6 = (bf16[5,32,1024]{2,1,0:T(8,128)(2,1)S(1)}, bf16[5,32,1024]{2,1,0:T(8,128)(2,1)S(1)}, u32[]{:S(2)}, u32[]{:S(2)}) collective-permute-start(bf16[5,32,1024]{2,1,0:T(8,128)(2,1)S(1)} %collective-permute-done.5), channel_id=1, source_target_pairs={{0,112},{16,0},{32,16},{48,32},{64,48},{80,64},{96,80},{112,96},{1... | collective-permute-start | bytes 983048 | tf_op jit(solution)/shard_map/ppermute | solution.py:56
  36.2 2.8 %collective-permute-done.3 = bf16[5,32,1024]{2,1,0:T(8,128)(2,1)S(1)} collective-permute-done((bf16[5,32,1024]{2,1,0:T(8,128)(2,1)S(1)}, bf16[5,32,1024]{2,1,0:T(8,128)(2,1)S(1)}, u32[]{:S(2)}, u32[]{:S(2)}) %collective-permute-start.3) | collective-permute-done | bytes 327712 | tf_op jit(solution)/shard_map/ppermute | solution.py:53
  51.2 17.9 %all-gather.2.cloned.1.call-done = bf16[5,512,1024]{2,1,0:T(8,128)(2,1)} async-done(((bf16[5,32,1024]{2,1,0:T(8,128)(2,1)}), bf16[5,512,1024]{2,1,0:T(8,128)(2,1)}) %all-gather.2.cloned.1.call-update) | async-done | bytes 5242896 | tf_op jit(solution)/shard_map/all_gather | solution.py:138
  69.1 5.2 %fusion.11 = (f32[5,256]{1,0:T(8,128)S(1)}, f32[5,512]{1,0:T(8,128)S(1)}, f32[5,256,512]{2,1,0:T(8,128)S(1)}) fusion(pred[5,256]{1,0:T(8,128)(4,1)S(1)} %broadcast_compare_fusion.1, pred[5,512]{1,0:T(8,128)(4,1)S(1)} %copy.30, bf16[5,512,1024]{2,1,0:T(8,128)(2,1)} %all-gather.2.cloned.1.call-done, ...), kind=kOutput, calls=%fused_computation.27 | convolution fusion | flops 1345450240 | bytes 10504964 | tf_op jit(solution)/shard_map/prd,pcd->prc/dot_general | solution.py:151
  74.3 1.5 copy-done.2
  75.8 1.9 fusion
  77.9 1.1 collective-permute-done.7
  79.0 1.5 collective-permute-start.8
  80.6 1.6 collective-permute-start.14
  82.9 1.8 collective-permute-done.14
  84.8 3.1 %collective-permute-start.15 = (f32[3,5,512]{2,0,1:T(4,128)S(1)}, f32[3,5,512]{2,0,1:T(4,128)S(1)}, u32[]{:S(2)}, u32[]{:S(2)}) collective-permute-start(f32[3,5,512]{2,0,1:T(4,128)S(1)} %pad_maximum_fusion.5), channel_id=1, source_target_pairs={{0,2},{1,3},{2,0},{3,1},{4,6},{5,7},{6,4},{7,5},{8,10},{9,11},{10,... | collective-permute-start | bytes 92168 | tf_op jit(solution)/shard_map/ppermute | solution.py:21
  88.0 2.7 %collective-permute-start.9 = (f32[2,5,256]{2,1,0:T(8,128)S(1)}, f32[2,5,256]{2,1,0:T(8,128)S(1)}, u32[]{:S(2)}, u32[]{:S(2)}) collective-permute-start(f32[2,5,256]{2,1,0:T(8,128)S(1)} %pad_maximum_fusion.10), channel_id=1, source_target_pairs={{0,64},{16,80},{32,96},{48,112},{64,0},{80,16},{96,32},{112,48},{1... | collective-permute-start | bytes 30728 | tf_op jit(solution)/shard_map/ppermute | solution.py:21
  90.8 1.2 collective-permute-start.16
  92.0 1.2 collective-permute-done.9
  93.2 1.7 collective-permute-done.16
  95.0 2.8 %collective-permute-start.17 = (f32[3,5,512]{2,0,1:T(4,128)S(1)}, f32[3,5,512]{2,0,1:T(4,128)S(1)}, u32[]{:S(2)}, u32[]{:S(2)}) collective-permute-start(f32[3,5,512]{2,0,1:T(4,128)S(1)} %pad_maximum_fusion.7), channel_id=1, source_target_pairs={{0,8},{1,9},{2,10},{3,11},{4,12},{5,13},{6,14},{7,15},{8,0},{9,1},... | collective-permute-start | bytes 92168 | tf_op jit(solution)/shard_map/ppermute | solution.py:21
  98.3 2.3 %collective-permute-done.17 = f32[3,5,512]{2,0,1:T(4,128)S(1)} collective-permute-done((f32[3,5,512]{2,0,1:T(4,128)S(1)}, f32[3,5,512]{2,0,1:T(4,128)S(1)}, u32[]{:S(2)}, u32[]{:S(2)}) %collective-permute-start.17) | collective-permute-done | bytes 30752 | tf_op jit(solution)/shard_map/ppermute | solution.py:21
  100.6 1.2 copy.34
  101.8 1.2 broadcast_select_fusion.1
  103.3 2.7 %fusion.4 = bf16[5,512,256]{1,2,0:T(8,128)(2,1)S(1)} fusion(f32[5,256,512]{2,1,0:T(8,128)} %copy-done.2, f32[5,256]{1,0:T(8,128)S(1)} %get-tuple-element.8, f32[5,512]{1,0:T(8,128)S(1)} %copy.37, f32[5]{0:T(128)S(1)} %get-tuple-element.49, pred[5,256]{1,0:T(8,128)(4,1)S(1)} %broadcast_compare_fusion.1, pred[5,512]{1,0:T(8,128)(4,1)S(1)} %copy.30), kind=kLoop, calls=%fused_computation.11 | loop fusion | flops 5898240 | bytes 3951380 | tf_op jit(solution)/shard_map/convert_element_type | solution.py:173
  106.1 6.8 %broadcast_multiply_fusion = f32[5,512,896]{2,1,0:T(8,128)} fusion(bf16[5,512,256]{1,2,0:T(8,128)(2,1)S(1)} %fusion.4, bf16[5,512,1024]{2,1,0:T(8,128)(2,1)} %constant_dynamic-update-slice_fusion, s32[]{:T(128)S(6)} %select_n.322), kind=kOutput, calls=%fused_computation.5 | convolution fusion | flops 1176698880 | bytes 12779524 | tf_op jit(solution)/shard_map/prc,pcd->prd/dot_general | solution.py:180
  113.1 4.0 %broadcast_multiply_fusion.1 = f32[5,256,1024]{2,1,0:T(8,128)S(1)} fusion(bf16[5,512,256]{1,2,0:T(8,128)(2,1)S(1)} %fusion.4, bf16[5,512,1024]{2,1,0:T(8,128)(2,1)} %all-gather.2.cloned.1.call-done), kind=kOutput, calls=%fused_computation.17 | convolution fusion | flops 1343488000 | bytes 11796480 | tf_op jit(solution)/shard_map/prc,prd->pcd/dot_general | solution.py:188
  117.4 2.1 maximum_maximum_fusion
  120.4 1.6 convolution_multiply_fusion
  122.2 1.5 collective-permute-start.22
  123.6 10.5 %collective-permute-done.22 = f32[5,4,32,128]{3,2,0,1:T(8,128)S(1)} collective-permute-done((f32[5,4,32,128]{3,2,0,1:T(8,128)S(1)}, f32[5,4,32,128]{3,2,0,1:T(8,128)S(1)}, u32[]{:S(2)}, u32[]{:S(2)}) %collective-permute-start.22) | collective-permute-done | bytes 327712 | tf_op jit(solution)/shard_map/ppermute | solution.py:112
  134.7 2.4 %slice.226 = f32[640,1024]{1,0:T(8,128)S(1)} slice(f32[648,1024]{1,0:T(8,128)} %collective-permute-done.18), slice={[0:640], [0:1024]} | slice | bytes 5242880 | tf_op jit(solution)/shard_map/slice | solution.py:72
  140.3 1.4 collective-permute-start.19
  141.7 6.9 %collective-permute-done.23 = f32[5,4,32,128]{3,2,0,1:T(8,128)S(1)} collective-permute-done((f32[5,4,32,128]{3,2,0,1:T(8,128)S(1)}, f32[5,4,32,128]{3,2,0,1:T(8,128)S(1)}, u32[]{:S(2)}, u32[]{:S(2)}) %collective-permute-start.23) | collective-permute-done | bytes 327712 | tf_op jit(solution)/shard_map/ppermute | solution.py:112
  148.9 2.1 collective-permute-start.10
  151.0 1.8 collective-permute-done.19
  152.8 1.2 fusion.12
  154.3 9.2 %collective-permute-done.24 = f32[5,4,32,128]{3,2,0,1:T(8,128)S(1)} collective-permute-done((f32[5,4,32,128]{3,2,0,1:T(8,128)S(1)}, f32[5,4,32,128]{3,2,0,1:T(8,128)S(1)}, u32[]{:S(2)}, u32[]{:S(2)}) %collective-permute-start.24) | collective-permute-done | bytes 327712 | tf_op jit(solution)/shard_map/ppermute | solution.py:112
  163.5 1.7 collective-permute-start.25
  166.0 6.4 %collective-permute-done.25 = f32[5,32,128]{2,1,0:T(8,128)S(1)} collective-permute-done((f32[5,32,128]{2,1,0:T(8,128)S(1)}, f32[5,32,128]{2,1,0:T(8,128)S(1)}, u32[]{:S(2)}, u32[]{:S(2)}) %collective-permute-start.25) | collective-permute-done | bytes 81952 | tf_op jit(solution)/shard_map/ppermute | solution.py:119
  173.0 1.6 collective-permute-start.12
  174.6 4.2 %collective-permute-done.26 = f32[5,32,128]{2,1,0:T(8,128)S(1)} collective-permute-done((f32[5,32,128]{2,1,0:T(8,128)S(1)}, f32[5,32,128]{2,1,0:T(8,128)S(1)}, u32[]{:S(2)}, u32[]{:S(2)}) %collective-permute-start.26) | collective-permute-done | bytes 81952 | tf_op jit(solution)/shard_map/ppermute | solution.py:119
  178.9 2.4 %collective-permute-start.13 = (f32[5]{0:T(128)S(1)}, f32[5]{0:T(128)S(1)}, u32[]{:S(2)}, u32[]{:S(2)}) collective-permute-start(f32[5]{0:T(128)S(1)} %fusion.49), channel_id=1, source_target_pairs={{0,8},{1,9},{2,10},{3,11},{4,12},{5,13},{6,14},{7,15},{8,0},{9,1},... | collective-permute-start | bytes 68 | tf_op jit(solution)/shard_map/ppermute | solution.py:32
  181.3 3.2 %collective-permute-done.27 = f32[5,32,128]{2,1,0:T(8,128)S(1)} collective-permute-done((f32[5,32,128]{2,1,0:T(8,128)S(1)}, f32[5,32,128]{2,1,0:T(8,128)S(1)}, u32[]{:S(2)}, u32[]{:S(2)}) %collective-permute-start.27) | collective-permute-done | bytes 81952 | tf_op jit(solution)/shard_map/ppermute | solution.py:119
  186.5 17.2 %reduce-scatter.2.cloned.1.call-done = f32[5,32,896]{2,1,0:T(8,128)} async-done(((f32[5,512,896]{2,1,0:T(8,128)}), f32[5,32,896]{2,1,0:T(8,128)}) %reduce-scatter.2.cloned.1.call-update) | async-done | bytes 573456 | tf_op jit(solution)/shard_map/reduce_scatter | solution.py:191
  203.7 2.4 %fusion.16 = (f32[5,32,1024]{2,1,0:T(8,128)}, f32[5,32,1024]{2,1,0:T(8,128)}) fusion(f32[5,32,1024]{2,1,0:T(8,128)S(1)} %bitcast.138, bf16[5,32,1024]{2,1,0:T(8,128)(2,1)S(1)} %copy-done.4, f32[5]{0:T(128)S(1)} %get-tuple-element.48, pred[5,32]{1,0:T(8,128)(4,1)S(1)} %broadcast_compare_fusion.2, bf16[5,32,1024]{2,1,0:T(8,128)(2,1)S(1)} %copy-done.3, ...), kind=kLoop, calls=%fused_computation.35 | loop fusion | flops 1474560 | bytes 3276980 | tf_op jit(solution)/shard_map/jit(_where)/select_n | solution.py:212
  (124 shorter events, 26.3 us)
Async XLA Ops:
  7.2 34.9 %copy-start.3 = (bf16[5,32,1024]{2,1,0:T(8,128)(2,1)S(1)}, bf16[5,32,1024]{2,1,0:T(8,128)(2,1)}, u32[]{:S(2)}) copy-start(bf16[5,32,1024]{2,1,0:T(8,128)(2,1)} %param.5) | copy-start | bytes 983044
  7.2 61.9 %all-gather.2.cloned.1.call-start = ((), (), s32[]{:S(2)}) async-start(), calls=%async_computation.1 | async-start | bytes 5570560 | tf_op jit(solution)/shard_map/all_gather | solution.py:138
  7.9 195.8 %reduce-scatter.2.cloned.1.call-start = ((), (), s32[]{:S(2)}) async-start(), calls=%async_computation.2 | async-start | bytes 9748480 | tf_op jit(solution)/shard_map/reduce_scatter | solution.py:191
  8.0 7.9 %collective-permute-start = (bf16[5,32,1024]{2,1,0:T(8,128)(2,1)}, bf16[5,32,1024]{2,1,0:T(8,128)(2,1)S(1)}, u32[]{:S(2)}, u32[]{:S(2)}) collective-permute-start(bf16[5,32,1024]{2,1,0:T(8,128)(2,1)} %param.5), channel_id=1, source_target_pairs={{0,16},{16,32},{32,48},{48,64},{64,80},{80,96},{96,112},{112,0},{1... | collective-permute-start | bytes 983048 | tf_op jit(solution)/shard_map/ppermute | solution.py:53
  8.0 17.2 %collective-permute-start.4 = (bf16[5,32,1024]{2,1,0:T(8,128)(2,1)}, bf16[5,32,1024]{2,1,0:T(8,128)(2,1)S(1)}, u32[]{:S(2)}, u32[]{:S(2)}) collective-permute-start(bf16[5,32,1024]{2,1,0:T(8,128)(2,1)} %param.5), channel_id=1, source_target_pairs={{0,112},{16,0},{32,16},{48,32},{64,48},{80,64},{96,80},{112,96},{1... | collective-permute-start | bytes 983048 | tf_op jit(solution)/shard_map/ppermute | solution.py:56
  15.9 7.7 %collective-permute-start.1 = (bf16[5,32,1024]{2,1,0:T(8,128)(2,1)S(1)}, bf16[5,32,1024]{2,1,0:T(8,128)(2,1)S(1)}, u32[]{:S(2)}, u32[]{:S(2)}) collective-permute-start(bf16[5,32,1024]{2,1,0:T(8,128)(2,1)S(1)} %collective-permute-done), channel_id=1, source_target_pairs={{0,16},{16,32},{32,48},{48,64},{64,80},{80,96},{96,112},{112,0},{1... | collective-permute-start | bytes 983048 | tf_op jit(solution)/shard_map/ppermute | solution.py:53
  23.6 7.7 %collective-permute-start.2 = (bf16[5,32,1024]{2,1,0:T(8,128)(2,1)S(1)}, bf16[5,32,1024]{2,1,0:T(8,128)(2,1)S(1)}, u32[]{:S(2)}, u32[]{:S(2)}) collective-permute-start(bf16[5,32,1024]{2,1,0:T(8,128)(2,1)S(1)} %collective-permute-done.1), channel_id=1, source_target_pairs={{0,16},{16,32},{32,48},{48,64},{64,80},{80,96},{96,112},{112,0},{1... | collective-permute-start | bytes 983048 | tf_op jit(solution)/shard_map/ppermute | solution.py:53
  25.2 7.5 %collective-permute-start.5 = (bf16[5,32,1024]{2,1,0:T(8,128)(2,1)S(1)}, bf16[5,32,1024]{2,1,0:T(8,128)(2,1)S(1)}, u32[]{:S(2)}, u32[]{:S(2)}) collective-permute-start(bf16[5,32,1024]{2,1,0:T(8,128)(2,1)S(1)} %collective-permute-done.4), channel_id=1, source_target_pairs={{0,112},{16,0},{32,16},{48,32},{64,48},{80,64},{96,80},{112,96},{1... | collective-permute-start | bytes 983048 | tf_op jit(solution)/shard_map/ppermute | solution.py:56
  31.3 7.7 %collective-permute-start.3 = (bf16[5,32,1024]{2,1,0:T(8,128)(2,1)S(1)}, bf16[5,32,1024]{2,1,0:T(8,128)(2,1)S(1)}, u32[]{:S(2)}, u32[]{:S(2)}) collective-permute-start(bf16[5,32,1024]{2,1,0:T(8,128)(2,1)S(1)} %collective-permute-done.2), channel_id=1, source_target_pairs={{0,16},{16,32},{32,48},{48,64},{64,80},{80,96},{96,112},{112,0},{1... | collective-permute-start | bytes 983048 | tf_op jit(solution)/shard_map/ppermute | solution.py:53
  32.7 11.7 %collective-permute-start.6 = (bf16[5,32,1024]{2,1,0:T(8,128)(2,1)S(1)}, bf16[5,32,1024]{2,1,0:T(8,128)(2,1)S(1)}, u32[]{:S(2)}, u32[]{:S(2)}) collective-permute-start(bf16[5,32,1024]{2,1,0:T(8,128)(2,1)S(1)} %collective-permute-done.5), channel_id=1, source_target_pairs={{0,112},{16,0},{32,16},{48,32},{64,48},{80,64},{96,80},{112,96},{1... | collective-permute-start | bytes 983048 | tf_op jit(solution)/shard_map/ppermute | solution.py:56
  74.3 1.5 copy-start.2
  74.3 3.5 %copy-start.6 = (f32[5]{0:T(128)S(1)}, f32[5]{0:T(128)}, u32[]{:S(2)}) copy-start(f32[5]{0:T(128)} %param.7) | copy-start | bytes 64
  74.3 23.5 %copy-start.5 = (s32[5]{0:T(128)S(1)}, s32[5]{0:T(128)}, u32[]{:S(2)}) copy-start(s32[5]{0:T(128)} %param.6) | copy-start | bytes 64
  77.7 1.3 collective-permute-start.7
  79.0 3.8 %collective-permute-start.8 = (f32[2,5,256]{2,1,0:T(8,128)S(1)}, f32[2,5,256]{2,1,0:T(8,128)S(1)}, u32[]{:S(2)}, u32[]{:S(2)}) collective-permute-start(f32[2,5,256]{2,1,0:T(8,128)S(1)} %pad_maximum_fusion.9), channel_id=1, source_target_pairs={{0,32},{16,48},{32,0},{48,16},{64,96},{80,112},{96,64},{112,80},{1... | collective-permute-start | bytes 30728 | tf_op jit(solution)/shard_map/ppermute | solution.py:21
  80.6 4.1 %collective-permute-start.14 = (f32[3,5,512]{2,0,1:T(4,128)S(1)}, f32[3,5,512]{2,0,1:T(4,128)S(1)}, u32[]{:S(2)}, u32[]{:S(2)}) collective-permute-start(f32[3,5,512]{2,0,1:T(4,128)S(1)} %pad_maximum_fusion.4), channel_id=1, source_target_pairs={{0,1},{1,0},{2,3},{3,2},{4,5},{5,4},{6,7},{7,6},{8,9},{9,8},{10,11... | collective-permute-start | bytes 92168 | tf_op jit(solution)/shard_map/ppermute | solution.py:21
  84.8 5.8 %collective-permute-start.15 = (f32[3,5,512]{2,0,1:T(4,128)S(1)}, f32[3,5,512]{2,0,1:T(4,128)S(1)}, u32[]{:S(2)}, u32[]{:S(2)}) collective-permute-start(f32[3,5,512]{2,0,1:T(4,128)S(1)} %pad_maximum_fusion.5), channel_id=1, source_target_pairs={{0,2},{1,3},{2,0},{3,1},{4,6},{5,7},{6,4},{7,5},{8,10},{9,11},{10,... | collective-permute-start | bytes 92168 | tf_op jit(solution)/shard_map/ppermute | solution.py:21
  88.0 5.2 %collective-permute-start.9 = (f32[2,5,256]{2,1,0:T(8,128)S(1)}, f32[2,5,256]{2,1,0:T(8,128)S(1)}, u32[]{:S(2)}, u32[]{:S(2)}) collective-permute-start(f32[2,5,256]{2,1,0:T(8,128)S(1)} %pad_maximum_fusion.10), channel_id=1, source_target_pairs={{0,64},{16,80},{32,96},{48,112},{64,0},{80,16},{96,32},{112,48},{1... | collective-permute-start | bytes 30728 | tf_op jit(solution)/shard_map/ppermute | solution.py:21
  90.8 4.1 %collective-permute-start.16 = (f32[3,5,512]{2,0,1:T(4,128)S(1)}, f32[3,5,512]{2,0,1:T(4,128)S(1)}, u32[]{:S(2)}, u32[]{:S(2)}) collective-permute-start(f32[3,5,512]{2,0,1:T(4,128)S(1)} %pad_maximum_fusion.6), channel_id=1, source_target_pairs={{0,4},{1,5},{2,6},{3,7},{4,0},{5,1},{6,2},{7,3},{8,12},{9,13},{10,... | collective-permute-start | bytes 92168 | tf_op jit(solution)/shard_map/ppermute | solution.py:21
  95.0 5.6 %collective-permute-start.17 = (f32[3,5,512]{2,0,1:T(4,128)S(1)}, f32[3,5,512]{2,0,1:T(4,128)S(1)}, u32[]{:S(2)}, u32[]{:S(2)}) collective-permute-start(f32[3,5,512]{2,0,1:T(4,128)S(1)} %pad_maximum_fusion.7), channel_id=1, source_target_pairs={{0,8},{1,9},{2,10},{3,11},{4,12},{5,13},{6,14},{7,15},{8,0},{9,1},... | collective-permute-start | bytes 92168 | tf_op jit(solution)/shard_map/ppermute | solution.py:21
  117.2 3.2 %copy-start = (f32[5,256,1024]{2,1,0:T(8,128)}, f32[5,256,1024]{2,1,0:T(8,128)S(1)}, u32[]{:S(2)}) copy-start(f32[5,256,1024]{2,1,0:T(8,128)S(1)} %broadcast_multiply_fusion.1) | copy-start | bytes 15728644
  120.4 14.3 %collective-permute-start.18 = (f32[648,1024]{1,0:T(8,128)}, f32[648,1024]{1,0:T(8,128)}, u32[]{:S(2)}, u32[]{:S(2)}) collective-permute-start(f32[648,1024]{1,0:T(8,128)} %maximum_maximum_fusion), channel_id=1, source_target_pairs={{0,16},{16,0},{32,48},{48,32},{64,80},{80,64},{96,112},{112,96},{1... | collective-permute-start | bytes 7962632 | tf_op jit(solution)/shard_map/ppermute | solution.py:71
  122.2 12.0 %collective-permute-start.22 = (f32[5,4,32,128]{3,2,0,1:T(8,128)S(1)}, f32[5,4,32,128]{3,2,0,1:T(8,128)S(1)}, u32[]{:S(2)}, u32[]{:S(2)}) collective-permute-start(f32[5,4,32,128]{3,2,0,1:T(8,128)S(1)} %bitcast.140), channel_id=1, source_target_pairs={{0,1},{1,2},{2,3},{3,0},{4,5},{5,6},{6,7},{7,4},{8,9},{9,10},{10,1... | collective-permute-start | bytes 983048 | tf_op jit(solution)/shard_map/ppermute | solution.py:112
  134.2 3.5 %copy-start.1 = (f32[5,256,1024]{2,1,0:T(8,128)S(1)}, f32[5,256,1024]{2,1,0:T(8,128)}, u32[]{:S(2)}) copy-start(f32[5,256,1024]{2,1,0:T(8,128)} %copy-done) | copy-start | bytes 15728644
  134.2 14.5 %collective-permute-start.23 = (f32[5,4,32,128]{3,2,0,1:T(8,128)S(1)}, f32[5,4,32,128]{3,2,0,1:T(8,128)S(1)}, u32[]{:S(2)}, u32[]{:S(2)}) collective-permute-start(f32[5,4,32,128]{3,2,0,1:T(8,128)S(1)} %bitcast_add_fusion.3), channel_id=1, source_target_pairs={{0,1},{1,2},{2,3},{3,0},{4,5},{5,6},{6,7},{7,4},{8,9},{9,10},{10,1... | collective-permute-start | bytes 983048 | tf_op jit(solution)/shard_map/ppermute | solution.py:112
  140.3 12.5 %collective-permute-start.19 = (f32[168,1024]{1,0:T(8,128)}, f32[168,1024]{1,0:T(8,128)}, u32[]{:S(2)}, u32[]{:S(2)}) collective-permute-start(f32[168,1024]{1,0:T(8,128)} %pad_maximum_fusion.3), channel_id=1, source_target_pairs={{0,32},{16,112},{32,64},{48,16},{64,96},{80,48},{96,0},{112,80},{1... | collective-permute-start | bytes 2064392 | tf_op jit(solution)/shard_map/ppermute | solution.py:85
  148.7 14.8 %collective-permute-start.24 = (f32[5,4,32,128]{3,2,0,1:T(8,128)S(1)}, f32[5,4,32,128]{3,2,0,1:T(8,128)S(1)}, u32[]{:S(2)}, u32[]{:S(2)}) collective-permute-start(f32[5,4,32,128]{3,2,0,1:T(8,128)S(1)} %bitcast_add_fusion.2), channel_id=1, source_target_pairs={{0,1},{1,2},{2,3},{3,0},{4,5},{5,6},{6,7},{7,4},{8,9},{9,10},{10,1... | collective-permute-start | bytes 983048 | tf_op jit(solution)/shard_map/ppermute | solution.py:112
  148.9 16.4 %collective-permute-start.10 = (f32[5]{0:T(128)S(1)}, f32[5]{0:T(128)S(1)}, u32[]{:S(2)}, u32[]{:S(2)}) collective-permute-start(f32[5]{0:T(128)S(1)} %get-tuple-element.7), channel_id=1, source_target_pairs={{0,1},{1,0},{2,3},{3,2},{4,5},{5,4},{6,7},{7,6},{8,9},{9,8},{10,11... | collective-permute-start | bytes 68 | tf_op jit(solution)/shard_map/ppermute | solution.py:32
  154.0 18.6 %collective-permute-start.20 = (f32[168,1024]{1,0:T(8,128)S(1)}, f32[168,1024]{1,0:T(8,128)S(1)}, u32[]{:S(2)}, u32[]{:S(2)}) collective-permute-start(f32[168,1024]{1,0:T(8,128)S(1)} %fusion.12), channel_id=1, source_target_pairs={{0,32},{16,112},{32,64},{48,16},{64,96},{80,48},{96,0},{112,80},{1... | collective-permute-start | bytes 2064392 | tf_op jit(solution)/shard_map/ppermute | solution.py:85
  163.5 8.9 %collective-permute-start.25 = (f32[5,32,128]{2,1,0:T(8,128)S(1)}, f32[5,32,128]{2,1,0:T(8,128)S(1)}, u32[]{:S(2)}, u32[]{:S(2)}) collective-permute-start(f32[5,32,128]{2,1,0:T(8,128)S(1)} %dynamic-slice_bitcast_fusion), channel_id=1, source_target_pairs={{0,4},{1,5},{2,6},{3,7},{4,8},{5,9},{6,10},{7,11},{8,12},{9,13},{1... | collective-permute-start | bytes 245768 | tf_op jit(solution)/shard_map/ppermute | solution.py:119
  165.3 7.7 %collective-permute-start.11 = (f32[5]{0:T(128)S(1)}, f32[5]{0:T(128)S(1)}, u32[]{:S(2)}, u32[]{:S(2)}) collective-permute-start(f32[5]{0:T(128)S(1)} %fusion.51), channel_id=1, source_target_pairs={{0,2},{1,3},{2,0},{3,1},{4,6},{5,7},{6,4},{7,5},{8,10},{9,11},{10,... | collective-permute-start | bytes 68 | tf_op jit(solution)/shard_map/ppermute | solution.py:32
  172.5 6.4 %collective-permute-start.26 = (f32[5,32,128]{2,1,0:T(8,128)S(1)}, f32[5,32,128]{2,1,0:T(8,128)S(1)}, u32[]{:S(2)}, u32[]{:S(2)}) collective-permute-start(f32[5,32,128]{2,1,0:T(8,128)S(1)} %bitcast_add_fusion.6), channel_id=1, source_target_pairs={{0,4},{1,5},{2,6},{3,7},{4,8},{5,9},{6,10},{7,11},{8,12},{9,13},{1... | collective-permute-start | bytes 245768 | tf_op jit(solution)/shard_map/ppermute | solution.py:119
  172.6 31.1 %copy-start.4 = (bf16[5,32,1024]{2,1,0:T(8,128)(2,1)S(1)}, bf16[5,32,1024]{2,1,0:T(8,128)(2,1)}, u32[]{:S(2)}) copy-start(bf16[5,32,1024]{2,1,0:T(8,128)(2,1)} %param.4) | copy-start | bytes 983044
  172.7 12.2 %collective-permute-start.21 = (f32[168,1024]{1,0:T(8,128)S(1)}, f32[168,1024]{1,0:T(8,128)S(1)}, u32[]{:S(2)}, u32[]{:S(2)}) collective-permute-start(f32[168,1024]{1,0:T(8,128)S(1)} %fusion.13), channel_id=1, source_target_pairs={{0,32},{16,112},{32,64},{48,16},{64,96},{80,48},{96,0},{112,80},{1... | collective-permute-start | bytes 2064392 | tf_op jit(solution)/shard_map/ppermute | solution.py:85
  173.0 5.9 %collective-permute-start.12 = (f32[5]{0:T(128)S(1)}, f32[5]{0:T(128)S(1)}, u32[]{:S(2)}, u32[]{:S(2)}) collective-permute-start(f32[5]{0:T(128)S(1)} %fusion.50), channel_id=1, source_target_pairs={{0,4},{1,5},{2,6},{3,7},{4,0},{5,1},{6,2},{7,3},{8,12},{9,13},{10,... | collective-permute-start | bytes 68 | tf_op jit(solution)/shard_map/ppermute | solution.py:32
  178.8 5.7 %collective-permute-start.27 = (f32[5,32,128]{2,1,0:T(8,128)S(1)}, f32[5,32,128]{2,1,0:T(8,128)S(1)}, u32[]{:S(2)}, u32[]{:S(2)}) collective-permute-start(f32[5,32,128]{2,1,0:T(8,128)S(1)} %bitcast_add_fusion.5), channel_id=1, source_target_pairs={{0,4},{1,5},{2,6},{3,7},{4,8},{5,9},{6,10},{7,11},{8,12},{9,13},{1... | collective-permute-start | bytes 245768 | tf_op jit(solution)/shard_map/ppermute | solution.py:119
  178.9 6.3 %collective-permute-start.13 = (f32[5]{0:T(128)S(1)}, f32[5]{0:T(128)S(1)}, u32[]{:S(2)}, u32[]{:S(2)}) collective-permute-start(f32[5]{0:T(128)S(1)} %fusion.49), channel_id=1, source_target_pairs={{0,8},{1,9},{2,10},{3,11},{4,12},{5,13},{6,14},{7,15},{8,0},{9,1},... | collective-permute-start | bytes 68 | tf_op jit(solution)/shard_map/ppermute | solution.py:32
Sparse Core Ops, SparseCore 0:
  10.2 58.9 all-gather.1
  113.0 90.6 reduce-scatter.1
